TPU v7x, 32 devices: a whole 2x2x4 slice. The times are simulated.
32 devices in a mesh: groups: 2 (over x), seq: 16 (over z, y, core).
Axes of the slice: x: 2, y: 2, z: 4, core: 2. Of those that a mesh axis runs over, the one named last changes fastest.
Arguments:
- query: bfloat16 [4096, 2048], P(('groups', 'seq')), parts along dimension 0, may hold values from -8 to 8
- keys: bfloat16 [4096, 2048], P(('groups', 'seq')), parts along dimension 0, may hold values from -8 to 8
- values: bfloat16 [4096, 2048], P(('groups', 'seq')), parts along dimension 0, may hold values from -6 to 6
- grad_out: bfloat16 [4096, 2048], P(('groups', 'seq')), parts along dimension 0, may hold values from -6 to 6
- global_blocks: int32 [4], P('groups'), parts along dimension 0, may hold values from 0 to 15
- random_blocks: int32 [32, 3], P('groups'), parts along dimension 0, may hold values from 0 to 15
Outputs:
- attended: bfloat16 [4096, 2048], P(('groups', 'seq')), parts along dimension 0
- grad_query: bfloat16 [4096, 2048], P(('groups', 'seq')), parts along dimension 0
- grad_keys: bfloat16 [4096, 2048], P(('groups', 'seq')), parts along dimension 0
- grad_values: bfloat16 [4096, 2048], P(('groups', 'seq')), parts along dimension 0
There are 2 independent parts, one for each index of `groups`. A program takes and returns all parts, laid end to end along the dimension named above; each array names one. Nothing has to cross between parts.
All inputs are finite; a program needn't handle non-finite values.
Results may differ from a plain program's by a relative error of at most 0.022.
Values may be sent and summed in bfloat16 or wider, within the bound.
No kernel may reach another device: no remote copies, remote signals or barrier semaphores. Data moves between devices by JAX's collectives and lax.ppermute only.
A program may use at most 192 MiB of HBM per device.

v0:
```python
import jax
import jax.numpy as jnp
from jax import lax
from jax.sharding import PartitionSpec as P

HD = 128
BLK = 128
G = 2


def attend_block(operands):
    query_blk, grad_blk, key_tiles, value_tiles = operands
    row_count, width = query_blk.shape
    keys_total = key_tiles.shape[0]
    head_size = HD
    head_count = width // head_size
    scaling = HD ** (-0.5)
    last_dims = (((1,), (1,)), ((), ()))
    first_dims = (((0,), (0,)), ((), ()))

    def one_head(head, carry):
        out_attended, out_gquery, out_gkeys, out_gvalues = carry
        start = head * head_size
        query_head = lax.dynamic_slice_in_dim(query_blk, start, head_size, 1)
        grad_head = lax.dynamic_slice_in_dim(grad_blk, start, head_size, 1)
        key_head = lax.dynamic_slice_in_dim(key_tiles, start, head_size, 1)
        value_head = lax.dynamic_slice_in_dim(value_tiles, start, head_size, 1)
        scores = (
            lax.dot_general(query_head, key_head, last_dims, preferred_element_type=jnp.float32)
            * scaling
        )
        probability = jax.nn.softmax(scores, axis=-1)
        weights = probability.astype(jnp.bfloat16)
        attended_head = jnp.dot(weights, value_head, preferred_element_type=jnp.float32).astype(
            jnp.bfloat16
        )
        deltas = jnp.sum(grad_head.astype(jnp.float32) * attended_head.astype(jnp.float32), axis=-1)
        grad_prob = lax.dot_general(
            grad_head, value_head, last_dims, preferred_element_type=jnp.float32
        )
        grad_score = (probability * (grad_prob - deltas[:, None])).astype(jnp.bfloat16)
        gquery_head = (
            jnp.dot(grad_score, key_head, preferred_element_type=jnp.float32) * scaling
        ).astype(jnp.bfloat16)
        gkeys_head = (
            lax.dot_general(grad_score, query_head, first_dims, preferred_element_type=jnp.float32)
            * scaling
        )
        gvalues_head = lax.dot_general(
            weights, grad_head, first_dims, preferred_element_type=jnp.float32
        )
        out_attended = lax.dynamic_update_slice_in_dim(out_attended, attended_head, start, 1)
        out_gquery = lax.dynamic_update_slice_in_dim(out_gquery, gquery_head, start, 1)
        out_gkeys = lax.dynamic_update_slice_in_dim(out_gkeys, gkeys_head, start, 1)
        out_gvalues = lax.dynamic_update_slice_in_dim(out_gvalues, gvalues_head, start, 1)
        return (out_attended, out_gquery, out_gkeys, out_gvalues)

    initial = (
        jnp.zeros((row_count, width), jnp.bfloat16),
        jnp.zeros((row_count, width), jnp.bfloat16),
        jnp.zeros((keys_total, width), jnp.float32),
        jnp.zeros((keys_total, width), jnp.float32),
    )
    return lax.fori_loop(0, head_count, one_head, initial)


def fetch_table(device_ids, block_count, total_blocks, global_blocks, random_blocks):
    owned_blocks = (
        device_ids[:, None] * block_count + jnp.arange(block_count, dtype=jnp.int32)[None, :]
    )
    pieces = []
    pieces.append(((owned_blocks - 1) % total_blocks)[:, :, None])
    pieces.append(((owned_blocks + 1) % total_blocks)[:, :, None])
    pieces.append(
        jnp.broadcast_to(
            global_blocks[None, None, :], owned_blocks.shape + (global_blocks.shape[0],)
        )
    )
    pieces.append(random_blocks[owned_blocks])
    return jnp.concatenate(pieces, axis=2).reshape(device_ids.shape[0], -1)


def shards(query, keys, values, grad_out, global_blocks, random_blocks):
    devices = lax.axis_size("seq")
    tok_rows, width = query.shape
    per_device = tok_rows // BLK
    total_blocks = per_device * devices
    row_share = BLK // devices
    key_blocks = keys.reshape(per_device, BLK, width)
    value_blocks = values.reshape(per_device, BLK, width)
    row_keys, row_values = (
        lax.all_to_all(
            keys.reshape(per_device, devices, row_share, width),
            "seq",
            split_axis=1,
            concat_axis=0,
            tiled=True,
        ),
        lax.all_to_all(
            values.reshape(per_device, devices, row_share, width),
            "seq",
            split_axis=1,
            concat_axis=0,
            tiled=True,
        ),
    )
    row_keys = row_keys.reshape(total_blocks, row_share, width)
    row_values = row_values.reshape(total_blocks, row_share, width)
    fetch_lists = fetch_table(
        jnp.arange(devices, dtype=jnp.int32), per_device, total_blocks, global_blocks, random_blocks
    )
    fetched = fetch_lists.shape[1]
    got_keys, got_values = (
        lax.all_to_all(row_keys[fetch_lists], "seq", split_axis=0, concat_axis=2, tiled=True),
        lax.all_to_all(row_values[fetch_lists], "seq", split_axis=0, concat_axis=2, tiled=True),
    )
    offset = 0
    window_keys = got_keys[:, 0:2]
    window_values = got_values[:, 0:2]
    offset = 2
    global_keys = got_keys[:, offset : offset + G]
    global_values = got_values[:, offset : offset + G]
    offset = offset + G
    random_keys = got_keys[:, offset:]
    random_values = got_values[:, offset:]
    tile_keys = jnp.concatenate(
        [key_blocks[:, None], window_keys, global_keys, random_keys], axis=1
    ).reshape(per_device, -1, width)
    tile_values = jnp.concatenate(
        [value_blocks[:, None], window_values, global_values, random_values], axis=1
    ).reshape(per_device, -1, width)
    attended, grad_query, tile_gkeys, tile_gvalues = lax.map(
        attend_block,
        (
            query.reshape(per_device, BLK, width),
            grad_out.reshape(per_device, BLK, width),
            tile_keys,
            tile_values,
        ),
    )
    tile_gkeys = tile_gkeys.reshape(per_device, -1, BLK, width)
    tile_gvalues = tile_gvalues.reshape(per_device, -1, BLK, width)
    window_gkeys = tile_gkeys[:, 1:3]
    window_gvalues = tile_gvalues[:, 1:3]
    global_gkeys = tile_gkeys[:, 3 : 3 + G]
    global_gvalues = tile_gvalues[:, 3 : 3 + G]
    back_keys = []
    back_values = []
    back_keys.append(window_gkeys)
    back_values.append(window_gvalues)
    back_keys.append(global_gkeys)
    back_values.append(global_gvalues)
    back_keys.append(tile_gkeys[:, 3 + G :])
    back_values.append(tile_gvalues[:, 3 + G :])
    back_keys = jnp.concatenate(back_keys, axis=1).reshape(1, fetched, devices, row_share, width)
    back_values = jnp.concatenate(back_values, axis=1).reshape(
        1, fetched, devices, row_share, width
    )
    recv_keys, recv_values = (
        lax.all_to_all(back_keys, "seq", split_axis=2, concat_axis=0, tiled=True),
        lax.all_to_all(back_values, "seq", split_axis=2, concat_axis=0, tiled=True),
    )
    flat_index = fetch_lists.reshape(-1)
    table_keys = (
        jnp.zeros((total_blocks, row_share, width), jnp.float32)
        .at[flat_index]
        .add(recv_keys.reshape(devices * fetched, row_share, width))
    )
    table_values = (
        jnp.zeros((total_blocks, row_share, width), jnp.float32)
        .at[flat_index]
        .add(recv_values.reshape(devices * fetched, row_share, width))
    )
    home_keys, home_values = (
        lax.all_to_all(
            table_keys.reshape(total_blocks, 1, row_share, width),
            "seq",
            split_axis=0,
            concat_axis=1,
            tiled=True,
        ),
        lax.all_to_all(
            table_values.reshape(total_blocks, 1, row_share, width),
            "seq",
            split_axis=0,
            concat_axis=1,
            tiled=True,
        ),
    )
    grad_key_blocks = tile_gkeys[:, 0] + home_keys.reshape(per_device, BLK, width)
    grad_value_blocks = tile_gvalues[:, 0] + home_values.reshape(per_device, BLK, width)
    return (
        attended.reshape(tok_rows, width),
        grad_query.reshape(tok_rows, width),
        grad_key_blocks.astype(jnp.bfloat16).reshape(tok_rows, width),
        grad_value_blocks.astype(jnp.bfloat16).reshape(tok_rows, width),
    )


def solution(mesh):
    placed = (
        P(("groups", "seq"), None),
        P(("groups", "seq"), None),
        P(("groups", "seq"), None),
        P(("groups", "seq"), None),
        P("groups"),
        P("groups", None),
    )
    return jax.shard_map(
        shards,
        mesh=mesh,
        in_specs=placed,
        out_specs=(
            P(("groups", "seq"), None),
            P(("groups", "seq"), None),
            P(("groups", "seq"), None),
            P(("groups", "seq"), None),
        ),
        check_vma=False,
    )
```

profile of v0, /device:TPU:10, one launch (start us, length us, event | category | flops | bytes accessed | tf_op | source)
XLA Modules:
  0.0 785.2 jit_solution(14915719466594909279)
XLA Ops:
  0.6 19.8 %all_to_all.102 = bf16[1,16,8,2048]{3,2,0,1:T(8,128)(2,1)S(1)} all-to-all(bf16[1,16,8,2048]{3,2,0,1:T(8,128)(2,1)} %bitcast.86), channel_id=1, replica_groups=mesh['groups'=2,'seq'=16] {'seq'}, dimensions={1} | all-to-all | bytes 1048576 | tf_op jit(solution)/shard_map/all_to_all | solution.py:99
  20.4 5.0 all-to-all-start
  27.8 2.7 gather_fusion.2
  30.5 8.3 %all-to-all-done = bf16[1,16,8,2048]{3,2,0,1:T(8,128)(2,1)S(1)} async-done(((bf16[1,16,8,2048]{3,2,0,1:T(8,128)(2,1)}), bf16[1,16,8,2048]{3,2,0,1:T(8,128)(2,1)S(1)}, u32[]{:S(2)}, u32[]{:S(2)}) %all-to-all-start) | async-done | bytes 524320 | tf_op jit(solution)/shard_map/all_to_all | solution.py:92
  38.9 5.1 all-to-all-start.3
  46.7 76.9 %all-to-all-done.3 = bf16[16,7,8,2048]{3,2,1,0:T(8,128)(2,1)} async-done(((bf16[16,7,8,2048]{3,2,1,0:T(8,128)(2,1)}), bf16[16,7,8,2048]{3,2,1,0:T(8,128)(2,1)}, u32[]{:S(2)}, u32[]{:S(2)}) %all-to-all-start.3) | async-done | bytes 3670048 | tf_op jit(solution)/shard_map/all_to_all | solution.py:115
  123.6 6.6 all-to-all-start.1
  135.0 74.7 %all-to-all-done.1 = bf16[16,7,8,2048]{3,2,1,0:T(8,128)(2,1)} async-done(((bf16[16,7,8,2048]{3,2,1,0:T(8,128)(2,1)}), bf16[16,7,8,2048]{3,2,1,0:T(8,128)(2,1)}, u32[]{:S(2)}, u32[]{:S(2)}) %all-to-all-start.1) | async-done | bytes 3670048 | tf_op jit(solution)/shard_map/all_to_all | solution.py:114
  214.6 4.3 broadcast.203
  218.9 4.3 broadcast.203.clone
  223.2 161.8 %while.32 = (s32[]{:T(128)}, bf16[128,2048]{1,0:T(8,128)(2,1)S(1)}, bf16[128,2048]{1,0:T(8,128)(2,1)S(1)}, f32[1024,2048]{1,0:T(8,128)}, f32[1024,2048]{1,0:T(8,...) while((s32[]{:T(128)}, bf16[128,2048]{1,0:T(8,128)(2,1)S(1)}, ...), condition=%wide.region_4.5_spmd, body=%wide.region_0.4_spmd.sunk | while | flops 203538048 | bytes 6007479 | solution.py:64
  385.1 4.4 slice_bitcast_fusion
  389.5 3.9 copy.49
  393.4 6.5 all-to-all-start.6
  399.9 4.0 slice_bitcast_fusion.1
  403.9 4.0 copy.48
  407.9 150.2 %all-to-all-done.6 = f32[1,7,16,8,2048]{4,3,1,0,2:T(8,128)} async-done(((f32[1,7,16,8,2048]{4,3,1,0,2:T(8,128)}), f32[1,7,16,8,2048]{4,3,1,0,2:T(8,128)}, u32[]{:S(2)}, u32[]{:S(2)}) %all-to-all-start.6) | async-done | bytes 7340064 | tf_op jit(solution)/shard_map/all_to_all | solution.py:161
  558.1 6.5 all-to-all-start.4
  565.8 22.6 %scatter_fusion.1 = f32[16,8,2048]{2,1,0:T(8,128)} fusion(f32[16,8,2048]{2,1,0:T(8,128)} %broadcast.209.clone.1, s32[112]{0:T(128)S(1)} %fusion.28, f32[112,8,2048]{2,1,0:T(8,128)} %bitcast.31), kind=kCustom, calls=%fused_computation.4 | custom fusion | flops 1835008 | bytes 22020544 | tf_op jit(solution)/shard_map/scatter-add | solution.py:172
  588.4 134.3 %all-to-all-done.4 = f32[1,7,16,8,2048]{4,3,1,0,2:T(8,128)} async-done(((f32[1,7,16,8,2048]{4,3,1,0,2:T(8,128)}), f32[1,7,16,8,2048]{4,3,1,0,2:T(8,128)}, u32[]{:S(2)}, u32[]{:S(2)}) %all-to-all-start.4) | async-done | bytes 7340064 | tf_op jit(solution)/shard_map/all_to_all | solution.py:160
  722.7 6.5 all-to-all-start.7
  730.3 22.7 %scatter_fusion = f32[16,8,2048]{2,1,0:T(8,128)} fusion(f32[16,8,2048]{2,1,0:T(8,128)} %broadcast.209.clone, s32[112]{0:T(128)S(1)} %fusion.28, f32[112,8,2048]{2,1,0:T(8,128)} %bitcast.23), kind=kCustom, calls=%fused_computation.3 | custom fusion | flops 1835008 | bytes 22020544 | tf_op jit(solution)/shard_map/scatter-add | solution.py:167
  753.2 5.7 all-to-all-start.5
  761.1 21.9 %all-to-all-done.5 = f32[16,1,8,2048]{3,2,1,0:T(8,128)S(1)} async-done(((f32[16,1,8,2048]{3,2,1,0:T(8,128)}), f32[16,1,8,2048]{3,2,1,0:T(8,128)S(1)}, u32[]{:S(2)}, u32[]{:S(2)}) %all-to-all-start.5) | async-done | bytes 1048608 | tf_op jit(solution)/shard_map/all_to_all | solution.py:175
  (211 shorter events, 182.7 us)
Async XLA Ops:
  20.4 18.4 %all-to-all-start = ((bf16[1,16,8,2048]{3,2,0,1:T(8,128)(2,1)}), bf16[1,16,8,2048]{3,2,0,1:T(8,128)(2,1)S(1)}, u32[]{:S(2)}, u32[]{:S(2)}) async-start(bf16[1,16,8,2048]{3,2,0,1:T(8,128)(2,1)} %bitcast.88), calls=%async_computation | async-start | bytes 1048576 | tf_op jit(solution)/shard_map/all_to_all | solution.py:92
  38.9 84.7 %all-to-all-start.3 = ((bf16[16,7,8,2048]{3,2,1,0:T(8,128)(2,1)}), bf16[16,7,8,2048]{3,2,1,0:T(8,128)(2,1)}, u32[]{:S(2)}, u32[]{:S(2)}) async-start(bf16[16,7,8,2048]{3,2,1,0:T(8,128)(2,1)} %bitcast.81), calls=%async_computation.3 | async-start | bytes 7340032 | tf_op jit(solution)/shard_map/all_to_all | solution.py:115
  123.6 9.1 %copy-start = (bf16[128,2048]{1,0:T(8,128)(2,1)S(1)}, bf16[128,2048]{1,0:T(8,128)(2,1)}, u32[]{:S(2)}) copy-start(bf16[128,2048]{1,0:T(8,128)(2,1)} %param.10) | copy-start | bytes 1572868
  123.6 86.1 %all-to-all-start.1 = ((bf16[16,7,8,2048]{3,2,1,0:T(8,128)(2,1)}), bf16[16,7,8,2048]{3,2,1,0:T(8,128)(2,1)}, u32[]{:S(2)}, u32[]{:S(2)}) async-start(bf16[16,7,8,2048]{3,2,1,0:T(8,128)(2,1)} %bitcast.80), calls=%async_computation.1 | async-start | bytes 7340032 | tf_op jit(solution)/shard_map/all_to_all | solution.py:114
  132.7 79.5 %copy-start.1 = (bf16[128,2048]{1,0:T(8,128)(2,1)S(1)}, bf16[128,2048]{1,0:T(8,128)(2,1)}, u32[]{:S(2)}) copy-start(bf16[128,2048]{1,0:T(8,128)(2,1)} %param.9) | copy-start | bytes 1572868
  385.1 4.4 copy-start.2
  385.1 4.4 copy-start.3
  393.4 164.7 %all-to-all-start.6 = ((f32[1,7,16,8,2048]{4,3,1,0,2:T(8,128)}), f32[1,7,16,8,2048]{4,3,1,0,2:T(8,128)}, u32[]{:S(2)}, u32[]{:S(2)}) async-start(f32[1,7,16,8,2048]{4,3,1,0,2:T(8,128)} %copy.49), calls=%async_computation.6 | async-start | bytes 14680064 | tf_op jit(solution)/shard_map/all_to_all | solution.py:161
  558.1 164.7 %all-to-all-start.4 = ((f32[1,7,16,8,2048]{4,3,1,0,2:T(8,128)}), f32[1,7,16,8,2048]{4,3,1,0,2:T(8,128)}, u32[]{:S(2)}, u32[]{:S(2)}) async-start(f32[1,7,16,8,2048]{4,3,1,0,2:T(8,128)} %copy.48), calls=%async_computation.4 | async-start | bytes 14680064 | tf_op jit(solution)/shard_map/all_to_all | solution.py:160
  722.7 30.5 %all-to-all-start.7 = ((f32[16,1,8,2048]{3,2,1,0:T(8,128)}), f32[16,1,8,2048]{3,2,1,0:T(8,128)S(1)}, u32[]{:S(2)}, u32[]{:S(2)}) async-start(f32[16,1,8,2048]{3,2,1,0:T(8,128)} %bitcast.33), calls=%async_computation.7 | async-start | bytes 2097152 | tf_op jit(solution)/shard_map/all_to_all | solution.py:182
  753.2 29.8 %all-to-all-start.5 = ((f32[16,1,8,2048]{3,2,1,0:T(8,128)}), f32[16,1,8,2048]{3,2,1,0:T(8,128)S(1)}, u32[]{:S(2)}, u32[]{:S(2)}) async-start(f32[16,1,8,2048]{3,2,1,0:T(8,128)} %bitcast.24), calls=%async_computation.5 | async-start | bytes 2097152 | tf_op jit(solution)/shard_map/all_to_all | solution.py:175
where the time goes:
time: 793 us; the launch traced here: 785 us
  waiting for transfers between devices  467 us (59%)
  matrix products  141 us (18%)
  other arithmetic  58.1 us (7%)
  local copies, waits for them, and re-layouts  56 us (7%)
  starting transfers between devices  41.8 us (5%)
  blocking collectives  19.8 us (2%)
    all_to_all x1, waiting for transfers between devices, shards(): lax.all_to_all(back_values, 'seq', split_axis=2, concat_axis=0, tiled=True)  150 us
    all_to_all x1, waiting for transfers between devices, shards(): lax.all_to_all(back_keys, 'seq', split_axis=2, concat_axis=0, tiled=True)  134 us
    all_to_all x1, waiting for transfers between devices, shards(): lax.all_to_all(row_values[fetch_lists], 'seq', split_axis=0, concat_axis=...  76.9 us
    all_to_all x1, waiting for transfers between devices, shards(): lax.all_to_all(row_keys[fetch_lists], 'seq', split_axis=0, concat_axis=2,...  74.7 us
    dot_general x16, matrix products, one_head(): lax.dot_general(weights, grad_head, first_dims, preferred_element_type=jn...  31.3 us
    dot_general x16, matrix products, one_head(): lax.dot_general(grad_score, query_head, first_dims, preferred_element_typ...  30.1 us
    scatter-add x1, other arithmetic, shards(): table_keys = jnp.zeros((total_blocks, row_share, width), jnp.float32).at[...  22.7 us
    scatter-add x1, other arithmetic, shards(): table_values = jnp.zeros((total_blocks, row_share, width), jnp.float32).a...  22.6 us
  transfers between devices with their start and end apart: 7, of which 7 were waited for; matrix products, arithmetic and copies ran while one was open for 9% of the time, Pallas kernels for 0%

commit v1 on v0

--- a/solution.py
+++ b/solution.py
@@ -1,6 +1,8 @@
 import jax
 import jax.numpy as jnp
 from jax import lax
+from jax.experimental import pallas as pl
+from jax.experimental.pallas import tpu as pltpu
 from jax.sharding import PartitionSpec as P
 
 HD = 128
@@ -80,7 +82,7 @@
     return jnp.concatenate(pieces, axis=2).reshape(device_ids.shape[0], -1)
 
 
-def shards(query, keys, values, grad_out, global_blocks, random_blocks):
+def shards_exchange(query, keys, values, grad_out, global_blocks, random_blocks):
     devices = lax.axis_size("seq")
     tok_rows, width = query.shape
     per_device = tok_rows // BLK
@@ -196,6 +198,144 @@
         grad_value_blocks.astype(jnp.bfloat16).reshape(tok_rows, width),
     )
 
+SLOTS = 3 + G + 3
+
+
+def _send(v, pairs):
+    return lax.ppermute(v.astype(jnp.bfloat16), "seq", pairs).astype(v.dtype)
+
+
+def gather_blocks(x, n):
+    line_len = n // 4
+    z = lax.axis_index("seq") // 4
+    ups, downs = [], []
+    up, down = x, x
+    for k in range(1, line_len):
+        up = _send(
+            up, [(4 * z0 + r, 4 * (z0 + 1) + r) for z0 in range(k - 1, line_len - 1) for r in range(4)]
+        )
+        down = _send(
+            down, [(4 * z0 + r, 4 * (z0 - 1) + r) for z0 in range(1, line_len - k + 1) for r in range(4)]
+        )
+        ups.append(up)
+        downs.append(down)
+    rel = jnp.stack(ups[::-1] + [x] + downs)
+    line = lax.dynamic_slice_in_dim(rel, line_len - 1 - z, line_len, axis=0)
+    other = _send(line, [(i, i ^ 2) for i in range(n)])
+    pair = jnp.stack([line, other])
+    sibling = _send(pair, [(i, i ^ 1) for i in range(n)])
+    return jnp.stack([pair, sibling])
+
+
+def _attend_kernel(pos_ref, q_ref, g_ref, *refs):
+    k_refs = refs[:SLOTS]
+    v_refs = refs[SLOTS : 2 * SLOTS]
+    att_ref, gq_ref, dk_ref, dv_ref = refs[2 * SLOTS :]
+    scale = HD ** (-0.5)
+    nt = (((1,), (1,)), ((), ()))
+    q = q_ref[...]
+    g = g_ref[...]
+    k_all = jnp.concatenate([r[...] for r in k_refs], axis=0)
+    v_all = jnp.concatenate([r[...] for r in v_refs], axis=0)
+    s = lax.dot_general(q, k_all, nt, preferred_element_type=jnp.float32) * scale
+    e = jnp.exp(s - jnp.max(s, axis=-1, keepdims=True))
+    p = e / jnp.sum(e, axis=-1, keepdims=True)
+    w = p.astype(jnp.bfloat16)
+    att = jnp.dot(w, v_all, preferred_element_type=jnp.float32).astype(jnp.bfloat16)
+    att_ref[...] = att
+    delta = jnp.sum(g.astype(jnp.float32) * att.astype(jnp.float32), axis=-1, keepdims=True)
+    gp = lax.dot_general(g, v_all, nt, preferred_element_type=jnp.float32)
+    gs32 = p * (gp - delta)
+    gs = gs32.astype(jnp.bfloat16)
+    gq_ref[...] = (jnp.dot(gs, k_all, preferred_element_type=jnp.float32) * scale).astype(
+        jnp.bfloat16
+    )
+    gk = jnp.dot(gs32.T.astype(jnp.bfloat16), q, preferred_element_type=jnp.float32) * scale
+    gv = jnp.dot(p.T.astype(jnp.bfloat16), g, preferred_element_type=jnp.float32)
+    dk_ref[...] = jnp.zeros(dk_ref.shape, jnp.float32)
+    dv_ref[...] = jnp.zeros(dv_ref.shape, jnp.float32)
+    rows = q.shape[0]
+    for j in range(SLOTS):
+        at = pos_ref[j]
+        dk_ref[at] = dk_ref[at] + gk[j * rows : (j + 1) * rows]
+        dv_ref[at] = dv_ref[at] + gv[j * rows : (j + 1) * rows]
+
+
+def attend_local(pos, query, grad_out, keys_local, values_local):
+    rows, width = query.shape
+    held = keys_local.shape[0]
+    heads = width // HD
+    head_spec = pl.BlockSpec((rows, HD), lambda h, pos: (0, h))
+    slot_specs = [
+        pl.BlockSpec((None, rows, HD), lambda h, pos, j=j: (pos[j], 0, h)) for j in range(SLOTS)
+    ]
+    part_spec = pl.BlockSpec((held, rows, HD), lambda h, pos: (0, 0, h))
+    flops = 12 * rows * SLOTS * rows * HD * heads
+    moved = 2 * SLOTS * rows * width * 2 + 4 * rows * width * 2 + 2 * held * rows * width * 4
+    call = pl.pallas_call(
+        _attend_kernel,
+        out_shape=(
+            jax.ShapeDtypeStruct((rows, width), jnp.bfloat16),
+            jax.ShapeDtypeStruct((rows, width), jnp.bfloat16),
+            jax.ShapeDtypeStruct((held, rows, width), jnp.float32),
+            jax.ShapeDtypeStruct((held, rows, width), jnp.float32),
+        ),
+        grid_spec=pltpu.PrefetchScalarGridSpec(
+            num_scalar_prefetch=1,
+            grid=(heads,),
+            in_specs=[head_spec, head_spec] + slot_specs + slot_specs,
+            out_specs=(head_spec, head_spec, part_spec, part_spec),
+        ),
+        compiler_params=pltpu.CompilerParams(dimension_semantics=("arbitrary",)),
+        cost_estimate=pl.CostEstimate(
+            flops=flops, transcendentals=rows * SLOTS * rows * heads, bytes_accessed=moved
+        ),
+    )
+    return call(
+        pos, query, grad_out, *([keys_local] * SLOTS), *([values_local] * SLOTS)
+    )
+
+
+def shards_gather(query, keys, values, grad_out, global_blocks, random_blocks):
+    n = lax.axis_size("seq")
+    rows, width = query.shape
+    line_len = n // 4
+    idx = lax.axis_index("seq")
+    listed = jnp.concatenate(
+        [
+            jnp.stack([idx, (idx - 1) % n, (idx + 1) % n]).astype(jnp.int32),
+            global_blocks.astype(jnp.int32),
+            random_blocks[idx].astype(jnp.int32),
+        ]
+    )
+    listed = jnp.clip(listed, 0, n - 1)
+    core = idx % 2
+    ypos = (idx // 2) % 2
+    pos = (((listed % 2) ^ core) * 2 + (((listed // 2) % 2) ^ ypos)) * line_len + listed // 4
+    keys_local = gather_blocks(keys, n).reshape(n, rows, width)
+    values_local = gather_blocks(values, n).reshape(n, rows, width)
+    attended, grad_query, part_keys, part_values = attend_local(
+        pos, query, grad_out, keys_local, values_local
+    )
+    scatter = jax.linear_transpose(
+        lambda t: gather_blocks(t, n), jax.ShapeDtypeStruct((rows, width), jnp.float32)
+    )
+    (grad_keys,) = scatter(part_keys.reshape(2, 2, line_len, rows, width))
+    (grad_values,) = scatter(part_values.reshape(2, 2, line_len, rows, width))
+    return (
+        attended,
+        grad_query,
+        grad_keys.astype(jnp.bfloat16),
+        grad_values.astype(jnp.bfloat16),
+    )
+
+
+def shards(query, keys, values, grad_out, global_blocks, random_blocks):
+    n = lax.axis_size("seq")
+    if query.shape[0] == BLK and n % 4 == 0 and n <= 32:
+        return shards_gather(query, keys, values, grad_out, global_blocks, random_blocks)
+    return shards_exchange(query, keys, values, grad_out, global_blocks, random_blocks)
+
 
 def solution(mesh):
     placed = (

time: 793 us -> 412 us (0.52)
  waiting for transfers between devices: 467 us -> 233 us
  matrix products: 141 us -> 0 us
  Pallas kernels: 0 us -> 26.9 us
  starting transfers between devices: 41.8 us -> 65.9 us
  local copies, waits for them, and re-layouts: 56 us -> 35.3 us
  blocking collectives: 19.8 us -> 0 us
  other arithmetic: 58.1 us -> 45.4 us
    all_to_all x7 -> x0, waiting for transfers between devices: 467 us -> none  [the longest x1 150 us: shards(): lax.all_to_all(back_values, 'seq', split_axis=2, concat_axis=0, tiled=True)]
    ppermute x0 -> x32, waiting for transfers between devices: none -> 233 us  [_send(): return lax.ppermute(v.astype(jnp.bfloat16), 'seq', pairs).astype(v.dtype)]
    dot_general x96 -> x0, matrix products: 141 us -> none  [the longest x16 31.3 us: one_head(): lax.dot_general(weights, grad_head, first_dims, preferred_element_type=jn...]
    ppermute x0 -> x32, starting transfers between devices: none -> 65.9 us  [_send(): return lax.ppermute(v.astype(jnp.bfloat16), 'seq', pairs).astype(v.dtype)]
    scatter-add x2 -> x0, other arithmetic: 45.3 us -> none  [the longest x1 22.7 us: shards(): table_keys = jnp.zeros((total_blocks, row_share, width), jnp.float32).at[...]
    all_to_all x7 -> x0, starting transfers between devices: 41.8 us -> none  [the longest x1 6.59 us: shards(): lax.all_to_all(row_keys[fetch_lists], 'seq', split_axis=0, concat_axis=2,...]
    pallas_call x0 -> x1, Pallas kernels: none -> 26.9 us  [attend_local(): call(pos, query, grad_out, *[keys_local] * SLOTS, *[values_local] * SLOTS)]
    another operation x0 -> x6, other arithmetic: none -> 22 us  [the longest x4 20.9 us: gather_blocks(): return jnp.stack([pair, sibling])]
  transfers between devices with their start and end apart: 7 -> 32, of which waited for: 7 -> 18; matrix products, arithmetic and copies ran while one was open for 9% -> 16% of each run, Pallas kernels for 0% -> 0%
where the time goes in v1:
time: 412 us; the launch traced here: 408 us
  waiting for transfers between devices  233 us (57%)
  starting transfers between devices  65.9 us (16%)
  other arithmetic  45.4 us (11%)
  local copies, waits for them, and re-layouts  35.3 us (9%)
  Pallas kernels  26.9 us (7%)
    ppermute x32, waiting for transfers between devices, _send(): return lax.ppermute(v.astype(jnp.bfloat16), 'seq', pairs).astype(v.dtype)  233 us
    ppermute x32, starting transfers between devices, _send(): return lax.ppermute(v.astype(jnp.bfloat16), 'seq', pairs).astype(v.dtype)  65.9 us
    pallas_call x1, Pallas kernels, attend_local(): call(pos, query, grad_out, *[keys_local] * SLOTS, *[values_local] * SLOTS)  26.9 us
    another operation x4, local copies, waits for them, and re-layouts, gather_blocks(): return jnp.stack([pair, sibling])  21 us
    another operation x4, other arithmetic, gather_blocks(): return jnp.stack([pair, sibling])  20.9 us
    add_any x2, other arithmetic, _send(): return lax.ppermute(v.astype(jnp.bfloat16), 'seq', pairs).astype(v.dtype)  14.7 us
  transfers between devices with their start and end apart: 32, of which 18 were waited for; matrix products, arithmetic and copies ran while one was open for 16% of the time, Pallas kernels for 0%

profile of v1, /device:TPU:10, one launch (start us, length us, event | category | flops | bytes accessed | tf_op | source)
XLA Modules:
  0.0 408.2 jit_solution(6655924015461079125)
XLA Ops:
  12.4 5.1 %collective-permute-done.8 = bf16[128,2048]{1,0:T(8,128)(2,1)S(1)} collective-permute-done((bf16[128,2048]{1,0:T(8,128)(2,1)}, bf16[128,2048]{1,0:T(8,128)(2,1)S(1)}, u32[]{:S(2)}, u32[]{:S(2)}) %collective-permute-start.8) | collective-permute-done | bytes 524320 | tf_op jit(solution)/shard_map/ppermute | solution.py:205
  17.5 4.3 %collective-permute-start.9 = (bf16[128,2048]{1,0:T(8,128)(2,1)S(1)}, bf16[128,2048]{1,0:T(8,128)(2,1)}, u32[]{:S(2)}, u32[]{:S(2)}) collective-permute-start(bf16[128,2048]{1,0:T(8,128)(2,1)S(1)} %collective-permute-done.8), channel_id=1, source_target_pairs={{4,8},{5,9},{6,10},{7,11},{8,12},{9,13},{10,14},{11,15},{20,24},{2... | collective-permute-start | bytes 1572872 | tf_op jit(solution)/shard_map/ppermute | solution.py:205
  28.0 4.3 %collective-permute-start.1 = (bf16[128,2048]{1,0:T(8,128)(2,1)S(1)}, bf16[128,2048]{1,0:T(8,128)(2,1)S(1)}, u32[]{:S(2)}, u32[]{:S(2)}) collective-permute-start(bf16[128,2048]{1,0:T(8,128)(2,1)S(1)} %collective-permute-done), channel_id=1, source_target_pairs={{4,8},{5,9},{6,10},{7,11},{8,12},{9,13},{10,14},{11,15},{20,24},{2... | collective-permute-start | bytes 1572872 | tf_op jit(solution)/shard_map/ppermute | solution.py:205
  34.7 4.5 %collective-permute-done.9 = bf16[128,2048]{1,0:T(8,128)(2,1)} collective-permute-done((bf16[128,2048]{1,0:T(8,128)(2,1)S(1)}, bf16[128,2048]{1,0:T(8,128)(2,1)}, u32[]{:S(2)}, u32[]{:S(2)}) %collective-permute-start.9) | collective-permute-done | bytes 524320 | tf_op jit(solution)/shard_map/ppermute | solution.py:205
  66.2 7.6 %collective-permute-done.5 = bf16[128,2048]{1,0:T(8,128)(2,1)S(1)} collective-permute-done((bf16[128,2048]{1,0:T(8,128)(2,1)S(1)}, bf16[128,2048]{1,0:T(8,128)(2,1)S(1)}, u32[]{:S(2)}, u32[]{:S(2)}) %collective-permute-start.5) | collective-permute-done | bytes 524320 | tf_op jit(solution)/shard_map/ppermute | solution.py:205
  75.8 37.0 %collective-permute-done.14 = bf16[4,128,2048]{2,1,0:T(8,128)(2,1)S(1)} collective-permute-done((bf16[4,128,2048]{2,1,0:T(8,128)(2,1)S(1)}, bf16[4,128,2048]{2,1,0:T(8,128)(2,1)S(1)}, u32[]{:S(2)}, u32[]{:S(2)}) %collective-permute-start.14) | collective-permute-done | bytes 2097184 | tf_op jit(solution)/shard_map/ppermute | solution.py:205
  116.6 37.5 %collective-permute-done.6 = bf16[4,128,2048]{2,1,0:T(8,128)(2,1)S(1)} collective-permute-done((bf16[4,128,2048]{2,1,0:T(8,128)(2,1)S(1)}, bf16[4,128,2048]{2,1,0:T(8,128)(2,1)S(1)}, u32[]{:S(2)}, u32[]{:S(2)}) %collective-permute-start.6) | collective-permute-done | bytes 2097184 | tf_op jit(solution)/shard_map/ppermute | solution.py:205
  158.5 7.6 %pad_maximum_fusion.1 = bf16[2,2,4,128,2048]{4,3,2,1,0:T(8,128)(2,1)} fusion(bf16[1,2,4,128,2048]{4,3,2,1,0:T(8,128)(2,1)} %bitcast.25, bf16[1,2,4,128,2048]{4,3,2,1,0:T(8,128)(2,1)} %get-tuple-element.16), kind=kLoop, calls=%fused_computation.3 | loop fusion | flops 4194304 | bytes 16777216 | tf_op jit(solution)/shard_map/stack | solution.py:227
  166.1 6.2 %pad_maximum_fusion = bf16[2,2,4,128,2048]{4,3,2,1,0:T(8,128)(2,1)} fusion(bf16[1,2,4,128,2048]{4,3,2,1,0:T(8,128)(2,1)} %bitcast.13, bf16[1,2,4,128,2048]{4,3,2,1,0:T(8,128)(2,1)S(1)} %copy-done.3), kind=kLoop, calls=%fused_computation.2 | loop fusion | flops 4194304 | bytes 16777216 | tf_op jit(solution)/shard_map/stack | solution.py:227
  172.3 26.9 %shard_map.93 = (bf16[128,2048]{1,0:T(8,128)(2,1)}, bf16[128,2048]{1,0:T(8,128)(2,1)}, f32[16,128,2048]{2,1,0:T(8,128)}, f32[16,128,2048]{2,1,0:T(8,128)}) custom-call(s32[8]{0:T(128)} %multiply_add_fusion.pos_ref, bf16[128,2048]{1,0:T(8,128)(2,1)} %q_ref.1, bf16[128,2048]{1,0:T(8,128)(2,1)} %g_ref.1, bf16[16,128,2048]{2,1,0:T(8,128)(2,1)} %bitcast.145, ...), custom_call_target="tpu_custom_call" | custom-call | flops 3221225472 | bytes 44040192 | tf_op jit(solution)/shard_map/pallas_call | solution.py:294
  199.3 6.3 %unstack.254 = bf16[8,128,2048]{2,1,0:T(8,128)(2,1)} slice(f32[16,128,2048]{2,1,0:T(8,128)} %get-tuple-element.11), slice={[8:16], [0:128], [0:2048]} | slice | bytes 8388608 | tf_op jit(solution)/shard_map/transpose()/unstack | solution.py:227
  206.0 6.9 %unstack.255 = bf16[8,128,2048]{2,1,0:T(8,128)(2,1)} slice(f32[16,128,2048]{2,1,0:T(8,128)} %get-tuple-element.10), slice={[8:16], [0:128], [0:2048]} | slice | bytes 8388608 | tf_op jit(solution)/shard_map/transpose()/unstack | solution.py:227
  220.8 10.0 %convert_add_fusion = f32[2,4,128,2048]{3,2,1,0:T(8,128)} fusion(f32[2,4,128,2048]{3,2,1,0:T(8,128)} %bitcast.154, bf16[2,4,128,2048]{3,2,1,0:T(8,128)(2,1)} %collective-permute-done.24), kind=kLoop, calls=%fused_computation.4 | loop fusion | flops 4194304 | bytes 20971520 | tf_op jit(solution)/shard_map/transpose()/add_any | solution.py:205
  236.2 4.7 %convert_add_fusion.1 = f32[2,4,128,2048]{3,2,1,0:T(8,128)} fusion(f32[2,4,128,2048]{3,2,1,0:T(8,128)S(1)} %bitcast.153, bf16[2,4,128,2048]{3,2,1,0:T(8,128)(2,1)S(1)} %collective-permute-done.16), kind=kLoop, calls=%fused_computation.5 | loop fusion | flops 4194304 | bytes 20971520 | tf_op jit(solution)/shard_map/transpose()/add_any | solution.py:205
  244.1 39.4 %collective-permute-done.25 = bf16[4,128,2048]{2,1,0:T(8,128)(2,1)} collective-permute-done((bf16[4,128,2048]{2,1,0:T(8,128)(2,1)}, bf16[4,128,2048]{2,1,0:T(8,128)(2,1)}, u32[]{:S(2)}, u32[]{:S(2)}) %collective-permute-start.25) | collective-permute-done | bytes 2097184 | tf_op jit(solution)/shard_map/transpose()/ppermute | solution.py:205
  289.5 38.4 %collective-permute-done.17 = bf16[4,128,2048]{2,1,0:T(8,128)(2,1)} collective-permute-done((bf16[4,128,2048]{2,1,0:T(8,128)(2,1)S(1)}, bf16[4,128,2048]{2,1,0:T(8,128)(2,1)}, u32[]{:S(2)}, u32[]{:S(2)}) %collective-permute-start.17) | collective-permute-done | bytes 2097184 | tf_op jit(solution)/shard_map/transpose()/ppermute | solution.py:205
  334.1 6.1 %collective-permute-start.27 = (bf16[128,2048]{1,0:T(8,128)(2,1)S(1)}, bf16[128,2048]{1,0:T(8,128)(2,1)S(1)}, u32[]{:S(2)}, u32[]{:S(2)}) collective-permute-start(bf16[128,2048]{1,0:T(8,128)(2,1)S(1)} %fusion.11), channel_id=1, source_target_pairs={{0,4},{1,5},{2,6},{3,7},{4,8},{5,9},{6,10},{7,11},{16,20},{17,21},... | collective-permute-start | bytes 1572872 | tf_op jit(solution)/shard_map/transpose()/ppermute | solution.py:205
  340.9 7.8 %collective-permute-done.18 = bf16[128,2048]{1,0:T(8,128)(2,1)S(1)} collective-permute-done((bf16[128,2048]{1,0:T(8,128)(2,1)S(1)}, bf16[128,2048]{1,0:T(8,128)(2,1)S(1)}, u32[]{:S(2)}, u32[]{:S(2)}) %collective-permute-start.18) | collective-permute-done | bytes 524320 | tf_op jit(solution)/shard_map/transpose()/ppermute | solution.py:205
  350.8 9.2 %collective-permute-done.27 = bf16[128,2048]{1,0:T(8,128)(2,1)S(1)} collective-permute-done((bf16[128,2048]{1,0:T(8,128)(2,1)S(1)}, bf16[128,2048]{1,0:T(8,128)(2,1)S(1)}, u32[]{:S(2)}, u32[]{:S(2)}) %collective-permute-start.27) | collective-permute-done | bytes 524320 | tf_op jit(solution)/shard_map/transpose()/ppermute | solution.py:205
  361.6 8.3 %collective-permute-done.19 = bf16[128,2048]{1,0:T(8,128)(2,1)S(1)} collective-permute-done((bf16[128,2048]{1,0:T(8,128)(2,1)S(1)}, bf16[128,2048]{1,0:T(8,128)(2,1)S(1)}, u32[]{:S(2)}, u32[]{:S(2)}) %collective-permute-start.19) | collective-permute-done | bytes 524320 | tf_op jit(solution)/shard_map/transpose()/ppermute | solution.py:205
  371.5 4.6 %collective-permute-start.28 = (bf16[128,2048]{1,0:T(8,128)(2,1)S(1)}, bf16[128,2048]{1,0:T(8,128)(2,1)S(1)}, u32[]{:S(2)}, u32[]{:S(2)}) collective-permute-start(bf16[128,2048]{1,0:T(8,128)(2,1)S(1)} %get-tuple-element.12), channel_id=1, source_target_pairs={{0,4},{1,5},{2,6},{3,7},{4,8},{5,9},{6,10},{7,11},{8,12},{9,13},{1... | collective-permute-start | bytes 1572872 | tf_op jit(solution)/shard_map/transpose()/ppermute | solution.py:205
  382.0 4.8 %collective-permute-done.22 = bf16[128,2048]{1,0:T(8,128)(2,1)S(1)} collective-permute-done((bf16[128,2048]{1,0:T(8,128)(2,1)S(1)}, bf16[128,2048]{1,0:T(8,128)(2,1)S(1)}, u32[]{:S(2)}, u32[]{:S(2)}) %collective-permute-start.22) | collective-permute-done | bytes 524320 | tf_op jit(solution)/shard_map/transpose()/ppermute | solution.py:205
  388.9 9.2 %collective-permute-done.31 = bf16[128,2048]{1,0:T(8,128)(2,1)S(1)} collective-permute-done((bf16[128,2048]{1,0:T(8,128)(2,1)S(1)}, bf16[128,2048]{1,0:T(8,128)(2,1)S(1)}, u32[]{:S(2)}, u32[]{:S(2)}) %collective-permute-start.31) | collective-permute-done | bytes 524320 | tf_op jit(solution)/shard_map/transpose()/ppermute | solution.py:205
  399.1 8.1 %collective-permute-done.23 = bf16[128,2048]{1,0:T(8,128)(2,1)S(1)} collective-permute-done((bf16[128,2048]{1,0:T(8,128)(2,1)S(1)}, bf16[128,2048]{1,0:T(8,128)(2,1)S(1)}, u32[]{:S(2)}, u32[]{:S(2)}) %collective-permute-start.23) | collective-permute-done | bytes 524320 | tf_op jit(solution)/shard_map/transpose()/ppermute | solution.py:205
  (109 shorter events, 102.2 us)
Async XLA Ops:
  4.1 17.7 %collective-permute-start.11 = (bf16[128,2048]{1,0:T(8,128)(2,1)}, bf16[128,2048]{1,0:T(8,128)(2,1)S(1)}, u32[]{:S(2)}, u32[]{:S(2)}) collective-permute-start(bf16[128,2048]{1,0:T(8,128)(2,1)} %param.8), channel_id=1, source_target_pairs={{4,0},{5,1},{6,2},{7,3},{8,4},{9,5},{10,6},{11,7},{12,8},{13,9},{1... | collective-permute-start | bytes 1572872 | tf_op jit(solution)/shard_map/ppermute | solution.py:205
  6.5 21.4 %collective-permute-start = (bf16[128,2048]{1,0:T(8,128)(2,1)}, bf16[128,2048]{1,0:T(8,128)(2,1)S(1)}, u32[]{:S(2)}, u32[]{:S(2)}) collective-permute-start(bf16[128,2048]{1,0:T(8,128)(2,1)} %param.7), channel_id=1, source_target_pairs={{0,4},{1,5},{2,6},{3,7},{4,8},{5,9},{6,10},{7,11},{8,12},{9,13},{1... | collective-permute-start | bytes 1572872 | tf_op jit(solution)/shard_map/ppermute | solution.py:205
  10.0 22.3 %collective-permute-start.3 = (bf16[128,2048]{1,0:T(8,128)(2,1)}, bf16[128,2048]{1,0:T(8,128)(2,1)S(1)}, u32[]{:S(2)}, u32[]{:S(2)}) collective-permute-start(bf16[128,2048]{1,0:T(8,128)(2,1)} %param.7), channel_id=1, source_target_pairs={{4,0},{5,1},{6,2},{7,3},{8,4},{9,5},{10,6},{11,7},{12,8},{13,9},{1... | collective-permute-start | bytes 1572872 | tf_op jit(solution)/shard_map/ppermute | solution.py:205
  17.5 21.6 %collective-permute-start.9 = (bf16[128,2048]{1,0:T(8,128)(2,1)S(1)}, bf16[128,2048]{1,0:T(8,128)(2,1)}, u32[]{:S(2)}, u32[]{:S(2)}) collective-permute-start(bf16[128,2048]{1,0:T(8,128)(2,1)S(1)} %collective-permute-done.8), channel_id=1, source_target_pairs={{4,8},{5,9},{6,10},{7,11},{8,12},{9,13},{10,14},{11,15},{20,24},{2... | collective-permute-start | bytes 1572872 | tf_op jit(solution)/shard_map/ppermute | solution.py:205
  21.8 21.8 %collective-permute-start.12 = (bf16[128,2048]{1,0:T(8,128)(2,1)S(1)}, bf16[128,2048]{1,0:T(8,128)(2,1)}, u32[]{:S(2)}, u32[]{:S(2)}) collective-permute-start(bf16[128,2048]{1,0:T(8,128)(2,1)S(1)} %collective-permute-done.11), channel_id=1, source_target_pairs={{4,0},{5,1},{6,2},{7,3},{8,4},{9,5},{10,6},{11,7},{20,16},{21,17},... | collective-permute-start | bytes 1572872 | tf_op jit(solution)/shard_map/ppermute | solution.py:205
  28.0 21.2 %collective-permute-start.1 = (bf16[128,2048]{1,0:T(8,128)(2,1)S(1)}, bf16[128,2048]{1,0:T(8,128)(2,1)S(1)}, u32[]{:S(2)}, u32[]{:S(2)}) collective-permute-start(bf16[128,2048]{1,0:T(8,128)(2,1)S(1)} %collective-permute-done), channel_id=1, source_target_pairs={{4,8},{5,9},{6,10},{7,11},{8,12},{9,13},{10,14},{11,15},{20,24},{2... | collective-permute-start | bytes 1572872 | tf_op jit(solution)/shard_map/ppermute | solution.py:205
  32.3 21.0 %collective-permute-start.4 = (bf16[128,2048]{1,0:T(8,128)(2,1)S(1)}, bf16[128,2048]{1,0:T(8,128)(2,1)S(1)}, u32[]{:S(2)}, u32[]{:S(2)}) collective-permute-start(bf16[128,2048]{1,0:T(8,128)(2,1)S(1)} %collective-permute-done.3), channel_id=1, source_target_pairs={{4,0},{5,1},{6,2},{7,3},{8,4},{9,5},{10,6},{11,7},{20,16},{21,17},... | collective-permute-start | bytes 1572872 | tf_op jit(solution)/shard_map/ppermute | solution.py:205
  39.1 18.0 %collective-permute-start.10 = (bf16[128,2048]{1,0:T(8,128)(2,1)}, bf16[128,2048]{1,0:T(8,128)(2,1)}, u32[]{:S(2)}, u32[]{:S(2)}) collective-permute-start(bf16[128,2048]{1,0:T(8,128)(2,1)} %collective-permute-done.9), channel_id=1, source_target_pairs={{8,12},{9,13},{10,14},{11,15},{24,28},{25,29},{26,30},{27,31}} | collective-permute-start | bytes 1572872 | tf_op jit(solution)/shard_map/ppermute | solution.py:205
  43.6 20.5 %collective-permute-start.13 = (bf16[128,2048]{1,0:T(8,128)(2,1)}, bf16[128,2048]{1,0:T(8,128)(2,1)S(1)}, u32[]{:S(2)}, u32[]{:S(2)}) collective-permute-start(bf16[128,2048]{1,0:T(8,128)(2,1)} %collective-permute-done.12), channel_id=1, source_target_pairs={{4,0},{5,1},{6,2},{7,3},{20,16},{21,17},{22,18},{23,19}} | collective-permute-start | bytes 1572872 | tf_op jit(solution)/shard_map/ppermute | solution.py:205
  53.3 20.5 %collective-permute-start.5 = (bf16[128,2048]{1,0:T(8,128)(2,1)S(1)}, bf16[128,2048]{1,0:T(8,128)(2,1)S(1)}, u32[]{:S(2)}, u32[]{:S(2)}) collective-permute-start(bf16[128,2048]{1,0:T(8,128)(2,1)S(1)} %collective-permute-done.4), channel_id=1, source_target_pairs={{4,0},{5,1},{6,2},{7,3},{20,16},{21,17},{22,18},{23,19}} | collective-permute-start | bytes 1572872 | tf_op jit(solution)/shard_map/ppermute | solution.py:205
  64.3 48.6 %collective-permute-start.14 = (bf16[4,128,2048]{2,1,0:T(8,128)(2,1)S(1)}, bf16[4,128,2048]{2,1,0:T(8,128)(2,1)S(1)}, u32[]{:S(2)}, u32[]{:S(2)}) collective-permute-start(bf16[4,128,2048]{2,1,0:T(8,128)(2,1)S(1)} %constant_dynamic-slice_fusion), channel_id=1, source_target_pairs={{0,2},{1,3},{2,0},{3,1},{4,6},{5,7},{6,4},{7,5},{8,10},{9,11},{10,... | collective-permute-start | bytes 6291464 | tf_op jit(solution)/shard_map/ppermute | solution.py:205
  74.1 80.0 %collective-permute-start.6 = (bf16[4,128,2048]{2,1,0:T(8,128)(2,1)S(1)}, bf16[4,128,2048]{2,1,0:T(8,128)(2,1)S(1)}, u32[]{:S(2)}, u32[]{:S(2)}) collective-permute-start(bf16[4,128,2048]{2,1,0:T(8,128)(2,1)S(1)} %constant_dynamic-slice_fusion.1), channel_id=1, source_target_pairs={{0,2},{1,3},{2,0},{3,1},{4,6},{5,7},{6,4},{7,5},{8,10},{9,11},{10,... | collective-permute-start | bytes 6291464 | tf_op jit(solution)/shard_map/ppermute | solution.py:205
  116.4 42.2 %collective-permute-start.15 = (bf16[2,4,128,2048]{3,2,1,0:T(8,128)(2,1)}, bf16[2,4,128,2048]{3,2,1,0:T(8,128)(2,1)}, u32[]{:S(2)}, u32[]{:S(2)}) collective-permute-start(bf16[2,4,128,2048]{3,2,1,0:T(8,128)(2,1)} %get-tuple-element.17), channel_id=1, source_target_pairs={{0,1},{1,0},{2,3},{3,2},{4,5},{5,4},{6,7},{7,6},{8,9},{9,8},{10,11... | collective-permute-start | bytes 12582920 | tf_op jit(solution)/shard_map/ppermute | solution.py:205
  212.9 23.3 %collective-permute-start.16 = (bf16[2,4,128,2048]{3,2,1,0:T(8,128)(2,1)}, bf16[2,4,128,2048]{3,2,1,0:T(8,128)(2,1)S(1)}, u32[]{:S(2)}, u32[]{:S(2)}) collective-permute-start(bf16[2,4,128,2048]{3,2,1,0:T(8,128)(2,1)} %bitcast.157), channel_id=1, source_target_pairs={{1,0},{0,1},{3,2},{2,3},{5,4},{4,5},{7,6},{6,7},{9,8},{8,9},{11,10... | collective-permute-start | bytes 12582920 | tf_op jit(solution)/shard_map/transpose()/ppermute | solution.py:205
  234.7 48.8 %collective-permute-start.25 = (bf16[4,128,2048]{2,1,0:T(8,128)(2,1)}, bf16[4,128,2048]{2,1,0:T(8,128)(2,1)}, u32[]{:S(2)}, u32[]{:S(2)}) collective-permute-start(bf16[4,128,2048]{2,1,0:T(8,128)(2,1)} %fusion.5), channel_id=1, source_target_pairs={{2,0},{3,1},{0,2},{1,3},{6,4},{7,5},{4,6},{5,7},{10,8},{11,9},{8,1... | collective-permute-start | bytes 6291464 | tf_op jit(solution)/shard_map/transpose()/ppermute | solution.py:205
  243.5 84.3 %collective-permute-start.17 = (bf16[4,128,2048]{2,1,0:T(8,128)(2,1)S(1)}, bf16[4,128,2048]{2,1,0:T(8,128)(2,1)}, u32[]{:S(2)}, u32[]{:S(2)}) collective-permute-start(bf16[4,128,2048]{2,1,0:T(8,128)(2,1)S(1)} %fusion.4), channel_id=1, source_target_pairs={{2,0},{3,1},{0,2},{1,3},{6,4},{7,5},{4,6},{5,7},{10,8},{11,9},{8,1... | collective-permute-start | bytes 6291464 | tf_op jit(solution)/shard_map/transpose()/ppermute | solution.py:205
  287.8 46.2 %collective-permute-start.26 = (bf16[128,2048]{1,0:T(8,128)(2,1)S(1)}, bf16[128,2048]{1,0:T(8,128)(2,1)S(1)}, u32[]{:S(2)}, u32[]{:S(2)}) collective-permute-start(bf16[128,2048]{1,0:T(8,128)(2,1)S(1)} %get-tuple-element.20), channel_id=1, source_target_pairs={{0,4},{1,5},{2,6},{3,7},{16,20},{17,21},{18,22},{19,23}} | collective-permute-start | bytes 1572872 | tf_op jit(solution)/shard_map/transpose()/ppermute | solution.py:205
  333.3 17.4 %collective-permute-start.29 = (bf16[128,2048]{1,0:T(8,128)(2,1)S(1)}, bf16[128,2048]{1,0:T(8,128)(2,1)S(1)}, u32[]{:S(2)}, u32[]{:S(2)}) collective-permute-start(bf16[128,2048]{1,0:T(8,128)(2,1)S(1)} %get-tuple-element.21), channel_id=1, source_target_pairs={{12,8},{13,9},{14,10},{15,11},{28,24},{29,25},{30,26},{31,27}} | collective-permute-start | bytes 1572872 | tf_op jit(solution)/shard_map/transpose()/ppermute | solution.py:205
  334.1 25.8 %collective-permute-start.27 = (bf16[128,2048]{1,0:T(8,128)(2,1)S(1)}, bf16[128,2048]{1,0:T(8,128)(2,1)S(1)}, u32[]{:S(2)}, u32[]{:S(2)}) collective-permute-start(bf16[128,2048]{1,0:T(8,128)(2,1)S(1)} %fusion.11), channel_id=1, source_target_pairs={{0,4},{1,5},{2,6},{3,7},{4,8},{5,9},{6,10},{7,11},{16,20},{17,21},... | collective-permute-start | bytes 1572872 | tf_op jit(solution)/shard_map/transpose()/ppermute | solution.py:205
  340.2 21.3 %collective-permute-start.21 = (bf16[128,2048]{1,0:T(8,128)(2,1)S(1)}, bf16[128,2048]{1,0:T(8,128)(2,1)S(1)}, u32[]{:S(2)}, u32[]{:S(2)}) collective-permute-start(bf16[128,2048]{1,0:T(8,128)(2,1)S(1)} %get-tuple-element.23), channel_id=1, source_target_pairs={{12,8},{13,9},{14,10},{15,11},{28,24},{29,25},{30,26},{31,27}} | collective-permute-start | bytes 1572872 | tf_op jit(solution)/shard_map/transpose()/ppermute | solution.py:205
  348.8 21.1 %collective-permute-start.19 = (bf16[128,2048]{1,0:T(8,128)(2,1)S(1)}, bf16[128,2048]{1,0:T(8,128)(2,1)S(1)}, u32[]{:S(2)}, u32[]{:S(2)}) collective-permute-start(bf16[128,2048]{1,0:T(8,128)(2,1)S(1)} %fusion.22), channel_id=1, source_target_pairs={{0,4},{1,5},{2,6},{3,7},{4,8},{5,9},{6,10},{7,11},{16,20},{17,21},... | collective-permute-start | bytes 1572872 | tf_op jit(solution)/shard_map/transpose()/ppermute | solution.py:205
  376.2 21.9 %collective-permute-start.31 = (bf16[128,2048]{1,0:T(8,128)(2,1)S(1)}, bf16[128,2048]{1,0:T(8,128)(2,1)S(1)}, u32[]{:S(2)}, u32[]{:S(2)}) collective-permute-start(bf16[128,2048]{1,0:T(8,128)(2,1)S(1)} %fusion.9), channel_id=1, source_target_pairs={{4,0},{5,1},{6,2},{7,3},{8,4},{9,5},{10,6},{11,7},{12,8},{13,9},{1... | collective-permute-start | bytes 1572872 | tf_op jit(solution)/shard_map/transpose()/ppermute | solution.py:205
  378.1 21.0 %collective-permute-start.20 = (bf16[128,2048]{1,0:T(8,128)(2,1)S(1)}, bf16[128,2048]{1,0:T(8,128)(2,1)S(1)}, u32[]{:S(2)}, u32[]{:S(2)}) collective-permute-start(bf16[128,2048]{1,0:T(8,128)(2,1)S(1)} %get-tuple-element.14), channel_id=1, source_target_pairs={{0,4},{1,5},{2,6},{3,7},{4,8},{5,9},{6,10},{7,11},{8,12},{9,13},{1... | collective-permute-start | bytes 1572872 | tf_op jit(solution)/shard_map/transpose()/ppermute | solution.py:205
  387.0 20.2 %collective-permute-start.23 = (bf16[128,2048]{1,0:T(8,128)(2,1)S(1)}, bf16[128,2048]{1,0:T(8,128)(2,1)S(1)}, u32[]{:S(2)}, u32[]{:S(2)}) collective-permute-start(bf16[128,2048]{1,0:T(8,128)(2,1)S(1)} %fusion.20), channel_id=1, source_target_pairs={{4,0},{5,1},{6,2},{7,3},{8,4},{9,5},{10,6},{11,7},{12,8},{13,9},{1... | collective-permute-start | bytes 1572872 | tf_op jit(solution)/shard_map/transpose()/ppermute | solution.py:205
  (17 other events, 467.5 us)

commit v2 on v1

--- a/solution.py
+++ b/solution.py
@@ -205,26 +205,48 @@
     return lax.ppermute(v.astype(jnp.bfloat16), "seq", pairs).astype(v.dtype)
 
 
-def gather_blocks(x, n):
+def _line_shifts(x, n):
     line_len = n // 4
     z = lax.axis_index("seq") // 4
-    ups, downs = [], []
-    up, down = x, x
-    for k in range(1, line_len):
-        up = _send(
-            up, [(4 * z0 + r, 4 * (z0 + 1) + r) for z0 in range(k - 1, line_len - 1) for r in range(4)]
-        )
-        down = _send(
-            down, [(4 * z0 + r, 4 * (z0 - 1) + r) for z0 in range(1, line_len - k + 1) for r in range(4)]
-        )
-        ups.append(up)
-        downs.append(down)
-    rel = jnp.stack(ups[::-1] + [x] + downs)
-    line = lax.dynamic_slice_in_dim(rel, line_len - 1 - z, line_len, axis=0)
+    got = {0: x}
+    for d in range(1, line_len):
+        for sign in (1, -1):
+            step = sign * d
+            pairs = [
+                (4 * z0 + r, 4 * (z0 + step) + r)
+                for z0 in range(line_len)
+                if 0 <= z0 + step < line_len
+                for r in range(4)
+            ]
+            got[-step] = _send(x, pairs)
+    rel = jnp.stack([got[m] for m in range(-(line_len - 1), line_len)])
+    return lax.dynamic_slice_in_dim(rel, line_len - 1 - z, line_len, axis=0)
+
+
+def _gather_z_first(x, n):
+    line = _line_shifts(x, n)
     other = _send(line, [(i, i ^ 2) for i in range(n)])
     pair = jnp.stack([line, other])
     sibling = _send(pair, [(i, i ^ 1) for i in range(n)])
     return jnp.stack([pair, sibling])
+
+
+def _gather_y_first(x, n):
+    other = _send(x, [(i, i ^ 2) for i in range(n)])
+    line = _line_shifts(jnp.stack([x, other]), n)
+    pair = jnp.moveaxis(line, 1, 0)
+    sibling = _send(pair, [(i, i ^ 1) for i in range(n)])
+    return jnp.stack([pair, sibling])
+
+
+Y_FIRST_HEADS = 3
+
+
+def gather_blocks(x, n):
+    split = x.shape[-1] - Y_FIRST_HEADS * HD
+    return jnp.concatenate(
+        [_gather_z_first(x[:, :split], n), _gather_y_first(x[:, split:], n)], axis=-1
+    )
 
 
 def _attend_kernel(pos_ref, q_ref, g_ref, *refs):

time: 412 us -> 466 us (1.13)
  starting transfers between devices: 65.9 us -> 134 us
  local copies, waits for them, and re-layouts: 35.3 us -> 21 us
  other arithmetic: 45.4 us -> 37.4 us
  waiting for transfers between devices: 233 us -> 241 us
    ppermute x32 -> x64, starting transfers between devices: 65.9 us -> 134 us  [_send(): return lax.ppermute(v.astype(jnp.bfloat16), 'seq', pairs).astype(v.dtype)]
    another operation x10 -> x14, local copies, waits for them, and re-layouts: 23.3 us -> 4.5 us  [the longest x2 2.46 us: _gather_y_first(): line = _line_shifts(jnp.stack([x, other]), n)]
    another operation x6 -> x9, other arithmetic: 22 us -> 10.2 us  [the longest x4 20.9 us: gather_blocks(): return jnp.stack([pair, sibling])]
    concatenate x0 -> x2, other arithmetic: none -> 7.87 us  [gather_blocks(): jnp.concatenate([_gather_z_first(x[:, :split], n), _gather_y_first(x[:, s...]
    ppermute x32 -> x64, waiting for transfers between devices: 233 us -> 241 us  [_send(): return lax.ppermute(v.astype(jnp.bfloat16), 'seq', pairs).astype(v.dtype)]
    convert_element_type x4 -> x12, local copies, waits for them, and re-layouts: 6.73 us -> 12.3 us  [_send(): return lax.ppermute(v.astype(jnp.bfloat16), 'seq', pairs).astype(v.dtype)]
    add_any x2 -> x8, other arithmetic: 14.7 us -> 12.6 us  [_send(): return lax.ppermute(v.astype(jnp.bfloat16), 'seq', pairs).astype(v.dtype)]
  transfers between devices with their start and end apart: 32 -> 64, of which waited for: 18 -> 24; matrix products, arithmetic and copies ran while one was open for 16% -> 9% of each run, Pallas kernels for 0% -> 0%
where the time goes in v2:
time: 466 us; the launch traced here: 462 us
  waiting for transfers between devices  241 us (52%)
  starting transfers between devices  134 us (29%)
  other arithmetic  37.4 us (8%)
  Pallas kernels  26.7 us (6%)
  local copies, waits for them, and re-layouts  21 us (5%)
    ppermute x64, waiting for transfers between devices, _send(): return lax.ppermute(v.astype(jnp.bfloat16), 'seq', pairs).astype(v.dtype)  241 us
    ppermute x64, starting transfers between devices, _send(): return lax.ppermute(v.astype(jnp.bfloat16), 'seq', pairs).astype(v.dtype)  134 us
    pallas_call x1, Pallas kernels, attend_local(): call(pos, query, grad_out, *[keys_local] * SLOTS, *[values_local] * SLOTS)  26.7 us
    add_any x8, other arithmetic, _send(): return lax.ppermute(v.astype(jnp.bfloat16), 'seq', pairs).astype(v.dtype)  12.6 us
    convert_element_type x12, local copies, waits for them, and re-layouts, _send(): return lax.ppermute(v.astype(jnp.bfloat16), 'seq', pairs).astype(v.dtype)  12.3 us
  transfers between devices with their start and end apart: 64, of which 24 were waited for; matrix products, arithmetic and copies ran while one was open for 9% of the time, Pallas kernels for 0%

profile of v2, /device:TPU:10, one launch (start us, length us, event | category | flops | bytes accessed | tf_op | source)
XLA Modules:
  0.0 462.3 jit_solution(8962811294883835135)
XLA Ops:
  2.5 5.1 %collective-permute-start.17 = (bf16[128,1664]{1,0:T(8,128)(2,1)S(1)}, bf16[128,1664]{1,0:T(8,128)(2,1)S(1)}, u32[]{:S(2)}, u32[]{:S(2)}) collective-permute-start(bf16[128,1664]{1,0:T(8,128)(2,1)S(1)} %slice.22), channel_id=1, source_target_pairs={{0,8},{1,9},{2,10},{3,11},{4,12},{5,13},{6,14},{7,15},{16,24},{17,... | collective-permute-start | bytes 1277960 | tf_op jit(solution)/shard_map/ppermute | solution.py:205
  26.5 8.1 %collective-permute-done.17 = bf16[128,1664]{1,0:T(8,128)(2,1)S(1)} collective-permute-done((bf16[128,1664]{1,0:T(8,128)(2,1)S(1)}, bf16[128,1664]{1,0:T(8,128)(2,1)S(1)}, u32[]{:S(2)}, u32[]{:S(2)}) %collective-permute-start.17) | collective-permute-done | bytes 426016 | tf_op jit(solution)/shard_map/ppermute | solution.py:205
  35.3 17.4 %collective-permute-done.18 = bf16[128,1664]{1,0:T(8,128)(2,1)S(1)} collective-permute-done((bf16[128,1664]{1,0:T(8,128)(2,1)S(1)}, bf16[128,1664]{1,0:T(8,128)(2,1)S(1)}, u32[]{:S(2)}, u32[]{:S(2)}) %collective-permute-start.18) | collective-permute-done | bytes 426016 | tf_op jit(solution)/shard_map/ppermute | solution.py:205
  64.4 9.0 %collective-permute-done.1 = bf16[128,1664]{1,0:T(8,128)(2,1)S(1)} collective-permute-done((bf16[128,1664]{1,0:T(8,128)(2,1)S(1)}, bf16[128,1664]{1,0:T(8,128)(2,1)S(1)}, u32[]{:S(2)}, u32[]{:S(2)}) %collective-permute-start.1) | collective-permute-done | bytes 426016 | tf_op jit(solution)/shard_map/ppermute | solution.py:205
  74.1 12.0 %collective-permute-done.2 = bf16[128,1664]{1,0:T(8,128)(2,1)S(1)} collective-permute-done((bf16[128,1664]{1,0:T(8,128)(2,1)S(1)}, bf16[128,1664]{1,0:T(8,128)(2,1)S(1)}, u32[]{:S(2)}, u32[]{:S(2)}) %collective-permute-start.2) | collective-permute-done | bytes 426016 | tf_op jit(solution)/shard_map/ppermute | solution.py:205
  93.5 9.3 %collective-permute-start.28 = (bf16[2,128,384]{2,1,0:T(8,128)(2,1)S(1)}, bf16[2,128,384]{2,1,0:T(8,128)(2,1)S(1)}, u32[]{:S(2)}, u32[]{:S(2)}) collective-permute-start(bf16[2,128,384]{2,1,0:T(8,128)(2,1)S(1)} %pad_maximum_fusion.7), channel_id=1, source_target_pairs={{4,0},{5,1},{6,2},{7,3},{8,4},{9,5},{10,6},{11,7},{12,8},{13,9},{1... | collective-permute-start | bytes 589832 | tf_op jit(solution)/shard_map/ppermute | solution.py:205
  107.4 35.5 %collective-permute-done.22 = bf16[4,128,1664]{2,1,0:T(8,128)(2,1)S(1)} collective-permute-done((bf16[4,128,1664]{2,1,0:T(8,128)(2,1)S(1)}, bf16[4,128,1664]{2,1,0:T(8,128)(2,1)S(1)}, u32[]{:S(2)}, u32[]{:S(2)}) %collective-permute-start.22) | collective-permute-done | bytes 1703968 | tf_op jit(solution)/shard_map/ppermute | solution.py:205
  143.7 33.4 %collective-permute-done.6 = bf16[4,128,1664]{2,1,0:T(8,128)(2,1)S(1)} collective-permute-done((bf16[4,128,1664]{2,1,0:T(8,128)(2,1)S(1)}, bf16[4,128,1664]{2,1,0:T(8,128)(2,1)S(1)}, u32[]{:S(2)}, u32[]{:S(2)}) %collective-permute-start.6) | collective-permute-done | bytes 1703968 | tf_op jit(solution)/shard_map/ppermute | solution.py:205
  178.4 9.6 %collective-permute-start.10 = (bf16[2,128,384]{2,1,0:T(8,128)(2,1)S(1)}, bf16[2,128,384]{2,1,0:T(8,128)(2,1)S(1)}, u32[]{:S(2)}, u32[]{:S(2)}) collective-permute-start(bf16[2,128,384]{2,1,0:T(8,128)(2,1)S(1)} %pad_maximum_fusion.6), channel_id=1, source_target_pairs={{0,8},{1,9},{2,10},{3,11},{4,12},{5,13},{6,14},{7,15},{16,24},{17,... | collective-permute-start | bytes 589832 | tf_op jit(solution)/shard_map/ppermute | solution.py:205
  198.5 9.6 %collective-permute-done.12 = bf16[2,128,384]{2,1,0:T(8,128)(2,1)S(1)} collective-permute-done((bf16[2,128,384]{2,1,0:T(8,128)(2,1)S(1)}, bf16[2,128,384]{2,1,0:T(8,128)(2,1)S(1)}, u32[]{:S(2)}, u32[]{:S(2)}) %collective-permute-start.12) | collective-permute-done | bytes 196640 | tf_op jit(solution)/shard_map/ppermute | solution.py:205
  218.3 26.7 %shard_map.93 = (bf16[128,2048]{1,0:T(8,128)(2,1)}, bf16[128,2048]{1,0:T(8,128)(2,1)}, f32[16,128,2048]{2,1,0:T(8,128)}, f32[16,128,2048]{2,1,0:T(8,128)}) custom-call(s32[8]{0:T(128)} %multiply_add_fusion.pos_ref, bf16[128,2048]{1,0:T(8,128)(2,1)} %q_ref.1, bf16[128,2048]{1,0:T(8,128)(2,1)} %g_ref.1, bf16[16,128,2048]{2,1,0:T(8,128)(2,1)} %bitcast.273, ...), custom_call_target="tpu_custom_call" | custom-call | flops 3221225472 | bytes 44040192 | tf_op jit(solution)/shard_map/pallas_call | solution.py:316
  245.0 8.2 %convert.57 = bf16[2,2,4,128,2048]{4,3,2,1,0:T(8,128)(2,1)S(1)} convert(f32[2,2,4,128,2048]{4,3,2,1,0:T(8,128)} %bitcast.281) | non-fusion elementwise | flops 4194304 | bytes 25165824 | tf_op jit(solution)/shard_map/convert.15
  256.4 5.0 %slice_bitcast_fusion.5 = bf16[2,4,128,1664]{3,2,0,1:T(8,128)(2,1)} fusion(f32[2,2,4,128,2048]{4,3,2,1,0:T(8,128)} %bitcast.289), kind=kLoop, calls=%fused_computation.15 | loop fusion | bytes 6815744 | tf_op jit(solution)/shard_map/transpose()/convert_element_type | solution.py:205
  264.0 9.8 %collective-permute-start.51 = (bf16[2,128,384]{2,1,0:T(8,128)(2,1)S(1)}, bf16[2,128,384]{2,1,0:T(8,128)(2,1)S(1)}, u32[]{:S(2)}, u32[]{:S(2)}) collective-permute-start(bf16[2,128,384]{2,1,0:T(8,128)(2,1)S(1)} %get-tuple-element.32), channel_id=1, source_target_pairs={{0,8},{1,9},{2,10},{3,11},{4,12},{5,13},{6,14},{7,15},{16,24},{17,... | collective-permute-start | bytes 589832 | tf_op jit(solution)/shard_map/transpose()/ppermute | solution.py:205
  289.8 9.3 %collective-permute-start.35 = (bf16[2,128,384]{2,1,0:T(8,128)(2,1)S(1)}, bf16[2,128,384]{2,1,0:T(8,128)(2,1)}, u32[]{:S(2)}, u32[]{:S(2)}) collective-permute-start(bf16[2,128,384]{2,1,0:T(8,128)(2,1)S(1)} %get-tuple-element.38), channel_id=1, source_target_pairs={{0,8},{1,9},{2,10},{3,11},{4,12},{5,13},{6,14},{7,15},{16,24},{17,... | collective-permute-start | bytes 589832 | tf_op jit(solution)/shard_map/transpose()/ppermute | solution.py:205
  300.6 5.7 %fusion = f32[2,4,128,1664]{3,2,1,0:T(8,128)} fusion(f32[2,2,4,128,2048]{4,3,2,1,0:T(8,128)S(1)} %bitcast.285, bf16[2,4,128,1664]{3,2,1,0:T(8,128)(2,1)} %collective-permute-done.56), kind=kLoop, calls=%fused_computation.3 | loop fusion | flops 3407872 | bytes 17039360 | tf_op jit(solution)/shard_map/transpose()/add_any | solution.py:205
  329.1 19.7 %collective-permute-done.57 = bf16[4,128,1664]{2,1,0:T(8,128)(2,1)S(1)} collective-permute-done((bf16[4,128,1664]{2,1,0:T(8,128)(2,1)S(1)}, bf16[4,128,1664]{2,1,0:T(8,128)(2,1)S(1)}, u32[]{:S(2)}, u32[]{:S(2)}) %collective-permute-start.57) | collective-permute-done | bytes 1703968 | tf_op jit(solution)/shard_map/transpose()/ppermute | solution.py:205
  351.7 34.1 %collective-permute-done.41 = bf16[4,128,1664]{2,1,0:T(8,128)(2,1)} collective-permute-done((bf16[4,128,1664]{2,1,0:T(8,128)(2,1)}, bf16[4,128,1664]{2,1,0:T(8,128)(2,1)}, u32[]{:S(2)}, u32[]{:S(2)}) %collective-permute-start.41) | collective-permute-done | bytes 1703968 | tf_op jit(solution)/shard_map/transpose()/ppermute | solution.py:205
  385.8 5.9 %collective-permute-start.60 = (bf16[128,1664]{1,0:T(8,128)(2,1)S(1)}, bf16[128,1664]{1,0:T(8,128)(2,1)S(1)}, u32[]{:S(2)}, u32[]{:S(2)}) collective-permute-start(bf16[128,1664]{1,0:T(8,128)(2,1)S(1)} %get-tuple-element.20), channel_id=1, source_target_pairs={{0,8},{1,9},{2,10},{3,11},{4,12},{5,13},{6,14},{7,15},{16,24},{17,... | collective-permute-start | bytes 1277960 | tf_op jit(solution)/shard_map/transpose()/ppermute | solution.py:205
  403.3 6.7 %collective-permute-done.61 = bf16[128,1664]{1,0:T(8,128)(2,1)S(1)} collective-permute-done((bf16[128,1664]{1,0:T(8,128)(2,1)S(1)}, bf16[128,1664]{1,0:T(8,128)(2,1)S(1)}, u32[]{:S(2)}, u32[]{:S(2)}) %collective-permute-start.61) | collective-permute-done | bytes 426016 | tf_op jit(solution)/shard_map/transpose()/ppermute | solution.py:205
  410.0 5.1 %collective-permute-start.44 = (bf16[128,1664]{1,0:T(8,128)(2,1)S(1)}, bf16[128,1664]{1,0:T(8,128)(2,1)S(1)}, u32[]{:S(2)}, u32[]{:S(2)}) collective-permute-start(bf16[128,1664]{1,0:T(8,128)(2,1)S(1)} %get-tuple-element.26), channel_id=1, source_target_pairs={{0,8},{1,9},{2,10},{3,11},{4,12},{5,13},{6,14},{7,15},{16,24},{17,... | collective-permute-start | bytes 1277960 | tf_op jit(solution)/shard_map/transpose()/ppermute | solution.py:205
  415.1 14.5 %collective-permute-done.62 = bf16[128,1664]{1,0:T(8,128)(2,1)S(1)} collective-permute-done((bf16[128,1664]{1,0:T(8,128)(2,1)S(1)}, bf16[128,1664]{1,0:T(8,128)(2,1)S(1)}, u32[]{:S(2)}, u32[]{:S(2)}) %collective-permute-start.62) | collective-permute-done | bytes 426016 | tf_op jit(solution)/shard_map/transpose()/ppermute | solution.py:205
  438.8 6.3 %collective-permute-done.45 = bf16[128,1664]{1,0:T(8,128)(2,1)S(1)} collective-permute-done((bf16[128,1664]{1,0:T(8,128)(2,1)S(1)}, bf16[128,1664]{1,0:T(8,128)(2,1)S(1)}, u32[]{:S(2)}, u32[]{:S(2)}) %collective-permute-start.45) | collective-permute-done | bytes 426016 | tf_op jit(solution)/shard_map/transpose()/ppermute | solution.py:205
  447.6 13.5 %collective-permute-done.47 = bf16[128,1664]{1,0:T(8,128)(2,1)S(1)} collective-permute-done((bf16[128,1664]{1,0:T(8,128)(2,1)S(1)}, bf16[128,1664]{1,0:T(8,128)(2,1)S(1)}, u32[]{:S(2)}, u32[]{:S(2)}) %collective-permute-start.47) | collective-permute-done | bytes 426016 | tf_op jit(solution)/shard_map/transpose()/ppermute | solution.py:205
  (209 shorter events, 140.8 us)
Async XLA Ops:
  7.6 45.2 %collective-permute-start.18 = (bf16[128,1664]{1,0:T(8,128)(2,1)S(1)}, bf16[128,1664]{1,0:T(8,128)(2,1)S(1)}, u32[]{:S(2)}, u32[]{:S(2)}) collective-permute-start(bf16[128,1664]{1,0:T(8,128)(2,1)S(1)} %slice.22), channel_id=1, source_target_pairs={{0,4},{1,5},{2,6},{3,7},{4,8},{5,9},{6,10},{7,11},{8,12},{9,13},{1... | collective-permute-start | bytes 1277960 | tf_op jit(solution)/shard_map/ppermute | solution.py:205
  9.5 44.7 %collective-permute-start.19 = (bf16[128,1664]{1,0:T(8,128)(2,1)S(1)}, bf16[128,1664]{1,0:T(8,128)(2,1)S(1)}, u32[]{:S(2)}, u32[]{:S(2)}) collective-permute-start(bf16[128,1664]{1,0:T(8,128)(2,1)S(1)} %slice.22), channel_id=1, source_target_pairs={{4,0},{5,1},{6,2},{7,3},{8,4},{9,5},{10,6},{11,7},{12,8},{13,9},{1... | collective-permute-start | bytes 1277960 | tf_op jit(solution)/shard_map/ppermute | solution.py:205
  24.5 34.2 %collective-permute-start.20 = (bf16[128,1664]{1,0:T(8,128)(2,1)S(1)}, bf16[128,1664]{1,0:T(8,128)(2,1)S(1)}, u32[]{:S(2)}, u32[]{:S(2)}) collective-permute-start(bf16[128,1664]{1,0:T(8,128)(2,1)S(1)} %slice.22), channel_id=1, source_target_pairs={{8,0},{9,1},{10,2},{11,3},{12,4},{13,5},{14,6},{15,7},{24,16},{25,... | collective-permute-start | bytes 1277960 | tf_op jit(solution)/shard_map/ppermute | solution.py:205
  25.8 36.3 %collective-permute-start.21 = (bf16[128,1664]{1,0:T(8,128)(2,1)S(1)}, bf16[128,1664]{1,0:T(8,128)(2,1)S(1)}, u32[]{:S(2)}, u32[]{:S(2)}) collective-permute-start(bf16[128,1664]{1,0:T(8,128)(2,1)S(1)} %slice.22), channel_id=1, source_target_pairs={{12,0},{13,1},{14,2},{15,3},{28,16},{29,17},{30,18},{31,19}} | collective-permute-start | bytes 1277960 | tf_op jit(solution)/shard_map/ppermute | solution.py:205
  63.6 39.2 %collective-permute-start.5 = (bf16[128,1664]{1,0:T(8,128)(2,1)S(1)}, bf16[128,1664]{1,0:T(8,128)(2,1)S(1)}, u32[]{:S(2)}, u32[]{:S(2)}) collective-permute-start(bf16[128,1664]{1,0:T(8,128)(2,1)S(1)} %slice.20), channel_id=1, source_target_pairs={{12,0},{13,1},{14,2},{15,3},{28,16},{29,17},{30,18},{31,19}} | collective-permute-start | bytes 1277960 | tf_op jit(solution)/shard_map/ppermute | solution.py:205
  93.5 84.9 %collective-permute-start.28 = (bf16[2,128,384]{2,1,0:T(8,128)(2,1)S(1)}, bf16[2,128,384]{2,1,0:T(8,128)(2,1)S(1)}, u32[]{:S(2)}, u32[]{:S(2)}) collective-permute-start(bf16[2,128,384]{2,1,0:T(8,128)(2,1)S(1)} %pad_maximum_fusion.7), channel_id=1, source_target_pairs={{4,0},{5,1},{6,2},{7,3},{8,4},{9,5},{10,6},{11,7},{12,8},{13,9},{1... | collective-permute-start | bytes 589832 | tf_op jit(solution)/shard_map/ppermute | solution.py:205
  102.8 40.1 %collective-permute-start.22 = (bf16[4,128,1664]{2,1,0:T(8,128)(2,1)S(1)}, bf16[4,128,1664]{2,1,0:T(8,128)(2,1)S(1)}, u32[]{:S(2)}, u32[]{:S(2)}) collective-permute-start(bf16[4,128,1664]{2,1,0:T(8,128)(2,1)S(1)} %constant_dynamic-slice_fusion), channel_id=1, source_target_pairs={{0,2},{1,3},{2,0},{3,1},{4,6},{5,7},{6,4},{7,5},{8,10},{9,11},{10,... | collective-permute-start | bytes 5111816 | tf_op jit(solution)/shard_map/ppermute | solution.py:205
  104.6 72.5 %collective-permute-start.6 = (bf16[4,128,1664]{2,1,0:T(8,128)(2,1)S(1)}, bf16[4,128,1664]{2,1,0:T(8,128)(2,1)S(1)}, u32[]{:S(2)}, u32[]{:S(2)}) collective-permute-start(bf16[4,128,1664]{2,1,0:T(8,128)(2,1)S(1)} %constant_dynamic-slice_fusion.1), channel_id=1, source_target_pairs={{0,2},{1,3},{2,0},{3,1},{4,6},{5,7},{6,4},{7,5},{8,10},{9,11},{10,... | collective-permute-start | bytes 5111816 | tf_op jit(solution)/shard_map/ppermute | solution.py:205
  105.2 82.8 %collective-permute-start.29 = (bf16[2,128,384]{2,1,0:T(8,128)(2,1)S(1)}, bf16[2,128,384]{2,1,0:T(8,128)(2,1)S(1)}, u32[]{:S(2)}, u32[]{:S(2)}) collective-permute-start(bf16[2,128,384]{2,1,0:T(8,128)(2,1)S(1)} %pad_maximum_fusion.7), channel_id=1, source_target_pairs={{8,0},{9,1},{10,2},{11,3},{12,4},{13,5},{14,6},{15,7},{24,16},{25,... | collective-permute-start | bytes 589832 | tf_op jit(solution)/shard_map/ppermute | solution.py:205
  106.5 83.4 %collective-permute-start.30 = (bf16[2,128,384]{2,1,0:T(8,128)(2,1)S(1)}, bf16[2,128,384]{2,1,0:T(8,128)(2,1)S(1)}, u32[]{:S(2)}, u32[]{:S(2)}) collective-permute-start(bf16[2,128,384]{2,1,0:T(8,128)(2,1)S(1)} %pad_maximum_fusion.7), channel_id=1, source_target_pairs={{12,0},{13,1},{14,2},{15,3},{28,16},{29,17},{30,18},{31,19}} | collective-permute-start | bytes 589832 | tf_op jit(solution)/shard_map/ppermute | solution.py:205
  143.4 67.0 %collective-permute-start.23 = (bf16[2,4,128,1664]{3,2,1,0:T(8,128)(2,1)S(1)}, bf16[2,4,128,1664]{3,2,1,0:T(8,128)(2,1)S(1)}, u32[]{:S(2)}, u32[]{:S(2)}) collective-permute-start(bf16[2,4,128,1664]{3,2,1,0:T(8,128)(2,1)S(1)} %get-tuple-element.13), channel_id=1, source_target_pairs={{0,1},{1,0},{2,3},{3,2},{4,5},{5,4},{6,7},{7,6},{8,9},{9,8},{10,11... | collective-permute-start | bytes 10223624 | tf_op jit(solution)/shard_map/ppermute | solution.py:205
  178.3 36.1 %collective-permute-start.7 = (bf16[2,4,128,1664]{3,2,1,0:T(8,128)(2,1)S(1)}, bf16[2,4,128,1664]{3,2,1,0:T(8,128)(2,1)S(1)}, u32[]{:S(2)}, u32[]{:S(2)}) collective-permute-start(bf16[2,4,128,1664]{3,2,1,0:T(8,128)(2,1)S(1)} %get-tuple-element.15), channel_id=1, source_target_pairs={{0,1},{1,0},{2,3},{3,2},{4,5},{5,4},{6,7},{7,6},{8,9},{9,8},{10,11... | collective-permute-start | bytes 10223624 | tf_op jit(solution)/shard_map/ppermute | solution.py:205
  253.6 45.7 %collective-permute-start.56 = (bf16[2,4,128,1664]{3,2,1,0:T(8,128)(2,1)S(1)}, bf16[2,4,128,1664]{3,2,1,0:T(8,128)(2,1)}, u32[]{:S(2)}, u32[]{:S(2)}) collective-permute-start(bf16[2,4,128,1664]{3,2,1,0:T(8,128)(2,1)S(1)} %slice_bitcast_fusion.3), channel_id=1, source_target_pairs={{1,0},{0,1},{3,2},{2,3},{5,4},{4,5},{7,6},{6,7},{9,8},{8,9},{11,10... | collective-permute-start | bytes 10223624 | tf_op jit(solution)/shard_map/transpose()/ppermute | solution.py:205
  261.4 47.2 %collective-permute-start.40 = (bf16[2,4,128,1664]{3,2,0,1:T(8,128)(2,1)}, bf16[2,4,128,1664]{3,2,0,1:T(8,128)(2,1)}, u32[]{:S(2)}, u32[]{:S(2)}) collective-permute-start(bf16[2,4,128,1664]{3,2,0,1:T(8,128)(2,1)} %slice_bitcast_fusion.5), channel_id=1, source_target_pairs={{1,0},{0,1},{3,2},{2,3},{5,4},{4,5},{7,6},{6,7},{9,8},{8,9},{11,10... | collective-permute-start | bytes 10223624 | tf_op jit(solution)/shard_map/transpose()/ppermute | solution.py:205
  308.6 40.1 %collective-permute-start.57 = (bf16[4,128,1664]{2,1,0:T(8,128)(2,1)S(1)}, bf16[4,128,1664]{2,1,0:T(8,128)(2,1)S(1)}, u32[]{:S(2)}, u32[]{:S(2)}) collective-permute-start(bf16[4,128,1664]{2,1,0:T(8,128)(2,1)S(1)} %fusion.7), channel_id=1, source_target_pairs={{2,0},{3,1},{0,2},{1,3},{6,4},{7,5},{4,6},{5,7},{10,8},{11,9},{8,1... | collective-permute-start | bytes 5111816 | tf_op jit(solution)/shard_map/transpose()/ppermute | solution.py:205
  322.0 72.7 %collective-permute-start.55 = (bf16[128,384]{1,0:T(8,128)(2,1)S(1)}, bf16[128,384]{1,0:T(8,128)(2,1)S(1)}, u32[]{:S(2)}, u32[]{:S(2)}) collective-permute-start(bf16[128,384]{1,0:T(8,128)(2,1)S(1)} %fusion.40), channel_id=1, source_target_pairs={{2,0},{3,1},{0,2},{1,3},{6,4},{7,5},{4,6},{5,7},{10,8},{11,9},{8,1... | collective-permute-start | bytes 294920 | tf_op jit(solution)/shard_map/transpose()/ppermute | solution.py:205
  322.6 63.2 %collective-permute-start.41 = (bf16[4,128,1664]{2,1,0:T(8,128)(2,1)}, bf16[4,128,1664]{2,1,0:T(8,128)(2,1)}, u32[]{:S(2)}, u32[]{:S(2)}) collective-permute-start(bf16[4,128,1664]{2,1,0:T(8,128)(2,1)} %fusion.6), channel_id=1, source_target_pairs={{2,0},{3,1},{0,2},{1,3},{6,4},{7,5},{4,6},{5,7},{10,8},{11,9},{8,1... | collective-permute-start | bytes 5111816 | tf_op jit(solution)/shard_map/transpose()/ppermute | solution.py:205
  328.4 67.5 %collective-permute-start.39 = (bf16[128,384]{1,0:T(8,128)(2,1)S(1)}, bf16[128,384]{1,0:T(8,128)(2,1)S(1)}, u32[]{:S(2)}, u32[]{:S(2)}) collective-permute-start(bf16[128,384]{1,0:T(8,128)(2,1)S(1)} %fusion.39), channel_id=1, source_target_pairs={{2,0},{3,1},{0,2},{1,3},{6,4},{7,5},{4,6},{5,7},{10,8},{11,9},{8,1... | collective-permute-start | bytes 294920 | tf_op jit(solution)/shard_map/transpose()/ppermute | solution.py:205
  350.3 47.6 %collective-permute-start.58 = (bf16[128,1664]{1,0:T(8,128)(2,1)S(1)}, bf16[128,1664]{1,0:T(8,128)(2,1)S(1)}, u32[]{:S(2)}, u32[]{:S(2)}) collective-permute-start(bf16[128,1664]{1,0:T(8,128)(2,1)S(1)} %get-tuple-element.16), channel_id=1, source_target_pairs={{0,12},{1,13},{2,14},{3,15},{16,28},{17,29},{18,30},{19,31}} | collective-permute-start | bytes 1277960 | tf_op jit(solution)/shard_map/transpose()/ppermute | solution.py:205
  351.0 50.9 %collective-permute-start.59 = (bf16[128,1664]{1,0:T(8,128)(2,1)S(1)}, bf16[128,1664]{1,0:T(8,128)(2,1)S(1)}, u32[]{:S(2)}, u32[]{:S(2)}) collective-permute-start(bf16[128,1664]{1,0:T(8,128)(2,1)S(1)} %get-tuple-element.21), channel_id=1, source_target_pairs={{12,0},{13,1},{14,2},{15,3},{28,16},{29,17},{30,18},{31,19}} | collective-permute-start | bytes 1277960 | tf_op jit(solution)/shard_map/transpose()/ppermute | solution.py:205
  396.0 33.6 %collective-permute-start.62 = (bf16[128,1664]{1,0:T(8,128)(2,1)S(1)}, bf16[128,1664]{1,0:T(8,128)(2,1)S(1)}, u32[]{:S(2)}, u32[]{:S(2)}) collective-permute-start(bf16[128,1664]{1,0:T(8,128)(2,1)S(1)} %get-tuple-element.18), channel_id=1, source_target_pairs={{0,4},{1,5},{2,6},{3,7},{4,8},{5,9},{6,10},{7,11},{8,12},{9,13},{1... | collective-permute-start | bytes 1277960 | tf_op jit(solution)/shard_map/transpose()/ppermute | solution.py:205
  397.9 33.0 %collective-permute-start.63 = (bf16[128,1664]{1,0:T(8,128)(2,1)S(1)}, bf16[128,1664]{1,0:T(8,128)(2,1)S(1)}, u32[]{:S(2)}, u32[]{:S(2)}) collective-permute-start(bf16[128,1664]{1,0:T(8,128)(2,1)S(1)} %get-tuple-element.17), channel_id=1, source_target_pairs={{4,0},{5,1},{6,2},{7,3},{8,4},{9,5},{10,6},{11,7},{12,8},{13,9},{1... | collective-permute-start | bytes 1277960 | tf_op jit(solution)/shard_map/transpose()/ppermute | solution.py:205
  401.9 33.5 %collective-permute-start.42 = (bf16[128,1664]{1,0:T(8,128)(2,1)S(1)}, bf16[128,1664]{1,0:T(8,128)(2,1)S(1)}, u32[]{:S(2)}, u32[]{:S(2)}) collective-permute-start(bf16[128,1664]{1,0:T(8,128)(2,1)S(1)} %get-tuple-element.22), channel_id=1, source_target_pairs={{0,12},{1,13},{2,14},{3,15},{16,28},{17,29},{18,30},{19,31}} | collective-permute-start | bytes 1277960 | tf_op jit(solution)/shard_map/transpose()/ppermute | solution.py:205
  402.6 35.9 %collective-permute-start.43 = (bf16[128,1664]{1,0:T(8,128)(2,1)S(1)}, bf16[128,1664]{1,0:T(8,128)(2,1)S(1)}, u32[]{:S(2)}, u32[]{:S(2)}) collective-permute-start(bf16[128,1664]{1,0:T(8,128)(2,1)S(1)} %get-tuple-element.27), channel_id=1, source_target_pairs={{12,0},{13,1},{14,2},{15,3},{28,16},{29,17},{30,18},{31,19}} | collective-permute-start | bytes 1277960 | tf_op jit(solution)/shard_map/transpose()/ppermute | solution.py:205
  (50 other events, 957.8 us)

commit v3 on v1

--- a/solution.py
+++ b/solution.py
@@ -296,6 +296,26 @@
     )
 
 
+STREAMS = 2
+
+
+def _stream(pos, query, grad_out, keys, values):
+    n = lax.axis_size("seq")
+    rows, width = query.shape
+    line_len = n // 4
+    keys_local = gather_blocks(keys, n).reshape(n, rows, width)
+    values_local = gather_blocks(values, n).reshape(n, rows, width)
+    attended, grad_query, part_keys, part_values = attend_local(
+        pos, query, grad_out, keys_local, values_local
+    )
+    scatter = jax.linear_transpose(
+        lambda t: gather_blocks(t, n), jax.ShapeDtypeStruct((rows, width), jnp.float32)
+    )
+    (grad_keys,) = scatter(part_keys.reshape(2, 2, line_len, rows, width))
+    (grad_values,) = scatter(part_values.reshape(2, 2, line_len, rows, width))
+    return attended, grad_query, grad_keys.astype(jnp.bfloat16), grad_values.astype(jnp.bfloat16)
+
+
 def shards_gather(query, keys, values, grad_out, global_blocks, random_blocks):
     n = lax.axis_size("seq")
     rows, width = query.shape
@@ -312,22 +332,15 @@
     core = idx % 2
     ypos = (idx // 2) % 2
     pos = (((listed % 2) ^ core) * 2 + (((listed // 2) % 2) ^ ypos)) * line_len + listed // 4
-    keys_local = gather_blocks(keys, n).reshape(n, rows, width)
-    values_local = gather_blocks(values, n).reshape(n, rows, width)
-    attended, grad_query, part_keys, part_values = attend_local(
-        pos, query, grad_out, keys_local, values_local
-    )
-    scatter = jax.linear_transpose(
-        lambda t: gather_blocks(t, n), jax.ShapeDtypeStruct((rows, width), jnp.float32)
-    )
-    (grad_keys,) = scatter(part_keys.reshape(2, 2, line_len, rows, width))
-    (grad_values,) = scatter(part_values.reshape(2, 2, line_len, rows, width))
-    return (
-        attended,
-        grad_query,
-        grad_keys.astype(jnp.bfloat16),
-        grad_values.astype(jnp.bfloat16),
-    )
+    cut = width // STREAMS
+    outs = []
+    for s in range(STREAMS):
+        cols = slice(s * cut, (s + 1) * cut)
+        with jax.named_scope(f"stream{s}"):
+            outs.append(
+                _stream(pos, query[:, cols], grad_out[:, cols], keys[:, cols], values[:, cols])
+            )
+    return tuple(jnp.concatenate(parts, axis=1) for parts in zip(*outs))
 
 
 def shards(query, keys, values, grad_out, global_blocks, random_blocks):

time: 412 us -> 425 us (1.032)
  starting transfers between devices: 65.9 us -> 138 us
  waiting for transfers between devices: 233 us -> 184 us
  local copies, waits for them, and re-layouts: 35.3 us -> 28.6 us
  other arithmetic: 45.4 us -> 39.8 us
    ppermute x32 -> x64, starting transfers between devices: 65.9 us -> 138 us  [_send(): return lax.ppermute(v.astype(jnp.bfloat16), 'seq', pairs).astype(v.dtype)]
    ppermute x32 -> x64, waiting for transfers between devices: 233 us -> 184 us  [_send(): return lax.ppermute(v.astype(jnp.bfloat16), 'seq', pairs).astype(v.dtype)]
    add_any x2 -> x4, other arithmetic: 14.7 us -> 7.54 us  [_send(): return lax.ppermute(v.astype(jnp.bfloat16), 'seq', pairs).astype(v.dtype)]
    convert_element_type x4 -> x8, local copies, waits for them, and re-layouts: 6.73 us -> 0.77 us  [_send(): return lax.ppermute(v.astype(jnp.bfloat16), 'seq', pairs).astype(v.dtype)]
    another operation x4 -> x8, local copies, waits for them, and re-layouts: 21 us -> 16.4 us  [gather_blocks(): return jnp.stack([pair, sibling])]
    slice x0 -> x4, local copies, waits for them, and re-layouts: none -> 4.49 us  [the longest x1 1.77 us: shards_gather(): keys[:, cols]]
    another operation x4 -> x8, other arithmetic: 20.9 us -> 24.4 us  [gather_blocks(): return jnp.stack([pair, sibling])]
    pallas_call x1 -> x2, Pallas kernels: 26.9 us -> 29.7 us  [attend_local(): call(pos, query, grad_out, *[keys_local] * SLOTS, *[values_local] * SLOTS)]
  transfers between devices with their start and end apart: 32 -> 64, of which waited for: 18 -> 26; matrix products, arithmetic and copies ran while one was open for 16% -> 15% of each run, Pallas kernels for 0% -> 7%
where the time goes in v3:
time: 425 us; the launch traced here: 422 us
  waiting for transfers between devices  184 us (43%)
  starting transfers between devices  138 us (32%)
  other arithmetic  39.8 us (9%)
  Pallas kernels  29.7 us (7%)
  local copies, waits for them, and re-layouts  28.6 us (7%)
    ppermute x64, waiting for transfers between devices, _send(): return lax.ppermute(v.astype(jnp.bfloat16), 'seq', pairs).astype(v.dtype)  184 us
    ppermute x64, starting transfers between devices, _send(): return lax.ppermute(v.astype(jnp.bfloat16), 'seq', pairs).astype(v.dtype)  138 us
    pallas_call x2, Pallas kernels, attend_local(): call(pos, query, grad_out, *[keys_local] * SLOTS, *[values_local] * SLOTS)  29.7 us
    another operation x8, other arithmetic, gather_blocks(): return jnp.stack([pair, sibling])  24.4 us
    another operation x8, local copies, waits for them, and re-layouts, gather_blocks(): return jnp.stack([pair, sibling])  16.4 us
  transfers between devices with their start and end apart: 64, of which 26 were waited for; matrix products, arithmetic and copies ran while one was open for 15% of the time, Pallas kernels for 7%

profile of v3, /device:TPU:10, one launch (start us, length us, event | category | flops | bytes accessed | tf_op | source)
XLA Modules:
  0.0 421.9 jit_solution(5343753911277459303)
XLA Ops:
  17.5 4.4 %collective-permute-start.25 = (bf16[128,1024]{1,0:T(8,128)(2,1)S(1)}, bf16[128,1024]{1,0:T(8,128)(2,1)S(1)}, u32[]{:S(2)}, u32[]{:S(2)}) collective-permute-start(bf16[128,1024]{1,0:T(8,128)(2,1)S(1)} %collective-permute-done.24), channel_id=1, source_target_pairs={{4,8},{5,9},{6,10},{7,11},{8,12},{9,13},{10,14},{11,15},{20,24},{2... | collective-permute-start | bytes 786440 | tf_op jit(solution)/shard_map/stream1/ppermute | solution.py:205
  27.5 7.2 %collective-permute-start = (bf16[128,1024]{1,0:T(8,128)(2,1)}, bf16[128,1024]{1,0:T(8,128)(2,1)S(1)}, u32[]{:S(2)}, u32[]{:S(2)}) collective-permute-start(bf16[128,1024]{1,0:T(8,128)(2,1)} %get-tuple-element.50), channel_id=1, source_target_pairs={{0,4},{1,5},{2,6},{3,7},{4,8},{5,9},{6,10},{7,11},{8,12},{9,13},{1... | collective-permute-start | bytes 786440 | tf_op jit(solution)/shard_map/stream0/ppermute | solution.py:205
  39.4 11.0 %collective-permute-start.16 = (bf16[128,1024]{1,0:T(8,128)(2,1)S(1)}, bf16[128,1024]{1,0:T(8,128)(2,1)S(1)}, u32[]{:S(2)}, u32[]{:S(2)}) collective-permute-start(bf16[128,1024]{1,0:T(8,128)(2,1)S(1)} %get-tuple-element.51), channel_id=1, source_target_pairs={{0,4},{1,5},{2,6},{3,7},{4,8},{5,9},{6,10},{7,11},{8,12},{9,13},{1... | collective-permute-start | bytes 786440 | tf_op jit(solution)/shard_map/stream1/ppermute | solution.py:205
  56.1 4.2 collective-permute-start.17
  78.4 4.4 %collective-permute-start.5 = (bf16[128,1024]{1,0:T(8,128)(2,1)S(1)}, bf16[128,1024]{1,0:T(8,128)(2,1)S(1)}, u32[]{:S(2)}, u32[]{:S(2)}) collective-permute-start(bf16[128,1024]{1,0:T(8,128)(2,1)S(1)} %collective-permute-done.4), channel_id=1, source_target_pairs={{4,0},{5,1},{6,2},{7,3},{20,16},{21,17},{22,18},{23,19}} | collective-permute-start | bytes 786440 | tf_op jit(solution)/shard_map/stream0/ppermute | solution.py:205
  84.0 4.4 %collective-permute-start.29 = (bf16[128,1024]{1,0:T(8,128)(2,1)S(1)}, bf16[128,1024]{1,0:T(8,128)(2,1)S(1)}, u32[]{:S(2)}, u32[]{:S(2)}) collective-permute-start(bf16[128,1024]{1,0:T(8,128)(2,1)S(1)} %collective-permute-done.28), channel_id=1, source_target_pairs={{4,0},{5,1},{6,2},{7,3},{20,16},{21,17},{22,18},{23,19}} | collective-permute-start | bytes 786440 | tf_op jit(solution)/shard_map/stream1/ppermute | solution.py:205
  89.7 4.4 %collective-permute-start.21 = (bf16[128,1024]{1,0:T(8,128)(2,1)S(1)}, bf16[128,1024]{1,0:T(8,128)(2,1)S(1)}, u32[]{:S(2)}, u32[]{:S(2)}) collective-permute-start(bf16[128,1024]{1,0:T(8,128)(2,1)S(1)} %collective-permute-done.20), channel_id=1, source_target_pairs={{4,0},{5,1},{6,2},{7,3},{20,16},{21,17},{22,18},{23,19}} | collective-permute-start | bytes 786440 | tf_op jit(solution)/shard_map/stream1/ppermute | solution.py:205
  101.1 19.2 %collective-permute-done.14 = bf16[4,128,1024]{2,1,0:T(8,128)(2,1)S(1)} collective-permute-done((bf16[4,128,1024]{2,1,0:T(8,128)(2,1)S(1)}, bf16[4,128,1024]{2,1,0:T(8,128)(2,1)S(1)}, u32[]{:S(2)}, u32[]{:S(2)}) %collective-permute-start.14) | collective-permute-done | bytes 1048608 | tf_op jit(solution)/shard_map/stream0/ppermute | solution.py:205
  121.9 20.8 %collective-permute-done.6 = bf16[4,128,1024]{2,1,0:T(8,128)(2,1)S(1)} collective-permute-done((bf16[4,128,1024]{2,1,0:T(8,128)(2,1)S(1)}, bf16[4,128,1024]{2,1,0:T(8,128)(2,1)S(1)}, u32[]{:S(2)}, u32[]{:S(2)}) %collective-permute-start.6) | collective-permute-done | bytes 1048608 | tf_op jit(solution)/shard_map/stream0/ppermute | solution.py:205
  145.1 15.8 %collective-permute-done.30 = bf16[4,128,1024]{2,1,0:T(8,128)(2,1)S(1)} collective-permute-done((bf16[4,128,1024]{2,1,0:T(8,128)(2,1)S(1)}, bf16[4,128,1024]{2,1,0:T(8,128)(2,1)S(1)}, u32[]{:S(2)}, u32[]{:S(2)}) %collective-permute-start.30) | collective-permute-done | bytes 1048608 | tf_op jit(solution)/shard_map/stream1/ppermute | solution.py:205
  167.1 5.0 %collective-permute-done.22 = bf16[4,128,1024]{2,1,0:T(8,128)(2,1)S(1)} collective-permute-done((bf16[4,128,1024]{2,1,0:T(8,128)(2,1)S(1)}, bf16[4,128,1024]{2,1,0:T(8,128)(2,1)S(1)}, u32[]{:S(2)}, u32[]{:S(2)}) %collective-permute-start.22) | collective-permute-done | bytes 1048608 | tf_op jit(solution)/shard_map/stream1/ppermute | solution.py:205
  176.9 4.1 pad_maximum_fusion.1
  185.0 14.8 %stream0.1 = (bf16[128,1024]{1,0:T(8,128)(2,1)}, bf16[128,1024]{1,0:T(8,128)(2,1)}, f32[16,128,1024]{2,1,0:T(8,128)}, f32[16,128,1024]{2,1,0:T(8,128)}) custom-call(s32[8]{0:T(128)} %multiply_add_fusion.pos_ref, bf16[128,1024]{1,0:T(8,128)(2,1)} %get-tuple-element.54.q_ref, bf16[128,1024]{1,0:T(8,128)(2,1)} %get-tuple-element.52.g_ref, ...), custom_call_target="tpu_custom_call" | custom-call | flops 1610612736 | bytes 22020096 | tf_op jit(solution)/shard_map/stream0/pallas_call | solution.py:294
  207.9 4.1 pad_maximum_fusion.3
  215.9 14.9 %stream1.1 = (bf16[128,1024]{1,0:T(8,128)(2,1)}, bf16[128,1024]{1,0:T(8,128)(2,1)}, f32[16,128,1024]{2,1,0:T(8,128)}, f32[16,128,1024]{2,1,0:T(8,128)}) custom-call(s32[8]{0:T(128)} %multiply_add_fusion.pos_ref, bf16[128,1024]{1,0:T(8,128)(2,1)} %get-tuple-element.55.q_ref, bf16[128,1024]{1,0:T(8,128)(2,1)} %get-tuple-element.53.g_ref, ...), custom_call_target="tpu_custom_call" | custom-call | flops 1610612736 | bytes 22020096 | tf_op jit(solution)/shard_map/stream1/pallas_call | solution.py:294
  261.5 16.0 %collective-permute-done.49 = bf16[4,128,1024]{2,1,0:T(8,128)(2,1)S(1)} collective-permute-done((bf16[4,128,1024]{2,1,0:T(8,128)(2,1)S(1)}, bf16[4,128,1024]{2,1,0:T(8,128)(2,1)S(1)}, u32[]{:S(2)}, u32[]{:S(2)}) %collective-permute-start.49) | collective-permute-done | bytes 1048608 | tf_op jit(solution)/shard_map/stream0/transpose()/ppermute | solution.py:205
  280.8 19.2 %collective-permute-done.57 = bf16[4,128,1024]{2,1,0:T(8,128)(2,1)S(1)} collective-permute-done((bf16[4,128,1024]{2,1,0:T(8,128)(2,1)S(1)}, bf16[4,128,1024]{2,1,0:T(8,128)(2,1)S(1)}, u32[]{:S(2)}, u32[]{:S(2)}) %collective-permute-start.57) | collective-permute-done | bytes 1048608 | tf_op jit(solution)/shard_map/stream1/transpose()/ppermute | solution.py:205
  302.6 19.9 %collective-permute-done.33 = bf16[4,128,1024]{2,1,0:T(8,128)(2,1)S(1)} collective-permute-done((bf16[4,128,1024]{2,1,0:T(8,128)(2,1)S(1)}, bf16[4,128,1024]{2,1,0:T(8,128)(2,1)S(1)}, u32[]{:S(2)}, u32[]{:S(2)}) %collective-permute-start.33) | collective-permute-done | bytes 1048608 | tf_op jit(solution)/shard_map/stream0/transpose()/ppermute | solution.py:205
  324.4 19.9 %collective-permute-done.41 = bf16[4,128,1024]{2,1,0:T(8,128)(2,1)S(1)} collective-permute-done((bf16[4,128,1024]{2,1,0:T(8,128)(2,1)S(1)}, bf16[4,128,1024]{2,1,0:T(8,128)(2,1)S(1)}, u32[]{:S(2)}, u32[]{:S(2)}) %collective-permute-start.41) | collective-permute-done | bytes 1048608 | tf_op jit(solution)/shard_map/stream1/transpose()/ppermute | solution.py:205
  349.2 6.1 %collective-permute-done.34 = bf16[128,1024]{1,0:T(8,128)(2,1)S(1)} collective-permute-done((bf16[128,1024]{1,0:T(8,128)(2,1)S(1)}, bf16[128,1024]{1,0:T(8,128)(2,1)S(1)}, u32[]{:S(2)}, u32[]{:S(2)}) %collective-permute-start.34) | collective-permute-done | bytes 262176 | tf_op jit(solution)/shard_map/stream0/transpose()/ppermute | solution.py:205
  374.3 4.6 %collective-permute-start.52 = (bf16[128,1024]{1,0:T(8,128)(2,1)S(1)}, bf16[128,1024]{1,0:T(8,128)(2,1)S(1)}, u32[]{:S(2)}, u32[]{:S(2)}) collective-permute-start(bf16[128,1024]{1,0:T(8,128)(2,1)S(1)} %get-tuple-element.20), channel_id=1, source_target_pairs={{0,4},{1,5},{2,6},{3,7},{4,8},{5,9},{6,10},{7,11},{8,12},{9,13},{1... | collective-permute-start | bytes 786440 | tf_op jit(solution)/shard_map/stream0/transpose()/ppermute | solution.py:205
  380.3 4.6 %collective-permute-start.60 = (bf16[128,1024]{1,0:T(8,128)(2,1)S(1)}, bf16[128,1024]{1,0:T(8,128)(2,1)S(1)}, u32[]{:S(2)}, u32[]{:S(2)}) collective-permute-start(bf16[128,1024]{1,0:T(8,128)(2,1)S(1)} %get-tuple-element.22), channel_id=1, source_target_pairs={{0,4},{1,5},{2,6},{3,7},{4,8},{5,9},{6,10},{7,11},{8,12},{9,13},{1... | collective-permute-start | bytes 786440 | tf_op jit(solution)/shard_map/stream1/transpose()/ppermute | solution.py:205
  386.3 4.6 %collective-permute-start.36 = (bf16[128,1024]{1,0:T(8,128)(2,1)S(1)}, bf16[128,1024]{1,0:T(8,128)(2,1)S(1)}, u32[]{:S(2)}, u32[]{:S(2)}) collective-permute-start(bf16[128,1024]{1,0:T(8,128)(2,1)S(1)} %get-tuple-element.24), channel_id=1, source_target_pairs={{0,4},{1,5},{2,6},{3,7},{4,8},{5,9},{6,10},{7,11},{8,12},{9,13},{1... | collective-permute-start | bytes 786440 | tf_op jit(solution)/shard_map/stream0/transpose()/ppermute | solution.py:205
  397.9 4.1 collective-permute-done.46
  (246 shorter events, 182.3 us)
Async XLA Ops:
  23.8 26.6 %collective-permute-start.11 = (bf16[128,1024]{1,0:T(8,128)(2,1)S(1)}, bf16[128,1024]{1,0:T(8,128)(2,1)S(1)}, u32[]{:S(2)}, u32[]{:S(2)}) collective-permute-start(bf16[128,1024]{1,0:T(8,128)(2,1)S(1)} %get-tuple-element.46), channel_id=1, source_target_pairs={{4,0},{5,1},{6,2},{7,3},{8,4},{9,5},{10,6},{11,7},{12,8},{13,9},{1... | collective-permute-start | bytes 786440 | tf_op jit(solution)/shard_map/stream0/ppermute | solution.py:205
  27.5 28.6 %collective-permute-start = (bf16[128,1024]{1,0:T(8,128)(2,1)}, bf16[128,1024]{1,0:T(8,128)(2,1)S(1)}, u32[]{:S(2)}, u32[]{:S(2)}) collective-permute-start(bf16[128,1024]{1,0:T(8,128)(2,1)} %get-tuple-element.50), channel_id=1, source_target_pairs={{0,4},{1,5},{2,6},{3,7},{4,8},{5,9},{6,10},{7,11},{8,12},{9,13},{1... | collective-permute-start | bytes 786440 | tf_op jit(solution)/shard_map/stream0/ppermute | solution.py:205
  36.7 27.5 %collective-permute-start.27 = (bf16[128,1024]{1,0:T(8,128)(2,1)S(1)}, bf16[128,1024]{1,0:T(8,128)(2,1)S(1)}, u32[]{:S(2)}, u32[]{:S(2)}) collective-permute-start(bf16[128,1024]{1,0:T(8,128)(2,1)S(1)} %get-tuple-element.47), channel_id=1, source_target_pairs={{4,0},{5,1},{6,2},{7,3},{8,4},{9,5},{10,6},{11,7},{12,8},{13,9},{1... | collective-permute-start | bytes 786440 | tf_op jit(solution)/shard_map/stream1/ppermute | solution.py:205
  94.2 26.1 %collective-permute-start.14 = (bf16[4,128,1024]{2,1,0:T(8,128)(2,1)S(1)}, bf16[4,128,1024]{2,1,0:T(8,128)(2,1)S(1)}, u32[]{:S(2)}, u32[]{:S(2)}) collective-permute-start(bf16[4,128,1024]{2,1,0:T(8,128)(2,1)S(1)} %constant_dynamic-slice_fusion.2), channel_id=1, source_target_pairs={{0,2},{1,3},{2,0},{3,1},{4,6},{5,7},{6,4},{7,5},{8,10},{9,11},{10,... | collective-permute-start | bytes 3145736 | tf_op jit(solution)/shard_map/stream0/ppermute | solution.py:205
  96.2 46.6 %collective-permute-start.6 = (bf16[4,128,1024]{2,1,0:T(8,128)(2,1)S(1)}, bf16[4,128,1024]{2,1,0:T(8,128)(2,1)S(1)}, u32[]{:S(2)}, u32[]{:S(2)}) collective-permute-start(bf16[4,128,1024]{2,1,0:T(8,128)(2,1)S(1)} %constant_dynamic-slice_fusion.3), channel_id=1, source_target_pairs={{0,2},{1,3},{2,0},{3,1},{4,6},{5,7},{6,4},{7,5},{8,10},{9,11},{10,... | collective-permute-start | bytes 3145736 | tf_op jit(solution)/shard_map/stream0/ppermute | solution.py:205
  97.2 63.8 %collective-permute-start.30 = (bf16[4,128,1024]{2,1,0:T(8,128)(2,1)S(1)}, bf16[4,128,1024]{2,1,0:T(8,128)(2,1)S(1)}, u32[]{:S(2)}, u32[]{:S(2)}) collective-permute-start(bf16[4,128,1024]{2,1,0:T(8,128)(2,1)S(1)} %constant_dynamic-slice_fusion), channel_id=1, source_target_pairs={{0,2},{1,3},{2,0},{3,1},{4,6},{5,7},{6,4},{7,5},{8,10},{9,11},{10,... | collective-permute-start | bytes 3145736 | tf_op jit(solution)/shard_map/stream1/ppermute | solution.py:205
  99.4 72.8 %collective-permute-start.22 = (bf16[4,128,1024]{2,1,0:T(8,128)(2,1)S(1)}, bf16[4,128,1024]{2,1,0:T(8,128)(2,1)S(1)}, u32[]{:S(2)}, u32[]{:S(2)}) collective-permute-start(bf16[4,128,1024]{2,1,0:T(8,128)(2,1)S(1)} %constant_dynamic-slice_fusion.1), channel_id=1, source_target_pairs={{0,2},{1,3},{2,0},{3,1},{4,6},{5,7},{6,4},{7,5},{8,10},{9,11},{10,... | collective-permute-start | bytes 3145736 | tf_op jit(solution)/shard_map/stream1/ppermute | solution.py:205
  121.9 55.0 %collective-permute-start.15 = (bf16[2,4,128,1024]{3,2,1,0:T(8,128)(2,1)}, bf16[2,4,128,1024]{3,2,1,0:T(8,128)(2,1)}, u32[]{:S(2)}, u32[]{:S(2)}) collective-permute-start(bf16[2,4,128,1024]{3,2,1,0:T(8,128)(2,1)} %get-tuple-element.29), channel_id=1, source_target_pairs={{0,1},{1,0},{2,3},{3,2},{4,5},{5,4},{6,7},{7,6},{8,9},{9,8},{10,11... | collective-permute-start | bytes 6291464 | tf_op jit(solution)/shard_map/stream0/ppermute | solution.py:205
  145.0 36.0 %collective-permute-start.7 = (bf16[2,4,128,1024]{3,2,1,0:T(8,128)(2,1)}, bf16[2,4,128,1024]{3,2,1,0:T(8,128)(2,1)}, u32[]{:S(2)}, u32[]{:S(2)}) collective-permute-start(bf16[2,4,128,1024]{3,2,1,0:T(8,128)(2,1)} %get-tuple-element.31), channel_id=1, source_target_pairs={{0,1},{1,0},{2,3},{3,2},{4,5},{5,4},{6,7},{7,6},{8,9},{9,8},{10,11... | collective-permute-start | bytes 6291464 | tf_op jit(solution)/shard_map/stream0/ppermute | solution.py:205
  163.2 44.7 %collective-permute-start.31 = (bf16[2,4,128,1024]{3,2,1,0:T(8,128)(2,1)}, bf16[2,4,128,1024]{3,2,1,0:T(8,128)(2,1)}, u32[]{:S(2)}, u32[]{:S(2)}) collective-permute-start(bf16[2,4,128,1024]{3,2,1,0:T(8,128)(2,1)} %get-tuple-element.33), channel_id=1, source_target_pairs={{0,1},{1,0},{2,3},{3,2},{4,5},{5,4},{6,7},{7,6},{8,9},{9,8},{10,11... | collective-permute-start | bytes 6291464 | tf_op jit(solution)/shard_map/stream1/ppermute | solution.py:205
  174.4 37.6 %collective-permute-start.23 = (bf16[2,4,128,1024]{3,2,1,0:T(8,128)(2,1)}, bf16[2,4,128,1024]{3,2,1,0:T(8,128)(2,1)}, u32[]{:S(2)}, u32[]{:S(2)}) collective-permute-start(bf16[2,4,128,1024]{3,2,1,0:T(8,128)(2,1)} %get-tuple-element.35), channel_id=1, source_target_pairs={{0,1},{1,0},{2,3},{3,2},{4,5},{5,4},{6,7},{7,6},{8,9},{9,8},{10,11... | collective-permute-start | bytes 6291464 | tf_op jit(solution)/shard_map/stream1/ppermute | solution.py:205
  203.8 45.2 %collective-permute-start.48 = (bf16[2,4,128,1024]{3,2,1,0:T(8,128)(2,1)}, bf16[2,4,128,1024]{3,2,1,0:T(8,128)(2,1)}, u32[]{:S(2)}, u32[]{:S(2)}) collective-permute-start(bf16[2,4,128,1024]{3,2,1,0:T(8,128)(2,1)} %bitcast.74), channel_id=1, source_target_pairs={{1,0},{0,1},{3,2},{2,3},{5,4},{4,5},{7,6},{6,7},{9,8},{8,9},{11,10... | collective-permute-start | bytes 6291464 | tf_op jit(solution)/shard_map/stream0/transpose()/ppermute | solution.py:205
  251.4 26.1 %collective-permute-start.49 = (bf16[4,128,1024]{2,1,0:T(8,128)(2,1)S(1)}, bf16[4,128,1024]{2,1,0:T(8,128)(2,1)S(1)}, u32[]{:S(2)}, u32[]{:S(2)}) collective-permute-start(bf16[4,128,1024]{2,1,0:T(8,128)(2,1)S(1)} %fusion.10), channel_id=1, source_target_pairs={{2,0},{3,1},{0,2},{1,3},{6,4},{7,5},{4,6},{5,7},{10,8},{11,9},{8,1... | collective-permute-start | bytes 3145736 | tf_op jit(solution)/shard_map/stream0/transpose()/ppermute | solution.py:205
  255.4 44.6 %collective-permute-start.57 = (bf16[4,128,1024]{2,1,0:T(8,128)(2,1)S(1)}, bf16[4,128,1024]{2,1,0:T(8,128)(2,1)S(1)}, u32[]{:S(2)}, u32[]{:S(2)}) collective-permute-start(bf16[4,128,1024]{2,1,0:T(8,128)(2,1)S(1)} %fusion.11), channel_id=1, source_target_pairs={{2,0},{3,1},{0,2},{1,3},{6,4},{7,5},{4,6},{5,7},{10,8},{11,9},{8,1... | collective-permute-start | bytes 3145736 | tf_op jit(solution)/shard_map/stream1/transpose()/ppermute | solution.py:205
  258.4 64.0 %collective-permute-start.33 = (bf16[4,128,1024]{2,1,0:T(8,128)(2,1)S(1)}, bf16[4,128,1024]{2,1,0:T(8,128)(2,1)S(1)}, u32[]{:S(2)}, u32[]{:S(2)}) collective-permute-start(bf16[4,128,1024]{2,1,0:T(8,128)(2,1)S(1)} %fusion.8), channel_id=1, source_target_pairs={{2,0},{3,1},{0,2},{1,3},{6,4},{7,5},{4,6},{5,7},{10,8},{11,9},{8,1... | collective-permute-start | bytes 3145736 | tf_op jit(solution)/shard_map/stream0/transpose()/ppermute | solution.py:205
  260.9 83.4 %collective-permute-start.41 = (bf16[4,128,1024]{2,1,0:T(8,128)(2,1)S(1)}, bf16[4,128,1024]{2,1,0:T(8,128)(2,1)S(1)}, u32[]{:S(2)}, u32[]{:S(2)}) collective-permute-start(bf16[4,128,1024]{2,1,0:T(8,128)(2,1)S(1)} %fusion.9), channel_id=1, source_target_pairs={{2,0},{3,1},{0,2},{1,3},{6,4},{7,5},{4,6},{5,7},{10,8},{11,9},{8,1... | collective-permute-start | bytes 3145736 | tf_op jit(solution)/shard_map/stream1/transpose()/ppermute | solution.py:205
  278.8 68.3 %collective-permute-start.50 = (bf16[128,1024]{1,0:T(8,128)(2,1)S(1)}, bf16[128,1024]{1,0:T(8,128)(2,1)S(1)}, u32[]{:S(2)}, u32[]{:S(2)}) collective-permute-start(bf16[128,1024]{1,0:T(8,128)(2,1)S(1)} %get-tuple-element.36), channel_id=1, source_target_pairs={{0,4},{1,5},{2,6},{3,7},{16,20},{17,21},{18,22},{19,23}} | collective-permute-start | bytes 786440 | tf_op jit(solution)/shard_map/stream0/transpose()/ppermute | solution.py:205
  280.1 81.6 %collective-permute-start.53 = (bf16[128,1024]{1,0:T(8,128)(2,1)S(1)}, bf16[128,1024]{1,0:T(8,128)(2,1)S(1)}, u32[]{:S(2)}, u32[]{:S(2)}) collective-permute-start(bf16[128,1024]{1,0:T(8,128)(2,1)S(1)} %get-tuple-element.37), channel_id=1, source_target_pairs={{12,8},{13,9},{14,10},{15,11},{28,24},{29,25},{30,26},{31,27}} | collective-permute-start | bytes 786440 | tf_op jit(solution)/shard_map/stream0/transpose()/ppermute | solution.py:205
  301.3 46.6 %collective-permute-start.58 = (bf16[128,1024]{1,0:T(8,128)(2,1)S(1)}, bf16[128,1024]{1,0:T(8,128)(2,1)S(1)}, u32[]{:S(2)}, u32[]{:S(2)}) collective-permute-start(bf16[128,1024]{1,0:T(8,128)(2,1)S(1)} %get-tuple-element.38), channel_id=1, source_target_pairs={{0,4},{1,5},{2,6},{3,7},{16,20},{17,21},{18,22},{19,23}} | collective-permute-start | bytes 786440 | tf_op jit(solution)/shard_map/stream1/transpose()/ppermute | solution.py:205
  322.5 46.2 %collective-permute-start.61 = (bf16[128,1024]{1,0:T(8,128)(2,1)S(1)}, bf16[128,1024]{1,0:T(8,128)(2,1)S(1)}, u32[]{:S(2)}, u32[]{:S(2)}) collective-permute-start(bf16[128,1024]{1,0:T(8,128)(2,1)S(1)} %get-tuple-element.39), channel_id=1, source_target_pairs={{12,8},{13,9},{14,10},{15,11},{28,24},{29,25},{30,26},{31,27}} | collective-permute-start | bytes 786440 | tf_op jit(solution)/shard_map/stream1/transpose()/ppermute | solution.py:205
  347.1 27.2 %collective-permute-start.37 = (bf16[128,1024]{1,0:T(8,128)(2,1)S(1)}, bf16[128,1024]{1,0:T(8,128)(2,1)S(1)}, u32[]{:S(2)}, u32[]{:S(2)}) collective-permute-start(bf16[128,1024]{1,0:T(8,128)(2,1)S(1)} %get-tuple-element.41), channel_id=1, source_target_pairs={{12,8},{13,9},{14,10},{15,11},{28,24},{29,25},{30,26},{31,27}} | collective-permute-start | bytes 786440 | tf_op jit(solution)/shard_map/stream0/transpose()/ppermute | solution.py:205
  374.3 29.8 %collective-permute-start.52 = (bf16[128,1024]{1,0:T(8,128)(2,1)S(1)}, bf16[128,1024]{1,0:T(8,128)(2,1)S(1)}, u32[]{:S(2)}, u32[]{:S(2)}) collective-permute-start(bf16[128,1024]{1,0:T(8,128)(2,1)S(1)} %get-tuple-element.20), channel_id=1, source_target_pairs={{0,4},{1,5},{2,6},{3,7},{4,8},{5,9},{6,10},{7,11},{8,12},{9,13},{1... | collective-permute-start | bytes 786440 | tf_op jit(solution)/shard_map/stream0/transpose()/ppermute | solution.py:205
  380.3 29.8 %collective-permute-start.60 = (bf16[128,1024]{1,0:T(8,128)(2,1)S(1)}, bf16[128,1024]{1,0:T(8,128)(2,1)S(1)}, u32[]{:S(2)}, u32[]{:S(2)}) collective-permute-start(bf16[128,1024]{1,0:T(8,128)(2,1)S(1)} %get-tuple-element.22), channel_id=1, source_target_pairs={{0,4},{1,5},{2,6},{3,7},{4,8},{5,9},{6,10},{7,11},{8,12},{9,13},{1... | collective-permute-start | bytes 786440 | tf_op jit(solution)/shard_map/stream1/transpose()/ppermute | solution.py:205
  386.3 27.9 %collective-permute-start.36 = (bf16[128,1024]{1,0:T(8,128)(2,1)S(1)}, bf16[128,1024]{1,0:T(8,128)(2,1)S(1)}, u32[]{:S(2)}, u32[]{:S(2)}) collective-permute-start(bf16[128,1024]{1,0:T(8,128)(2,1)S(1)} %get-tuple-element.24), channel_id=1, source_target_pairs={{0,4},{1,5},{2,6},{3,7},{4,8},{5,9},{6,10},{7,11},{8,12},{9,13},{1... | collective-permute-start | bytes 786440 | tf_op jit(solution)/shard_map/stream0/transpose()/ppermute | solution.py:205
  (59 other events, 849.8 us)

commit v4 on v3

--- a/solution.py
+++ b/solution.py
@@ -299,10 +299,12 @@
 STREAMS = 2
 
 
-def _stream(pos, query, grad_out, keys, values):
+def _stream(pos, query, grad_out, keys, values, after=None):
     n = lax.axis_size("seq")
     rows, width = query.shape
     line_len = n // 4
+    if after is not None:
+        keys, values, _ = lax.optimization_barrier((keys, values, after))
     keys_local = gather_blocks(keys, n).reshape(n, rows, width)
     values_local = gather_blocks(values, n).reshape(n, rows, width)
     attended, grad_query, part_keys, part_values = attend_local(
@@ -313,7 +315,8 @@
     )
     (grad_keys,) = scatter(part_keys.reshape(2, 2, line_len, rows, width))
     (grad_values,) = scatter(part_values.reshape(2, 2, line_len, rows, width))
-    return attended, grad_query, grad_keys.astype(jnp.bfloat16), grad_values.astype(jnp.bfloat16)
+    outs = (attended, grad_query, grad_keys.astype(jnp.bfloat16), grad_values.astype(jnp.bfloat16))
+    return outs, (keys_local, values_local)
 
 
 def shards_gather(query, keys, values, grad_out, global_blocks, random_blocks):
@@ -334,12 +337,14 @@
     pos = (((listed % 2) ^ core) * 2 + (((listed // 2) % 2) ^ ypos)) * line_len + listed // 4
     cut = width // STREAMS
     outs = []
+    after = None
     for s in range(STREAMS):
         cols = slice(s * cut, (s + 1) * cut)
         with jax.named_scope(f"stream{s}"):
-            outs.append(
-                _stream(pos, query[:, cols], grad_out[:, cols], keys[:, cols], values[:, cols])
+            out, after = _stream(
+                pos, query[:, cols], grad_out[:, cols], keys[:, cols], values[:, cols], after
             )
+            outs.append(out)
     return tuple(jnp.concatenate(parts, axis=1) for parts in zip(*outs))
 
 

time: 425 us -> 388 us (0.913)
  starting transfers between devices: 138 us -> 115 us
  other arithmetic: 39.8 us -> 29.8 us
    ppermute x64, starting transfers between devices: 138 us -> 115 us  [_send(): return lax.ppermute(v.astype(jnp.bfloat16), 'seq', pairs).astype(v.dtype)]
    another operation x8, other arithmetic: 24.4 us -> 13.9 us  [gather_blocks(): return jnp.stack([pair, sibling])]
  transfers between devices with their start and end apart: 64 -> 64, of which waited for: 26 -> 24; matrix products, arithmetic and copies ran while one was open for 15% -> 12% of each run, Pallas kernels for 7% -> 8%
where the time goes in v4:
time: 388 us; the launch traced here: 384 us
  waiting for transfers between devices  182 us (47%)
  starting transfers between devices  115 us (30%)
  other arithmetic  29.8 us (8%)
  Pallas kernels  29.7 us (8%)
  local copies, waits for them, and re-layouts  25 us (6%)
    ppermute x64, waiting for transfers between devices, _send(): return lax.ppermute(v.astype(jnp.bfloat16), 'seq', pairs).astype(v.dtype)  182 us
    ppermute x64, starting transfers between devices, _send(): return lax.ppermute(v.astype(jnp.bfloat16), 'seq', pairs).astype(v.dtype)  115 us
    pallas_call x2, Pallas kernels, attend_local(): call(pos, query, grad_out, *[keys_local] * SLOTS, *[values_local] * SLOTS)  29.7 us
    another operation x8, other arithmetic, gather_blocks(): return jnp.stack([pair, sibling])  13.9 us
    another operation x8, local copies, waits for them, and re-layouts, gather_blocks(): return jnp.stack([pair, sibling])  12.3 us
  transfers between devices with their start and end apart: 64, of which 24 were waited for; matrix products, arithmetic and copies ran while one was open for 12% of the time, Pallas kernels for 8%

profile of v4, /device:TPU:10, one launch (start us, length us, event | category | flops | bytes accessed | tf_op | source)
XLA Modules:
  0.0 383.7 jit_solution(18405273316422982964)
XLA Ops:
  20.0 3.9 %collective-permute-start.1 = (bf16[128,1024]{1,0:T(8,128)(2,1)S(1)}, bf16[128,1024]{1,0:T(8,128)(2,1)S(1)}, u32[]{:S(2)}, u32[]{:S(2)}) collective-permute-start(bf16[128,1024]{1,0:T(8,128)(2,1)S(1)} %collective-permute-done), channel_id=1, source_target_pairs={{4,8},{5,9},{6,10},{7,11},{8,12},{9,13},{10,14},{11,15},{20,24},{2... | collective-permute-start | bytes 786440 | tf_op jit(solution)/shard_map/stream0/ppermute | solution.py:205
  32.6 4.4 %collective-permute-start.5 = (bf16[128,1024]{1,0:T(8,128)(2,1)S(1)}, bf16[128,1024]{1,0:T(8,128)(2,1)S(1)}, u32[]{:S(2)}, u32[]{:S(2)}) collective-permute-start(bf16[128,1024]{1,0:T(8,128)(2,1)S(1)} %collective-permute-done.4), channel_id=1, source_target_pairs={{4,0},{5,1},{6,2},{7,3},{20,16},{21,17},{22,18},{23,19}} | collective-permute-start | bytes 786440 | tf_op jit(solution)/shard_map/stream0/ppermute | solution.py:205
  43.5 20.9 %collective-permute-done.14 = bf16[4,128,1024]{2,1,0:T(8,128)(2,1)S(1)} collective-permute-done((bf16[4,128,1024]{2,1,0:T(8,128)(2,1)S(1)}, bf16[4,128,1024]{2,1,0:T(8,128)(2,1)S(1)}, u32[]{:S(2)}, u32[]{:S(2)}) %collective-permute-start.14) | collective-permute-done | bytes 1048608 | tf_op jit(solution)/shard_map/stream0/ppermute | solution.py:205
  64.9 17.0 %collective-permute-done.6 = bf16[4,128,1024]{2,1,0:T(8,128)(2,1)S(1)} collective-permute-done((bf16[4,128,1024]{2,1,0:T(8,128)(2,1)S(1)}, bf16[4,128,1024]{2,1,0:T(8,128)(2,1)S(1)}, u32[]{:S(2)}, u32[]{:S(2)}) %collective-permute-start.6) | collective-permute-done | bytes 1048608 | tf_op jit(solution)/shard_map/stream0/ppermute | solution.py:205
  90.7 3.9 %collective-permute-start.27 = (bf16[128,1024]{1,0:T(8,128)(2,1)S(1)}, bf16[128,1024]{1,0:T(8,128)(2,1)S(1)}, u32[]{:S(2)}, u32[]{:S(2)}) collective-permute-start(bf16[128,1024]{1,0:T(8,128)(2,1)S(1)} %get-tuple-element.16), channel_id=1, source_target_pairs={{4,0},{5,1},{6,2},{7,3},{8,4},{9,5},{10,6},{11,7},{12,8},{13,9},{1... | collective-permute-start | bytes 786440 | tf_op jit(solution)/shard_map/stream1/ppermute | solution.py:205
  106.7 3.9 %collective-permute-start.17 = (bf16[128,1024]{1,0:T(8,128)(2,1)S(1)}, bf16[128,1024]{1,0:T(8,128)(2,1)S(1)}, u32[]{:S(2)}, u32[]{:S(2)}) collective-permute-start(bf16[128,1024]{1,0:T(8,128)(2,1)S(1)} %collective-permute-done.16), channel_id=1, source_target_pairs={{4,8},{5,9},{6,10},{7,11},{8,12},{9,13},{10,14},{11,15},{20,24},{2... | collective-permute-start | bytes 786440 | tf_op jit(solution)/shard_map/stream1/ppermute | solution.py:205
  113.8 14.8 %stream0.1 = (bf16[128,1024]{1,0:T(8,128)(2,1)}, bf16[128,1024]{1,0:T(8,128)(2,1)}, f32[16,128,1024]{2,1,0:T(8,128)}, f32[16,128,1024]{2,1,0:T(8,128)}) custom-call(s32[8]{0:T(128)} %multiply_add_fusion.pos_ref, bf16[128,1024]{1,0:T(8,128)(2,1)} %get-tuple-element.50.q_ref, bf16[128,1024]{1,0:T(8,128)(2,1)} %get-tuple-element.48.g_ref, ...), custom_call_target="tpu_custom_call" | custom-call | flops 1610612736 | bytes 22020096 | tf_op jit(solution)/shard_map/stream0/pallas_call | solution.py:294
  135.1 4.3 %collective-permute-done.29 = bf16[128,1024]{1,0:T(8,128)(2,1)S(1)} collective-permute-done((bf16[128,1024]{1,0:T(8,128)(2,1)S(1)}, bf16[128,1024]{1,0:T(8,128)(2,1)S(1)}, u32[]{:S(2)}, u32[]{:S(2)}) %collective-permute-start.29) | collective-permute-done | bytes 262176 | tf_op jit(solution)/shard_map/stream1/ppermute | solution.py:205
  149.8 15.8 %collective-permute-done.30 = bf16[4,128,1024]{2,1,0:T(8,128)(2,1)S(1)} collective-permute-done((bf16[4,128,1024]{2,1,0:T(8,128)(2,1)S(1)}, bf16[4,128,1024]{2,1,0:T(8,128)(2,1)S(1)}, u32[]{:S(2)}, u32[]{:S(2)}) %collective-permute-start.30) | collective-permute-done | bytes 1048608 | tf_op jit(solution)/shard_map/stream1/ppermute | solution.py:205
  165.9 20.8 %collective-permute-done.22 = bf16[4,128,1024]{2,1,0:T(8,128)(2,1)S(1)} collective-permute-done((bf16[4,128,1024]{2,1,0:T(8,128)(2,1)S(1)}, bf16[4,128,1024]{2,1,0:T(8,128)(2,1)S(1)}, u32[]{:S(2)}, u32[]{:S(2)}) %collective-permute-start.22) | collective-permute-done | bytes 1048608 | tf_op jit(solution)/shard_map/stream1/ppermute | solution.py:205
  193.3 22.4 %collective-permute-done.49 = bf16[4,128,1024]{2,1,0:T(8,128)(2,1)} collective-permute-done((bf16[4,128,1024]{2,1,0:T(8,128)(2,1)}, bf16[4,128,1024]{2,1,0:T(8,128)(2,1)}, u32[]{:S(2)}, u32[]{:S(2)}) %collective-permute-start.49) | collective-permute-done | bytes 1048608 | tf_op jit(solution)/shard_map/stream0/transpose()/ppermute | solution.py:205
  219.6 4.0 %pad_maximum_fusion.3 = bf16[2,2,4,128,1024]{4,3,2,1,0:T(8,128)(2,1)} fusion(bf16[1,2,4,128,1024]{4,3,2,1,0:T(8,128)(2,1)} %bitcast.49, bf16[1,2,4,128,1024]{4,3,2,1,0:T(8,128)(2,1)S(1)} %get-tuple-element.32), kind=kLoop, calls=%fused_computation.7 | loop fusion | flops 2097152 | bytes 8388608 | tf_op jit(solution)/shard_map/stream1/stack | solution.py:227
  223.6 4.1 %pad_maximum_fusion.2 = bf16[2,2,4,128,1024]{4,3,2,1,0:T(8,128)(2,1)} fusion(bf16[1,2,4,128,1024]{4,3,2,1,0:T(8,128)(2,1)} %bitcast.37, bf16[1,2,4,128,1024]{4,3,2,1,0:T(8,128)(2,1)S(1)} %get-tuple-element.34), kind=kLoop, calls=%fused_computation.6 | loop fusion | flops 2097152 | bytes 8388608 | tf_op jit(solution)/shard_map/stream1/stack | solution.py:227
  227.6 14.9 %stream1.1 = (bf16[128,1024]{1,0:T(8,128)(2,1)}, bf16[128,1024]{1,0:T(8,128)(2,1)}, f32[16,128,1024]{2,1,0:T(8,128)}, f32[16,128,1024]{2,1,0:T(8,128)}) custom-call(s32[8]{0:T(128)} %multiply_add_fusion.pos_ref, bf16[128,1024]{1,0:T(8,128)(2,1)} %get-tuple-element.51.q_ref, bf16[128,1024]{1,0:T(8,128)(2,1)} %get-tuple-element.49.g_ref, ...), custom_call_target="tpu_custom_call" | custom-call | flops 1610612736 | bytes 22020096 | tf_op jit(solution)/shard_map/stream1/pallas_call | solution.py:294
  258.2 4.9 %collective-permute-done.34 = bf16[128,1024]{1,0:T(8,128)(2,1)S(1)} collective-permute-done((bf16[128,1024]{1,0:T(8,128)(2,1)S(1)}, bf16[128,1024]{1,0:T(8,128)(2,1)S(1)}, u32[]{:S(2)}, u32[]{:S(2)}) %collective-permute-start.34) | collective-permute-done | bytes 262176 | tf_op jit(solution)/shard_map/stream0/transpose()/ppermute | solution.py:205
  271.0 4.5 %collective-permute-start.52 = (bf16[128,1024]{1,0:T(8,128)(2,1)}, bf16[128,1024]{1,0:T(8,128)(2,1)S(1)}, u32[]{:S(2)}, u32[]{:S(2)}) collective-permute-start(bf16[128,1024]{1,0:T(8,128)(2,1)} %get-tuple-element.24), channel_id=1, source_target_pairs={{0,4},{1,5},{2,6},{3,7},{4,8},{5,9},{6,10},{7,11},{8,12},{9,13},{1... | collective-permute-start | bytes 786440 | tf_op jit(solution)/shard_map/stream0/transpose()/ppermute | solution.py:205
  282.7 4.8 %collective-permute-start.36 = (bf16[128,1024]{1,0:T(8,128)(2,1)}, bf16[128,1024]{1,0:T(8,128)(2,1)S(1)}, u32[]{:S(2)}, u32[]{:S(2)}) collective-permute-start(bf16[128,1024]{1,0:T(8,128)(2,1)} %get-tuple-element.28), channel_id=1, source_target_pairs={{0,4},{1,5},{2,6},{3,7},{4,8},{5,9},{6,10},{7,11},{8,12},{9,13},{1... | collective-permute-start | bytes 786440 | tf_op jit(solution)/shard_map/stream0/transpose()/ppermute | solution.py:205
  294.2 20.6 %collective-permute-done.57 = bf16[4,128,1024]{2,1,0:T(8,128)(2,1)S(1)} collective-permute-done((bf16[4,128,1024]{2,1,0:T(8,128)(2,1)S(1)}, bf16[4,128,1024]{2,1,0:T(8,128)(2,1)S(1)}, u32[]{:S(2)}, u32[]{:S(2)}) %collective-permute-start.57) | collective-permute-done | bytes 1048608 | tf_op jit(solution)/shard_map/stream1/transpose()/ppermute | solution.py:205
  317.9 16.2 %collective-permute-done.41 = bf16[4,128,1024]{2,1,0:T(8,128)(2,1)S(1)} collective-permute-done((bf16[4,128,1024]{2,1,0:T(8,128)(2,1)S(1)}, bf16[4,128,1024]{2,1,0:T(8,128)(2,1)S(1)}, u32[]{:S(2)}, u32[]{:S(2)}) %collective-permute-start.41) | collective-permute-done | bytes 1048608 | tf_op jit(solution)/shard_map/stream1/transpose()/ppermute | solution.py:205
  336.6 5.7 %collective-permute-done.58 = bf16[128,1024]{1,0:T(8,128)(2,1)S(1)} collective-permute-done((bf16[128,1024]{1,0:T(8,128)(2,1)S(1)}, bf16[128,1024]{1,0:T(8,128)(2,1)S(1)}, u32[]{:S(2)}, u32[]{:S(2)}) %collective-permute-start.58) | collective-permute-done | bytes 262176 | tf_op jit(solution)/shard_map/stream1/transpose()/ppermute | solution.py:205
  346.4 5.1 %collective-permute-done.42 = bf16[128,1024]{1,0:T(8,128)(2,1)S(1)} collective-permute-done((bf16[128,1024]{1,0:T(8,128)(2,1)S(1)}, bf16[128,1024]{1,0:T(8,128)(2,1)S(1)}, u32[]{:S(2)}, u32[]{:S(2)}) %collective-permute-start.42) | collective-permute-done | bytes 262176 | tf_op jit(solution)/shard_map/stream1/transpose()/ppermute | solution.py:205
  358.6 4.6 %collective-permute-start.60 = (bf16[128,1024]{1,0:T(8,128)(2,1)S(1)}, bf16[128,1024]{1,0:T(8,128)(2,1)S(1)}, u32[]{:S(2)}, u32[]{:S(2)}) collective-permute-start(bf16[128,1024]{1,0:T(8,128)(2,1)S(1)} %get-tuple-element.26), channel_id=1, source_target_pairs={{0,4},{1,5},{2,6},{3,7},{4,8},{5,9},{6,10},{7,11},{8,12},{9,13},{1... | collective-permute-start | bytes 786440 | tf_op jit(solution)/shard_map/stream1/transpose()/ppermute | solution.py:205
  370.5 3.9 %collective-permute-start.44 = (bf16[128,1024]{1,0:T(8,128)(2,1)S(1)}, bf16[128,1024]{1,0:T(8,128)(2,1)S(1)}, u32[]{:S(2)}, u32[]{:S(2)}) collective-permute-start(bf16[128,1024]{1,0:T(8,128)(2,1)S(1)} %get-tuple-element.30), channel_id=1, source_target_pairs={{0,4},{1,5},{2,6},{3,7},{4,8},{5,9},{6,10},{7,11},{8,12},{9,13},{1... | collective-permute-start | bytes 786440 | tf_op jit(solution)/shard_map/stream1/transpose()/ppermute | solution.py:205
  378.7 4.0 %collective-permute-done.47 = bf16[128,1024]{1,0:T(8,128)(2,1)S(1)} collective-permute-done((bf16[128,1024]{1,0:T(8,128)(2,1)S(1)}, bf16[128,1024]{1,0:T(8,128)(2,1)S(1)}, u32[]{:S(2)}, u32[]{:S(2)}) %collective-permute-start.47) | collective-permute-done | bytes 262176 | tf_op jit(solution)/shard_map/stream1/transpose()/ppermute | solution.py:205
  (245 shorter events, 152.0 us)
Async XLA Ops:
  38.3 26.1 %collective-permute-start.14 = (bf16[4,128,1024]{2,1,0:T(8,128)(2,1)S(1)}, bf16[4,128,1024]{2,1,0:T(8,128)(2,1)S(1)}, u32[]{:S(2)}, u32[]{:S(2)}) collective-permute-start(bf16[4,128,1024]{2,1,0:T(8,128)(2,1)S(1)} %constant_dynamic-slice_fusion.2), channel_id=1, source_target_pairs={{0,2},{1,3},{2,0},{3,1},{4,6},{5,7},{6,4},{7,5},{8,10},{9,11},{10,... | collective-permute-start | bytes 3145736 | tf_op jit(solution)/shard_map/stream0/ppermute | solution.py:205
  41.9 40.0 %collective-permute-start.6 = (bf16[4,128,1024]{2,1,0:T(8,128)(2,1)S(1)}, bf16[4,128,1024]{2,1,0:T(8,128)(2,1)S(1)}, u32[]{:S(2)}, u32[]{:S(2)}) collective-permute-start(bf16[4,128,1024]{2,1,0:T(8,128)(2,1)S(1)} %constant_dynamic-slice_fusion.3), channel_id=1, source_target_pairs={{0,2},{1,3},{2,0},{3,1},{4,6},{5,7},{6,4},{7,5},{8,10},{9,11},{10,... | collective-permute-start | bytes 3145736 | tf_op jit(solution)/shard_map/stream0/ppermute | solution.py:205
  104.7 26.7 %collective-permute-start.28 = (bf16[128,1024]{1,0:T(8,128)(2,1)S(1)}, bf16[128,1024]{1,0:T(8,128)(2,1)S(1)}, u32[]{:S(2)}, u32[]{:S(2)}) collective-permute-start(bf16[128,1024]{1,0:T(8,128)(2,1)S(1)} %collective-permute-done.27), channel_id=1, source_target_pairs={{4,0},{5,1},{6,2},{7,3},{8,4},{9,5},{10,6},{11,7},{20,16},{21,17},... | collective-permute-start | bytes 786440 | tf_op jit(solution)/shard_map/stream1/ppermute | solution.py:205
  106.7 26.1 %collective-permute-start.17 = (bf16[128,1024]{1,0:T(8,128)(2,1)S(1)}, bf16[128,1024]{1,0:T(8,128)(2,1)S(1)}, u32[]{:S(2)}, u32[]{:S(2)}) collective-permute-start(bf16[128,1024]{1,0:T(8,128)(2,1)S(1)} %collective-permute-done.16), channel_id=1, source_target_pairs={{4,8},{5,9},{6,10},{7,11},{8,12},{9,13},{10,14},{11,15},{20,24},{2... | collective-permute-start | bytes 786440 | tf_op jit(solution)/shard_map/stream1/ppermute | solution.py:205
  110.6 22.8 %collective-permute-start.20 = (bf16[128,1024]{1,0:T(8,128)(2,1)S(1)}, bf16[128,1024]{1,0:T(8,128)(2,1)S(1)}, u32[]{:S(2)}, u32[]{:S(2)}) collective-permute-start(bf16[128,1024]{1,0:T(8,128)(2,1)S(1)} %collective-permute-done.19), channel_id=1, source_target_pairs={{4,0},{5,1},{6,2},{7,3},{8,4},{9,5},{10,6},{11,7},{20,16},{21,17},... | collective-permute-start | bytes 786440 | tf_op jit(solution)/shard_map/stream1/ppermute | solution.py:205
  112.6 22.4 %collective-permute-start.26 = (bf16[128,1024]{1,0:T(8,128)(2,1)S(1)}, bf16[128,1024]{1,0:T(8,128)(2,1)S(1)}, u32[]{:S(2)}, u32[]{:S(2)}) collective-permute-start(bf16[128,1024]{1,0:T(8,128)(2,1)S(1)} %collective-permute-done.25), channel_id=1, source_target_pairs={{8,12},{9,13},{10,14},{11,15},{24,28},{25,29},{26,30},{27,31}} | collective-permute-start | bytes 786440 | tf_op jit(solution)/shard_map/stream1/ppermute | solution.py:205
  131.3 55.8 %collective-permute-start.48 = (bf16[2,4,128,1024]{3,2,1,0:T(8,128)(2,1)S(1)}, bf16[2,4,128,1024]{3,2,1,0:T(8,128)(2,1)S(1)}, u32[]{:S(2)}, u32[]{:S(2)}) collective-permute-start(bf16[2,4,128,1024]{3,2,1,0:T(8,128)(2,1)S(1)} %bitcast.309), channel_id=1, source_target_pairs={{1,0},{0,1},{3,2},{2,3},{5,4},{4,5},{7,6},{6,7},{9,8},{8,9},{11,10... | collective-permute-start | bytes 6291464 | tf_op jit(solution)/shard_map/stream0/transpose()/ppermute | solution.py:205
  139.5 26.1 %collective-permute-start.30 = (bf16[4,128,1024]{2,1,0:T(8,128)(2,1)S(1)}, bf16[4,128,1024]{2,1,0:T(8,128)(2,1)S(1)}, u32[]{:S(2)}, u32[]{:S(2)}) collective-permute-start(bf16[4,128,1024]{2,1,0:T(8,128)(2,1)S(1)} %constant_dynamic-slice_fusion), channel_id=1, source_target_pairs={{0,2},{1,3},{2,0},{3,1},{4,6},{5,7},{6,4},{7,5},{8,10},{9,11},{10,... | collective-permute-start | bytes 3145736 | tf_op jit(solution)/shard_map/stream1/ppermute | solution.py:205
  144.9 41.9 %collective-permute-start.22 = (bf16[4,128,1024]{2,1,0:T(8,128)(2,1)S(1)}, bf16[4,128,1024]{2,1,0:T(8,128)(2,1)S(1)}, u32[]{:S(2)}, u32[]{:S(2)}) collective-permute-start(bf16[4,128,1024]{2,1,0:T(8,128)(2,1)S(1)} %constant_dynamic-slice_fusion.1), channel_id=1, source_target_pairs={{0,2},{1,3},{2,0},{3,1},{4,6},{5,7},{6,4},{7,5},{8,10},{9,11},{10,... | collective-permute-start | bytes 3145736 | tf_op jit(solution)/shard_map/stream1/ppermute | solution.py:205
  146.9 44.7 %collective-permute-start.32 = (bf16[2,4,128,1024]{3,2,1,0:T(8,128)(2,1)S(1)}, bf16[2,4,128,1024]{3,2,1,0:T(8,128)(2,1)S(1)}, u32[]{:S(2)}, u32[]{:S(2)}) collective-permute-start(bf16[2,4,128,1024]{3,2,1,0:T(8,128)(2,1)S(1)} %bitcast.312), channel_id=1, source_target_pairs={{1,0},{0,1},{3,2},{2,3},{5,4},{4,5},{7,6},{6,7},{9,8},{8,9},{11,10... | collective-permute-start | bytes 6291464 | tf_op jit(solution)/shard_map/stream0/transpose()/ppermute | solution.py:205
  165.9 53.7 %collective-permute-start.31 = (bf16[2,4,128,1024]{3,2,1,0:T(8,128)(2,1)S(1)}, bf16[2,4,128,1024]{3,2,1,0:T(8,128)(2,1)}, u32[]{:S(2)}, u32[]{:S(2)}) collective-permute-start(bf16[2,4,128,1024]{3,2,1,0:T(8,128)(2,1)S(1)} %get-tuple-element.33), channel_id=1, source_target_pairs={{0,1},{1,0},{2,3},{3,2},{4,5},{5,4},{6,7},{7,6},{8,9},{9,8},{10,11... | collective-permute-start | bytes 6291464 | tf_op jit(solution)/shard_map/stream1/ppermute | solution.py:205
  187.1 36.5 %collective-permute-start.23 = (bf16[2,4,128,1024]{3,2,1,0:T(8,128)(2,1)S(1)}, bf16[2,4,128,1024]{3,2,1,0:T(8,128)(2,1)}, u32[]{:S(2)}, u32[]{:S(2)}) collective-permute-start(bf16[2,4,128,1024]{3,2,1,0:T(8,128)(2,1)S(1)} %get-tuple-element.35), channel_id=1, source_target_pairs={{0,1},{1,0},{2,3},{3,2},{4,5},{5,4},{6,7},{7,6},{8,9},{9,8},{10,11... | collective-permute-start | bytes 6291464 | tf_op jit(solution)/shard_map/stream1/ppermute | solution.py:205
  189.4 26.3 %collective-permute-start.49 = (bf16[4,128,1024]{2,1,0:T(8,128)(2,1)}, bf16[4,128,1024]{2,1,0:T(8,128)(2,1)}, u32[]{:S(2)}, u32[]{:S(2)}) collective-permute-start(bf16[4,128,1024]{2,1,0:T(8,128)(2,1)} %fusion.10), channel_id=1, source_target_pairs={{2,0},{3,1},{0,2},{1,3},{6,4},{7,5},{4,6},{5,7},{10,8},{11,9},{8,1... | collective-permute-start | bytes 3145736 | tf_op jit(solution)/shard_map/stream0/transpose()/ppermute | solution.py:205
  192.8 54.0 %collective-permute-start.33 = (bf16[4,128,1024]{2,1,0:T(8,128)(2,1)S(1)}, bf16[4,128,1024]{2,1,0:T(8,128)(2,1)}, u32[]{:S(2)}, u32[]{:S(2)}) collective-permute-start(bf16[4,128,1024]{2,1,0:T(8,128)(2,1)S(1)} %fusion.8), channel_id=1, source_target_pairs={{2,0},{3,1},{0,2},{1,3},{6,4},{7,5},{4,6},{5,7},{10,8},{11,9},{8,1... | collective-permute-start | bytes 3145736 | tf_op jit(solution)/shard_map/stream0/transpose()/ppermute | solution.py:205
  245.0 37.7 %collective-permute-start.56 = (bf16[2,4,128,1024]{3,2,1,0:T(8,128)(2,1)S(1)}, bf16[2,4,128,1024]{3,2,1,0:T(8,128)(2,1)S(1)}, u32[]{:S(2)}, u32[]{:S(2)}) collective-permute-start(bf16[2,4,128,1024]{3,2,1,0:T(8,128)(2,1)S(1)} %bitcast.310), channel_id=1, source_target_pairs={{1,0},{0,1},{3,2},{2,3},{5,4},{4,5},{7,6},{6,7},{9,8},{8,9},{11,10... | collective-permute-start | bytes 6291464 | tf_op jit(solution)/shard_map/stream1/transpose()/ppermute | solution.py:205
  251.3 37.4 %collective-permute-start.40 = (bf16[2,4,128,1024]{3,2,1,0:T(8,128)(2,1)S(1)}, bf16[2,4,128,1024]{3,2,1,0:T(8,128)(2,1)S(1)}, u32[]{:S(2)}, u32[]{:S(2)}) collective-permute-start(bf16[2,4,128,1024]{3,2,1,0:T(8,128)(2,1)S(1)} %bitcast.311), channel_id=1, source_target_pairs={{1,0},{0,1},{3,2},{2,3},{5,4},{4,5},{7,6},{6,7},{9,8},{8,9},{11,10... | collective-permute-start | bytes 6291464 | tf_op jit(solution)/shard_map/stream1/transpose()/ppermute | solution.py:205
  269.7 22.0 %collective-permute-start.54 = (bf16[128,1024]{1,0:T(8,128)(2,1)}, bf16[128,1024]{1,0:T(8,128)(2,1)S(1)}, u32[]{:S(2)}, u32[]{:S(2)}) collective-permute-start(bf16[128,1024]{1,0:T(8,128)(2,1)} %get-tuple-element.25), channel_id=1, source_target_pairs={{8,4},{9,5},{10,6},{11,7},{12,8},{13,9},{14,10},{15,11},{24,20},{2... | collective-permute-start | bytes 786440 | tf_op jit(solution)/shard_map/stream0/transpose()/ppermute | solution.py:205
  271.0 72.7 %collective-permute-start.52 = (bf16[128,1024]{1,0:T(8,128)(2,1)}, bf16[128,1024]{1,0:T(8,128)(2,1)S(1)}, u32[]{:S(2)}, u32[]{:S(2)}) collective-permute-start(bf16[128,1024]{1,0:T(8,128)(2,1)} %get-tuple-element.24), channel_id=1, source_target_pairs={{0,4},{1,5},{2,6},{3,7},{4,8},{5,9},{6,10},{7,11},{8,12},{9,13},{1... | collective-permute-start | bytes 786440 | tf_op jit(solution)/shard_map/stream0/transpose()/ppermute | solution.py:205
  282.7 87.6 %collective-permute-start.36 = (bf16[128,1024]{1,0:T(8,128)(2,1)}, bf16[128,1024]{1,0:T(8,128)(2,1)S(1)}, u32[]{:S(2)}, u32[]{:S(2)}) collective-permute-start(bf16[128,1024]{1,0:T(8,128)(2,1)} %get-tuple-element.28), channel_id=1, source_target_pairs={{0,4},{1,5},{2,6},{3,7},{4,8},{5,9},{6,10},{7,11},{8,12},{9,13},{1... | collective-permute-start | bytes 786440 | tf_op jit(solution)/shard_map/stream0/transpose()/ppermute | solution.py:205
  288.7 26.1 %collective-permute-start.57 = (bf16[4,128,1024]{2,1,0:T(8,128)(2,1)S(1)}, bf16[4,128,1024]{2,1,0:T(8,128)(2,1)S(1)}, u32[]{:S(2)}, u32[]{:S(2)}) collective-permute-start(bf16[4,128,1024]{2,1,0:T(8,128)(2,1)S(1)} %fusion.11), channel_id=1, source_target_pairs={{2,0},{3,1},{0,2},{1,3},{6,4},{7,5},{4,6},{5,7},{10,8},{11,9},{8,1... | collective-permute-start | bytes 3145736 | tf_op jit(solution)/shard_map/stream1/transpose()/ppermute | solution.py:205
  291.6 42.4 %collective-permute-start.41 = (bf16[4,128,1024]{2,1,0:T(8,128)(2,1)S(1)}, bf16[4,128,1024]{2,1,0:T(8,128)(2,1)S(1)}, u32[]{:S(2)}, u32[]{:S(2)}) collective-permute-start(bf16[4,128,1024]{2,1,0:T(8,128)(2,1)S(1)} %fusion.9), channel_id=1, source_target_pairs={{2,0},{3,1},{0,2},{1,3},{6,4},{7,5},{4,6},{5,7},{10,8},{11,9},{8,1... | collective-permute-start | bytes 3145736 | tf_op jit(solution)/shard_map/stream1/transpose()/ppermute | solution.py:205
  292.2 52.2 %collective-permute-start.55 = (bf16[128,1024]{1,0:T(8,128)(2,1)S(1)}, bf16[128,1024]{1,0:T(8,128)(2,1)S(1)}, u32[]{:S(2)}, u32[]{:S(2)}) collective-permute-start(bf16[128,1024]{1,0:T(8,128)(2,1)S(1)} %fusion.26), channel_id=1, source_target_pairs={{4,0},{5,1},{6,2},{7,3},{8,4},{9,5},{10,6},{11,7},{12,8},{13,9},{1... | collective-permute-start | bytes 786440 | tf_op jit(solution)/shard_map/stream0/transpose()/ppermute | solution.py:205
  314.8 55.5 %collective-permute-start.39 = (bf16[128,1024]{1,0:T(8,128)(2,1)S(1)}, bf16[128,1024]{1,0:T(8,128)(2,1)S(1)}, u32[]{:S(2)}, u32[]{:S(2)}) collective-permute-start(bf16[128,1024]{1,0:T(8,128)(2,1)S(1)} %fusion.48), channel_id=1, source_target_pairs={{4,0},{5,1},{6,2},{7,3},{8,4},{9,5},{10,6},{11,7},{12,8},{13,9},{1... | collective-permute-start | bytes 786440 | tf_op jit(solution)/shard_map/stream0/transpose()/ppermute | solution.py:205
  358.6 17.9 %collective-permute-start.60 = (bf16[128,1024]{1,0:T(8,128)(2,1)S(1)}, bf16[128,1024]{1,0:T(8,128)(2,1)S(1)}, u32[]{:S(2)}, u32[]{:S(2)}) collective-permute-start(bf16[128,1024]{1,0:T(8,128)(2,1)S(1)} %get-tuple-element.26), channel_id=1, source_target_pairs={{0,4},{1,5},{2,6},{3,7},{4,8},{5,9},{6,10},{7,11},{8,12},{9,13},{1... | collective-permute-start | bytes 786440 | tf_op jit(solution)/shard_map/stream1/transpose()/ppermute | solution.py:205
  (58 other events, 695.4 us)

commit v5 on v4

--- a/solution.py
+++ b/solution.py
@@ -208,6 +208,8 @@
 def gather_blocks(x, n):
     line_len = n // 4
     z = lax.axis_index("seq") // 4
+    y_swap = [(i, i ^ 2) for i in range(n)]
+    other_own = _send(x, y_swap)
     ups, downs = [], []
     up, down = x, x
     for k in range(1, line_len):
@@ -219,10 +221,12 @@
         )
         ups.append(up)
         downs.append(down)
-    rel = jnp.stack(ups[::-1] + [x] + downs)
-    line = lax.dynamic_slice_in_dim(rel, line_len - 1 - z, line_len, axis=0)
-    other = _send(line, [(i, i ^ 2) for i in range(n)])
-    pair = jnp.stack([line, other])
+    rest = lax.dynamic_slice_in_dim(
+        jnp.stack(ups[::-1] + downs), line_len - 1 - z, line_len - 1, axis=0
+    )
+    mine = jnp.concatenate([x[None], rest])
+    other = jnp.concatenate([other_own[None], _send(rest, y_swap)])
+    pair = jnp.stack([mine, other])
     sibling = _send(pair, [(i, i ^ 1) for i in range(n)])
     return jnp.stack([pair, sibling])
 
@@ -230,7 +234,7 @@
 def _attend_kernel(pos_ref, q_ref, g_ref, *refs):
     k_refs = refs[:SLOTS]
     v_refs = refs[SLOTS : 2 * SLOTS]
-    att_ref, gq_ref, dk_ref, dv_ref = refs[2 * SLOTS :]
+    att_ref, gq_ref, part_ref = refs[2 * SLOTS :]
     scale = HD ** (-0.5)
     nt = (((1,), (1,)), ((), ()))
     q = q_ref[...]
@@ -252,24 +256,27 @@
     )
     gk = jnp.dot(gs32.T.astype(jnp.bfloat16), q, preferred_element_type=jnp.float32) * scale
     gv = jnp.dot(p.T.astype(jnp.bfloat16), g, preferred_element_type=jnp.float32)
-    dk_ref[...] = jnp.zeros(dk_ref.shape, jnp.float32)
-    dv_ref[...] = jnp.zeros(dv_ref.shape, jnp.float32)
+    part_ref[...] = jnp.zeros(part_ref.shape, jnp.float32)
     rows = q.shape[0]
     for j in range(SLOTS):
         at = pos_ref[j]
-        dk_ref[at] = dk_ref[at] + gk[j * rows : (j + 1) * rows]
-        dv_ref[at] = dv_ref[at] + gv[j * rows : (j + 1) * rows]
-
-
-def attend_local(pos, query, grad_out, keys_local, values_local):
+        part_ref[at, 0] = part_ref[at, 0] + gk[j * rows : (j + 1) * rows]
+        part_ref[at, 1] = part_ref[at, 1] + gv[j * rows : (j + 1) * rows]
+
+
+def attend_local(pos, query, grad_out, kv_local):
     rows, width = query.shape
-    held = keys_local.shape[0]
+    held = kv_local.shape[0] // 2
     heads = width // HD
     head_spec = pl.BlockSpec((rows, HD), lambda h, pos: (0, h))
-    slot_specs = [
-        pl.BlockSpec((None, rows, HD), lambda h, pos, j=j: (pos[j], 0, h)) for j in range(SLOTS)
+    key_specs = [
+        pl.BlockSpec((None, rows, HD), lambda h, pos, j=j: (2 * pos[j], 0, h)) for j in range(SLOTS)
     ]
-    part_spec = pl.BlockSpec((held, rows, HD), lambda h, pos: (0, 0, h))
+    value_specs = [
+        pl.BlockSpec((None, rows, HD), lambda h, pos, j=j: (2 * pos[j] + 1, 0, h))
+        for j in range(SLOTS)
+    ]
+    part_spec = pl.BlockSpec((held, 2, rows, HD), lambda h, pos: (0, 0, 0, h))
     flops = 12 * rows * SLOTS * rows * HD * heads
     moved = 2 * SLOTS * rows * width * 2 + 4 * rows * width * 2 + 2 * held * rows * width * 4
     call = pl.pallas_call(
@@ -277,23 +284,20 @@
         out_shape=(
             jax.ShapeDtypeStruct((rows, width), jnp.bfloat16),
             jax.ShapeDtypeStruct((rows, width), jnp.bfloat16),
-            jax.ShapeDtypeStruct((held, rows, width), jnp.float32),
-            jax.ShapeDtypeStruct((held, rows, width), jnp.float32),
+            jax.ShapeDtypeStruct((held, 2, rows, width), jnp.float32),
         ),
         grid_spec=pltpu.PrefetchScalarGridSpec(
             num_scalar_prefetch=1,
             grid=(heads,),
-            in_specs=[head_spec, head_spec] + slot_specs + slot_specs,
-            out_specs=(head_spec, head_spec, part_spec, part_spec),
+            in_specs=[head_spec, head_spec] + key_specs + value_specs,
+            out_specs=(head_spec, head_spec, part_spec),
         ),
         compiler_params=pltpu.CompilerParams(dimension_semantics=("arbitrary",)),
         cost_estimate=pl.CostEstimate(
             flops=flops, transcendentals=rows * SLOTS * rows * heads, bytes_accessed=moved
         ),
     )
-    return call(
-        pos, query, grad_out, *([keys_local] * SLOTS), *([values_local] * SLOTS)
-    )
+    return call(pos, query, grad_out, *([kv_local] * (2 * SLOTS)))
 
 
 STREAMS = 2
@@ -303,20 +307,17 @@
     n = lax.axis_size("seq")
     rows, width = query.shape
     line_len = n // 4
+    both = jnp.stack([keys, values])
     if after is not None:
-        keys, values, _ = lax.optimization_barrier((keys, values, after))
-    keys_local = gather_blocks(keys, n).reshape(n, rows, width)
-    values_local = gather_blocks(values, n).reshape(n, rows, width)
-    attended, grad_query, part_keys, part_values = attend_local(
-        pos, query, grad_out, keys_local, values_local
-    )
+        both, _ = lax.optimization_barrier((both, after))
+    kv_local = gather_blocks(both, n).reshape(2 * n, rows, width)
+    attended, grad_query, parts = attend_local(pos, query, grad_out, kv_local)
     scatter = jax.linear_transpose(
-        lambda t: gather_blocks(t, n), jax.ShapeDtypeStruct((rows, width), jnp.float32)
-    )
-    (grad_keys,) = scatter(part_keys.reshape(2, 2, line_len, rows, width))
-    (grad_values,) = scatter(part_values.reshape(2, 2, line_len, rows, width))
-    outs = (attended, grad_query, grad_keys.astype(jnp.bfloat16), grad_values.astype(jnp.bfloat16))
-    return outs, (keys_local, values_local)
+        lambda t: gather_blocks(t, n), jax.ShapeDtypeStruct((2, rows, width), jnp.float32)
+    )
+    (grads,) = scatter(parts.reshape(2, 2, line_len, 2, rows, width))
+    grads = grads.astype(jnp.bfloat16)
+    return (attended, grad_query, grads[0], grads[1]), kv_local
 
 
 def shards_gather(query, keys, values, grad_out, global_blocks, random_blocks):
@@ -334,7 +335,10 @@
     listed = jnp.clip(listed, 0, n - 1)
     core = idx % 2
     ypos = (idx // 2) % 2
-    pos = (((listed % 2) ^ core) * 2 + (((listed // 2) % 2) ^ ypos)) * line_len + listed // 4
+    zpos = idx // 4
+    plane = listed // 4
+    in_line = jnp.where(plane == zpos, 0, jnp.where(plane < zpos, plane + 1, plane))
+    pos = (((listed % 2) ^ core) * 2 + (((listed // 2) % 2) ^ ypos)) * line_len + in_line
     cut = width // STREAMS
     outs = []
     after = None

time: 388 us -> 429 us (1.11)
  waiting for transfers between devices: 182 us -> 240 us
  starting transfers between devices: 115 us -> 64.9 us
  other arithmetic: 29.8 us -> 49.9 us
  local copies, waits for them, and re-layouts: 25 us -> 40.6 us
    ppermute x64 -> x36, waiting for transfers between devices: 182 us -> 240 us  [_send(): return lax.ppermute(v.astype(jnp.bfloat16), 'seq', pairs).astype(v.dtype)]
    ppermute x64 -> x36, starting transfers between devices: 115 us -> 64.9 us  [_send(): return lax.ppermute(v.astype(jnp.bfloat16), 'seq', pairs).astype(v.dtype)]
    another operation x4 -> x9, other arithmetic: 1.15 us -> 22.2 us
    another operation x8 -> x4, local copies, waits for them, and re-layouts: 12.3 us -> 29 us  [gather_blocks(): return jnp.stack([pair, sibling])]
    another operation x8 -> x4, other arithmetic: 13.9 us -> 16.7 us  [gather_blocks(): return jnp.stack([pair, sibling])]
  transfers between devices with their start and end apart: 64 -> 36, of which waited for: 24 -> 21; matrix products, arithmetic and copies ran while one was open for 12% -> 17% of each run, Pallas kernels for 8% -> 7%
where the time goes in v5:
time: 429 us; the launch traced here: 427 us
  waiting for transfers between devices  240 us (56%)
  starting transfers between devices  64.9 us (15%)
  other arithmetic  49.9 us (12%)
  local copies, waits for them, and re-layouts  40.6 us (9%)
  Pallas kernels  29.9 us (7%)
    ppermute x36, waiting for transfers between devices, _send(): return lax.ppermute(v.astype(jnp.bfloat16), 'seq', pairs).astype(v.dtype)  240 us
    ppermute x36, starting transfers between devices, _send(): return lax.ppermute(v.astype(jnp.bfloat16), 'seq', pairs).astype(v.dtype)  64.9 us
    pallas_call x2, Pallas kernels, attend_local(): return call(pos, query, grad_out, *[kv_local] * (2 * SLOTS))  29.9 us
    another operation x4, local copies, waits for them, and re-layouts, gather_blocks(): return jnp.stack([pair, sibling])  29 us
    another operation x4, other arithmetic  21.4 us
    another operation x4, other arithmetic, gather_blocks(): return jnp.stack([pair, sibling])  16.7 us
  transfers between devices with their start and end apart: 36, of which 21 were waited for; matrix products, arithmetic and copies ran while one was open for 17% of the time, Pallas kernels for 7%

profile of v5, /device:TPU:10, one launch (start us, length us, event | category | flops | bytes accessed | tf_op | source)
XLA Modules:
  0.0 426.5 jit_solution(10069197745209969344)
XLA Ops:
  7.9 9.7 %collective-permute-done = bf16[2,128,1024]{2,1,0:T(8,128)(2,1)S(1)} collective-permute-done((bf16[2,128,1024]{2,1,0:T(8,128)(2,1)S(1)}, bf16[2,128,1024]{2,1,0:T(8,128)(2,1)S(1)}, u32[]{:S(2)}, u32[]{:S(2)}) %collective-permute-start) | collective-permute-done | bytes 524320 | tf_op jit(solution)/shard_map/stream0/ppermute | solution.py:205
  23.8 7.6 %collective-permute-done.1 = bf16[2,128,1024]{2,1,0:T(8,128)(2,1)} collective-permute-done((bf16[2,128,1024]{2,1,0:T(8,128)(2,1)S(1)}, bf16[2,128,1024]{2,1,0:T(8,128)(2,1)}, u32[]{:S(2)}, u32[]{:S(2)}) %collective-permute-start.1) | collective-permute-done | bytes 524320 | tf_op jit(solution)/shard_map/stream0/ppermute | solution.py:205
  41.9 6.4 %collective-permute-done.5 = bf16[2,128,1024]{2,1,0:T(8,128)(2,1)S(1)} collective-permute-done((bf16[2,128,1024]{2,1,0:T(8,128)(2,1)}, bf16[2,128,1024]{2,1,0:T(8,128)(2,1)S(1)}, u32[]{:S(2)}, u32[]{:S(2)}) %collective-permute-start.5) | collective-permute-done | bytes 524320 | tf_op jit(solution)/shard_map/stream0/ppermute | solution.py:205
  50.8 42.6 %collective-permute-done.6 = bf16[2,128,1024]{2,1,0:T(8,128)(2,1)S(1)} collective-permute-done((bf16[2,128,1024]{2,1,0:T(8,128)(2,1)S(1)}, bf16[2,128,1024]{2,1,0:T(8,128)(2,1)S(1)}, u32[]{:S(2)}, u32[]{:S(2)}) %collective-permute-start.6) | collective-permute-done | bytes 524320 | tf_op jit(solution)/shard_map/stream0/ppermute | solution.py:205
  94.3 7.1 %collective-permute-done.8 = bf16[2,4,2,128,1024]{4,3,2,1,0:T(8,128)(2,1)S(1)} collective-permute-done((bf16[2,4,2,128,1024]{4,3,2,1,0:T(8,128)(2,1)S(1)}, bf16[2,4,2,128,1024]{4,3,2,1,0:T(8,128)(2,1)S(1)}, u32[]{:S(2)}, u32[]{:S(2)}) %collective-permute-start.8) | collective-permute-done | bytes 4194336 | tf_op jit(solution)/shard_map/stream0/ppermute | solution.py:205
  103.4 6.3 %pad_maximum_fusion = bf16[2,2,4,2,128,1024]{5,4,3,2,1,0:T(8,128)(2,1)} fusion(bf16[1,2,4,2,128,1024]{5,4,3,2,1,0:T(8,128)(2,1)} %bitcast.200, bf16[1,2,4,2,128,1024]{5,4,3,2,1,0:T(8,128)(2,1)S(1)} %get-tuple-element.28), kind=kLoop, calls=%fused_computation.2 | loop fusion | flops 4194304 | bytes 16777216 | tf_op jit(solution)/shard_map/stream0/stack | solution.py:231
  115.7 9.8 %collective-permute-done.9 = bf16[2,128,1024]{2,1,0:T(8,128)(2,1)S(1)} collective-permute-done((bf16[2,128,1024]{2,1,0:T(8,128)(2,1)S(1)}, bf16[2,128,1024]{2,1,0:T(8,128)(2,1)S(1)}, u32[]{:S(2)}, u32[]{:S(2)}) %collective-permute-start.9) | collective-permute-done | bytes 524320 | tf_op jit(solution)/shard_map/stream1/ppermute | solution.py:205
  132.0 8.2 %collective-permute-done.10 = bf16[2,128,1024]{2,1,0:T(8,128)(2,1)S(1)} collective-permute-done((bf16[2,128,1024]{2,1,0:T(8,128)(2,1)S(1)}, bf16[2,128,1024]{2,1,0:T(8,128)(2,1)S(1)}, u32[]{:S(2)}, u32[]{:S(2)}) %collective-permute-start.10) | collective-permute-done | bytes 524320 | tf_op jit(solution)/shard_map/stream1/ppermute | solution.py:205
  147.5 9.8 %collective-permute-done.14 = bf16[2,128,1024]{2,1,0:T(8,128)(2,1)S(1)} collective-permute-done((bf16[2,128,1024]{2,1,0:T(8,128)(2,1)S(1)}, bf16[2,128,1024]{2,1,0:T(8,128)(2,1)S(1)}, u32[]{:S(2)}, u32[]{:S(2)}) %collective-permute-start.14) | collective-permute-done | bytes 524320 | tf_op jit(solution)/shard_map/stream1/ppermute | solution.py:205
  159.7 43.2 %collective-permute-done.15 = bf16[2,128,1024]{2,1,0:T(8,128)(2,1)S(1)} collective-permute-done((bf16[2,128,1024]{2,1,0:T(8,128)(2,1)S(1)}, bf16[2,128,1024]{2,1,0:T(8,128)(2,1)S(1)}, u32[]{:S(2)}, u32[]{:S(2)}) %collective-permute-start.15) | collective-permute-done | bytes 524320 | tf_op jit(solution)/shard_map/stream1/ppermute | solution.py:205
  208.6 14.9 %stream0.1 = (bf16[128,1024]{1,0:T(8,128)(2,1)}, bf16[128,1024]{1,0:T(8,128)(2,1)}, f32[16,2,128,1024]{3,2,1,0:T(8,128)}) custom-call(s32[8]{0:T(128)} %fusion.28.pos_ref, bf16[128,1024]{1,0:T(8,128)(2,1)} %get-tuple-element.51.q_ref, bf16[128,1024]{1,0:T(8,128)(2,1)} %get-tuple-element.38.g_ref, bf16[32,128,1024]{2,1,0:T(8,128)(2,1)} %bitcast.164, ...), custom_call_target="tpu_custom_call" | custom-call | flops 1610612736 | bytes 22020096 | tf_op jit(solution)/shard_map/stream0/pallas_call | solution.py:300
  223.5 6.3 %unstack.183 = bf16[8,2,128,1024]{3,2,1,0:T(8,128)(2,1)} slice(f32[16,2,128,1024]{3,2,1,0:T(8,128)} %get-tuple-element.16), slice={[8:16], [0:2], [0:128], [0:1024]} | slice | bytes 8388608 | tf_op jit(solution)/shard_map/stream0/transpose()/unstack | solution.py:231
  230.3 6.2 %pad_maximum_fusion.1 = bf16[2,2,4,2,128,1024]{5,4,3,2,1,0:T(8,128)(2,1)} fusion(bf16[1,2,4,2,128,1024]{5,4,3,2,1,0:T(8,128)(2,1)} %bitcast.31, bf16[1,2,4,2,128,1024]{5,4,3,2,1,0:T(8,128)(2,1)S(1)} %copy-done.2), kind=kLoop, calls=%fused_computation.3 | loop fusion | flops 4194304 | bytes 16777216 | tf_op jit(solution)/shard_map/stream1/stack | solution.py:231
  236.5 15.0 %stream1.1 = (bf16[128,1024]{1,0:T(8,128)(2,1)}, bf16[128,1024]{1,0:T(8,128)(2,1)}, f32[16,2,128,1024]{3,2,1,0:T(8,128)}) custom-call(s32[8]{0:T(128)} %fusion.28.pos_ref, bf16[128,1024]{1,0:T(8,128)(2,1)} %get-tuple-element.50.q_ref, bf16[128,1024]{1,0:T(8,128)(2,1)} %get-tuple-element.39.g_ref, bf16[32,128,1024]{2,1,0:T(8,128)(2,1)} %bitcast.180, ...), custom_call_target="tpu_custom_call" | custom-call | flops 1610612736 | bytes 22020096 | tf_op jit(solution)/shard_map/stream1/pallas_call | solution.py:300
  257.6 8.3 %unstack.96 = f32[8,2,128,1024]{3,2,1,0:T(8,128)} slice(f32[16,2,128,1024]{3,2,1,0:T(8,128)} %get-tuple-element.16), slice={[0:8], [0:2], [0:128], [0:1024]} | slice | bytes 16777216 | tf_op jit(solution)/shard_map/stream0/transpose()/unstack | solution.py:231
  265.9 10.2 %fusion.37 = (bf16[2,4,2,128,1024]{4,3,2,1,0:T(8,128)(2,1)S(1)}, f32[2,4,2,128,1024]{4,3,2,1,0:T(8,128)}) fusion(f32[2,4,2,128,1024]{4,3,2,1,0:T(8,128)} %bitcast.196, bf16[2,4,2,128,1024]{4,3,2,1,0:T(8,128)(2,1)} %collective-permute-done.18), kind=kLoop, calls=%fused_computation.111 | loop fusion | flops 6291456 | bytes 25165824 | tf_op jit(solution)/shard_map/convert.8
  278.1 8.3 %unstack.109 = f32[8,2,128,1024]{3,2,1,0:T(8,128)} slice(f32[16,2,128,1024]{3,2,1,0:T(8,128)} %get-tuple-element.17), slice={[0:8], [0:2], [0:128], [0:1024]} | slice | bytes 16777216 | tf_op jit(solution)/shard_map/stream1/transpose()/unstack | solution.py:231
  286.5 10.2 %fusion.38 = (bf16[2,4,2,128,1024]{4,3,2,1,0:T(8,128)(2,1)S(1)}, f32[2,4,2,128,1024]{4,3,2,1,0:T(8,128)}) fusion(f32[2,4,2,128,1024]{4,3,2,1,0:T(8,128)} %bitcast.197, bf16[2,4,2,128,1024]{4,3,2,1,0:T(8,128)(2,1)} %collective-permute-done.27), kind=kLoop, calls=%fused_computation.112 | loop fusion | flops 6291456 | bytes 25165824 | tf_op jit(solution)/shard_map/convert.3
  298.2 15.5 %collective-permute-done.19 = bf16[3,2,128,1024]{3,2,1,0:T(8,128)(2,1)} collective-permute-done((bf16[3,2,128,1024]{3,2,1,0:T(8,128)(2,1)S(1)}, bf16[3,2,128,1024]{3,2,1,0:T(8,128)(2,1)}, u32[]{:S(2)}, u32[]{:S(2)}) %collective-permute-start.19) | collective-permute-done | bytes 1572896 | tf_op jit(solution)/shard_map/stream0/transpose()/ppermute | solution.py:205
  320.4 26.5 %collective-permute-done.28 = bf16[3,2,128,1024]{3,2,1,0:T(8,128)(2,1)S(1)} collective-permute-done((bf16[3,2,128,1024]{3,2,1,0:T(8,128)(2,1)S(1)}, bf16[3,2,128,1024]{3,2,1,0:T(8,128)(2,1)S(1)}, u32[]{:S(2)}, u32[]{:S(2)}) %collective-permute-start.28) | collective-permute-done | bytes 1572896 | tf_op jit(solution)/shard_map/stream1/transpose()/ppermute | solution.py:205
  356.1 9.6 %collective-permute-done.29 = bf16[2,128,1024]{2,1,0:T(8,128)(2,1)S(1)} collective-permute-done((bf16[2,128,1024]{2,1,0:T(8,128)(2,1)S(1)}, bf16[2,128,1024]{2,1,0:T(8,128)(2,1)S(1)}, u32[]{:S(2)}, u32[]{:S(2)}) %collective-permute-start.29) | collective-permute-done | bytes 524320 | tf_op jit(solution)/shard_map/stream1/transpose()/ppermute | solution.py:205
  367.9 9.0 %collective-permute-done.21 = bf16[2,128,1024]{2,1,0:T(8,128)(2,1)S(1)} collective-permute-done((bf16[2,128,1024]{2,1,0:T(8,128)(2,1)S(1)}, bf16[2,128,1024]{2,1,0:T(8,128)(2,1)S(1)}, u32[]{:S(2)}, u32[]{:S(2)}) %collective-permute-start.21) | collective-permute-done | bytes 524320 | tf_op jit(solution)/shard_map/stream0/transpose()/ppermute | solution.py:205
  394.3 10.9 %collective-permute-done.33 = bf16[2,128,1024]{2,1,0:T(8,128)(2,1)S(1)} collective-permute-done((bf16[2,128,1024]{2,1,0:T(8,128)(2,1)S(1)}, bf16[2,128,1024]{2,1,0:T(8,128)(2,1)S(1)}, u32[]{:S(2)}, u32[]{:S(2)}) %collective-permute-start.33) | collective-permute-done | bytes 524320 | tf_op jit(solution)/shard_map/stream1/transpose()/ppermute | solution.py:205
  418.1 6.4 %collective-permute-done.34 = bf16[2,128,1024]{2,1,0:T(8,128)(2,1)S(1)} collective-permute-done((bf16[2,128,1024]{2,1,0:T(8,128)(2,1)S(1)}, bf16[2,128,1024]{2,1,0:T(8,128)(2,1)S(1)}, u32[]{:S(2)}, u32[]{:S(2)}) %collective-permute-start.34) | collective-permute-done | bytes 524320 | tf_op jit(solution)/shard_map/stream1/transpose()/ppermute | solution.py:205
  (140 shorter events, 117.3 us)
Async XLA Ops:
  5.5 16.4 %collective-permute-start.3 = (bf16[2,128,1024]{2,1,0:T(8,128)(2,1)S(1)}, bf16[2,128,1024]{2,1,0:T(8,128)(2,1)S(1)}, u32[]{:S(2)}, u32[]{:S(2)}) collective-permute-start(bf16[2,128,1024]{2,1,0:T(8,128)(2,1)S(1)} %get-tuple-element.43), channel_id=1, source_target_pairs={{4,0},{5,1},{6,2},{7,3},{8,4},{9,5},{10,6},{11,7},{12,8},{13,9},{1... | collective-permute-start | bytes 1572872 | tf_op jit(solution)/shard_map/stream0/ppermute | solution.py:205
  48.5 44.9 %collective-permute-start.7 = (bf16[3,2,128,1024]{3,2,1,0:T(8,128)(2,1)S(1)}, bf16[3,2,128,1024]{3,2,1,0:T(8,128)(2,1)S(1)}, u32[]{:S(2)}, u32[]{:S(2)}) collective-permute-start(bf16[3,2,128,1024]{3,2,1,0:T(8,128)(2,1)S(1)} %constant_dynamic-slice_fusion.1), channel_id=1, source_target_pairs={{0,2},{1,3},{2,0},{3,1},{4,6},{5,7},{6,4},{7,5},{8,10},{9,11},{10,... | collective-permute-start | bytes 4718600 | tf_op jit(solution)/shard_map/stream0/ppermute | solution.py:205
  50.1 43.3 %collective-permute-start.6 = (bf16[2,128,1024]{2,1,0:T(8,128)(2,1)S(1)}, bf16[2,128,1024]{2,1,0:T(8,128)(2,1)S(1)}, u32[]{:S(2)}, u32[]{:S(2)}) collective-permute-start(bf16[2,128,1024]{2,1,0:T(8,128)(2,1)S(1)} %get-tuple-element.43), channel_id=1, source_target_pairs={{0,2},{1,3},{2,0},{3,1},{4,6},{5,7},{6,4},{7,5},{8,10},{9,11},{10,... | collective-permute-start | bytes 1572872 | tf_op jit(solution)/shard_map/stream0/ppermute | solution.py:205
  109.6 15.9 %collective-permute-start.9 = (bf16[2,128,1024]{2,1,0:T(8,128)(2,1)S(1)}, bf16[2,128,1024]{2,1,0:T(8,128)(2,1)S(1)}, u32[]{:S(2)}, u32[]{:S(2)}) collective-permute-start(bf16[2,128,1024]{2,1,0:T(8,128)(2,1)S(1)} %pad_maximum_fusion.5), channel_id=1, source_target_pairs={{0,4},{1,5},{2,6},{3,7},{4,8},{5,9},{6,10},{7,11},{8,12},{9,13},{1... | collective-permute-start | bytes 1572872 | tf_op jit(solution)/shard_map/stream1/ppermute | solution.py:205
  113.7 16.3 %collective-permute-start.12 = (bf16[2,128,1024]{2,1,0:T(8,128)(2,1)S(1)}, bf16[2,128,1024]{2,1,0:T(8,128)(2,1)S(1)}, u32[]{:S(2)}, u32[]{:S(2)}) collective-permute-start(bf16[2,128,1024]{2,1,0:T(8,128)(2,1)S(1)} %pad_maximum_fusion.5), channel_id=1, source_target_pairs={{4,0},{5,1},{6,2},{7,3},{8,4},{9,5},{10,6},{11,7},{12,8},{13,9},{1... | collective-permute-start | bytes 1572872 | tf_op jit(solution)/shard_map/stream1/ppermute | solution.py:205
  157.5 45.5 %collective-permute-start.16 = (bf16[3,2,128,1024]{3,2,1,0:T(8,128)(2,1)S(1)}, bf16[3,2,128,1024]{3,2,1,0:T(8,128)(2,1)S(1)}, u32[]{:S(2)}, u32[]{:S(2)}) collective-permute-start(bf16[3,2,128,1024]{3,2,1,0:T(8,128)(2,1)S(1)} %constant_dynamic-slice_fusion), channel_id=1, source_target_pairs={{0,2},{1,3},{2,0},{3,1},{4,6},{5,7},{6,4},{7,5},{8,10},{9,11},{10,... | collective-permute-start | bytes 4718600 | tf_op jit(solution)/shard_map/stream1/ppermute | solution.py:205
  159.0 43.9 %collective-permute-start.15 = (bf16[2,128,1024]{2,1,0:T(8,128)(2,1)S(1)}, bf16[2,128,1024]{2,1,0:T(8,128)(2,1)S(1)}, u32[]{:S(2)}, u32[]{:S(2)}) collective-permute-start(bf16[2,128,1024]{2,1,0:T(8,128)(2,1)S(1)} %pad_maximum_fusion.5), channel_id=1, source_target_pairs={{0,2},{1,3},{2,0},{3,1},{4,6},{5,7},{6,4},{7,5},{8,10},{9,11},{10,... | collective-permute-start | bytes 1572872 | tf_op jit(solution)/shard_map/stream1/ppermute | solution.py:205
  206.7 23.6 %collective-permute-start.17 = (bf16[2,4,2,128,1024]{4,3,2,1,0:T(8,128)(2,1)}, bf16[2,4,2,128,1024]{4,3,2,1,0:T(8,128)(2,1)}, u32[]{:S(2)}, u32[]{:S(2)}) collective-permute-start(bf16[2,4,2,128,1024]{4,3,2,1,0:T(8,128)(2,1)} %get-tuple-element.27), channel_id=1, source_target_pairs={{0,1},{1,0},{2,3},{3,2},{4,5},{5,4},{6,7},{7,6},{8,9},{9,8},{10,11... | collective-permute-start | bytes 12582920 | tf_op jit(solution)/shard_map/stream1/ppermute | solution.py:205
  229.8 36.1 %collective-permute-start.18 = (bf16[2,4,2,128,1024]{4,3,2,1,0:T(8,128)(2,1)}, bf16[2,4,2,128,1024]{4,3,2,1,0:T(8,128)(2,1)}, u32[]{:S(2)}, u32[]{:S(2)}) collective-permute-start(bf16[2,4,2,128,1024]{4,3,2,1,0:T(8,128)(2,1)} %bitcast.34), channel_id=1, source_target_pairs={{1,0},{0,1},{3,2},{2,3},{5,4},{4,5},{7,6},{6,7},{9,8},{8,9},{11,10... | collective-permute-start | bytes 12582920 | tf_op jit(solution)/shard_map/stream0/transpose()/ppermute | solution.py:205
  257.6 28.9 %collective-permute-start.27 = (bf16[2,4,2,128,1024]{4,3,2,1,0:T(8,128)(2,1)}, bf16[2,4,2,128,1024]{4,3,2,1,0:T(8,128)(2,1)}, u32[]{:S(2)}, u32[]{:S(2)}) collective-permute-start(bf16[2,4,2,128,1024]{4,3,2,1,0:T(8,128)(2,1)} %bitcast.47), channel_id=1, source_target_pairs={{1,0},{0,1},{3,2},{2,3},{5,4},{4,5},{7,6},{6,7},{9,8},{8,9},{11,10... | collective-permute-start | bytes 12582920 | tf_op jit(solution)/shard_map/stream1/transpose()/ppermute | solution.py:205
  276.3 37.4 %collective-permute-start.19 = (bf16[3,2,128,1024]{3,2,1,0:T(8,128)(2,1)S(1)}, bf16[3,2,128,1024]{3,2,1,0:T(8,128)(2,1)}, u32[]{:S(2)}, u32[]{:S(2)}) collective-permute-start(bf16[3,2,128,1024]{3,2,1,0:T(8,128)(2,1)S(1)} %slice_bitcast_fusion.3), channel_id=1, source_target_pairs={{2,0},{3,1},{0,2},{1,3},{6,4},{7,5},{4,6},{5,7},{10,8},{11,9},{8,1... | collective-permute-start | bytes 4718600 | tf_op jit(solution)/shard_map/stream0/transpose()/ppermute | solution.py:205
  296.9 50.0 %collective-permute-start.28 = (bf16[3,2,128,1024]{3,2,1,0:T(8,128)(2,1)S(1)}, bf16[3,2,128,1024]{3,2,1,0:T(8,128)(2,1)S(1)}, u32[]{:S(2)}, u32[]{:S(2)}) collective-permute-start(bf16[3,2,128,1024]{3,2,1,0:T(8,128)(2,1)S(1)} %slice_bitcast_fusion.2), channel_id=1, source_target_pairs={{2,0},{3,1},{0,2},{1,3},{6,4},{7,5},{4,6},{5,7},{10,8},{11,9},{8,1... | collective-permute-start | bytes 4718600 | tf_op jit(solution)/shard_map/stream1/transpose()/ppermute | solution.py:205
  318.3 32.0 %collective-permute-start.20 = (bf16[2,128,1024]{2,1,0:T(8,128)(2,1)S(1)}, bf16[2,128,1024]{2,1,0:T(8,128)(2,1)S(1)}, u32[]{:S(2)}, u32[]{:S(2)}) collective-permute-start(bf16[2,128,1024]{2,1,0:T(8,128)(2,1)S(1)} %get-tuple-element.30), channel_id=1, source_target_pairs={{0,4},{1,5},{2,6},{3,7},{16,20},{17,21},{18,22},{19,23}} | collective-permute-start | bytes 1572872 | tf_op jit(solution)/shard_map/stream0/transpose()/ppermute | solution.py:205
  319.7 48.2 %collective-permute-start.23 = (bf16[2,128,1024]{2,1,0:T(8,128)(2,1)S(1)}, bf16[2,128,1024]{2,1,0:T(8,128)(2,1)S(1)}, u32[]{:S(2)}, u32[]{:S(2)}) collective-permute-start(bf16[2,128,1024]{2,1,0:T(8,128)(2,1)S(1)} %get-tuple-element.31), channel_id=1, source_target_pairs={{12,8},{13,9},{14,10},{15,11},{28,24},{29,25},{30,26},{31,27}} | collective-permute-start | bytes 1572872 | tf_op jit(solution)/shard_map/stream0/transpose()/ppermute | solution.py:205
  349.0 16.7 %collective-permute-start.29 = (bf16[2,128,1024]{2,1,0:T(8,128)(2,1)S(1)}, bf16[2,128,1024]{2,1,0:T(8,128)(2,1)S(1)}, u32[]{:S(2)}, u32[]{:S(2)}) collective-permute-start(bf16[2,128,1024]{2,1,0:T(8,128)(2,1)S(1)} %get-tuple-element.32), channel_id=1, source_target_pairs={{0,4},{1,5},{2,6},{3,7},{16,20},{17,21},{18,22},{19,23}} | collective-permute-start | bytes 1572872 | tf_op jit(solution)/shard_map/stream1/transpose()/ppermute | solution.py:205
  350.5 26.5 %collective-permute-start.21 = (bf16[2,128,1024]{2,1,0:T(8,128)(2,1)S(1)}, bf16[2,128,1024]{2,1,0:T(8,128)(2,1)S(1)}, u32[]{:S(2)}, u32[]{:S(2)}) collective-permute-start(bf16[2,128,1024]{2,1,0:T(8,128)(2,1)S(1)} %fusion.21), channel_id=1, source_target_pairs={{0,4},{1,5},{2,6},{3,7},{4,8},{5,9},{6,10},{7,11},{16,20},{17,21},... | collective-permute-start | bytes 1572872 | tf_op jit(solution)/shard_map/stream0/transpose()/ppermute | solution.py:205
  353.5 53.8 %collective-permute-start.26 = (bf16[2,128,1024]{2,1,0:T(8,128)(2,1)S(1)}, bf16[2,128,1024]{2,1,0:T(8,128)(2,1)S(1)}, u32[]{:S(2)}, u32[]{:S(2)}) collective-permute-start(bf16[2,128,1024]{2,1,0:T(8,128)(2,1)S(1)} %slice_bitcast_fusion.17), channel_id=1, source_target_pairs={{2,0},{3,1},{0,2},{1,3},{6,4},{7,5},{4,6},{5,7},{10,8},{11,9},{8,1... | collective-permute-start | bytes 1572872 | tf_op jit(solution)/shard_map/stream0/transpose()/ppermute | solution.py:205
  355.3 29.6 %collective-permute-start.32 = (bf16[2,128,1024]{2,1,0:T(8,128)(2,1)S(1)}, bf16[2,128,1024]{2,1,0:T(8,128)(2,1)S(1)}, u32[]{:S(2)}, u32[]{:S(2)}) collective-permute-start(bf16[2,128,1024]{2,1,0:T(8,128)(2,1)S(1)} %get-tuple-element.33), channel_id=1, source_target_pairs={{12,8},{13,9},{14,10},{15,11},{28,24},{29,25},{30,26},{31,27}} | collective-permute-start | bytes 1572872 | tf_op jit(solution)/shard_map/stream1/transpose()/ppermute | solution.py:205
  365.9 22.3 %collective-permute-start.30 = (bf16[2,128,1024]{2,1,0:T(8,128)(2,1)S(1)}, bf16[2,128,1024]{2,1,0:T(8,128)(2,1)S(1)}, u32[]{:S(2)}, u32[]{:S(2)}) collective-permute-start(bf16[2,128,1024]{2,1,0:T(8,128)(2,1)S(1)} %fusion.9), channel_id=1, source_target_pairs={{0,4},{1,5},{2,6},{3,7},{4,8},{5,9},{6,10},{7,11},{16,20},{17,21},... | collective-permute-start | bytes 1572872 | tf_op jit(solution)/shard_map/stream1/transpose()/ppermute | solution.py:205
  378.6 32.7 %collective-permute-start.22 = (bf16[2,128,1024]{2,1,0:T(8,128)(2,1)S(1)}, bf16[2,128,1024]{2,1,0:T(8,128)(2,1)S(1)}, u32[]{:S(2)}, u32[]{:S(2)}) collective-permute-start(bf16[2,128,1024]{2,1,0:T(8,128)(2,1)S(1)} %get-tuple-element.22), channel_id=1, source_target_pairs={{0,4},{1,5},{2,6},{3,7},{4,8},{5,9},{6,10},{7,11},{8,12},{9,13},{1... | collective-permute-start | bytes 1572872 | tf_op jit(solution)/shard_map/stream0/transpose()/ppermute | solution.py:205
  388.5 16.7 %collective-permute-start.33 = (bf16[2,128,1024]{2,1,0:T(8,128)(2,1)S(1)}, bf16[2,128,1024]{2,1,0:T(8,128)(2,1)S(1)}, u32[]{:S(2)}, u32[]{:S(2)}) collective-permute-start(bf16[2,128,1024]{2,1,0:T(8,128)(2,1)S(1)} %get-tuple-element.25), channel_id=1, source_target_pairs={{8,4},{9,5},{10,6},{11,7},{12,8},{13,9},{14,10},{15,11},{24,20},{2... | collective-permute-start | bytes 1572872 | tf_op jit(solution)/shard_map/stream1/transpose()/ppermute | solution.py:205
  390.9 25.5 %collective-permute-start.25 = (bf16[2,128,1024]{2,1,0:T(8,128)(2,1)S(1)}, bf16[2,128,1024]{2,1,0:T(8,128)(2,1)S(1)}, u32[]{:S(2)}, u32[]{:S(2)}) collective-permute-start(bf16[2,128,1024]{2,1,0:T(8,128)(2,1)S(1)} %fusion.19), channel_id=1, source_target_pairs={{4,0},{5,1},{6,2},{7,3},{8,4},{9,5},{10,6},{11,7},{12,8},{13,9},{1... | collective-permute-start | bytes 1572872 | tf_op jit(solution)/shard_map/stream0/transpose()/ppermute | solution.py:205
  392.9 25.2 %collective-permute-start.35 = (bf16[2,128,1024]{2,1,0:T(8,128)(2,1)S(1)}, bf16[2,128,1024]{2,1,0:T(8,128)(2,1)S(1)}, u32[]{:S(2)}, u32[]{:S(2)}) collective-permute-start(bf16[2,128,1024]{2,1,0:T(8,128)(2,1)S(1)} %slice_bitcast_fusion.14), channel_id=1, source_target_pairs={{2,0},{3,1},{0,2},{1,3},{6,4},{7,5},{4,6},{5,7},{10,8},{11,9},{8,1... | collective-permute-start | bytes 1572872 | tf_op jit(solution)/shard_map/stream1/transpose()/ppermute | solution.py:205
  407.3 17.2 %collective-permute-start.34 = (bf16[2,128,1024]{2,1,0:T(8,128)(2,1)S(1)}, bf16[2,128,1024]{2,1,0:T(8,128)(2,1)S(1)}, u32[]{:S(2)}, u32[]{:S(2)}) collective-permute-start(bf16[2,128,1024]{2,1,0:T(8,128)(2,1)S(1)} %fusion.7), channel_id=1, source_target_pairs={{4,0},{5,1},{6,2},{7,3},{8,4},{9,5},{10,6},{11,7},{12,8},{13,9},{1... | collective-permute-start | bytes 1572872 | tf_op jit(solution)/shard_map/stream1/transpose()/ppermute | solution.py:205
  (26 other events, 547.5 us)

commit v6 on v5

--- a/solution.py
+++ b/solution.py
@@ -205,11 +205,9 @@
     return lax.ppermute(v.astype(jnp.bfloat16), "seq", pairs).astype(v.dtype)
 
 
-def gather_blocks(x, n):
+def _line(x, n):
     line_len = n // 4
     z = lax.axis_index("seq") // 4
-    y_swap = [(i, i ^ 2) for i in range(n)]
-    other_own = _send(x, y_swap)
     ups, downs = [], []
     up, down = x, x
     for k in range(1, line_len):
@@ -221,14 +219,30 @@
         )
         ups.append(up)
         downs.append(down)
-    rest = lax.dynamic_slice_in_dim(
-        jnp.stack(ups[::-1] + downs), line_len - 1 - z, line_len - 1, axis=0
-    )
-    mine = jnp.concatenate([x[None], rest])
-    other = jnp.concatenate([other_own[None], _send(rest, y_swap)])
-    pair = jnp.stack([mine, other])
-    sibling = _send(pair, [(i, i ^ 1) for i in range(n)])
-    return jnp.stack([pair, sibling])
+    rel = jnp.stack(ups[::-1] + [x] + downs)
+    return lax.dynamic_slice_in_dim(rel, line_len - 1 - z, line_len, axis=0)
+
+
+def _z_then_y(x, n):
+    line = _line(x, n)
+    pair = jnp.stack([line, _send(line, [(i, i ^ 2) for i in range(n)])])
+    return jnp.stack([pair, _send(pair, [(i, i ^ 1) for i in range(n)])])
+
+
+def _y_then_z(x, n):
+    both = jnp.stack([x, _send(x, [(i, i ^ 2) for i in range(n)])])
+    pair = jnp.moveaxis(_line(both, n), 1, 0)
+    return jnp.stack([pair, _send(pair, [(i, i ^ 1) for i in range(n)])])
+
+
+Y_FIRST_HEADS = 6
+
+
+def gather_blocks(x, n):
+    split = x.shape[-1] - Y_FIRST_HEADS * HD
+    return jnp.concatenate(
+        [_z_then_y(x[..., :split], n), _y_then_z(x[..., split:], n)], axis=-1
+    )
 
 
 def _attend_kernel(pos_ref, q_ref, g_ref, *refs):
@@ -300,7 +314,7 @@
     return call(pos, query, grad_out, *([kv_local] * (2 * SLOTS)))
 
 
-STREAMS = 2
+STREAMS = 1
 
 
 def _stream(pos, query, grad_out, keys, values, after=None):
@@ -335,10 +349,7 @@
     listed = jnp.clip(listed, 0, n - 1)
     core = idx % 2
     ypos = (idx // 2) % 2
-    zpos = idx // 4
-    plane = listed // 4
-    in_line = jnp.where(plane == zpos, 0, jnp.where(plane < zpos, plane + 1, plane))
-    pos = (((listed % 2) ^ core) * 2 + (((listed // 2) % 2) ^ ypos)) * line_len + in_line
+    pos = (((listed % 2) ^ core) * 2 + (((listed // 2) % 2) ^ ypos)) * line_len + listed // 4
     cut = width // STREAMS
     outs = []
     after = None

time: 429 us -> 425 us (level)
  other arithmetic: 49.9 us -> 70.4 us
  local copies, waits for them, and re-layouts: 40.6 us -> 21 us
  starting transfers between devices: 64.9 us -> 57.5 us
    another operation x9 -> x4, local copies, waits for them, and re-layouts: 31.9 us -> 2.69 us  [the longest x1 2.41 us: _y_then_z(): return jnp.stack([pair, _send(pair, [(i, i ^ 1) for i in range(n)])])]
    another operation x12 -> x6, other arithmetic: 38.8 us -> 25.9 us
    add_any x0 -> x4, other arithmetic: none -> 12.6 us  [_send(): return lax.ppermute(v.astype(jnp.bfloat16), 'seq', pairs).astype(v.dtype)]
    concatenate x4 -> x1, other arithmetic: 3.32 us -> 12.8 us  [gather_blocks(): jnp.concatenate([_z_then_y(x[..., :split], n), _y_then_z(x[..., split:],...]
    ppermute x36 -> x32, starting transfers between devices: 64.9 us -> 57.5 us  [_send(): return lax.ppermute(v.astype(jnp.bfloat16), 'seq', pairs).astype(v.dtype)]
    dynamic_update_slice x2, other arithmetic: 3.87 us -> 11 us  [_line(): return lax.dynamic_slice_in_dim(rel, line_len - 1 - z, line_len, axis=0)]
    broadcast_in_dim x0 -> x2, local copies, waits for them, and re-layouts: none -> 5.73 us  [_line(): return lax.dynamic_slice_in_dim(rel, line_len - 1 - z, line_len, axis=0)]
    convert_element_type x6, local copies, waits for them, and re-layouts: 1.65 us -> 6.84 us  [_send(): return lax.ppermute(v.astype(jnp.bfloat16), 'seq', pairs).astype(v.dtype)]
  transfers between devices with their start and end apart: 36 -> 32, of which waited for: 21 -> 18; matrix products, arithmetic and copies ran while one was open for 17% -> 14% of each run, Pallas kernels for 7% -> 0%
where the time goes in v6:
time: 425 us; the launch traced here: 421 us
  waiting for transfers between devices  244 us (57%)
  other arithmetic  70.4 us (17%)
  starting transfers between devices  57.5 us (14%)
  Pallas kernels  27 us (6%)
  local copies, waits for them, and re-layouts  21 us (5%)
    ppermute x32, waiting for transfers between devices, _send(): return lax.ppermute(v.astype(jnp.bfloat16), 'seq', pairs).astype(v.dtype)  244 us
    ppermute x32, starting transfers between devices, _send(): return lax.ppermute(v.astype(jnp.bfloat16), 'seq', pairs).astype(v.dtype)  57.5 us
    pallas_call x1, Pallas kernels, attend_local(): return call(pos, query, grad_out, *[kv_local] * (2 * SLOTS))  27 us
    another operation x3, other arithmetic  19.4 us
    concatenate x1, other arithmetic, gather_blocks(): jnp.concatenate([_z_then_y(x[..., :split], n), _y_then_z(x[..., split:],...  12.8 us
    add_any x4, other arithmetic, _send(): return lax.ppermute(v.astype(jnp.bfloat16), 'seq', pairs).astype(v.dtype)  12.6 us
    dynamic_update_slice x2, other arithmetic, _line(): return lax.dynamic_slice_in_dim(rel, line_len - 1 - z, line_len, axis=0)  11 us
  transfers between devices with their start and end apart: 32, of which 18 were waited for; matrix products, arithmetic and copies ran while one was open for 14% of the time, Pallas kernels for 0%

profile of v6, /device:TPU:10, one launch (start us, length us, event | category | flops | bytes accessed | tf_op | source)
XLA Modules:
  0.0 421.2 jit_solution(7515697449353335545)
XLA Ops:
  7.8 12.5 %collective-permute-done = bf16[2,128,1280]{2,1,0:T(8,128)(2,1)S(1)} collective-permute-done((bf16[2,128,1280]{2,1,0:T(8,128)(2,1)S(1)}, bf16[2,128,1280]{2,1,0:T(8,128)(2,1)S(1)}, u32[]{:S(2)}, u32[]{:S(2)}) %collective-permute-start) | collective-permute-done | bytes 655392 | tf_op jit(solution)/shard_map/stream0/ppermute | solution.py:205
  26.5 10.4 %collective-permute-done.1 = bf16[2,128,1280]{2,1,0:T(8,128)(2,1)} collective-permute-done((bf16[2,128,1280]{2,1,0:T(8,128)(2,1)S(1)}, bf16[2,128,1280]{2,1,0:T(8,128)(2,1)}, u32[]{:S(2)}, u32[]{:S(2)}) %collective-permute-start.1) | collective-permute-done | bytes 655392 | tf_op jit(solution)/shard_map/stream0/ppermute | solution.py:205
  46.6 9.7 %collective-permute-done.5 = bf16[2,128,1280]{2,1,0:T(8,128)(2,1)S(1)} collective-permute-done((bf16[2,128,1280]{2,1,0:T(8,128)(2,1)S(1)}, bf16[2,128,1280]{2,1,0:T(8,128)(2,1)S(1)}, u32[]{:S(2)}, u32[]{:S(2)}) %collective-permute-start.5) | collective-permute-done | bytes 655392 | tf_op jit(solution)/shard_map/stream0/ppermute | solution.py:205
  58.7 62.3 %collective-permute-done.8 = bf16[2,128,768]{2,1,0:T(8,128)(2,1)S(1)} collective-permute-done((bf16[2,128,768]{2,1,0:T(8,128)(2,1)S(1)}, bf16[2,128,768]{2,1,0:T(8,128)(2,1)S(1)}, u32[]{:S(2)}, u32[]{:S(2)}) %collective-permute-start.8) | collective-permute-done | bytes 393248 | tf_op jit(solution)/shard_map/stream0/ppermute | solution.py:205
  127.0 12.0 %collective-permute-done.9 = bf16[2,2,128,768]{3,2,1,0:T(8,128)(2,1)S(1)} collective-permute-done((bf16[2,2,128,768]{3,2,1,0:T(8,128)(2,1)S(1)}, bf16[2,2,128,768]{3,2,1,0:T(8,128)(2,1)S(1)}, u32[]{:S(2)}, u32[]{:S(2)}) %collective-permute-start.9) | collective-permute-done | bytes 786464 | tf_op jit(solution)/shard_map/stream0/ppermute | solution.py:205
  144.9 10.1 %collective-permute-done.10 = bf16[2,2,128,768]{3,2,1,0:T(8,128)(2,1)S(1)} collective-permute-done((bf16[2,2,128,768]{3,2,1,0:T(8,128)(2,1)S(1)}, bf16[2,2,128,768]{3,2,1,0:T(8,128)(2,1)S(1)}, u32[]{:S(2)}, u32[]{:S(2)}) %collective-permute-start.10) | collective-permute-done | bytes 786464 | tf_op jit(solution)/shard_map/stream0/ppermute | solution.py:205
  157.5 6.4 %fusion.34 = (bf16[1,2,4,2,128,1280]{5,4,3,2,1,0:T(8,128)(2,1)}, bf16[2,4,2,128,1280]{4,3,2,1,0:T(8,128)(2,1)}) fusion(bf16[1,4,2,128,1280]{4,3,2,1,0:T(8,128)(2,1)} %bitcast.181, bf16[1,4,2,128,1280]{4,3,2,1,0:T(8,128)(2,1)S(1)} %fusion.35), kind=kLoop, calls=%fused_computation.97 | loop fusion | flops 2621440 | bytes 15728640 | tf_op jit(solution)/shard_map/stream0/stack | solution.py:229
  165.6 17.3 %collective-permute-done.14 = bf16[2,2,128,768]{3,2,1,0:T(8,128)(2,1)S(1)} collective-permute-done((bf16[2,2,128,768]{3,2,1,0:T(8,128)(2,1)S(1)}, bf16[2,2,128,768]{3,2,1,0:T(8,128)(2,1)S(1)}, u32[]{:S(2)}, u32[]{:S(2)}) %collective-permute-start.14) | collective-permute-done | bytes 786464 | tf_op jit(solution)/shard_map/stream0/ppermute | solution.py:205
  186.2 5.2 %collective-permute-done.15 = bf16[2,4,2,128,768]{4,3,2,0,1:T(8,128)(2,1)} collective-permute-done((bf16[2,4,2,128,768]{4,3,2,0,1:T(8,128)(2,1)}, bf16[2,4,2,128,768]{4,3,2,0,1:T(8,128)(2,1)}, u32[]{:S(2)}, u32[]{:S(2)}) %collective-permute-start.15) | collective-permute-done | bytes 3145760 | tf_op jit(solution)/shard_map/stream0/ppermute | solution.py:205
  191.4 12.8 %pad_maximum_fusion = bf16[2,2,4,2,128,2048]{5,4,3,2,1,0:T(8,128)(2,1)} fusion(bf16[1,2,4,2,128,1280]{5,4,3,2,1,0:T(8,128)(2,1)} %bitcast.15, bf16[1,2,4,2,128,1280]{5,4,3,2,1,0:T(8,128)(2,1)} %get-tuple-element.18, bf16[1,2,4,2,128,768]{5,4,3,1,2,0:T(8,128)(2,1)} %bitcast.27, bf16[1,2,4,2,128,768]{5,4,3,1,2,0:T(8,128)(2,1)S(1)} %get-tuple-element.16), kind=kLoop, calls=%fused_computation | loop fusion | flops 53477376 | bytes 33554432 | tf_op jit(solution)/shard_map/stream0/concatenate | solution.py:243
  204.2 27.0 %stream0.1 = (bf16[128,2048]{1,0:T(8,128)(2,1)}, bf16[128,2048]{1,0:T(8,128)(2,1)}, f32[16,2,128,2048]{3,2,1,0:T(8,128)}) custom-call(s32[8]{0:T(128)} %multiply_add_fusion.pos_ref, bf16[128,2048]{1,0:T(8,128)(2,1)} %q_ref.1, bf16[128,2048]{1,0:T(8,128)(2,1)} %g_ref.1, bf16[32,128,2048]{2,1,0:T(8,128)(2,1)} %bitcast.154, bf16[32,128,2048]{2,1,0:T(8,128)(2,1)} %bitcast.155, ...), custom_call_target="tpu_custom_call" | custom-call | flops 3221225472 | bytes 44040192 | tf_op jit(solution)/shard_map/stream0/pallas_call | solution.py:314
  231.2 12.1 %convert.18 = bf16[2,2,4,2,128,2048]{5,4,3,2,1,0:T(8,128)(2,1)S(1)} convert(f32[2,2,4,2,128,2048]{5,4,3,2,1,0:T(8,128)} %bitcast.170) | non-fusion elementwise | flops 8388608 | bytes 50331648 | tf_op jit(solution)/shard_map/convert.7
  245.0 7.8 %collective-permute-done.24 = bf16[2,4,2,128,1280]{4,3,2,1,0:T(8,128)(2,1)} collective-permute-done((bf16[2,4,2,128,1280]{4,3,2,1,0:T(8,128)(2,1)S(1)}, bf16[2,4,2,128,1280]{4,3,2,1,0:T(8,128)(2,1)}, u32[]{:S(2)}, u32[]{:S(2)}) %collective-permute-start.24) | collective-permute-done | bytes 5242912 | tf_op jit(solution)/shard_map/stream0/transpose()/ppermute | solution.py:205
  252.9 10.6 %fusion = f32[2,4,2,128,1280]{4,3,2,1,0:T(8,128)} fusion(f32[2,2,4,2,128,2048]{5,4,3,2,1,0:T(8,128)} %bitcast.171, bf16[2,4,2,128,1280]{4,3,2,1,0:T(8,128)(2,1)} %collective-permute-done.24), kind=kLoop, calls=%fused_computation.2 | loop fusion | flops 5242880 | bytes 26214400 | tf_op jit(solution)/shard_map/stream0/transpose()/add_any | solution.py:205
  270.5 4.8 %copy_dynamic-update-slice_fusion = f32[7,2,2,128,768]{4,3,2,1,0:T(8,128)S(1)} fusion(f32[7,2,2,128,768]{4,3,2,1,0:T(8,128)S(1)} %broadcast_in_dim.6, s32[]{:T(128)S(6)} %select_n.69, f32[2,2,4,2,128,2048]{5,4,3,2,1,0:T(8,128)} %bitcast.172, bf16[2,4,2,128,768]{4,3,2,1,0:T(8,128)(2,1)} %collective-permute-done.16), kind=kLoop, calls=%fused_computation.7 | loop fusion | flops 3145728 | bytes 15728644 | tf_op jit(solution)/shard_map/stream0/transpose()/dynamic_update_slice | solution.py:223
  282.2 19.1 %collective-permute-done.17 = bf16[2,2,128,768]{3,2,1,0:T(8,128)(2,1)S(1)} collective-permute-done((bf16[2,2,128,768]{3,2,1,0:T(8,128)(2,1)S(1)}, bf16[2,2,128,768]{3,2,1,0:T(8,128)(2,1)S(1)}, u32[]{:S(2)}, u32[]{:S(2)}) %collective-permute-start.17) | collective-permute-done | bytes 786464 | tf_op jit(solution)/shard_map/stream0/transpose()/ppermute | solution.py:205
  303.4 23.5 %collective-permute-done.25 = bf16[4,2,128,1280]{3,2,1,0:T(8,128)(2,1)} collective-permute-done((bf16[4,2,128,1280]{3,2,1,0:T(8,128)(2,1)}, bf16[4,2,128,1280]{3,2,1,0:T(8,128)(2,1)}, u32[]{:S(2)}, u32[]{:S(2)}) %collective-permute-start.25) | collective-permute-done | bytes 2621472 | tf_op jit(solution)/shard_map/stream0/transpose()/ppermute | solution.py:205
  327.0 4.5 %broadcast_in_dim.7 = f32[7,2,128,1280]{3,2,1,0:T(8,128)} broadcast(f32[]{:T(128)} %constant.107.clone.1), dimensions={} | broadcast | bytes 9175044 | tf_op jit(solution)/shard_map/stream0/transpose()/broadcast_in_dim | solution.py:223
  331.5 6.2 %fusion.4 = f32[7,2,128,1280]{3,2,1,0:T(8,128)} fusion(f32[7,2,128,1280]{3,2,1,0:T(8,128)} %broadcast_in_dim.7, s32[]{:T(128)S(6)} %select_n.69, f32[2,4,2,128,1280]{4,3,2,1,0:T(8,128)} %fusion, bf16[4,2,128,1280]{3,2,1,0:T(8,128)(2,1)} %collective-permute-done.25), kind=kLoop, calls=%fused_computation.11 | loop fusion | flops 2621440 | bytes 13107204 | tf_op jit(solution)/shard_map/stream0/transpose()/dynamic_update_slice | solution.py:223
  345.8 14.1 %collective-permute-done.26 = bf16[2,128,1280]{2,1,0:T(8,128)(2,1)S(1)} collective-permute-done((bf16[2,128,1280]{2,1,0:T(8,128)(2,1)S(1)}, bf16[2,128,1280]{2,1,0:T(8,128)(2,1)S(1)}, u32[]{:S(2)}, u32[]{:S(2)}) %collective-permute-start.26) | collective-permute-done | bytes 655392 | tf_op jit(solution)/shard_map/stream0/transpose()/ppermute | solution.py:205
  369.4 11.4 %collective-permute-done.27 = bf16[2,128,1280]{2,1,0:T(8,128)(2,1)S(1)} collective-permute-done((bf16[2,128,1280]{2,1,0:T(8,128)(2,1)S(1)}, bf16[2,128,1280]{2,1,0:T(8,128)(2,1)S(1)}, u32[]{:S(2)}, u32[]{:S(2)}) %collective-permute-start.27) | collective-permute-done | bytes 655392 | tf_op jit(solution)/shard_map/stream0/transpose()/ppermute | solution.py:205
  384.3 11.1 %collective-permute-done.19 = bf16[2,2,128,768]{3,2,1,0:T(8,128)(2,1)S(1)} collective-permute-done((bf16[2,2,128,768]{3,2,1,0:T(8,128)(2,1)S(1)}, bf16[2,2,128,768]{3,2,1,0:T(8,128)(2,1)S(1)}, u32[]{:S(2)}, u32[]{:S(2)}) %collective-permute-start.19) | collective-permute-done | bytes 786464 | tf_op jit(solution)/shard_map/stream0/transpose()/ppermute | solution.py:205
  404.8 8.5 %collective-permute-done.28 = bf16[2,128,1280]{2,1,0:T(8,128)(2,1)S(1)} collective-permute-done((bf16[2,128,1280]{2,1,0:T(8,128)(2,1)S(1)}, bf16[2,128,1280]{2,1,0:T(8,128)(2,1)S(1)}, u32[]{:S(2)}, u32[]{:S(2)}) %collective-permute-start.28) | collective-permute-done | bytes 655392 | tf_op jit(solution)/shard_map/stream0/transpose()/ppermute | solution.py:205
  413.3 5.2 %collective-permute-done.31 = bf16[2,128,1280]{2,1,0:T(8,128)(2,1)S(1)} collective-permute-done((bf16[2,128,1280]{2,1,0:T(8,128)(2,1)S(1)}, bf16[2,128,1280]{2,1,0:T(8,128)(2,1)S(1)}, u32[]{:S(2)}, u32[]{:S(2)}) %collective-permute-start.31) | collective-permute-done | bytes 655392 | tf_op jit(solution)/shard_map/stream0/transpose()/ppermute | solution.py:205
  (104 shorter events, 95.4 us)
Async XLA Ops:
  1.9 18.4 %collective-permute-start = (bf16[2,128,1280]{2,1,0:T(8,128)(2,1)S(1)}, bf16[2,128,1280]{2,1,0:T(8,128)(2,1)S(1)}, u32[]{:S(2)}, u32[]{:S(2)}) collective-permute-start(bf16[2,128,1280]{2,1,0:T(8,128)(2,1)S(1)} %fusion.27), channel_id=1, source_target_pairs={{0,4},{1,5},{2,6},{3,7},{4,8},{5,9},{6,10},{7,11},{8,12},{9,13},{1... | collective-permute-start | bytes 1966088 | tf_op jit(solution)/shard_map/stream0/ppermute | solution.py:205
  5.4 19.2 %collective-permute-start.3 = (bf16[2,128,1280]{2,1,0:T(8,128)(2,1)S(1)}, bf16[2,128,1280]{2,1,0:T(8,128)(2,1)S(1)}, u32[]{:S(2)}, u32[]{:S(2)}) collective-permute-start(bf16[2,128,1280]{2,1,0:T(8,128)(2,1)S(1)} %fusion.27), channel_id=1, source_target_pairs={{4,0},{5,1},{6,2},{7,3},{8,4},{9,5},{10,6},{11,7},{12,8},{13,9},{1... | collective-permute-start | bytes 1966088 | tf_op jit(solution)/shard_map/stream0/ppermute | solution.py:205
  20.3 16.6 %collective-permute-start.1 = (bf16[2,128,1280]{2,1,0:T(8,128)(2,1)S(1)}, bf16[2,128,1280]{2,1,0:T(8,128)(2,1)}, u32[]{:S(2)}, u32[]{:S(2)}) collective-permute-start(bf16[2,128,1280]{2,1,0:T(8,128)(2,1)S(1)} %collective-permute-done), channel_id=1, source_target_pairs={{4,8},{5,9},{6,10},{7,11},{8,12},{9,13},{10,14},{11,15},{20,24},{2... | collective-permute-start | bytes 1966088 | tf_op jit(solution)/shard_map/stream0/ppermute | solution.py:205
  24.6 17.2 %collective-permute-start.4 = (bf16[2,128,1280]{2,1,0:T(8,128)(2,1)S(1)}, bf16[2,128,1280]{2,1,0:T(8,128)(2,1)S(1)}, u32[]{:S(2)}, u32[]{:S(2)}) collective-permute-start(bf16[2,128,1280]{2,1,0:T(8,128)(2,1)S(1)} %collective-permute-done.3), channel_id=1, source_target_pairs={{4,0},{5,1},{6,2},{7,3},{8,4},{9,5},{10,6},{11,7},{20,16},{21,17},... | collective-permute-start | bytes 1966088 | tf_op jit(solution)/shard_map/stream0/ppermute | solution.py:205
  56.5 99.4 %collective-permute-start.6 = (bf16[4,2,128,1280]{3,2,1,0:T(8,128)(2,1)S(1)}, bf16[4,2,128,1280]{3,2,1,0:T(8,128)(2,1)S(1)}, u32[]{:S(2)}, u32[]{:S(2)}) collective-permute-start(bf16[4,2,128,1280]{3,2,1,0:T(8,128)(2,1)S(1)} %constant_dynamic-slice_fusion), channel_id=1, source_target_pairs={{0,2},{1,3},{2,0},{3,1},{4,6},{5,7},{6,4},{7,5},{8,10},{9,11},{10,... | collective-permute-start | bytes 7864328 | tf_op jit(solution)/shard_map/stream0/ppermute | solution.py:205
  58.1 62.9 %collective-permute-start.8 = (bf16[2,128,768]{2,1,0:T(8,128)(2,1)S(1)}, bf16[2,128,768]{2,1,0:T(8,128)(2,1)S(1)}, u32[]{:S(2)}, u32[]{:S(2)}) collective-permute-start(bf16[2,128,768]{2,1,0:T(8,128)(2,1)S(1)} %pad_maximum_fusion.4), channel_id=1, source_target_pairs={{0,2},{1,3},{2,0},{3,1},{4,6},{5,7},{6,4},{7,5},{8,10},{9,11},{10,... | collective-permute-start | bytes 1179656 | tf_op jit(solution)/shard_map/stream0/ppermute | solution.py:205
  121.1 17.9 %collective-permute-start.9 = (bf16[2,2,128,768]{3,2,1,0:T(8,128)(2,1)S(1)}, bf16[2,2,128,768]{3,2,1,0:T(8,128)(2,1)S(1)}, u32[]{:S(2)}, u32[]{:S(2)}) collective-permute-start(bf16[2,2,128,768]{3,2,1,0:T(8,128)(2,1)S(1)} %pad_maximum_fusion.3), channel_id=1, source_target_pairs={{0,4},{1,5},{2,6},{3,7},{4,8},{5,9},{6,10},{7,11},{8,12},{9,13},{1... | collective-permute-start | bytes 2359304 | tf_op jit(solution)/shard_map/stream0/ppermute | solution.py:205
  124.8 18.2 %collective-permute-start.12 = (bf16[2,2,128,768]{3,2,1,0:T(8,128)(2,1)S(1)}, bf16[2,2,128,768]{3,2,1,0:T(8,128)(2,1)S(1)}, u32[]{:S(2)}, u32[]{:S(2)}) collective-permute-start(bf16[2,2,128,768]{3,2,1,0:T(8,128)(2,1)S(1)} %pad_maximum_fusion.3), channel_id=1, source_target_pairs={{4,0},{5,1},{6,2},{7,3},{8,4},{9,5},{10,6},{11,7},{12,8},{13,9},{1... | collective-permute-start | bytes 2359304 | tf_op jit(solution)/shard_map/stream0/ppermute | solution.py:205
  143.0 20.9 %collective-permute-start.13 = (bf16[2,2,128,768]{3,2,1,0:T(8,128)(2,1)S(1)}, bf16[2,2,128,768]{3,2,1,0:T(8,128)(2,1)S(1)}, u32[]{:S(2)}, u32[]{:S(2)}) collective-permute-start(bf16[2,2,128,768]{3,2,1,0:T(8,128)(2,1)S(1)} %collective-permute-done.12), channel_id=1, source_target_pairs={{4,0},{5,1},{6,2},{7,3},{8,4},{9,5},{10,6},{11,7},{20,16},{21,17},... | collective-permute-start | bytes 2359304 | tf_op jit(solution)/shard_map/stream0/ppermute | solution.py:205
  163.9 27.5 %collective-permute-start.7 = (bf16[2,4,2,128,1280]{4,3,2,1,0:T(8,128)(2,1)}, bf16[2,4,2,128,1280]{4,3,2,1,0:T(8,128)(2,1)}, u32[]{:S(2)}, u32[]{:S(2)}) collective-permute-start(bf16[2,4,2,128,1280]{4,3,2,1,0:T(8,128)(2,1)} %get-tuple-element.19), channel_id=1, source_target_pairs={{0,1},{1,0},{2,3},{3,2},{4,5},{5,4},{6,7},{7,6},{8,9},{9,8},{10,11... | collective-permute-start | bytes 15728648 | tf_op jit(solution)/shard_map/stream0/ppermute | solution.py:205
  163.9 19.0 %collective-permute-start.14 = (bf16[2,2,128,768]{3,2,1,0:T(8,128)(2,1)S(1)}, bf16[2,2,128,768]{3,2,1,0:T(8,128)(2,1)S(1)}, u32[]{:S(2)}, u32[]{:S(2)}) collective-permute-start(bf16[2,2,128,768]{3,2,1,0:T(8,128)(2,1)S(1)} %collective-permute-done.13), channel_id=1, source_target_pairs={{4,0},{5,1},{6,2},{7,3},{20,16},{21,17},{22,18},{23,19}} | collective-permute-start | bytes 2359304 | tf_op jit(solution)/shard_map/stream0/ppermute | solution.py:205
  244.6 24.7 %collective-permute-start.16 = (bf16[2,4,2,128,768]{4,3,2,1,0:T(8,128)(2,1)S(1)}, bf16[2,4,2,128,768]{4,3,2,1,0:T(8,128)(2,1)}, u32[]{:S(2)}, u32[]{:S(2)}) collective-permute-start(bf16[2,4,2,128,768]{4,3,2,1,0:T(8,128)(2,1)S(1)} %slice_bitcast_fusion.4), channel_id=1, source_target_pairs={{1,0},{0,1},{3,2},{2,3},{5,4},{4,5},{7,6},{6,7},{9,8},{8,9},{11,10... | collective-permute-start | bytes 9437192 | tf_op jit(solution)/shard_map/stream0/transpose()/ppermute | solution.py:205
  267.7 59.2 %collective-permute-start.25 = (bf16[4,2,128,1280]{3,2,1,0:T(8,128)(2,1)}, bf16[4,2,128,1280]{3,2,1,0:T(8,128)(2,1)}, u32[]{:S(2)}, u32[]{:S(2)}) collective-permute-start(bf16[4,2,128,1280]{3,2,1,0:T(8,128)(2,1)} %fusion.5), channel_id=1, source_target_pairs={{2,0},{3,1},{0,2},{1,3},{6,4},{7,5},{4,6},{5,7},{10,8},{11,9},{8,1... | collective-permute-start | bytes 7864328 | tf_op jit(solution)/shard_map/stream0/transpose()/ppermute | solution.py:205
  280.0 21.3 %collective-permute-start.17 = (bf16[2,2,128,768]{3,2,1,0:T(8,128)(2,1)S(1)}, bf16[2,2,128,768]{3,2,1,0:T(8,128)(2,1)S(1)}, u32[]{:S(2)}, u32[]{:S(2)}) collective-permute-start(bf16[2,2,128,768]{3,2,1,0:T(8,128)(2,1)S(1)} %get-tuple-element.14), channel_id=1, source_target_pairs={{0,4},{1,5},{2,6},{3,7},{16,20},{17,21},{18,22},{19,23}} | collective-permute-start | bytes 2359304 | tf_op jit(solution)/shard_map/stream0/transpose()/ppermute | solution.py:205
  281.3 61.9 %collective-permute-start.20 = (bf16[2,2,128,768]{3,2,1,0:T(8,128)(2,1)S(1)}, bf16[2,2,128,768]{3,2,1,0:T(8,128)(2,1)S(1)}, u32[]{:S(2)}, u32[]{:S(2)}) collective-permute-start(bf16[2,2,128,768]{3,2,1,0:T(8,128)(2,1)S(1)} %get-tuple-element.15), channel_id=1, source_target_pairs={{12,8},{13,9},{14,10},{15,11},{28,24},{29,25},{30,26},{31,27}} | collective-permute-start | bytes 2359304 | tf_op jit(solution)/shard_map/stream0/transpose()/ppermute | solution.py:205
  301.5 41.7 %collective-permute-start.18 = (bf16[2,2,128,768]{3,2,1,0:T(8,128)(2,1)S(1)}, bf16[2,2,128,768]{3,2,1,0:T(8,128)(2,1)S(1)}, u32[]{:S(2)}, u32[]{:S(2)}) collective-permute-start(bf16[2,2,128,768]{3,2,1,0:T(8,128)(2,1)S(1)} %fusion.11), channel_id=1, source_target_pairs={{0,4},{1,5},{2,6},{3,7},{4,8},{5,9},{6,10},{7,11},{16,20},{17,21},... | collective-permute-start | bytes 2359304 | tf_op jit(solution)/shard_map/stream0/transpose()/ppermute | solution.py:205
  341.9 18.0 %collective-permute-start.26 = (bf16[2,128,1280]{2,1,0:T(8,128)(2,1)S(1)}, bf16[2,128,1280]{2,1,0:T(8,128)(2,1)S(1)}, u32[]{:S(2)}, u32[]{:S(2)}) collective-permute-start(bf16[2,128,1280]{2,1,0:T(8,128)(2,1)S(1)} %get-tuple-element.20), channel_id=1, source_target_pairs={{0,4},{1,5},{2,6},{3,7},{16,20},{17,21},{18,22},{19,23}} | collective-permute-start | bytes 1966088 | tf_op jit(solution)/shard_map/stream0/transpose()/ppermute | solution.py:205
  343.8 21.4 %collective-permute-start.21 = (bf16[2,2,128,768]{3,2,1,0:T(8,128)(2,1)S(1)}, bf16[2,2,128,768]{3,2,1,0:T(8,128)(2,1)S(1)}, u32[]{:S(2)}, u32[]{:S(2)}) collective-permute-start(bf16[2,2,128,768]{3,2,1,0:T(8,128)(2,1)S(1)} %get-tuple-element.11), channel_id=1, source_target_pairs={{8,4},{9,5},{10,6},{11,7},{12,8},{13,9},{14,10},{15,11},{24,20},{2... | collective-permute-start | bytes 2359304 | tf_op jit(solution)/shard_map/stream0/transpose()/ppermute | solution.py:205
  345.1 24.4 %collective-permute-start.29 = (bf16[2,128,1280]{2,1,0:T(8,128)(2,1)S(1)}, bf16[2,128,1280]{2,1,0:T(8,128)(2,1)S(1)}, u32[]{:S(2)}, u32[]{:S(2)}) collective-permute-start(bf16[2,128,1280]{2,1,0:T(8,128)(2,1)S(1)} %get-tuple-element.21), channel_id=1, source_target_pairs={{12,8},{13,9},{14,10},{15,11},{28,24},{29,25},{30,26},{31,27}} | collective-permute-start | bytes 1966088 | tf_op jit(solution)/shard_map/stream0/transpose()/ppermute | solution.py:205
  361.3 19.5 %collective-permute-start.27 = (bf16[2,128,1280]{2,1,0:T(8,128)(2,1)S(1)}, bf16[2,128,1280]{2,1,0:T(8,128)(2,1)S(1)}, u32[]{:S(2)}, u32[]{:S(2)}) collective-permute-start(bf16[2,128,1280]{2,1,0:T(8,128)(2,1)S(1)} %fusion.21), channel_id=1, source_target_pairs={{0,4},{1,5},{2,6},{3,7},{4,8},{5,9},{6,10},{7,11},{16,20},{17,21},... | collective-permute-start | bytes 1966088 | tf_op jit(solution)/shard_map/stream0/transpose()/ppermute | solution.py:205
  363.3 32.1 %collective-permute-start.19 = (bf16[2,2,128,768]{3,2,1,0:T(8,128)(2,1)S(1)}, bf16[2,2,128,768]{3,2,1,0:T(8,128)(2,1)S(1)}, u32[]{:S(2)}, u32[]{:S(2)}) collective-permute-start(bf16[2,2,128,768]{3,2,1,0:T(8,128)(2,1)S(1)} %get-tuple-element.10), channel_id=1, source_target_pairs={{0,4},{1,5},{2,6},{3,7},{4,8},{5,9},{6,10},{7,11},{8,12},{9,13},{1... | collective-permute-start | bytes 2359304 | tf_op jit(solution)/shard_map/stream0/transpose()/ppermute | solution.py:205
  365.5 29.9 %collective-permute-start.22 = (bf16[2,2,128,768]{3,2,1,0:T(8,128)(2,1)S(1)}, bf16[2,2,128,768]{3,2,1,0:T(8,128)(2,1)S(1)}, u32[]{:S(2)}, u32[]{:S(2)}) collective-permute-start(bf16[2,2,128,768]{3,2,1,0:T(8,128)(2,1)S(1)} %fusion.9), channel_id=1, source_target_pairs={{4,0},{5,1},{6,2},{7,3},{8,4},{9,5},{10,6},{11,7},{12,8},{13,9},{1... | collective-permute-start | bytes 2359304 | tf_op jit(solution)/shard_map/stream0/transpose()/ppermute | solution.py:205
  383.0 16.6 %collective-permute-start.30 = (bf16[2,128,1280]{2,1,0:T(8,128)(2,1)S(1)}, bf16[2,128,1280]{2,1,0:T(8,128)(2,1)S(1)}, u32[]{:S(2)}, u32[]{:S(2)}) collective-permute-start(bf16[2,128,1280]{2,1,0:T(8,128)(2,1)S(1)} %get-tuple-element.13), channel_id=1, source_target_pairs={{8,4},{9,5},{10,6},{11,7},{12,8},{13,9},{14,10},{15,11},{24,20},{2... | collective-permute-start | bytes 1966088 | tf_op jit(solution)/shard_map/stream0/transpose()/ppermute | solution.py:205
  401.0 17.5 %collective-permute-start.31 = (bf16[2,128,1280]{2,1,0:T(8,128)(2,1)S(1)}, bf16[2,128,1280]{2,1,0:T(8,128)(2,1)S(1)}, u32[]{:S(2)}, u32[]{:S(2)}) collective-permute-start(bf16[2,128,1280]{2,1,0:T(8,128)(2,1)S(1)} %fusion.19), channel_id=1, source_target_pairs={{4,0},{5,1},{6,2},{7,3},{8,4},{9,5},{10,6},{11,7},{12,8},{13,9},{1... | collective-permute-start | bytes 1966088 | tf_op jit(solution)/shard_map/stream0/transpose()/ppermute | solution.py:205
  (14 other events, 384.7 us)

commit v7 on v6

--- a/solution.py
+++ b/solution.py
@@ -223,26 +223,23 @@
     return lax.dynamic_slice_in_dim(rel, line_len - 1 - z, line_len, axis=0)
 
 
-def _z_then_y(x, n):
-    line = _line(x, n)
-    pair = jnp.stack([line, _send(line, [(i, i ^ 2) for i in range(n)])])
-    return jnp.stack([pair, _send(pair, [(i, i ^ 1) for i in range(n)])])
-
-
-def _y_then_z(x, n):
-    both = jnp.stack([x, _send(x, [(i, i ^ 2) for i in range(n)])])
-    pair = jnp.moveaxis(_line(both, n), 1, 0)
-    return jnp.stack([pair, _send(pair, [(i, i ^ 1) for i in range(n)])])
-
-
 Y_FIRST_HEADS = 6
 
 
 def gather_blocks(x, n):
     split = x.shape[-1] - Y_FIRST_HEADS * HD
-    return jnp.concatenate(
-        [_z_then_y(x[..., :split], n), _y_then_z(x[..., split:], n)], axis=-1
-    )
+    x1, x2 = x[..., :split], x[..., split:]
+    y_swap = [(i, i ^ 2) for i in range(n)]
+    c_swap = [(i, i ^ 1) for i in range(n)]
+    both2 = jnp.stack([x2, _send(x2, y_swap)])
+    x1, both2 = lax.optimization_barrier((x1, both2))
+    line1 = _line(x1, n)
+    line1, both2 = lax.optimization_barrier((line1, both2))
+    pair1 = jnp.stack([line1, _send(line1, y_swap)])
+    pair2 = jnp.moveaxis(_line(both2, n), 1, 0)
+    out1 = jnp.stack([pair1, _send(pair1, c_swap)])
+    out2 = jnp.stack([pair2, _send(pair2, c_swap)])
+    return jnp.concatenate([out1, out2], axis=-1)
 
 
 def _attend_kernel(pos_ref, q_ref, g_ref, *refs):

time: 425 us -> 411 us (0.967)
  other arithmetic: 70.4 us -> 60.4 us
  waiting for transfers between devices: 244 us -> 236 us
  starting transfers between devices: 57.5 us -> 63.7 us
    ppermute x32, waiting for transfers between devices: 244 us -> 236 us  [_send(): return lax.ppermute(v.astype(jnp.bfloat16), 'seq', pairs).astype(v.dtype)]
    dynamic_update_slice x2 -> x1, other arithmetic: 11 us -> 4.02 us  [_line(): return lax.dynamic_slice_in_dim(rel, line_len - 1 - z, line_len, axis=0)]
    ppermute x32, starting transfers between devices: 57.5 us -> 63.7 us  [_send(): return lax.ppermute(v.astype(jnp.bfloat16), 'seq', pairs).astype(v.dtype)]
    add_any x4 -> x5, other arithmetic: 12.6 us -> 13.1 us  [_send(): return lax.ppermute(v.astype(jnp.bfloat16), 'seq', pairs).astype(v.dtype)]
  transfers between devices with their start and end apart: 32 -> 32, of which waited for: 18 -> 22; matrix products, arithmetic and copies ran while one was open for 14% -> 11% of each run, Pallas kernels for 0% -> 0%
where the time goes in v7:
time: 411 us; the launch traced here: 407 us
  waiting for transfers between devices  236 us (57%)
  starting transfers between devices  63.7 us (15%)
  other arithmetic  60.4 us (15%)
  Pallas kernels  27 us (7%)
  local copies, waits for them, and re-layouts  18.4 us (4%)
    ppermute x32, waiting for transfers between devices, _send(): return lax.ppermute(v.astype(jnp.bfloat16), 'seq', pairs).astype(v.dtype)  236 us
    ppermute x32, starting transfers between devices, _send(): return lax.ppermute(v.astype(jnp.bfloat16), 'seq', pairs).astype(v.dtype)  63.7 us
    pallas_call x1, Pallas kernels, attend_local(): return call(pos, query, grad_out, *[kv_local] * (2 * SLOTS))  27 us
    another operation x3, other arithmetic  16.2 us
    add_any x5, other arithmetic, _send(): return lax.ppermute(v.astype(jnp.bfloat16), 'seq', pairs).astype(v.dtype)  13.1 us
    concatenate x1, other arithmetic, gather_blocks(): return jnp.concatenate([out1, out2], axis=-1)  12.8 us
    convert_element_type x6, local copies, waits for them, and re-layouts, _send(): return lax.ppermute(v.astype(jnp.bfloat16), 'seq', pairs).astype(v.dtype)  8.95 us
  transfers between devices with their start and end apart: 32, of which 22 were waited for; matrix products, arithmetic and copies ran while one was open for 11% of the time, Pallas kernels for 0%

profile of v7, /device:TPU:10, one launch (start us, length us, event | category | flops | bytes accessed | tf_op | source)
XLA Modules:
  0.0 406.9 jit_solution(11876206862083939400)
XLA Ops:
  5.5 7.1 %collective-permute-done = bf16[2,128,768]{2,1,0:T(8,128)(2,1)S(1)} collective-permute-done((bf16[2,128,768]{2,1,0:T(8,128)(2,1)S(1)}, bf16[2,128,768]{2,1,0:T(8,128)(2,1)S(1)}, u32[]{:S(2)}, u32[]{:S(2)}) %collective-permute-start) | collective-permute-done | bytes 393248 | tf_op jit(solution)/shard_map/stream0/ppermute | solution.py:205
  18.6 11.6 %collective-permute-done.1 = bf16[2,128,1280]{2,1,0:T(8,128)(2,1)S(1)} collective-permute-done((bf16[2,128,1280]{2,1,0:T(8,128)(2,1)S(1)}, bf16[2,128,1280]{2,1,0:T(8,128)(2,1)S(1)}, u32[]{:S(2)}, u32[]{:S(2)}) %collective-permute-start.1) | collective-permute-done | bytes 655392 | tf_op jit(solution)/shard_map/stream0/ppermute | solution.py:205
  36.5 9.5 %collective-permute-done.2 = bf16[2,128,1280]{2,1,0:T(8,128)(2,1)} collective-permute-done((bf16[2,128,1280]{2,1,0:T(8,128)(2,1)S(1)}, bf16[2,128,1280]{2,1,0:T(8,128)(2,1)}, u32[]{:S(2)}, u32[]{:S(2)}) %collective-permute-start.2) | collective-permute-done | bytes 655392 | tf_op jit(solution)/shard_map/stream0/ppermute | solution.py:205
  55.6 8.9 %collective-permute-done.6 = bf16[2,128,1280]{2,1,0:T(8,128)(2,1)S(1)} collective-permute-done((bf16[2,128,1280]{2,1,0:T(8,128)(2,1)S(1)}, bf16[2,128,1280]{2,1,0:T(8,128)(2,1)S(1)}, u32[]{:S(2)}, u32[]{:S(2)}) %collective-permute-start.6) | collective-permute-done | bytes 655392 | tf_op jit(solution)/shard_map/stream0/ppermute | solution.py:205
  72.2 11.7 %collective-permute-done.9 = bf16[2,2,128,768]{3,2,1,0:T(8,128)(2,1)S(1)} collective-permute-done((bf16[2,2,128,768]{3,2,1,0:T(8,128)(2,1)S(1)}, bf16[2,2,128,768]{3,2,1,0:T(8,128)(2,1)S(1)}, u32[]{:S(2)}, u32[]{:S(2)}) %collective-permute-start.9) | collective-permute-done | bytes 786464 | tf_op jit(solution)/shard_map/stream0/ppermute | solution.py:205
  90.1 9.8 %collective-permute-done.10 = bf16[2,2,128,768]{3,2,1,0:T(8,128)(2,1)S(1)} collective-permute-done((bf16[2,2,128,768]{3,2,1,0:T(8,128)(2,1)S(1)}, bf16[2,2,128,768]{3,2,1,0:T(8,128)(2,1)S(1)}, u32[]{:S(2)}, u32[]{:S(2)}) %collective-permute-start.10) | collective-permute-done | bytes 786464 | tf_op jit(solution)/shard_map/stream0/ppermute | solution.py:205
  100.6 19.4 %collective-permute-done.7 = bf16[4,2,128,1280]{3,2,1,0:T(8,128)(2,1)S(1)} collective-permute-done((bf16[4,2,128,1280]{3,2,1,0:T(8,128)(2,1)S(1)}, bf16[4,2,128,1280]{3,2,1,0:T(8,128)(2,1)S(1)}, u32[]{:S(2)}, u32[]{:S(2)}) %collective-permute-start.7) | collective-permute-done | bytes 2621472 | tf_op jit(solution)/shard_map/stream0/ppermute | solution.py:205
  120.0 4.6 %fusion.32 = (bf16[1,2,4,2,128,1280]{5,4,3,2,1,0:T(8,128)(2,1)}, bf16[2,4,2,128,1280]{4,3,2,1,0:T(8,128)(2,1)}) fusion(bf16[1,4,2,128,1280]{4,3,2,1,0:T(8,128)(2,1)S(1)} %bitcast.175, bf16[1,4,2,128,1280]{4,3,2,1,0:T(8,128)(2,1)S(1)} %bitcast.168), kind=kLoop, calls=%fused_computation.96 | loop fusion | flops 2621440 | bytes 15728640 | tf_op jit(solution)/shard_map/stream0/stack | solution.py:240
  129.4 17.0 %collective-permute-done.14 = bf16[2,2,128,768]{3,2,1,0:T(8,128)(2,1)S(1)} collective-permute-done((bf16[2,2,128,768]{3,2,1,0:T(8,128)(2,1)S(1)}, bf16[2,2,128,768]{3,2,1,0:T(8,128)(2,1)S(1)}, u32[]{:S(2)}, u32[]{:S(2)}) %collective-permute-start.14) | collective-permute-done | bytes 786464 | tf_op jit(solution)/shard_map/stream0/ppermute | solution.py:205
  149.7 5.2 %collective-permute-done.15 = bf16[2,4,2,128,768]{4,3,2,0,1:T(8,128)(2,1)} collective-permute-done((bf16[2,4,2,128,768]{4,3,2,0,1:T(8,128)(2,1)}, bf16[2,4,2,128,768]{4,3,2,0,1:T(8,128)(2,1)}, u32[]{:S(2)}, u32[]{:S(2)}) %collective-permute-start.15) | collective-permute-done | bytes 3145760 | tf_op jit(solution)/shard_map/stream0/ppermute | solution.py:205
  154.9 12.8 %pad_maximum_fusion = bf16[2,2,4,2,128,2048]{5,4,3,2,1,0:T(8,128)(2,1)} fusion(bf16[1,2,4,2,128,1280]{5,4,3,2,1,0:T(8,128)(2,1)} %bitcast.17, bf16[1,2,4,2,128,1280]{5,4,3,2,1,0:T(8,128)(2,1)} %get-tuple-element.34, bf16[1,2,4,2,128,768]{5,4,3,1,2,0:T(8,128)(2,1)} %bitcast.27, bf16[1,2,4,2,128,768]{5,4,3,1,2,0:T(8,128)(2,1)S(1)} %get-tuple-element.32), kind=kLoop, calls=%fused_computation | loop fusion | flops 53477376 | bytes 33554432 | tf_op jit(solution)/shard_map/stream0/concatenate | solution.py:242
  167.7 27.0 %stream0.1 = (bf16[128,2048]{1,0:T(8,128)(2,1)}, bf16[128,2048]{1,0:T(8,128)(2,1)}, f32[16,2,128,2048]{3,2,1,0:T(8,128)}) custom-call(s32[8]{0:T(128)} %multiply_add_fusion.pos_ref, bf16[128,2048]{1,0:T(8,128)(2,1)} %q_ref.1, bf16[128,2048]{1,0:T(8,128)(2,1)} %g_ref.1, bf16[32,128,2048]{2,1,0:T(8,128)(2,1)} %bitcast.149, bf16[32,128,2048]{2,1,0:T(8,128)(2,1)} %bitcast.150, ...), custom_call_target="tpu_custom_call" | custom-call | flops 3221225472 | bytes 44040192 | tf_op jit(solution)/shard_map/stream0/pallas_call | solution.py:311
  194.7 12.1 %convert.18 = bf16[2,2,4,2,128,2048]{5,4,3,2,1,0:T(8,128)(2,1)S(1)} convert(f32[2,2,4,2,128,2048]{5,4,3,2,1,0:T(8,128)} %bitcast.165) | non-fusion elementwise | flops 8388608 | bytes 50331648 | tf_op jit(solution)/shard_map/convert.7
  210.8 12.4 %collective-permute-done.18 = bf16[2,4,2,128,768]{4,3,2,1,0:T(8,128)(2,1)S(1)} collective-permute-done((bf16[2,4,2,128,768]{4,3,2,1,0:T(8,128)(2,1)S(1)}, bf16[2,4,2,128,768]{4,3,2,1,0:T(8,128)(2,1)S(1)}, u32[]{:S(2)}, u32[]{:S(2)}) %collective-permute-start.18) | collective-permute-done | bytes 3145760 | tf_op jit(solution)/shard_map/stream0/transpose()/ppermute | solution.py:205
  236.7 19.6 %collective-permute-done.19 = bf16[2,2,128,768]{3,2,1,0:T(8,128)(2,1)S(1)} collective-permute-done((bf16[2,2,128,768]{3,2,1,0:T(8,128)(2,1)S(1)}, bf16[2,2,128,768]{3,2,1,0:T(8,128)(2,1)S(1)}, u32[]{:S(2)}, u32[]{:S(2)}) %collective-permute-start.19) | collective-permute-done | bytes 786464 | tf_op jit(solution)/shard_map/stream0/transpose()/ppermute | solution.py:205
  259.5 10.7 %fusion = f32[2,4,2,128,1280]{4,3,2,1,0:T(8,128)} fusion(f32[2,2,4,2,128,2048]{5,4,3,2,1,0:T(8,128)} %bitcast.167, bf16[2,4,2,128,1280]{4,3,2,1,0:T(8,128)(2,1)} %collective-permute-done.16), kind=kLoop, calls=%fused_computation.2 | loop fusion | flops 5242880 | bytes 26214400 | tf_op jit(solution)/shard_map/stream0/transpose()/add_any | solution.py:205
  286.9 14.0 %collective-permute-done.23 = bf16[2,2,128,768]{3,2,1,0:T(8,128)(2,1)S(1)} collective-permute-done((bf16[2,2,128,768]{3,2,1,0:T(8,128)(2,1)S(1)}, bf16[2,2,128,768]{3,2,1,0:T(8,128)(2,1)S(1)}, u32[]{:S(2)}, u32[]{:S(2)}) %collective-permute-start.23) | collective-permute-done | bytes 786464 | tf_op jit(solution)/shard_map/stream0/transpose()/ppermute | solution.py:205
  304.5 17.1 %collective-permute-done.24 = bf16[2,2,128,768]{3,2,1,0:T(8,128)(2,1)S(1)} collective-permute-done((bf16[2,2,128,768]{3,2,1,0:T(8,128)(2,1)S(1)}, bf16[2,2,128,768]{3,2,1,0:T(8,128)(2,1)S(1)}, u32[]{:S(2)}, u32[]{:S(2)}) %collective-permute-start.24) | collective-permute-done | bytes 786464 | tf_op jit(solution)/shard_map/stream0/transpose()/ppermute | solution.py:205
  323.2 7.9 %collective-permute-done.17 = bf16[4,2,128,1280]{3,2,1,0:T(8,128)(2,1)S(1)} collective-permute-done((bf16[4,2,128,1280]{3,2,1,0:T(8,128)(2,1)S(1)}, bf16[4,2,128,1280]{3,2,1,0:T(8,128)(2,1)S(1)}, u32[]{:S(2)}, u32[]{:S(2)}) %collective-permute-start.17) | collective-permute-done | bytes 2621472 | tf_op jit(solution)/shard_map/stream0/transpose()/ppermute | solution.py:205
  335.8 15.1 %collective-permute-done.25 = bf16[2,128,1280]{2,1,0:T(8,128)(2,1)S(1)} collective-permute-done((bf16[2,128,1280]{2,1,0:T(8,128)(2,1)S(1)}, bf16[2,128,1280]{2,1,0:T(8,128)(2,1)S(1)}, u32[]{:S(2)}, u32[]{:S(2)}) %collective-permute-start.25) | collective-permute-done | bytes 655392 | tf_op jit(solution)/shard_map/stream0/transpose()/ppermute | solution.py:205
  352.9 14.3 %collective-permute-done.26 = bf16[2,128,1280]{2,1,0:T(8,128)(2,1)S(1)} collective-permute-done((bf16[2,128,1280]{2,1,0:T(8,128)(2,1)S(1)}, bf16[2,128,1280]{2,1,0:T(8,128)(2,1)S(1)}, u32[]{:S(2)}, u32[]{:S(2)}) %collective-permute-start.26) | collective-permute-done | bytes 655392 | tf_op jit(solution)/shard_map/stream0/transpose()/ppermute | solution.py:205
  373.4 9.5 %collective-permute-done.29 = bf16[2,128,1280]{2,1,0:T(8,128)(2,1)S(1)} collective-permute-done((bf16[2,128,1280]{2,1,0:T(8,128)(2,1)S(1)}, bf16[2,128,1280]{2,1,0:T(8,128)(2,1)S(1)}, u32[]{:S(2)}, u32[]{:S(2)}) %collective-permute-start.29) | collective-permute-done | bytes 655392 | tf_op jit(solution)/shard_map/stream0/transpose()/ppermute | solution.py:205
  384.9 12.6 %collective-permute-done.30 = bf16[2,128,1280]{2,1,0:T(8,128)(2,1)S(1)} collective-permute-done((bf16[2,128,1280]{2,1,0:T(8,128)(2,1)S(1)}, bf16[2,128,1280]{2,1,0:T(8,128)(2,1)S(1)}, u32[]{:S(2)}, u32[]{:S(2)}) %collective-permute-start.30) | collective-permute-done | bytes 655392 | tf_op jit(solution)/shard_map/stream0/transpose()/ppermute | solution.py:205
  399.7 5.9 %collective-permute-done.31 = bf16[2,128,768]{2,1,0:T(8,128)(2,1)S(1)} collective-permute-done((bf16[2,128,768]{2,1,0:T(8,128)(2,1)S(1)}, bf16[2,128,768]{2,1,0:T(8,128)(2,1)S(1)}, u32[]{:S(2)}, u32[]{:S(2)}) %collective-permute-start.31) | collective-permute-done | bytes 393248 | tf_op jit(solution)/shard_map/stream0/transpose()/ppermute | solution.py:205
  (102 shorter events, 110.0 us)
Async XLA Ops:
  12.7 17.5 %collective-permute-start.1 = (bf16[2,128,1280]{2,1,0:T(8,128)(2,1)S(1)}, bf16[2,128,1280]{2,1,0:T(8,128)(2,1)S(1)}, u32[]{:S(2)}, u32[]{:S(2)}) collective-permute-start(bf16[2,128,1280]{2,1,0:T(8,128)(2,1)S(1)} %fusion.25), channel_id=1, source_target_pairs={{0,4},{1,5},{2,6},{3,7},{4,8},{5,9},{6,10},{7,11},{8,12},{9,13},{1... | collective-permute-start | bytes 1966088 | tf_op jit(solution)/shard_map/stream0/ppermute | solution.py:205
  16.2 18.3 %collective-permute-start.4 = (bf16[2,128,1280]{2,1,0:T(8,128)(2,1)S(1)}, bf16[2,128,1280]{2,1,0:T(8,128)(2,1)S(1)}, u32[]{:S(2)}, u32[]{:S(2)}) collective-permute-start(bf16[2,128,1280]{2,1,0:T(8,128)(2,1)S(1)} %fusion.25), channel_id=1, source_target_pairs={{4,0},{5,1},{6,2},{7,3},{8,4},{9,5},{10,6},{11,7},{12,8},{13,9},{1... | collective-permute-start | bytes 1966088 | tf_op jit(solution)/shard_map/stream0/ppermute | solution.py:205
  30.2 15.7 %collective-permute-start.2 = (bf16[2,128,1280]{2,1,0:T(8,128)(2,1)S(1)}, bf16[2,128,1280]{2,1,0:T(8,128)(2,1)}, u32[]{:S(2)}, u32[]{:S(2)}) collective-permute-start(bf16[2,128,1280]{2,1,0:T(8,128)(2,1)S(1)} %collective-permute-done.1), channel_id=1, source_target_pairs={{4,8},{5,9},{6,10},{7,11},{8,12},{9,13},{10,14},{11,15},{20,24},{2... | collective-permute-start | bytes 1966088 | tf_op jit(solution)/shard_map/stream0/ppermute | solution.py:205
  34.5 16.4 %collective-permute-start.5 = (bf16[2,128,1280]{2,1,0:T(8,128)(2,1)S(1)}, bf16[2,128,1280]{2,1,0:T(8,128)(2,1)S(1)}, u32[]{:S(2)}, u32[]{:S(2)}) collective-permute-start(bf16[2,128,1280]{2,1,0:T(8,128)(2,1)S(1)} %collective-permute-done.4), channel_id=1, source_target_pairs={{4,0},{5,1},{6,2},{7,3},{8,4},{9,5},{10,6},{11,7},{20,16},{21,17},... | collective-permute-start | bytes 1966088 | tf_op jit(solution)/shard_map/stream0/ppermute | solution.py:205
  64.7 55.2 %collective-permute-start.7 = (bf16[4,2,128,1280]{3,2,1,0:T(8,128)(2,1)S(1)}, bf16[4,2,128,1280]{3,2,1,0:T(8,128)(2,1)S(1)}, u32[]{:S(2)}, u32[]{:S(2)}) collective-permute-start(bf16[4,2,128,1280]{3,2,1,0:T(8,128)(2,1)S(1)} %constant_dynamic-slice_fusion), channel_id=1, source_target_pairs={{0,2},{1,3},{2,0},{3,1},{4,6},{5,7},{6,4},{7,5},{8,10},{9,11},{10,... | collective-permute-start | bytes 7864328 | tf_op jit(solution)/shard_map/stream0/ppermute | solution.py:205
  66.3 17.6 %collective-permute-start.9 = (bf16[2,2,128,768]{3,2,1,0:T(8,128)(2,1)S(1)}, bf16[2,2,128,768]{3,2,1,0:T(8,128)(2,1)S(1)}, u32[]{:S(2)}, u32[]{:S(2)}) collective-permute-start(bf16[2,2,128,768]{3,2,1,0:T(8,128)(2,1)S(1)} %pad_maximum_fusion.3), channel_id=1, source_target_pairs={{0,4},{1,5},{2,6},{3,7},{4,8},{5,9},{6,10},{7,11},{8,12},{9,13},{1... | collective-permute-start | bytes 2359304 | tf_op jit(solution)/shard_map/stream0/ppermute | solution.py:205
  70.0 18.2 %collective-permute-start.12 = (bf16[2,2,128,768]{3,2,1,0:T(8,128)(2,1)S(1)}, bf16[2,2,128,768]{3,2,1,0:T(8,128)(2,1)S(1)}, u32[]{:S(2)}, u32[]{:S(2)}) collective-permute-start(bf16[2,2,128,768]{3,2,1,0:T(8,128)(2,1)S(1)} %pad_maximum_fusion.3), channel_id=1, source_target_pairs={{4,0},{5,1},{6,2},{7,3},{8,4},{9,5},{10,6},{11,7},{12,8},{13,9},{1... | collective-permute-start | bytes 2359304 | tf_op jit(solution)/shard_map/stream0/ppermute | solution.py:205
  83.9 16.0 %collective-permute-start.10 = (bf16[2,2,128,768]{3,2,1,0:T(8,128)(2,1)S(1)}, bf16[2,2,128,768]{3,2,1,0:T(8,128)(2,1)S(1)}, u32[]{:S(2)}, u32[]{:S(2)}) collective-permute-start(bf16[2,2,128,768]{3,2,1,0:T(8,128)(2,1)S(1)} %collective-permute-done.9), channel_id=1, source_target_pairs={{4,8},{5,9},{6,10},{7,11},{8,12},{9,13},{10,14},{11,15},{20,24},{2... | collective-permute-start | bytes 2359304 | tf_op jit(solution)/shard_map/stream0/ppermute | solution.py:205
  88.2 36.4 %collective-permute-start.13 = (bf16[2,2,128,768]{3,2,1,0:T(8,128)(2,1)S(1)}, bf16[2,2,128,768]{3,2,1,0:T(8,128)(2,1)S(1)}, u32[]{:S(2)}, u32[]{:S(2)}) collective-permute-start(bf16[2,2,128,768]{3,2,1,0:T(8,128)(2,1)S(1)} %collective-permute-done.12), channel_id=1, source_target_pairs={{4,0},{5,1},{6,2},{7,3},{8,4},{9,5},{10,6},{11,7},{20,16},{21,17},... | collective-permute-start | bytes 2359304 | tf_op jit(solution)/shard_map/stream0/ppermute | solution.py:205
  99.9 29.1 %collective-permute-start.11 = (bf16[2,2,128,768]{3,2,1,0:T(8,128)(2,1)S(1)}, bf16[2,2,128,768]{3,2,1,0:T(8,128)(2,1)S(1)}, u32[]{:S(2)}, u32[]{:S(2)}) collective-permute-start(bf16[2,2,128,768]{3,2,1,0:T(8,128)(2,1)S(1)} %collective-permute-done.10), channel_id=1, source_target_pairs={{8,12},{9,13},{10,14},{11,15},{24,28},{25,29},{26,30},{27,31}} | collective-permute-start | bytes 2359304 | tf_op jit(solution)/shard_map/stream0/ppermute | solution.py:205
  124.6 30.3 %collective-permute-start.8 = (bf16[2,4,2,128,1280]{4,3,2,1,0:T(8,128)(2,1)}, bf16[2,4,2,128,1280]{4,3,2,1,0:T(8,128)(2,1)}, u32[]{:S(2)}, u32[]{:S(2)}) collective-permute-start(bf16[2,4,2,128,1280]{4,3,2,1,0:T(8,128)(2,1)} %get-tuple-element.35), channel_id=1, source_target_pairs={{0,1},{1,0},{2,3},{3,2},{4,5},{5,4},{6,7},{7,6},{8,9},{9,8},{10,11... | collective-permute-start | bytes 15728648 | tf_op jit(solution)/shard_map/stream0/ppermute | solution.py:205
  124.6 21.8 %collective-permute-start.14 = (bf16[2,2,128,768]{3,2,1,0:T(8,128)(2,1)S(1)}, bf16[2,2,128,768]{3,2,1,0:T(8,128)(2,1)S(1)}, u32[]{:S(2)}, u32[]{:S(2)}) collective-permute-start(bf16[2,2,128,768]{3,2,1,0:T(8,128)(2,1)S(1)} %collective-permute-done.13), channel_id=1, source_target_pairs={{4,0},{5,1},{6,2},{7,3},{20,16},{21,17},{22,18},{23,19}} | collective-permute-start | bytes 2359304 | tf_op jit(solution)/shard_map/stream0/ppermute | solution.py:205
  209.8 49.6 %collective-permute-start.16 = (bf16[2,4,2,128,1280]{4,3,2,1,0:T(8,128)(2,1)}, bf16[2,4,2,128,1280]{4,3,2,1,0:T(8,128)(2,1)}, u32[]{:S(2)}, u32[]{:S(2)}) collective-permute-start(bf16[2,4,2,128,1280]{4,3,2,1,0:T(8,128)(2,1)} %slice_bitcast_fusion.3), channel_id=1, source_target_pairs={{1,0},{0,1},{3,2},{2,3},{5,4},{4,5},{7,6},{6,7},{9,8},{8,9},{11,10... | collective-permute-start | bytes 15728648 | tf_op jit(solution)/shard_map/stream0/transpose()/ppermute | solution.py:205
  234.7 21.6 %collective-permute-start.19 = (bf16[2,2,128,768]{3,2,1,0:T(8,128)(2,1)S(1)}, bf16[2,2,128,768]{3,2,1,0:T(8,128)(2,1)S(1)}, u32[]{:S(2)}, u32[]{:S(2)}) collective-permute-start(bf16[2,2,128,768]{3,2,1,0:T(8,128)(2,1)S(1)} %get-tuple-element.30), channel_id=1, source_target_pairs={{0,4},{1,5},{2,6},{3,7},{16,20},{17,21},{18,22},{19,23}} | collective-permute-start | bytes 2359304 | tf_op jit(solution)/shard_map/stream0/transpose()/ppermute | solution.py:205
  236.0 38.6 %collective-permute-start.22 = (bf16[2,2,128,768]{3,2,1,0:T(8,128)(2,1)S(1)}, bf16[2,2,128,768]{3,2,1,0:T(8,128)(2,1)S(1)}, u32[]{:S(2)}, u32[]{:S(2)}) collective-permute-start(bf16[2,2,128,768]{3,2,1,0:T(8,128)(2,1)S(1)} %get-tuple-element.31), channel_id=1, source_target_pairs={{12,8},{13,9},{14,10},{15,11},{28,24},{29,25},{30,26},{31,27}} | collective-permute-start | bytes 2359304 | tf_op jit(solution)/shard_map/stream0/transpose()/ppermute | solution.py:205
  257.4 20.9 %collective-permute-start.20 = (bf16[2,2,128,768]{3,2,1,0:T(8,128)(2,1)}, bf16[2,2,128,768]{3,2,1,0:T(8,128)(2,1)S(1)}, u32[]{:S(2)}, u32[]{:S(2)}) collective-permute-start(bf16[2,2,128,768]{3,2,1,0:T(8,128)(2,1)} %fusion.10), channel_id=1, source_target_pairs={{0,4},{1,5},{2,6},{3,7},{4,8},{5,9},{6,10},{7,11},{16,20},{17,21},... | collective-permute-start | bytes 2359304 | tf_op jit(solution)/shard_map/stream0/transpose()/ppermute | solution.py:205
  272.9 58.2 %collective-permute-start.17 = (bf16[4,2,128,1280]{3,2,1,0:T(8,128)(2,1)S(1)}, bf16[4,2,128,1280]{3,2,1,0:T(8,128)(2,1)S(1)}, u32[]{:S(2)}, u32[]{:S(2)}) collective-permute-start(bf16[4,2,128,1280]{3,2,1,0:T(8,128)(2,1)S(1)} %fusion.4), channel_id=1, source_target_pairs={{2,0},{3,1},{0,2},{1,3},{6,4},{7,5},{4,6},{5,7},{10,8},{11,9},{8,1... | collective-permute-start | bytes 7864328 | tf_op jit(solution)/shard_map/stream0/transpose()/ppermute | solution.py:205
  280.8 20.2 %collective-permute-start.23 = (bf16[2,2,128,768]{3,2,1,0:T(8,128)(2,1)S(1)}, bf16[2,2,128,768]{3,2,1,0:T(8,128)(2,1)S(1)}, u32[]{:S(2)}, u32[]{:S(2)}) collective-permute-start(bf16[2,2,128,768]{3,2,1,0:T(8,128)(2,1)S(1)} %get-tuple-element.27), channel_id=1, source_target_pairs={{8,4},{9,5},{10,6},{11,7},{12,8},{13,9},{14,10},{15,11},{24,20},{2... | collective-permute-start | bytes 2359304 | tf_op jit(solution)/shard_map/stream0/transpose()/ppermute | solution.py:205
  282.4 22.1 %collective-permute-start.21 = (bf16[2,2,128,768]{3,2,1,0:T(8,128)(2,1)S(1)}, bf16[2,2,128,768]{3,2,1,0:T(8,128)(2,1)S(1)}, u32[]{:S(2)}, u32[]{:S(2)}) collective-permute-start(bf16[2,2,128,768]{3,2,1,0:T(8,128)(2,1)S(1)} %get-tuple-element.26), channel_id=1, source_target_pairs={{0,4},{1,5},{2,6},{3,7},{4,8},{5,9},{6,10},{7,11},{8,12},{9,13},{1... | collective-permute-start | bytes 2359304 | tf_op jit(solution)/shard_map/stream0/transpose()/ppermute | solution.py:205
  302.5 19.0 %collective-permute-start.24 = (bf16[2,2,128,768]{3,2,1,0:T(8,128)(2,1)S(1)}, bf16[2,2,128,768]{3,2,1,0:T(8,128)(2,1)S(1)}, u32[]{:S(2)}, u32[]{:S(2)}) collective-permute-start(bf16[2,2,128,768]{3,2,1,0:T(8,128)(2,1)S(1)} %fusion.8), channel_id=1, source_target_pairs={{4,0},{5,1},{6,2},{7,3},{8,4},{9,5},{10,6},{11,7},{12,8},{13,9},{1... | collective-permute-start | bytes 2359304 | tf_op jit(solution)/shard_map/stream0/transpose()/ppermute | solution.py:205
  333.8 17.1 %collective-permute-start.25 = (bf16[2,128,1280]{2,1,0:T(8,128)(2,1)S(1)}, bf16[2,128,1280]{2,1,0:T(8,128)(2,1)S(1)}, u32[]{:S(2)}, u32[]{:S(2)}) collective-permute-start(bf16[2,128,1280]{2,1,0:T(8,128)(2,1)S(1)} %get-tuple-element.36), channel_id=1, source_target_pairs={{0,4},{1,5},{2,6},{3,7},{16,20},{17,21},{18,22},{19,23}} | collective-permute-start | bytes 1966088 | tf_op jit(solution)/shard_map/stream0/transpose()/ppermute | solution.py:205
  335.1 17.8 %collective-permute-start.28 = (bf16[2,128,1280]{2,1,0:T(8,128)(2,1)S(1)}, bf16[2,128,1280]{2,1,0:T(8,128)(2,1)S(1)}, u32[]{:S(2)}, u32[]{:S(2)}) collective-permute-start(bf16[2,128,1280]{2,1,0:T(8,128)(2,1)S(1)} %get-tuple-element.37), channel_id=1, source_target_pairs={{12,8},{13,9},{14,10},{15,11},{28,24},{29,25},{30,26},{31,27}} | collective-permute-start | bytes 1966088 | tf_op jit(solution)/shard_map/stream0/transpose()/ppermute | solution.py:205
  351.0 16.2 %collective-permute-start.26 = (bf16[2,128,1280]{2,1,0:T(8,128)(2,1)S(1)}, bf16[2,128,1280]{2,1,0:T(8,128)(2,1)S(1)}, u32[]{:S(2)}, u32[]{:S(2)}) collective-permute-start(bf16[2,128,1280]{2,1,0:T(8,128)(2,1)S(1)} %fusion.20), channel_id=1, source_target_pairs={{0,4},{1,5},{2,6},{3,7},{4,8},{5,9},{6,10},{7,11},{16,20},{17,21},... | collective-permute-start | bytes 1966088 | tf_op jit(solution)/shard_map/stream0/transpose()/ppermute | solution.py:205
  368.8 16.1 %collective-permute-start.27 = (bf16[2,128,1280]{2,1,0:T(8,128)(2,1)S(1)}, bf16[2,128,1280]{2,1,0:T(8,128)(2,1)S(1)}, u32[]{:S(2)}, u32[]{:S(2)}) collective-permute-start(bf16[2,128,1280]{2,1,0:T(8,128)(2,1)S(1)} %get-tuple-element.28), channel_id=1, source_target_pairs={{0,4},{1,5},{2,6},{3,7},{4,8},{5,9},{6,10},{7,11},{8,12},{9,13},{1... | collective-permute-start | bytes 1966088 | tf_op jit(solution)/shard_map/stream0/transpose()/ppermute | solution.py:205
  (13 other events, 360.9 us)

commit v8 on v6

--- a/solution.py
+++ b/solution.py
@@ -223,26 +223,10 @@
     return lax.dynamic_slice_in_dim(rel, line_len - 1 - z, line_len, axis=0)
 
 
-def _z_then_y(x, n):
+def gather_blocks(x, n):
     line = _line(x, n)
     pair = jnp.stack([line, _send(line, [(i, i ^ 2) for i in range(n)])])
     return jnp.stack([pair, _send(pair, [(i, i ^ 1) for i in range(n)])])
-
-
-def _y_then_z(x, n):
-    both = jnp.stack([x, _send(x, [(i, i ^ 2) for i in range(n)])])
-    pair = jnp.moveaxis(_line(both, n), 1, 0)
-    return jnp.stack([pair, _send(pair, [(i, i ^ 1) for i in range(n)])])
-
-
-Y_FIRST_HEADS = 6
-
-
-def gather_blocks(x, n):
-    split = x.shape[-1] - Y_FIRST_HEADS * HD
-    return jnp.concatenate(
-        [_z_then_y(x[..., :split], n), _y_then_z(x[..., split:], n)], axis=-1
-    )
 
 
 def _attend_kernel(pos_ref, q_ref, g_ref, *refs):
@@ -314,7 +298,7 @@
     return call(pos, query, grad_out, *([kv_local] * (2 * SLOTS)))
 
 
-STREAMS = 1
+STREAMS = 2
 
 
 def _stream(pos, query, grad_out, keys, values, after=None):

time: 425 us -> 447 us (1.052)
  waiting for transfers between devices: 244 us -> 277 us
  other arithmetic: 70.4 us -> 40.5 us
  local copies, waits for them, and re-layouts: 21 us -> 37 us
    ppermute x32, waiting for transfers between devices: 244 us -> 277 us  [_send(): return lax.ppermute(v.astype(jnp.bfloat16), 'seq', pairs).astype(v.dtype)]
    another operation x2 -> x9, local copies, waits for them, and re-layouts: 2.59 us -> 24.2 us  [the longest x4 20.8 us: gather_blocks(): return jnp.stack([pair, _send(pair, [(i, i ^ 1) for i in range(n)])])]
    concatenate x1 -> x4, other arithmetic: 12.8 us -> 3.32 us  [shards_gather(): return tuple((jnp.concatenate(parts, axis=1) for parts in zip(*outs)))]
    another operation x6, other arithmetic: 25.9 us -> 17.8 us  [the longest x4 16.6 us: gather_blocks(): return jnp.stack([pair, _send(pair, [(i, i ^ 1) for i in range(n)])])]
    dynamic_update_slice x2, other arithmetic: 11 us -> 5.09 us  [_line(): return lax.dynamic_slice_in_dim(rel, line_len - 1 - z, line_len, axis=0)]
    broadcast_in_dim x2 -> x0, local copies, waits for them, and re-layouts: 5.73 us -> none  [_line(): return lax.dynamic_slice_in_dim(rel, line_len - 1 - z, line_len, axis=0)]
    convert_element_type x6, other arithmetic: 6.04 us -> 1.33 us  [_send(): return lax.ppermute(v.astype(jnp.bfloat16), 'seq', pairs).astype(v.dtype)]
    pallas_call x1 -> x2, Pallas kernels: 27 us -> 30 us  [attend_local(): return call(pos, query, grad_out, *[kv_local] * (2 * SLOTS))]
  transfers between devices with their start and end apart: 32 -> 32, of which waited for: 18 -> 21; matrix products, arithmetic and copies ran while one was open for 14% -> 14% of each run, Pallas kernels for 0% -> 7%
where the time goes in v8:
time: 447 us; the launch traced here: 445 us
  waiting for transfers between devices  277 us (62%)
  starting transfers between devices  58.7 us (13%)
  other arithmetic  40.5 us (9%)
  local copies, waits for them, and re-layouts  37 us (8%)
  Pallas kernels  30 us (7%)
    ppermute x32, waiting for transfers between devices, _send(): return lax.ppermute(v.astype(jnp.bfloat16), 'seq', pairs).astype(v.dtype)  277 us
    ppermute x32, starting transfers between devices, _send(): return lax.ppermute(v.astype(jnp.bfloat16), 'seq', pairs).astype(v.dtype)  58.7 us
    pallas_call x2, Pallas kernels, attend_local(): return call(pos, query, grad_out, *[kv_local] * (2 * SLOTS))  30 us
    another operation x4, local copies, waits for them, and re-layouts, gather_blocks(): return jnp.stack([pair, _send(pair, [(i, i ^ 1) for i in range(n)])])  20.8 us
    another operation x4, other arithmetic, gather_blocks(): return jnp.stack([pair, _send(pair, [(i, i ^ 1) for i in range(n)])])  16.6 us
    add_any x2, other arithmetic, _send(): return lax.ppermute(v.astype(jnp.bfloat16), 'seq', pairs).astype(v.dtype)  11.7 us
  transfers between devices with their start and end apart: 32, of which 21 were waited for; matrix products, arithmetic and copies ran while one was open for 14% of the time, Pallas kernels for 7%

profile of v8, /device:TPU:10, one launch (start us, length us, event | category | flops | bytes accessed | tf_op | source)
XLA Modules:
  0.0 444.8 jit_solution(11533213805462367969)
XLA Ops:
  7.9 9.7 %collective-permute-done = bf16[2,128,1024]{2,1,0:T(8,128)(2,1)S(1)} collective-permute-done((bf16[2,128,1024]{2,1,0:T(8,128)(2,1)S(1)}, bf16[2,128,1024]{2,1,0:T(8,128)(2,1)S(1)}, u32[]{:S(2)}, u32[]{:S(2)}) %collective-permute-start) | collective-permute-done | bytes 524320 | tf_op jit(solution)/shard_map/stream0/ppermute | solution.py:205
  23.7 7.6 %collective-permute-done.1 = bf16[2,128,1024]{2,1,0:T(8,128)(2,1)} collective-permute-done((bf16[2,128,1024]{2,1,0:T(8,128)(2,1)S(1)}, bf16[2,128,1024]{2,1,0:T(8,128)(2,1)}, u32[]{:S(2)}, u32[]{:S(2)}) %collective-permute-start.1) | collective-permute-done | bytes 524320 | tf_op jit(solution)/shard_map/stream0/ppermute | solution.py:205
  40.8 7.1 %collective-permute-done.5 = bf16[2,128,1024]{2,1,0:T(8,128)(2,1)S(1)} collective-permute-done((bf16[2,128,1024]{2,1,0:T(8,128)(2,1)S(1)}, bf16[2,128,1024]{2,1,0:T(8,128)(2,1)S(1)}, u32[]{:S(2)}, u32[]{:S(2)}) %collective-permute-start.5) | collective-permute-done | bytes 524320 | tf_op jit(solution)/shard_map/stream0/ppermute | solution.py:205
  49.9 43.1 %collective-permute-done.6 = bf16[4,2,128,1024]{3,2,1,0:T(8,128)(2,1)S(1)} collective-permute-done((bf16[4,2,128,1024]{3,2,1,0:T(8,128)(2,1)S(1)}, bf16[4,2,128,1024]{3,2,1,0:T(8,128)(2,1)S(1)}, u32[]{:S(2)}, u32[]{:S(2)}) %collective-permute-start.6) | collective-permute-done | bytes 2097184 | tf_op jit(solution)/shard_map/stream0/ppermute | solution.py:205
  93.7 7.1 %collective-permute-done.7 = bf16[2,4,2,128,1024]{4,3,2,1,0:T(8,128)(2,1)S(1)} collective-permute-done((bf16[2,4,2,128,1024]{4,3,2,1,0:T(8,128)(2,1)S(1)}, bf16[2,4,2,128,1024]{4,3,2,1,0:T(8,128)(2,1)S(1)}, u32[]{:S(2)}, u32[]{:S(2)}) %collective-permute-start.7) | collective-permute-done | bytes 4194336 | tf_op jit(solution)/shard_map/stream0/ppermute | solution.py:205
  102.8 6.3 %pad_maximum_fusion = bf16[2,2,4,2,128,1024]{5,4,3,2,1,0:T(8,128)(2,1)} fusion(bf16[1,2,4,2,128,1024]{5,4,3,2,1,0:T(8,128)(2,1)} %bitcast.189, bf16[1,2,4,2,128,1024]{5,4,3,2,1,0:T(8,128)(2,1)S(1)} %get-tuple-element.24), kind=kLoop, calls=%fused_computation.2 | loop fusion | flops 4194304 | bytes 16777216 | tf_op jit(solution)/shard_map/stream0/stack | solution.py:229
  114.9 10.1 %collective-permute-done.8 = bf16[2,128,1024]{2,1,0:T(8,128)(2,1)S(1)} collective-permute-done((bf16[2,128,1024]{2,1,0:T(8,128)(2,1)S(1)}, bf16[2,128,1024]{2,1,0:T(8,128)(2,1)S(1)}, u32[]{:S(2)}, u32[]{:S(2)}) %collective-permute-start.8) | collective-permute-done | bytes 524320 | tf_op jit(solution)/shard_map/stream1/ppermute | solution.py:205
  130.8 8.2 %collective-permute-done.9 = bf16[2,128,1024]{2,1,0:T(8,128)(2,1)S(1)} collective-permute-done((bf16[2,128,1024]{2,1,0:T(8,128)(2,1)S(1)}, bf16[2,128,1024]{2,1,0:T(8,128)(2,1)S(1)}, u32[]{:S(2)}, u32[]{:S(2)}) %collective-permute-start.9) | collective-permute-done | bytes 524320 | tf_op jit(solution)/shard_map/stream1/ppermute | solution.py:205
  146.4 9.7 %collective-permute-done.13 = bf16[2,128,1024]{2,1,0:T(8,128)(2,1)S(1)} collective-permute-done((bf16[2,128,1024]{2,1,0:T(8,128)(2,1)S(1)}, bf16[2,128,1024]{2,1,0:T(8,128)(2,1)S(1)}, u32[]{:S(2)}, u32[]{:S(2)}) %collective-permute-start.13) | collective-permute-done | bytes 524320 | tf_op jit(solution)/shard_map/stream1/ppermute | solution.py:205
  158.1 43.7 %collective-permute-done.14 = bf16[4,2,128,1024]{3,2,1,0:T(8,128)(2,1)S(1)} collective-permute-done((bf16[4,2,128,1024]{3,2,1,0:T(8,128)(2,1)S(1)}, bf16[4,2,128,1024]{3,2,1,0:T(8,128)(2,1)S(1)}, u32[]{:S(2)}, u32[]{:S(2)}) %collective-permute-start.14) | collective-permute-done | bytes 2097184 | tf_op jit(solution)/shard_map/stream1/ppermute | solution.py:205
  207.2 15.0 %stream0.1 = (bf16[128,1024]{1,0:T(8,128)(2,1)}, bf16[128,1024]{1,0:T(8,128)(2,1)}, f32[16,2,128,1024]{3,2,1,0:T(8,128)}) custom-call(s32[8]{0:T(128)} %multiply_add_fusion.pos_ref, bf16[128,1024]{1,0:T(8,128)(2,1)} %get-tuple-element.45.q_ref, bf16[128,1024]{1,0:T(8,128)(2,1)} %get-tuple-element.34.g_ref, bf16[32,128,1024]{2,1,0:T(8,128)(2,1)} %bitcast.153, ...), custom_call_target="tpu_custom_call" | custom-call | flops 1610612736 | bytes 22020096 | tf_op jit(solution)/shard_map/stream0/pallas_call | solution.py:298
  222.2 6.2 %unstack.255 = bf16[8,2,128,1024]{3,2,1,0:T(8,128)(2,1)} slice(f32[16,2,128,1024]{3,2,1,0:T(8,128)} %get-tuple-element.16), slice={[8:16], [0:2], [0:128], [0:1024]} | slice | bytes 8388608 | tf_op jit(solution)/shard_map/stream0/transpose()/unstack | solution.py:229
  228.9 6.2 %pad_maximum_fusion.1 = bf16[2,2,4,2,128,1024]{5,4,3,2,1,0:T(8,128)(2,1)} fusion(bf16[1,2,4,2,128,1024]{5,4,3,2,1,0:T(8,128)(2,1)} %bitcast.29, bf16[1,2,4,2,128,1024]{5,4,3,2,1,0:T(8,128)(2,1)S(1)} %copy-done.2), kind=kLoop, calls=%fused_computation.3 | loop fusion | flops 4194304 | bytes 16777216 | tf_op jit(solution)/shard_map/stream1/stack | solution.py:229
  235.1 15.0 %stream1.1 = (bf16[128,1024]{1,0:T(8,128)(2,1)}, bf16[128,1024]{1,0:T(8,128)(2,1)}, f32[16,2,128,1024]{3,2,1,0:T(8,128)}) custom-call(s32[8]{0:T(128)} %multiply_add_fusion.pos_ref, bf16[128,1024]{1,0:T(8,128)(2,1)} %get-tuple-element.44.q_ref, bf16[128,1024]{1,0:T(8,128)(2,1)} %get-tuple-element.35.g_ref, bf16[32,128,1024]{2,1,0:T(8,128)(2,1)} %bitcast.169, ...), custom_call_target="tpu_custom_call" | custom-call | flops 1610612736 | bytes 22020096 | tf_op jit(solution)/shard_map/stream1/pallas_call | solution.py:298
  250.1 6.1 %unstack.254 = bf16[8,2,128,1024]{3,2,1,0:T(8,128)(2,1)} slice(f32[16,2,128,1024]{3,2,1,0:T(8,128)} %get-tuple-element.17), slice={[8:16], [0:2], [0:128], [0:1024]} | slice | bytes 8388608 | tf_op jit(solution)/shard_map/stream1/transpose()/unstack | solution.py:229
  260.5 7.0 %convert_add_fusion.1 = f32[2,4,2,128,1024]{4,3,2,1,0:T(8,128)} fusion(f32[2,4,2,128,1024]{4,3,2,1,0:T(8,128)S(1)} %bitcast.185, bf16[2,4,2,128,1024]{4,3,2,1,0:T(8,128)(2,1)} %collective-permute-done.16), kind=kLoop, calls=%fused_computation.5 | loop fusion | flops 4194304 | bytes 20971520 | tf_op jit(solution)/shard_map/stream0/transpose()/add_any | solution.py:205
  284.9 35.4 %collective-permute-done.17 = bf16[4,2,128,1024]{3,2,1,0:T(8,128)(2,1)} collective-permute-done((bf16[4,2,128,1024]{3,2,1,0:T(8,128)(2,1)}, bf16[4,2,128,1024]{3,2,1,0:T(8,128)(2,1)}, u32[]{:S(2)}, u32[]{:S(2)}) %collective-permute-start.17) | collective-permute-done | bytes 2097184 | tf_op jit(solution)/shard_map/stream0/transpose()/ppermute | solution.py:205
  327.3 37.3 %collective-permute-done.25 = bf16[4,2,128,1024]{3,2,1,0:T(8,128)(2,1)S(1)} collective-permute-done((bf16[4,2,128,1024]{3,2,1,0:T(8,128)(2,1)S(1)}, bf16[4,2,128,1024]{3,2,1,0:T(8,128)(2,1)S(1)}, u32[]{:S(2)}, u32[]{:S(2)}) %collective-permute-start.25) | collective-permute-done | bytes 2097184 | tf_op jit(solution)/shard_map/stream1/transpose()/ppermute | solution.py:205
  372.1 11.9 %collective-permute-done.26 = bf16[2,128,1024]{2,1,0:T(8,128)(2,1)S(1)} collective-permute-done((bf16[2,128,1024]{2,1,0:T(8,128)(2,1)S(1)}, bf16[2,128,1024]{2,1,0:T(8,128)(2,1)S(1)}, u32[]{:S(2)}, u32[]{:S(2)}) %collective-permute-start.26) | collective-permute-done | bytes 524320 | tf_op jit(solution)/shard_map/stream1/transpose()/ppermute | solution.py:205
  386.1 9.1 %collective-permute-done.19 = bf16[2,128,1024]{2,1,0:T(8,128)(2,1)S(1)} collective-permute-done((bf16[2,128,1024]{2,1,0:T(8,128)(2,1)S(1)}, bf16[2,128,1024]{2,1,0:T(8,128)(2,1)S(1)}, u32[]{:S(2)}, u32[]{:S(2)}) %collective-permute-start.19) | collective-permute-done | bytes 524320 | tf_op jit(solution)/shard_map/stream0/transpose()/ppermute | solution.py:205
  397.1 4.7 %collective-permute-start.20 = (bf16[2,128,1024]{2,1,0:T(8,128)(2,1)S(1)}, bf16[2,128,1024]{2,1,0:T(8,128)(2,1)S(1)}, u32[]{:S(2)}, u32[]{:S(2)}) collective-permute-start(bf16[2,128,1024]{2,1,0:T(8,128)(2,1)S(1)} %get-tuple-element.18), channel_id=1, source_target_pairs={{0,4},{1,5},{2,6},{3,7},{4,8},{5,9},{6,10},{7,11},{8,12},{9,13},{1... | collective-permute-start | bytes 1572872 | tf_op jit(solution)/shard_map/stream0/transpose()/ppermute | solution.py:205
  417.0 6.5 %collective-permute-done.30 = bf16[2,128,1024]{2,1,0:T(8,128)(2,1)S(1)} collective-permute-done((bf16[2,128,1024]{2,1,0:T(8,128)(2,1)S(1)}, bf16[2,128,1024]{2,1,0:T(8,128)(2,1)S(1)}, u32[]{:S(2)}, u32[]{:S(2)}) %collective-permute-start.30) | collective-permute-done | bytes 524320 | tf_op jit(solution)/shard_map/stream1/transpose()/ppermute | solution.py:205
  425.6 9.1 %collective-permute-done.23 = bf16[2,128,1024]{2,1,0:T(8,128)(2,1)S(1)} collective-permute-done((bf16[2,128,1024]{2,1,0:T(8,128)(2,1)S(1)}, bf16[2,128,1024]{2,1,0:T(8,128)(2,1)S(1)}, u32[]{:S(2)}, u32[]{:S(2)}) %collective-permute-start.23) | collective-permute-done | bytes 524320 | tf_op jit(solution)/shard_map/stream0/transpose()/ppermute | solution.py:205
  435.1 7.7 %collective-permute-done.31 = bf16[2,128,1024]{2,1,0:T(8,128)(2,1)S(1)} collective-permute-done((bf16[2,128,1024]{2,1,0:T(8,128)(2,1)S(1)}, bf16[2,128,1024]{2,1,0:T(8,128)(2,1)S(1)}, u32[]{:S(2)}, u32[]{:S(2)}) %collective-permute-start.31) | collective-permute-done | bytes 524320 | tf_op jit(solution)/shard_map/stream1/transpose()/ppermute | solution.py:205
  (128 shorter events, 113.7 us)
Async XLA Ops:
  2.0 15.6 %collective-permute-start = (bf16[2,128,1024]{2,1,0:T(8,128)(2,1)S(1)}, bf16[2,128,1024]{2,1,0:T(8,128)(2,1)S(1)}, u32[]{:S(2)}, u32[]{:S(2)}) collective-permute-start(bf16[2,128,1024]{2,1,0:T(8,128)(2,1)S(1)} %pad_maximum_fusion.4), channel_id=1, source_target_pairs={{0,4},{1,5},{2,6},{3,7},{4,8},{5,9},{6,10},{7,11},{8,12},{9,13},{1... | collective-permute-start | bytes 1572872 | tf_op jit(solution)/shard_map/stream0/ppermute | solution.py:205
  5.5 16.4 %collective-permute-start.3 = (bf16[2,128,1024]{2,1,0:T(8,128)(2,1)S(1)}, bf16[2,128,1024]{2,1,0:T(8,128)(2,1)S(1)}, u32[]{:S(2)}, u32[]{:S(2)}) collective-permute-start(bf16[2,128,1024]{2,1,0:T(8,128)(2,1)S(1)} %pad_maximum_fusion.4), channel_id=1, source_target_pairs={{4,0},{5,1},{6,2},{7,3},{8,4},{9,5},{10,6},{11,7},{12,8},{13,9},{1... | collective-permute-start | bytes 1572872 | tf_op jit(solution)/shard_map/stream0/ppermute | solution.py:205
  21.8 14.4 %collective-permute-start.4 = (bf16[2,128,1024]{2,1,0:T(8,128)(2,1)S(1)}, bf16[2,128,1024]{2,1,0:T(8,128)(2,1)S(1)}, u32[]{:S(2)}, u32[]{:S(2)}) collective-permute-start(bf16[2,128,1024]{2,1,0:T(8,128)(2,1)S(1)} %collective-permute-done.3), channel_id=1, source_target_pairs={{4,0},{5,1},{6,2},{7,3},{8,4},{9,5},{10,6},{11,7},{20,16},{21,17},... | collective-permute-start | bytes 1572872 | tf_op jit(solution)/shard_map/stream0/ppermute | solution.py:205
  48.1 44.9 %collective-permute-start.6 = (bf16[4,2,128,1024]{3,2,1,0:T(8,128)(2,1)S(1)}, bf16[4,2,128,1024]{3,2,1,0:T(8,128)(2,1)S(1)}, u32[]{:S(2)}, u32[]{:S(2)}) collective-permute-start(bf16[4,2,128,1024]{3,2,1,0:T(8,128)(2,1)S(1)} %constant_dynamic-slice_fusion.1), channel_id=1, source_target_pairs={{0,2},{1,3},{2,0},{3,1},{4,6},{5,7},{6,4},{7,5},{8,10},{9,11},{10,... | collective-permute-start | bytes 6291464 | tf_op jit(solution)/shard_map/stream0/ppermute | solution.py:205
  109.0 16.0 %collective-permute-start.8 = (bf16[2,128,1024]{2,1,0:T(8,128)(2,1)S(1)}, bf16[2,128,1024]{2,1,0:T(8,128)(2,1)S(1)}, u32[]{:S(2)}, u32[]{:S(2)}) collective-permute-start(bf16[2,128,1024]{2,1,0:T(8,128)(2,1)S(1)} %pad_maximum_fusion.5), channel_id=1, source_target_pairs={{0,4},{1,5},{2,6},{3,7},{4,8},{5,9},{6,10},{7,11},{8,12},{9,13},{1... | collective-permute-start | bytes 1572872 | tf_op jit(solution)/shard_map/stream1/ppermute | solution.py:205
  112.5 16.3 %collective-permute-start.11 = (bf16[2,128,1024]{2,1,0:T(8,128)(2,1)S(1)}, bf16[2,128,1024]{2,1,0:T(8,128)(2,1)S(1)}, u32[]{:S(2)}, u32[]{:S(2)}) collective-permute-start(bf16[2,128,1024]{2,1,0:T(8,128)(2,1)S(1)} %pad_maximum_fusion.5), channel_id=1, source_target_pairs={{4,0},{5,1},{6,2},{7,3},{8,4},{9,5},{10,6},{11,7},{12,8},{13,9},{1... | collective-permute-start | bytes 1572872 | tf_op jit(solution)/shard_map/stream1/ppermute | solution.py:205
  128.9 15.0 %collective-permute-start.12 = (bf16[2,128,1024]{2,1,0:T(8,128)(2,1)S(1)}, bf16[2,128,1024]{2,1,0:T(8,128)(2,1)S(1)}, u32[]{:S(2)}, u32[]{:S(2)}) collective-permute-start(bf16[2,128,1024]{2,1,0:T(8,128)(2,1)S(1)} %collective-permute-done.11), channel_id=1, source_target_pairs={{4,0},{5,1},{6,2},{7,3},{8,4},{9,5},{10,6},{11,7},{20,16},{21,17},... | collective-permute-start | bytes 1572872 | tf_op jit(solution)/shard_map/stream1/ppermute | solution.py:205
  156.3 45.5 %collective-permute-start.14 = (bf16[4,2,128,1024]{3,2,1,0:T(8,128)(2,1)S(1)}, bf16[4,2,128,1024]{3,2,1,0:T(8,128)(2,1)S(1)}, u32[]{:S(2)}, u32[]{:S(2)}) collective-permute-start(bf16[4,2,128,1024]{3,2,1,0:T(8,128)(2,1)S(1)} %constant_dynamic-slice_fusion), channel_id=1, source_target_pairs={{0,2},{1,3},{2,0},{3,1},{4,6},{5,7},{6,4},{7,5},{8,10},{9,11},{10,... | collective-permute-start | bytes 6291464 | tf_op jit(solution)/shard_map/stream1/ppermute | solution.py:205
  205.4 23.5 %collective-permute-start.15 = (bf16[2,4,2,128,1024]{4,3,2,1,0:T(8,128)(2,1)}, bf16[2,4,2,128,1024]{4,3,2,1,0:T(8,128)(2,1)}, u32[]{:S(2)}, u32[]{:S(2)}) collective-permute-start(bf16[2,4,2,128,1024]{4,3,2,1,0:T(8,128)(2,1)} %get-tuple-element.23), channel_id=1, source_target_pairs={{0,1},{1,0},{2,3},{3,2},{4,5},{5,4},{6,7},{7,6},{8,9},{9,8},{10,11... | collective-permute-start | bytes 12582920 | tf_op jit(solution)/shard_map/stream1/ppermute | solution.py:205
  228.4 32.1 %collective-permute-start.16 = (bf16[2,4,2,128,1024]{4,3,2,1,0:T(8,128)(2,1)}, bf16[2,4,2,128,1024]{4,3,2,1,0:T(8,128)(2,1)}, u32[]{:S(2)}, u32[]{:S(2)}) collective-permute-start(bf16[2,4,2,128,1024]{4,3,2,1,0:T(8,128)(2,1)} %bitcast.32), channel_id=1, source_target_pairs={{1,0},{0,1},{3,2},{2,3},{5,4},{4,5},{7,6},{6,7},{9,8},{8,9},{11,10... | collective-permute-start | bytes 12582920 | tf_op jit(solution)/shard_map/stream0/transpose()/ppermute | solution.py:205
  256.2 20.9 %collective-permute-start.24 = (bf16[2,4,2,128,1024]{4,3,2,1,0:T(8,128)(2,1)}, bf16[2,4,2,128,1024]{4,3,2,1,0:T(8,128)(2,1)S(1)}, u32[]{:S(2)}, u32[]{:S(2)}) collective-permute-start(bf16[2,4,2,128,1024]{4,3,2,1,0:T(8,128)(2,1)} %bitcast.44), channel_id=1, source_target_pairs={{1,0},{0,1},{3,2},{2,3},{5,4},{4,5},{7,6},{6,7},{9,8},{8,9},{11,10... | collective-permute-start | bytes 12582920 | tf_op jit(solution)/shard_map/stream1/transpose()/ppermute | solution.py:205
  271.4 48.8 %collective-permute-start.17 = (bf16[4,2,128,1024]{3,2,1,0:T(8,128)(2,1)}, bf16[4,2,128,1024]{3,2,1,0:T(8,128)(2,1)}, u32[]{:S(2)}, u32[]{:S(2)}) collective-permute-start(bf16[4,2,128,1024]{3,2,1,0:T(8,128)(2,1)} %fusion.4), channel_id=1, source_target_pairs={{2,0},{3,1},{0,2},{1,3},{6,4},{7,5},{4,6},{5,7},{10,8},{11,9},{8,1... | collective-permute-start | bytes 6291464 | tf_op jit(solution)/shard_map/stream0/transpose()/ppermute | solution.py:205
  284.3 80.3 %collective-permute-start.25 = (bf16[4,2,128,1024]{3,2,1,0:T(8,128)(2,1)S(1)}, bf16[4,2,128,1024]{3,2,1,0:T(8,128)(2,1)S(1)}, u32[]{:S(2)}, u32[]{:S(2)}) collective-permute-start(bf16[4,2,128,1024]{3,2,1,0:T(8,128)(2,1)S(1)} %fusion.5), channel_id=1, source_target_pairs={{2,0},{3,1},{0,2},{1,3},{6,4},{7,5},{4,6},{5,7},{10,8},{11,9},{8,1... | collective-permute-start | bytes 6291464 | tf_op jit(solution)/shard_map/stream1/transpose()/ppermute | solution.py:205
  325.9 43.4 %collective-permute-start.18 = (bf16[2,128,1024]{2,1,0:T(8,128)(2,1)S(1)}, bf16[2,128,1024]{2,1,0:T(8,128)(2,1)S(1)}, u32[]{:S(2)}, u32[]{:S(2)}) collective-permute-start(bf16[2,128,1024]{2,1,0:T(8,128)(2,1)S(1)} %get-tuple-element.26), channel_id=1, source_target_pairs={{0,4},{1,5},{2,6},{3,7},{16,20},{17,21},{18,22},{19,23}} | collective-permute-start | bytes 1572872 | tf_op jit(solution)/shard_map/stream0/transpose()/ppermute | solution.py:205
  367.3 16.7 %collective-permute-start.26 = (bf16[2,128,1024]{2,1,0:T(8,128)(2,1)S(1)}, bf16[2,128,1024]{2,1,0:T(8,128)(2,1)S(1)}, u32[]{:S(2)}, u32[]{:S(2)}) collective-permute-start(bf16[2,128,1024]{2,1,0:T(8,128)(2,1)S(1)} %get-tuple-element.28), channel_id=1, source_target_pairs={{0,4},{1,5},{2,6},{3,7},{16,20},{17,21},{18,22},{19,23}} | collective-permute-start | bytes 1572872 | tf_op jit(solution)/shard_map/stream1/transpose()/ppermute | solution.py:205
  368.6 17.5 %collective-permute-start.21 = (bf16[2,128,1024]{2,1,0:T(8,128)(2,1)S(1)}, bf16[2,128,1024]{2,1,0:T(8,128)(2,1)S(1)}, u32[]{:S(2)}, u32[]{:S(2)}) collective-permute-start(bf16[2,128,1024]{2,1,0:T(8,128)(2,1)S(1)} %get-tuple-element.27), channel_id=1, source_target_pairs={{12,8},{13,9},{14,10},{15,11},{28,24},{29,25},{30,26},{31,27}} | collective-permute-start | bytes 1572872 | tf_op jit(solution)/shard_map/stream0/transpose()/ppermute | solution.py:205
  369.5 25.8 %collective-permute-start.19 = (bf16[2,128,1024]{2,1,0:T(8,128)(2,1)S(1)}, bf16[2,128,1024]{2,1,0:T(8,128)(2,1)S(1)}, u32[]{:S(2)}, u32[]{:S(2)}) collective-permute-start(bf16[2,128,1024]{2,1,0:T(8,128)(2,1)S(1)} %fusion.22), channel_id=1, source_target_pairs={{0,4},{1,5},{2,6},{3,7},{4,8},{5,9},{6,10},{7,11},{16,20},{17,21},... | collective-permute-start | bytes 1572872 | tf_op jit(solution)/shard_map/stream0/transpose()/ppermute | solution.py:205
  371.4 30.4 %collective-permute-start.29 = (bf16[2,128,1024]{2,1,0:T(8,128)(2,1)S(1)}, bf16[2,128,1024]{2,1,0:T(8,128)(2,1)S(1)}, u32[]{:S(2)}, u32[]{:S(2)}) collective-permute-start(bf16[2,128,1024]{2,1,0:T(8,128)(2,1)S(1)} %get-tuple-element.29), channel_id=1, source_target_pairs={{12,8},{13,9},{14,10},{15,11},{28,24},{29,25},{30,26},{31,27}} | collective-permute-start | bytes 1572872 | tf_op jit(solution)/shard_map/stream1/transpose()/ppermute | solution.py:205
  384.2 22.3 %collective-permute-start.27 = (bf16[2,128,1024]{2,1,0:T(8,128)(2,1)S(1)}, bf16[2,128,1024]{2,1,0:T(8,128)(2,1)S(1)}, u32[]{:S(2)}, u32[]{:S(2)}) collective-permute-start(bf16[2,128,1024]{2,1,0:T(8,128)(2,1)S(1)} %fusion.11), channel_id=1, source_target_pairs={{0,4},{1,5},{2,6},{3,7},{4,8},{5,9},{6,10},{7,11},{16,20},{17,21},... | collective-permute-start | bytes 1572872 | tf_op jit(solution)/shard_map/stream1/transpose()/ppermute | solution.py:205
  397.1 28.5 %collective-permute-start.20 = (bf16[2,128,1024]{2,1,0:T(8,128)(2,1)S(1)}, bf16[2,128,1024]{2,1,0:T(8,128)(2,1)S(1)}, u32[]{:S(2)}, u32[]{:S(2)}) collective-permute-start(bf16[2,128,1024]{2,1,0:T(8,128)(2,1)S(1)} %get-tuple-element.18), channel_id=1, source_target_pairs={{0,4},{1,5},{2,6},{3,7},{4,8},{5,9},{6,10},{7,11},{8,12},{9,13},{1... | collective-permute-start | bytes 1572872 | tf_op jit(solution)/shard_map/stream0/transpose()/ppermute | solution.py:205
  406.8 16.7 %collective-permute-start.30 = (bf16[2,128,1024]{2,1,0:T(8,128)(2,1)S(1)}, bf16[2,128,1024]{2,1,0:T(8,128)(2,1)S(1)}, u32[]{:S(2)}, u32[]{:S(2)}) collective-permute-start(bf16[2,128,1024]{2,1,0:T(8,128)(2,1)S(1)} %get-tuple-element.21), channel_id=1, source_target_pairs={{8,4},{9,5},{10,6},{11,7},{12,8},{13,9},{14,10},{15,11},{24,20},{2... | collective-permute-start | bytes 1572872 | tf_op jit(solution)/shard_map/stream1/transpose()/ppermute | solution.py:205
  409.5 25.3 %collective-permute-start.23 = (bf16[2,128,1024]{2,1,0:T(8,128)(2,1)S(1)}, bf16[2,128,1024]{2,1,0:T(8,128)(2,1)S(1)}, u32[]{:S(2)}, u32[]{:S(2)}) collective-permute-start(bf16[2,128,1024]{2,1,0:T(8,128)(2,1)S(1)} %fusion.20), channel_id=1, source_target_pairs={{4,0},{5,1},{6,2},{7,3},{8,4},{9,5},{10,6},{11,7},{12,8},{13,9},{1... | collective-permute-start | bytes 1572872 | tf_op jit(solution)/shard_map/stream0/transpose()/ppermute | solution.py:205
  413.1 22.0 %collective-permute-start.28 = (bf16[2,128,1024]{2,1,0:T(8,128)(2,1)S(1)}, bf16[2,128,1024]{2,1,0:T(8,128)(2,1)S(1)}, u32[]{:S(2)}, u32[]{:S(2)}) collective-permute-start(bf16[2,128,1024]{2,1,0:T(8,128)(2,1)S(1)} %get-tuple-element.20), channel_id=1, source_target_pairs={{0,4},{1,5},{2,6},{3,7},{4,8},{5,9},{6,10},{7,11},{8,12},{9,13},{1... | collective-permute-start | bytes 1572872 | tf_op jit(solution)/shard_map/stream1/transpose()/ppermute | solution.py:205
  423.7 19.1 %collective-permute-start.31 = (bf16[2,128,1024]{2,1,0:T(8,128)(2,1)S(1)}, bf16[2,128,1024]{2,1,0:T(8,128)(2,1)S(1)}, u32[]{:S(2)}, u32[]{:S(2)}) collective-permute-start(bf16[2,128,1024]{2,1,0:T(8,128)(2,1)S(1)} %fusion.9), channel_id=1, source_target_pairs={{4,0},{5,1},{6,2},{7,3},{8,4},{9,5},{10,6},{11,7},{12,8},{13,9},{1... | collective-permute-start | bytes 1572872 | tf_op jit(solution)/shard_map/stream1/transpose()/ppermute | solution.py:205
  (21 other events, 469.4 us)

commit v9 on v4

--- a/solution.py
+++ b/solution.py
@@ -299,7 +299,7 @@
 STREAMS = 2
 
 
-def _stream(pos, query, grad_out, keys, values, after=None):
+def _stream(pos, query, grad_out, keys, values, after=None, before_kernel=None):
     n = lax.axis_size("seq")
     rows, width = query.shape
     line_len = n // 4
@@ -307,6 +307,10 @@
         keys, values, _ = lax.optimization_barrier((keys, values, after))
     keys_local = gather_blocks(keys, n).reshape(n, rows, width)
     values_local = gather_blocks(values, n).reshape(n, rows, width)
+    if before_kernel is not None:
+        keys_local, values_local, _ = lax.optimization_barrier(
+            (keys_local, values_local, before_kernel)
+        )
     attended, grad_query, part_keys, part_values = attend_local(
         pos, query, grad_out, keys_local, values_local
     )
@@ -316,7 +320,7 @@
     (grad_keys,) = scatter(part_keys.reshape(2, 2, line_len, rows, width))
     (grad_values,) = scatter(part_values.reshape(2, 2, line_len, rows, width))
     outs = (attended, grad_query, grad_keys.astype(jnp.bfloat16), grad_values.astype(jnp.bfloat16))
-    return outs, (keys_local, values_local)
+    return outs, (attended, outs[2:])
 
 
 def shards_gather(query, keys, values, grad_out, global_blocks, random_blocks):
@@ -337,13 +341,20 @@
     pos = (((listed % 2) ^ core) * 2 + (((listed // 2) % 2) ^ ypos)) * line_len + listed // 4
     cut = width // STREAMS
     outs = []
-    after = None
+    after = before_kernel = None
     for s in range(STREAMS):
         cols = slice(s * cut, (s + 1) * cut)
         with jax.named_scope(f"stream{s}"):
-            out, after = _stream(
-                pos, query[:, cols], grad_out[:, cols], keys[:, cols], values[:, cols], after
+            out, tie = _stream(
+                pos,
+                query[:, cols],
+                grad_out[:, cols],
+                keys[:, cols],
+                values[:, cols],
+                after,
+                before_kernel,
             )
+            after, before_kernel = tie
             outs.append(out)
     return tuple(jnp.concatenate(parts, axis=1) for parts in zip(*outs))
 

time: 388 us -> 408 us (1.052)
  waiting for transfers between devices: 182 us -> 202 us
    ppermute x64, waiting for transfers between devices: 182 us -> 202 us  [_send(): return lax.ppermute(v.astype(jnp.bfloat16), 'seq', pairs).astype(v.dtype)]
  transfers between devices with their start and end apart: 64 -> 64, of which waited for: 24 -> 26; matrix products, arithmetic and copies ran while one was open for 12% -> 11% of each run, Pallas kernels for 8% -> 0%
where the time goes in v9:
time: 408 us; the launch traced here: 404 us
  waiting for transfers between devices  202 us (50%)
  starting transfers between devices  116 us (28%)
  Pallas kernels  29.7 us (7%)
  other arithmetic  28.7 us (7%)
  local copies, waits for them, and re-layouts  25.5 us (6%)
    ppermute x64, waiting for transfers between devices, _send(): return lax.ppermute(v.astype(jnp.bfloat16), 'seq', pairs).astype(v.dtype)  202 us
    ppermute x64, starting transfers between devices, _send(): return lax.ppermute(v.astype(jnp.bfloat16), 'seq', pairs).astype(v.dtype)  116 us
    pallas_call x2, Pallas kernels, attend_local(): call(pos, query, grad_out, *[keys_local] * SLOTS, *[values_local] * SLOTS)  29.7 us
    another operation x8, other arithmetic, gather_blocks(): return jnp.stack([pair, sibling])  17.3 us
    another operation x8, local copies, waits for them, and re-layouts, gather_blocks(): return jnp.stack([pair, sibling])  14.9 us
  transfers between devices with their start and end apart: 64, of which 26 were waited for; matrix products, arithmetic and copies ran while one was open for 11% of the time, Pallas kernels for 0%

profile of v9, /device:TPU:10, one launch (start us, length us, event | category | flops | bytes accessed | tf_op | source)
XLA Modules:
  0.0 403.6 jit_solution(10170463664441954876)
XLA Ops:
  1.8 3.5 collective-permute-start.8
  20.0 3.9 collective-permute-start.1
  32.6 4.4 %collective-permute-start.5 = (bf16[128,1024]{1,0:T(8,128)(2,1)S(1)}, bf16[128,1024]{1,0:T(8,128)(2,1)S(1)}, u32[]{:S(2)}, u32[]{:S(2)}) collective-permute-start(bf16[128,1024]{1,0:T(8,128)(2,1)S(1)} %collective-permute-done.4), channel_id=1, source_target_pairs={{4,0},{5,1},{6,2},{7,3},{20,16},{21,17},{22,18},{23,19}} | collective-permute-start | bytes 786440 | tf_op jit(solution)/shard_map/stream0/ppermute | solution.py:205
  43.5 20.9 %collective-permute-done.14 = bf16[4,128,1024]{2,1,0:T(8,128)(2,1)S(1)} collective-permute-done((bf16[4,128,1024]{2,1,0:T(8,128)(2,1)S(1)}, bf16[4,128,1024]{2,1,0:T(8,128)(2,1)S(1)}, u32[]{:S(2)}, u32[]{:S(2)}) %collective-permute-start.14) | collective-permute-done | bytes 1048608 | tf_op jit(solution)/shard_map/stream0/ppermute | solution.py:205
  66.1 15.8 %collective-permute-done.6 = bf16[4,128,1024]{2,1,0:T(8,128)(2,1)S(1)} collective-permute-done((bf16[4,128,1024]{2,1,0:T(8,128)(2,1)S(1)}, bf16[4,128,1024]{2,1,0:T(8,128)(2,1)S(1)}, u32[]{:S(2)}, u32[]{:S(2)}) %collective-permute-start.6) | collective-permute-done | bytes 1048608 | tf_op jit(solution)/shard_map/stream0/ppermute | solution.py:205
  87.7 4.1 %pad_maximum_fusion.1 = bf16[2,2,4,128,1024]{4,3,2,1,0:T(8,128)(2,1)} fusion(bf16[1,2,4,128,1024]{4,3,2,1,0:T(8,128)(2,1)} %bitcast.25, bf16[1,2,4,128,1024]{4,3,2,1,0:T(8,128)(2,1)S(1)} %get-tuple-element.40), kind=kLoop, calls=%fused_computation.5 | loop fusion | flops 2097152 | bytes 8388608 | tf_op jit(solution)/shard_map/stream0/stack | solution.py:227
  91.9 4.0 pad_maximum_fusion
  95.9 14.8 %stream0.1 = (bf16[128,1024]{1,0:T(8,128)(2,1)}, bf16[128,1024]{1,0:T(8,128)(2,1)}, f32[16,128,1024]{2,1,0:T(8,128)}, f32[16,128,1024]{2,1,0:T(8,128)}) custom-call(s32[8]{0:T(128)} %multiply_add_fusion.pos_ref, bf16[128,1024]{1,0:T(8,128)(2,1)} %get-tuple-element.58.q_ref, bf16[128,1024]{1,0:T(8,128)(2,1)} %get-tuple-element.56.g_ref, ...), custom_call_target="tpu_custom_call" | custom-call | flops 1610612736 | bytes 22020096 | tf_op jit(solution)/shard_map/stream0/pallas_call | solution.py:294
  112.6 3.9 collective-permute-start.27
  118.8 3.6 collective-permute-start.19
  146.5 4.3 %collective-permute-done.29 = bf16[128,1024]{1,0:T(8,128)(2,1)S(1)} collective-permute-done((bf16[128,1024]{1,0:T(8,128)(2,1)S(1)}, bf16[128,1024]{1,0:T(8,128)(2,1)S(1)}, u32[]{:S(2)}, u32[]{:S(2)}) %collective-permute-start.29) | collective-permute-done | bytes 262176 | tf_op jit(solution)/shard_map/stream1/ppermute | solution.py:205
  161.6 15.4 %collective-permute-done.30 = bf16[4,128,1024]{2,1,0:T(8,128)(2,1)S(1)} collective-permute-done((bf16[4,128,1024]{2,1,0:T(8,128)(2,1)S(1)}, bf16[4,128,1024]{2,1,0:T(8,128)(2,1)S(1)}, u32[]{:S(2)}, u32[]{:S(2)}) %collective-permute-start.30) | collective-permute-done | bytes 1048608 | tf_op jit(solution)/shard_map/stream1/ppermute | solution.py:205
  177.4 22.1 %collective-permute-done.22 = bf16[4,128,1024]{2,1,0:T(8,128)(2,1)S(1)} collective-permute-done((bf16[4,128,1024]{2,1,0:T(8,128)(2,1)S(1)}, bf16[4,128,1024]{2,1,0:T(8,128)(2,1)S(1)}, u32[]{:S(2)}, u32[]{:S(2)}) %collective-permute-start.22) | collective-permute-done | bytes 1048608 | tf_op jit(solution)/shard_map/stream1/ppermute | solution.py:205
  199.9 22.1 %collective-permute-done.41 = bf16[4,128,1024]{2,1,0:T(8,128)(2,1)S(1)} collective-permute-done((bf16[4,128,1024]{2,1,0:T(8,128)(2,1)S(1)}, bf16[4,128,1024]{2,1,0:T(8,128)(2,1)S(1)}, u32[]{:S(2)}, u32[]{:S(2)}) %collective-permute-start.41) | collective-permute-done | bytes 1048608 | tf_op jit(solution)/shard_map/stream0/transpose()/ppermute | solution.py:205
  224.5 17.8 %collective-permute-done.33 = bf16[4,128,1024]{2,1,0:T(8,128)(2,1)S(1)} collective-permute-done((bf16[4,128,1024]{2,1,0:T(8,128)(2,1)S(1)}, bf16[4,128,1024]{2,1,0:T(8,128)(2,1)S(1)}, u32[]{:S(2)}, u32[]{:S(2)}) %collective-permute-start.33) | collective-permute-done | bytes 1048608 | tf_op jit(solution)/shard_map/stream0/transpose()/ppermute | solution.py:205
  247.7 7.1 %collective-permute-done.34 = bf16[128,1024]{1,0:T(8,128)(2,1)S(1)} collective-permute-done((bf16[128,1024]{1,0:T(8,128)(2,1)S(1)}, bf16[128,1024]{1,0:T(8,128)(2,1)S(1)}, u32[]{:S(2)}, u32[]{:S(2)}) %collective-permute-start.34) | collective-permute-done | bytes 262176 | tf_op jit(solution)/shard_map/stream0/transpose()/ppermute | solution.py:205
  265.2 4.6 %collective-permute-start.44 = (bf16[128,1024]{1,0:T(8,128)(2,1)S(1)}, bf16[128,1024]{1,0:T(8,128)(2,1)S(1)}, u32[]{:S(2)}, u32[]{:S(2)}) collective-permute-start(bf16[128,1024]{1,0:T(8,128)(2,1)S(1)} %get-tuple-element.32), channel_id=1, source_target_pairs={{0,4},{1,5},{2,6},{3,7},{4,8},{5,9},{6,10},{7,11},{8,12},{9,13},{1... | collective-permute-start | bytes 786440 | tf_op jit(solution)/shard_map/stream0/transpose()/ppermute | solution.py:205
  285.8 14.8 %stream1.1 = (bf16[128,1024]{1,0:T(8,128)(2,1)}, bf16[128,1024]{1,0:T(8,128)(2,1)}, f32[16,128,1024]{2,1,0:T(8,128)}, f32[16,128,1024]{2,1,0:T(8,128)}) custom-call(s32[8]{0:T(128)} %multiply_add_fusion.pos_ref, bf16[128,1024]{1,0:T(8,128)(2,1)} %get-tuple-element.59.q_ref, bf16[128,1024]{1,0:T(8,128)(2,1)} %get-tuple-element.57.g_ref, ...), custom_call_target="tpu_custom_call" | custom-call | flops 1610612736 | bytes 22020096 | tf_op jit(solution)/shard_map/stream1/pallas_call | solution.py:294
  314.6 22.7 %collective-permute-done.57 = bf16[4,128,1024]{2,1,0:T(8,128)(2,1)S(1)} collective-permute-done((bf16[4,128,1024]{2,1,0:T(8,128)(2,1)S(1)}, bf16[4,128,1024]{2,1,0:T(8,128)(2,1)S(1)}, u32[]{:S(2)}, u32[]{:S(2)}) %collective-permute-start.57) | collective-permute-done | bytes 1048608 | tf_op jit(solution)/shard_map/stream1/transpose()/ppermute | solution.py:205
  339.9 19.0 %collective-permute-done.49 = bf16[4,128,1024]{2,1,0:T(8,128)(2,1)S(1)} collective-permute-done((bf16[4,128,1024]{2,1,0:T(8,128)(2,1)S(1)}, bf16[4,128,1024]{2,1,0:T(8,128)(2,1)S(1)}, u32[]{:S(2)}, u32[]{:S(2)}) %collective-permute-start.49) | collective-permute-done | bytes 1048608 | tf_op jit(solution)/shard_map/stream1/transpose()/ppermute | solution.py:205
  365.7 5.5 %collective-permute-done.50 = bf16[128,1024]{1,0:T(8,128)(2,1)S(1)} collective-permute-done((bf16[128,1024]{1,0:T(8,128)(2,1)S(1)}, bf16[128,1024]{1,0:T(8,128)(2,1)S(1)}, u32[]{:S(2)}, u32[]{:S(2)}) %collective-permute-start.50) | collective-permute-done | bytes 262176 | tf_op jit(solution)/shard_map/stream1/transpose()/ppermute | solution.py:205
  373.2 3.6 collective-permute-done.59
  378.5 4.6 %collective-permute-start.60 = (bf16[128,1024]{1,0:T(8,128)(2,1)S(1)}, bf16[128,1024]{1,0:T(8,128)(2,1)S(1)}, u32[]{:S(2)}, u32[]{:S(2)}) collective-permute-start(bf16[128,1024]{1,0:T(8,128)(2,1)S(1)} %get-tuple-element.28), channel_id=1, source_target_pairs={{0,4},{1,5},{2,6},{3,7},{4,8},{5,9},{6,10},{7,11},{8,12},{9,13},{1... | collective-permute-start | bytes 786440 | tf_op jit(solution)/shard_map/stream1/transpose()/ppermute | solution.py:205
  390.3 3.9 collective-permute-start.52
  (237 shorter events, 155.0 us)
Async XLA Ops:
  38.3 26.1 %collective-permute-start.14 = (bf16[4,128,1024]{2,1,0:T(8,128)(2,1)S(1)}, bf16[4,128,1024]{2,1,0:T(8,128)(2,1)S(1)}, u32[]{:S(2)}, u32[]{:S(2)}) collective-permute-start(bf16[4,128,1024]{2,1,0:T(8,128)(2,1)S(1)} %constant_dynamic-slice_fusion.2), channel_id=1, source_target_pairs={{0,2},{1,3},{2,0},{3,1},{4,6},{5,7},{6,4},{7,5},{8,10},{9,11},{10,... | collective-permute-start | bytes 3145736 | tf_op jit(solution)/shard_map/stream0/ppermute | solution.py:205
  41.9 40.0 %collective-permute-start.6 = (bf16[4,128,1024]{2,1,0:T(8,128)(2,1)S(1)}, bf16[4,128,1024]{2,1,0:T(8,128)(2,1)S(1)}, u32[]{:S(2)}, u32[]{:S(2)}) collective-permute-start(bf16[4,128,1024]{2,1,0:T(8,128)(2,1)S(1)} %constant_dynamic-slice_fusion.3), channel_id=1, source_target_pairs={{0,2},{1,3},{2,0},{3,1},{4,6},{5,7},{6,4},{7,5},{8,10},{9,11},{10,... | collective-permute-start | bytes 3145736 | tf_op jit(solution)/shard_map/stream0/ppermute | solution.py:205
  66.0 21.7 %collective-permute-start.15 = (bf16[2,4,128,1024]{3,2,1,0:T(8,128)(2,1)}, bf16[2,4,128,1024]{3,2,1,0:T(8,128)(2,1)}, u32[]{:S(2)}, u32[]{:S(2)}) collective-permute-start(bf16[2,4,128,1024]{3,2,1,0:T(8,128)(2,1)} %get-tuple-element.41), channel_id=1, source_target_pairs={{0,1},{1,0},{2,3},{3,2},{4,5},{5,4},{6,7},{7,6},{8,9},{9,8},{10,11... | collective-permute-start | bytes 6291464 | tf_op jit(solution)/shard_map/stream0/ppermute | solution.py:205
  124.7 17.6 %collective-permute-start.28 = (bf16[128,1024]{1,0:T(8,128)(2,1)S(1)}, bf16[128,1024]{1,0:T(8,128)(2,1)S(1)}, u32[]{:S(2)}, u32[]{:S(2)}) collective-permute-start(bf16[128,1024]{1,0:T(8,128)(2,1)S(1)} %collective-permute-done.27), channel_id=1, source_target_pairs={{4,0},{5,1},{6,2},{7,3},{8,4},{9,5},{10,6},{11,7},{20,16},{21,17},... | collective-permute-start | bytes 786440 | tf_op jit(solution)/shard_map/stream1/ppermute | solution.py:205
  127.3 15.5 %collective-permute-start.17 = (bf16[128,1024]{1,0:T(8,128)(2,1)S(1)}, bf16[128,1024]{1,0:T(8,128)(2,1)S(1)}, u32[]{:S(2)}, u32[]{:S(2)}) collective-permute-start(bf16[128,1024]{1,0:T(8,128)(2,1)S(1)} %collective-permute-done.16), channel_id=1, source_target_pairs={{4,8},{5,9},{6,10},{7,11},{8,12},{9,13},{10,14},{11,15},{20,24},{2... | collective-permute-start | bytes 786440 | tf_op jit(solution)/shard_map/stream1/ppermute | solution.py:205
  130.7 13.5 %collective-permute-start.20 = (bf16[128,1024]{1,0:T(8,128)(2,1)S(1)}, bf16[128,1024]{1,0:T(8,128)(2,1)S(1)}, u32[]{:S(2)}, u32[]{:S(2)}) collective-permute-start(bf16[128,1024]{1,0:T(8,128)(2,1)S(1)} %collective-permute-done.19), channel_id=1, source_target_pairs={{4,0},{5,1},{6,2},{7,3},{8,4},{9,5},{10,6},{11,7},{20,16},{21,17},... | collective-permute-start | bytes 786440 | tf_op jit(solution)/shard_map/stream1/ppermute | solution.py:205
  142.3 15.4 %collective-permute-start.40 = (bf16[2,4,128,1024]{3,2,1,0:T(8,128)(2,1)S(1)}, bf16[2,4,128,1024]{3,2,1,0:T(8,128)(2,1)S(1)}, u32[]{:S(2)}, u32[]{:S(2)}) collective-permute-start(bf16[2,4,128,1024]{3,2,1,0:T(8,128)(2,1)S(1)} %bitcast.310), channel_id=1, source_target_pairs={{1,0},{0,1},{3,2},{2,3},{5,4},{4,5},{7,6},{6,7},{9,8},{8,9},{11,10... | collective-permute-start | bytes 6291464 | tf_op jit(solution)/shard_map/stream0/transpose()/ppermute | solution.py:205
  142.3 16.7 %collective-permute-start.32 = (bf16[2,4,128,1024]{3,2,1,0:T(8,128)(2,1)S(1)}, bf16[2,4,128,1024]{3,2,1,0:T(8,128)(2,1)S(1)}, u32[]{:S(2)}, u32[]{:S(2)}) collective-permute-start(bf16[2,4,128,1024]{3,2,1,0:T(8,128)(2,1)S(1)} %bitcast.309), channel_id=1, source_target_pairs={{1,0},{0,1},{3,2},{2,3},{5,4},{4,5},{7,6},{6,7},{9,8},{8,9},{11,10... | collective-permute-start | bytes 6291464 | tf_op jit(solution)/shard_map/stream0/transpose()/ppermute | solution.py:205
  150.9 26.1 %collective-permute-start.30 = (bf16[4,128,1024]{2,1,0:T(8,128)(2,1)S(1)}, bf16[4,128,1024]{2,1,0:T(8,128)(2,1)S(1)}, u32[]{:S(2)}, u32[]{:S(2)}) collective-permute-start(bf16[4,128,1024]{2,1,0:T(8,128)(2,1)S(1)} %constant_dynamic-slice_fusion), channel_id=1, source_target_pairs={{0,2},{1,3},{2,0},{3,1},{4,6},{5,7},{6,4},{7,5},{8,10},{9,11},{10,... | collective-permute-start | bytes 3145736 | tf_op jit(solution)/shard_map/stream1/ppermute | solution.py:205
  155.9 43.6 %collective-permute-start.22 = (bf16[4,128,1024]{2,1,0:T(8,128)(2,1)S(1)}, bf16[4,128,1024]{2,1,0:T(8,128)(2,1)S(1)}, u32[]{:S(2)}, u32[]{:S(2)}) collective-permute-start(bf16[4,128,1024]{2,1,0:T(8,128)(2,1)S(1)} %constant_dynamic-slice_fusion.1), channel_id=1, source_target_pairs={{0,2},{1,3},{2,0},{3,1},{4,6},{5,7},{6,4},{7,5},{8,10},{9,11},{10,... | collective-permute-start | bytes 3145736 | tf_op jit(solution)/shard_map/stream1/ppermute | solution.py:205
  158.5 63.4 %collective-permute-start.41 = (bf16[4,128,1024]{2,1,0:T(8,128)(2,1)S(1)}, bf16[4,128,1024]{2,1,0:T(8,128)(2,1)S(1)}, u32[]{:S(2)}, u32[]{:S(2)}) collective-permute-start(bf16[4,128,1024]{2,1,0:T(8,128)(2,1)S(1)} %fusion.9), channel_id=1, source_target_pairs={{2,0},{3,1},{0,2},{1,3},{6,4},{7,5},{4,6},{5,7},{10,8},{11,9},{8,1... | collective-permute-start | bytes 3145736 | tf_op jit(solution)/shard_map/stream0/transpose()/ppermute | solution.py:205
  159.9 82.5 %collective-permute-start.33 = (bf16[4,128,1024]{2,1,0:T(8,128)(2,1)S(1)}, bf16[4,128,1024]{2,1,0:T(8,128)(2,1)S(1)}, u32[]{:S(2)}, u32[]{:S(2)}) collective-permute-start(bf16[4,128,1024]{2,1,0:T(8,128)(2,1)S(1)} %fusion.8), channel_id=1, source_target_pairs={{2,0},{3,1},{0,2},{1,3},{6,4},{7,5},{4,6},{5,7},{10,8},{11,9},{8,1... | collective-permute-start | bytes 3145736 | tf_op jit(solution)/shard_map/stream0/transpose()/ppermute | solution.py:205
  177.3 99.5 %collective-permute-start.31 = (bf16[2,4,128,1024]{3,2,1,0:T(8,128)(2,1)S(1)}, bf16[2,4,128,1024]{3,2,1,0:T(8,128)(2,1)S(1)}, u32[]{:S(2)}, u32[]{:S(2)}) collective-permute-start(bf16[2,4,128,1024]{3,2,1,0:T(8,128)(2,1)S(1)} %get-tuple-element.37), channel_id=1, source_target_pairs={{0,1},{1,0},{2,3},{3,2},{4,5},{5,4},{6,7},{7,6},{8,9},{9,8},{10,11... | collective-permute-start | bytes 6291464 | tf_op jit(solution)/shard_map/stream1/ppermute | solution.py:205
  199.8 81.5 %collective-permute-start.23 = (bf16[2,4,128,1024]{3,2,1,0:T(8,128)(2,1)S(1)}, bf16[2,4,128,1024]{3,2,1,0:T(8,128)(2,1)S(1)}, u32[]{:S(2)}, u32[]{:S(2)}) collective-permute-start(bf16[2,4,128,1024]{3,2,1,0:T(8,128)(2,1)S(1)} %get-tuple-element.39), channel_id=1, source_target_pairs={{0,1},{1,0},{2,3},{3,2},{4,5},{5,4},{6,7},{7,6},{8,9},{9,8},{10,11... | collective-permute-start | bytes 6291464 | tf_op jit(solution)/shard_map/stream1/ppermute | solution.py:205
  223.2 22.4 %collective-permute-start.42 = (bf16[128,1024]{1,0:T(8,128)(2,1)S(1)}, bf16[128,1024]{1,0:T(8,128)(2,1)S(1)}, u32[]{:S(2)}, u32[]{:S(2)}) collective-permute-start(bf16[128,1024]{1,0:T(8,128)(2,1)S(1)} %get-tuple-element.48), channel_id=1, source_target_pairs={{0,4},{1,5},{2,6},{3,7},{16,20},{17,21},{18,22},{19,23}} | collective-permute-start | bytes 786440 | tf_op jit(solution)/shard_map/stream0/transpose()/ppermute | solution.py:205
  245.7 14.6 %collective-permute-start.43 = (bf16[128,1024]{1,0:T(8,128)(2,1)S(1)}, bf16[128,1024]{1,0:T(8,128)(2,1)S(1)}, u32[]{:S(2)}, u32[]{:S(2)}) collective-permute-start(bf16[128,1024]{1,0:T(8,128)(2,1)S(1)} %fusion.39), channel_id=1, source_target_pairs={{0,4},{1,5},{2,6},{3,7},{4,8},{5,9},{6,10},{7,11},{16,20},{17,21},... | collective-permute-start | bytes 786440 | tf_op jit(solution)/shard_map/stream0/transpose()/ppermute | solution.py:205
  265.2 18.5 %collective-permute-start.44 = (bf16[128,1024]{1,0:T(8,128)(2,1)S(1)}, bf16[128,1024]{1,0:T(8,128)(2,1)S(1)}, u32[]{:S(2)}, u32[]{:S(2)}) collective-permute-start(bf16[128,1024]{1,0:T(8,128)(2,1)S(1)} %get-tuple-element.32), channel_id=1, source_target_pairs={{0,4},{1,5},{2,6},{3,7},{4,8},{5,9},{6,10},{7,11},{8,12},{9,13},{1... | collective-permute-start | bytes 786440 | tf_op jit(solution)/shard_map/stream0/transpose()/ppermute | solution.py:205
  270.8 13.1 %collective-permute-start.36 = (bf16[128,1024]{1,0:T(8,128)(2,1)S(1)}, bf16[128,1024]{1,0:T(8,128)(2,1)S(1)}, u32[]{:S(2)}, u32[]{:S(2)}) collective-permute-start(bf16[128,1024]{1,0:T(8,128)(2,1)S(1)} %get-tuple-element.34), channel_id=1, source_target_pairs={{0,4},{1,5},{2,6},{3,7},{4,8},{5,9},{6,10},{7,11},{8,12},{9,13},{1... | collective-permute-start | bytes 786440 | tf_op jit(solution)/shard_map/stream0/transpose()/ppermute | solution.py:205
  311.2 26.1 %collective-permute-start.57 = (bf16[4,128,1024]{2,1,0:T(8,128)(2,1)S(1)}, bf16[4,128,1024]{2,1,0:T(8,128)(2,1)S(1)}, u32[]{:S(2)}, u32[]{:S(2)}) collective-permute-start(bf16[4,128,1024]{2,1,0:T(8,128)(2,1)S(1)} %fusion.11), channel_id=1, source_target_pairs={{2,0},{3,1},{0,2},{1,3},{6,4},{7,5},{4,6},{5,7},{10,8},{11,9},{8,1... | collective-permute-start | bytes 3145736 | tf_op jit(solution)/shard_map/stream1/transpose()/ppermute | solution.py:205
  314.1 44.7 %collective-permute-start.49 = (bf16[4,128,1024]{2,1,0:T(8,128)(2,1)S(1)}, bf16[4,128,1024]{2,1,0:T(8,128)(2,1)S(1)}, u32[]{:S(2)}, u32[]{:S(2)}) collective-permute-start(bf16[4,128,1024]{2,1,0:T(8,128)(2,1)S(1)} %fusion.10), channel_id=1, source_target_pairs={{2,0},{3,1},{0,2},{1,3},{6,4},{7,5},{4,6},{5,7},{10,8},{11,9},{8,1... | collective-permute-start | bytes 3145736 | tf_op jit(solution)/shard_map/stream1/transpose()/ppermute | solution.py:205
  338.6 23.5 %collective-permute-start.58 = (bf16[128,1024]{1,0:T(8,128)(2,1)S(1)}, bf16[128,1024]{1,0:T(8,128)(2,1)S(1)}, u32[]{:S(2)}, u32[]{:S(2)}) collective-permute-start(bf16[128,1024]{1,0:T(8,128)(2,1)S(1)} %get-tuple-element.44), channel_id=1, source_target_pairs={{0,4},{1,5},{2,6},{3,7},{16,20},{17,21},{18,22},{19,23}} | collective-permute-start | bytes 786440 | tf_op jit(solution)/shard_map/stream1/transpose()/ppermute | solution.py:205
  362.2 14.6 %collective-permute-start.59 = (bf16[128,1024]{1,0:T(8,128)(2,1)S(1)}, bf16[128,1024]{1,0:T(8,128)(2,1)S(1)}, u32[]{:S(2)}, u32[]{:S(2)}) collective-permute-start(bf16[128,1024]{1,0:T(8,128)(2,1)S(1)} %fusion.17), channel_id=1, source_target_pairs={{0,4},{1,5},{2,6},{3,7},{4,8},{5,9},{6,10},{7,11},{16,20},{17,21},... | collective-permute-start | bytes 786440 | tf_op jit(solution)/shard_map/stream1/transpose()/ppermute | solution.py:205
  365.0 18.0 %collective-permute-start.53 = (bf16[128,1024]{1,0:T(8,128)(2,1)S(1)}, bf16[128,1024]{1,0:T(8,128)(2,1)S(1)}, u32[]{:S(2)}, u32[]{:S(2)}) collective-permute-start(bf16[128,1024]{1,0:T(8,128)(2,1)S(1)} %get-tuple-element.47), channel_id=1, source_target_pairs={{12,8},{13,9},{14,10},{15,11},{28,24},{29,25},{30,26},{31,27}} | collective-permute-start | bytes 786440 | tf_op jit(solution)/shard_map/stream1/transpose()/ppermute | solution.py:205
  378.5 17.8 %collective-permute-start.60 = (bf16[128,1024]{1,0:T(8,128)(2,1)S(1)}, bf16[128,1024]{1,0:T(8,128)(2,1)S(1)}, u32[]{:S(2)}, u32[]{:S(2)}) collective-permute-start(bf16[128,1024]{1,0:T(8,128)(2,1)S(1)} %get-tuple-element.28), channel_id=1, source_target_pairs={{0,4},{1,5},{2,6},{3,7},{4,8},{5,9},{6,10},{7,11},{8,12},{9,13},{1... | collective-permute-start | bytes 786440 | tf_op jit(solution)/shard_map/stream1/transpose()/ppermute | solution.py:205
  (54 other events, 618.5 us)

commit v10 on v4

--- a/solution.py
+++ b/solution.py
@@ -250,8 +250,9 @@
     gq_ref[...] = (jnp.dot(gs, k_all, preferred_element_type=jnp.float32) * scale).astype(
         jnp.bfloat16
     )
-    gk = jnp.dot(gs32.T.astype(jnp.bfloat16), q, preferred_element_type=jnp.float32) * scale
-    gv = jnp.dot(p.T.astype(jnp.bfloat16), g, preferred_element_type=jnp.float32)
+    tn = (((0,), (0,)), ((), ()))
+    gk = lax.dot_general(gs, q, tn, preferred_element_type=jnp.float32) * scale
+    gv = lax.dot_general(w, g, tn, preferred_element_type=jnp.float32)
     dk_ref[...] = jnp.zeros(dk_ref.shape, jnp.float32)
     dv_ref[...] = jnp.zeros(dv_ref.shape, jnp.float32)
     rows = q.shape[0]

time: 388 us -> 388 us (level)
  no operation moved by 1% of the time
where the time goes in v10:
time: 388 us; the launch traced here: 384 us
  waiting for transfers between devices  182 us (47%)
  starting transfers between devices  115 us (30%)
  other arithmetic  29.8 us (8%)
  Pallas kernels  29.6 us (8%)
  local copies, waits for them, and re-layouts  25 us (6%)
    ppermute x64, waiting for transfers between devices, _send(): return lax.ppermute(v.astype(jnp.bfloat16), 'seq', pairs).astype(v.dtype)  182 us
    ppermute x64, starting transfers between devices, _send(): return lax.ppermute(v.astype(jnp.bfloat16), 'seq', pairs).astype(v.dtype)  115 us
    pallas_call x2, Pallas kernels, attend_local(): call(pos, query, grad_out, *[keys_local] * SLOTS, *[values_local] * SLOTS)  29.6 us
    another operation x8, other arithmetic, gather_blocks(): return jnp.stack([pair, sibling])  13.9 us
    another operation x8, local copies, waits for them, and re-layouts, gather_blocks(): return jnp.stack([pair, sibling])  12.3 us
  transfers between devices with their start and end apart: 64, of which 24 were waited for; matrix products, arithmetic and copies ran while one was open for 12% of the time, Pallas kernels for 8%

profile of v10, /device:TPU:10, one launch (start us, length us, event | category | flops | bytes accessed | tf_op | source)
XLA Modules:
  0.0 383.5 jit_solution(9126151561233732283)
XLA Ops:
  20.0 3.9 %collective-permute-start.1 = (bf16[128,1024]{1,0:T(8,128)(2,1)S(1)}, bf16[128,1024]{1,0:T(8,128)(2,1)S(1)}, u32[]{:S(2)}, u32[]{:S(2)}) collective-permute-start(bf16[128,1024]{1,0:T(8,128)(2,1)S(1)} %collective-permute-done), channel_id=1, source_target_pairs={{4,8},{5,9},{6,10},{7,11},{8,12},{9,13},{10,14},{11,15},{20,24},{2... | collective-permute-start | bytes 786440 | tf_op jit(solution)/shard_map/stream0/ppermute | solution.py:205
  32.6 4.4 %collective-permute-start.5 = (bf16[128,1024]{1,0:T(8,128)(2,1)S(1)}, bf16[128,1024]{1,0:T(8,128)(2,1)S(1)}, u32[]{:S(2)}, u32[]{:S(2)}) collective-permute-start(bf16[128,1024]{1,0:T(8,128)(2,1)S(1)} %collective-permute-done.4), channel_id=1, source_target_pairs={{4,0},{5,1},{6,2},{7,3},{20,16},{21,17},{22,18},{23,19}} | collective-permute-start | bytes 786440 | tf_op jit(solution)/shard_map/stream0/ppermute | solution.py:205
  43.5 20.9 %collective-permute-done.14 = bf16[4,128,1024]{2,1,0:T(8,128)(2,1)S(1)} collective-permute-done((bf16[4,128,1024]{2,1,0:T(8,128)(2,1)S(1)}, bf16[4,128,1024]{2,1,0:T(8,128)(2,1)S(1)}, u32[]{:S(2)}, u32[]{:S(2)}) %collective-permute-start.14) | collective-permute-done | bytes 1048608 | tf_op jit(solution)/shard_map/stream0/ppermute | solution.py:205
  64.9 17.0 %collective-permute-done.6 = bf16[4,128,1024]{2,1,0:T(8,128)(2,1)S(1)} collective-permute-done((bf16[4,128,1024]{2,1,0:T(8,128)(2,1)S(1)}, bf16[4,128,1024]{2,1,0:T(8,128)(2,1)S(1)}, u32[]{:S(2)}, u32[]{:S(2)}) %collective-permute-start.6) | collective-permute-done | bytes 1048608 | tf_op jit(solution)/shard_map/stream0/ppermute | solution.py:205
  90.7 3.9 %collective-permute-start.27 = (bf16[128,1024]{1,0:T(8,128)(2,1)S(1)}, bf16[128,1024]{1,0:T(8,128)(2,1)S(1)}, u32[]{:S(2)}, u32[]{:S(2)}) collective-permute-start(bf16[128,1024]{1,0:T(8,128)(2,1)S(1)} %get-tuple-element.16), channel_id=1, source_target_pairs={{4,0},{5,1},{6,2},{7,3},{8,4},{9,5},{10,6},{11,7},{12,8},{13,9},{1... | collective-permute-start | bytes 786440 | tf_op jit(solution)/shard_map/stream1/ppermute | solution.py:205
  106.7 3.9 %collective-permute-start.17 = (bf16[128,1024]{1,0:T(8,128)(2,1)S(1)}, bf16[128,1024]{1,0:T(8,128)(2,1)S(1)}, u32[]{:S(2)}, u32[]{:S(2)}) collective-permute-start(bf16[128,1024]{1,0:T(8,128)(2,1)S(1)} %collective-permute-done.16), channel_id=1, source_target_pairs={{4,8},{5,9},{6,10},{7,11},{8,12},{9,13},{10,14},{11,15},{20,24},{2... | collective-permute-start | bytes 786440 | tf_op jit(solution)/shard_map/stream1/ppermute | solution.py:205
  113.8 14.8 %stream0.1 = (bf16[128,1024]{1,0:T(8,128)(2,1)}, bf16[128,1024]{1,0:T(8,128)(2,1)}, f32[16,128,1024]{2,1,0:T(8,128)}, f32[16,128,1024]{2,1,0:T(8,128)}) custom-call(s32[8]{0:T(128)} %multiply_add_fusion.pos_ref, bf16[128,1024]{1,0:T(8,128)(2,1)} %get-tuple-element.50.q_ref, bf16[128,1024]{1,0:T(8,128)(2,1)} %get-tuple-element.48.g_ref, ...), custom_call_target="tpu_custom_call" | custom-call | flops 1610612736 | bytes 22020096 | tf_op jit(solution)/shard_map/stream0/pallas_call | solution.py:295
  135.1 4.3 %collective-permute-done.29 = bf16[128,1024]{1,0:T(8,128)(2,1)S(1)} collective-permute-done((bf16[128,1024]{1,0:T(8,128)(2,1)S(1)}, bf16[128,1024]{1,0:T(8,128)(2,1)S(1)}, u32[]{:S(2)}, u32[]{:S(2)}) %collective-permute-start.29) | collective-permute-done | bytes 262176 | tf_op jit(solution)/shard_map/stream1/ppermute | solution.py:205
  149.7 15.9 %collective-permute-done.30 = bf16[4,128,1024]{2,1,0:T(8,128)(2,1)S(1)} collective-permute-done((bf16[4,128,1024]{2,1,0:T(8,128)(2,1)S(1)}, bf16[4,128,1024]{2,1,0:T(8,128)(2,1)S(1)}, u32[]{:S(2)}, u32[]{:S(2)}) %collective-permute-start.30) | collective-permute-done | bytes 1048608 | tf_op jit(solution)/shard_map/stream1/ppermute | solution.py:205
  165.9 20.8 %collective-permute-done.22 = bf16[4,128,1024]{2,1,0:T(8,128)(2,1)S(1)} collective-permute-done((bf16[4,128,1024]{2,1,0:T(8,128)(2,1)S(1)}, bf16[4,128,1024]{2,1,0:T(8,128)(2,1)S(1)}, u32[]{:S(2)}, u32[]{:S(2)}) %collective-permute-start.22) | collective-permute-done | bytes 1048608 | tf_op jit(solution)/shard_map/stream1/ppermute | solution.py:205
  193.3 22.4 %collective-permute-done.49 = bf16[4,128,1024]{2,1,0:T(8,128)(2,1)} collective-permute-done((bf16[4,128,1024]{2,1,0:T(8,128)(2,1)}, bf16[4,128,1024]{2,1,0:T(8,128)(2,1)}, u32[]{:S(2)}, u32[]{:S(2)}) %collective-permute-start.49) | collective-permute-done | bytes 1048608 | tf_op jit(solution)/shard_map/stream0/transpose()/ppermute | solution.py:205
  219.5 4.0 %pad_maximum_fusion.3 = bf16[2,2,4,128,1024]{4,3,2,1,0:T(8,128)(2,1)} fusion(bf16[1,2,4,128,1024]{4,3,2,1,0:T(8,128)(2,1)} %bitcast.49, bf16[1,2,4,128,1024]{4,3,2,1,0:T(8,128)(2,1)S(1)} %get-tuple-element.32), kind=kLoop, calls=%fused_computation.7 | loop fusion | flops 2097152 | bytes 8388608 | tf_op jit(solution)/shard_map/stream1/stack | solution.py:227
  223.5 4.1 %pad_maximum_fusion.2 = bf16[2,2,4,128,1024]{4,3,2,1,0:T(8,128)(2,1)} fusion(bf16[1,2,4,128,1024]{4,3,2,1,0:T(8,128)(2,1)} %bitcast.37, bf16[1,2,4,128,1024]{4,3,2,1,0:T(8,128)(2,1)S(1)} %get-tuple-element.34), kind=kLoop, calls=%fused_computation.6 | loop fusion | flops 2097152 | bytes 8388608 | tf_op jit(solution)/shard_map/stream1/stack | solution.py:227
  227.6 14.8 %stream1.1 = (bf16[128,1024]{1,0:T(8,128)(2,1)}, bf16[128,1024]{1,0:T(8,128)(2,1)}, f32[16,128,1024]{2,1,0:T(8,128)}, f32[16,128,1024]{2,1,0:T(8,128)}) custom-call(s32[8]{0:T(128)} %multiply_add_fusion.pos_ref, bf16[128,1024]{1,0:T(8,128)(2,1)} %get-tuple-element.51.q_ref, bf16[128,1024]{1,0:T(8,128)(2,1)} %get-tuple-element.49.g_ref, ...), custom_call_target="tpu_custom_call" | custom-call | flops 1610612736 | bytes 22020096 | tf_op jit(solution)/shard_map/stream1/pallas_call | solution.py:295
  258.0 5.0 %collective-permute-done.34 = bf16[128,1024]{1,0:T(8,128)(2,1)S(1)} collective-permute-done((bf16[128,1024]{1,0:T(8,128)(2,1)S(1)}, bf16[128,1024]{1,0:T(8,128)(2,1)S(1)}, u32[]{:S(2)}, u32[]{:S(2)}) %collective-permute-start.34) | collective-permute-done | bytes 262176 | tf_op jit(solution)/shard_map/stream0/transpose()/ppermute | solution.py:205
  270.8 4.5 %collective-permute-start.52 = (bf16[128,1024]{1,0:T(8,128)(2,1)}, bf16[128,1024]{1,0:T(8,128)(2,1)S(1)}, u32[]{:S(2)}, u32[]{:S(2)}) collective-permute-start(bf16[128,1024]{1,0:T(8,128)(2,1)} %get-tuple-element.24), channel_id=1, source_target_pairs={{0,4},{1,5},{2,6},{3,7},{4,8},{5,9},{6,10},{7,11},{8,12},{9,13},{1... | collective-permute-start | bytes 786440 | tf_op jit(solution)/shard_map/stream0/transpose()/ppermute | solution.py:205
  282.6 4.8 %collective-permute-start.36 = (bf16[128,1024]{1,0:T(8,128)(2,1)}, bf16[128,1024]{1,0:T(8,128)(2,1)S(1)}, u32[]{:S(2)}, u32[]{:S(2)}) collective-permute-start(bf16[128,1024]{1,0:T(8,128)(2,1)} %get-tuple-element.28), channel_id=1, source_target_pairs={{0,4},{1,5},{2,6},{3,7},{4,8},{5,9},{6,10},{7,11},{8,12},{9,13},{1... | collective-permute-start | bytes 786440 | tf_op jit(solution)/shard_map/stream0/transpose()/ppermute | solution.py:205
  294.0 20.6 %collective-permute-done.57 = bf16[4,128,1024]{2,1,0:T(8,128)(2,1)S(1)} collective-permute-done((bf16[4,128,1024]{2,1,0:T(8,128)(2,1)S(1)}, bf16[4,128,1024]{2,1,0:T(8,128)(2,1)S(1)}, u32[]{:S(2)}, u32[]{:S(2)}) %collective-permute-start.57) | collective-permute-done | bytes 1048608 | tf_op jit(solution)/shard_map/stream1/transpose()/ppermute | solution.py:205
  317.8 16.2 %collective-permute-done.41 = bf16[4,128,1024]{2,1,0:T(8,128)(2,1)S(1)} collective-permute-done((bf16[4,128,1024]{2,1,0:T(8,128)(2,1)S(1)}, bf16[4,128,1024]{2,1,0:T(8,128)(2,1)S(1)}, u32[]{:S(2)}, u32[]{:S(2)}) %collective-permute-start.41) | collective-permute-done | bytes 1048608 | tf_op jit(solution)/shard_map/stream1/transpose()/ppermute | solution.py:205
  336.4 5.7 %collective-permute-done.58 = bf16[128,1024]{1,0:T(8,128)(2,1)S(1)} collective-permute-done((bf16[128,1024]{1,0:T(8,128)(2,1)S(1)}, bf16[128,1024]{1,0:T(8,128)(2,1)S(1)}, u32[]{:S(2)}, u32[]{:S(2)}) %collective-permute-start.58) | collective-permute-done | bytes 262176 | tf_op jit(solution)/shard_map/stream1/transpose()/ppermute | solution.py:205
  346.3 5.1 %collective-permute-done.42 = bf16[128,1024]{1,0:T(8,128)(2,1)S(1)} collective-permute-done((bf16[128,1024]{1,0:T(8,128)(2,1)S(1)}, bf16[128,1024]{1,0:T(8,128)(2,1)S(1)}, u32[]{:S(2)}, u32[]{:S(2)}) %collective-permute-start.42) | collective-permute-done | bytes 262176 | tf_op jit(solution)/shard_map/stream1/transpose()/ppermute | solution.py:205
  358.4 4.6 %collective-permute-start.60 = (bf16[128,1024]{1,0:T(8,128)(2,1)S(1)}, bf16[128,1024]{1,0:T(8,128)(2,1)S(1)}, u32[]{:S(2)}, u32[]{:S(2)}) collective-permute-start(bf16[128,1024]{1,0:T(8,128)(2,1)S(1)} %get-tuple-element.26), channel_id=1, source_target_pairs={{0,4},{1,5},{2,6},{3,7},{4,8},{5,9},{6,10},{7,11},{8,12},{9,13},{1... | collective-permute-start | bytes 786440 | tf_op jit(solution)/shard_map/stream1/transpose()/ppermute | solution.py:205
  370.3 3.9 %collective-permute-start.44 = (bf16[128,1024]{1,0:T(8,128)(2,1)S(1)}, bf16[128,1024]{1,0:T(8,128)(2,1)S(1)}, u32[]{:S(2)}, u32[]{:S(2)}) collective-permute-start(bf16[128,1024]{1,0:T(8,128)(2,1)S(1)} %get-tuple-element.30), channel_id=1, source_target_pairs={{0,4},{1,5},{2,6},{3,7},{4,8},{5,9},{6,10},{7,11},{8,12},{9,13},{1... | collective-permute-start | bytes 786440 | tf_op jit(solution)/shard_map/stream1/transpose()/ppermute | solution.py:205
  378.6 4.0 %collective-permute-done.47 = bf16[128,1024]{1,0:T(8,128)(2,1)S(1)} collective-permute-done((bf16[128,1024]{1,0:T(8,128)(2,1)S(1)}, bf16[128,1024]{1,0:T(8,128)(2,1)S(1)}, u32[]{:S(2)}, u32[]{:S(2)}) %collective-permute-start.47) | collective-permute-done | bytes 262176 | tf_op jit(solution)/shard_map/stream1/transpose()/ppermute | solution.py:205
  (245 shorter events, 151.9 us)
Async XLA Ops:
  38.3 26.1 %collective-permute-start.14 = (bf16[4,128,1024]{2,1,0:T(8,128)(2,1)S(1)}, bf16[4,128,1024]{2,1,0:T(8,128)(2,1)S(1)}, u32[]{:S(2)}, u32[]{:S(2)}) collective-permute-start(bf16[4,128,1024]{2,1,0:T(8,128)(2,1)S(1)} %constant_dynamic-slice_fusion.2), channel_id=1, source_target_pairs={{0,2},{1,3},{2,0},{3,1},{4,6},{5,7},{6,4},{7,5},{8,10},{9,11},{10,... | collective-permute-start | bytes 3145736 | tf_op jit(solution)/shard_map/stream0/ppermute | solution.py:205
  41.9 40.0 %collective-permute-start.6 = (bf16[4,128,1024]{2,1,0:T(8,128)(2,1)S(1)}, bf16[4,128,1024]{2,1,0:T(8,128)(2,1)S(1)}, u32[]{:S(2)}, u32[]{:S(2)}) collective-permute-start(bf16[4,128,1024]{2,1,0:T(8,128)(2,1)S(1)} %constant_dynamic-slice_fusion.3), channel_id=1, source_target_pairs={{0,2},{1,3},{2,0},{3,1},{4,6},{5,7},{6,4},{7,5},{8,10},{9,11},{10,... | collective-permute-start | bytes 3145736 | tf_op jit(solution)/shard_map/stream0/ppermute | solution.py:205
  104.7 26.6 %collective-permute-start.28 = (bf16[128,1024]{1,0:T(8,128)(2,1)S(1)}, bf16[128,1024]{1,0:T(8,128)(2,1)S(1)}, u32[]{:S(2)}, u32[]{:S(2)}) collective-permute-start(bf16[128,1024]{1,0:T(8,128)(2,1)S(1)} %collective-permute-done.27), channel_id=1, source_target_pairs={{4,0},{5,1},{6,2},{7,3},{8,4},{9,5},{10,6},{11,7},{20,16},{21,17},... | collective-permute-start | bytes 786440 | tf_op jit(solution)/shard_map/stream1/ppermute | solution.py:205
  106.7 26.0 %collective-permute-start.17 = (bf16[128,1024]{1,0:T(8,128)(2,1)S(1)}, bf16[128,1024]{1,0:T(8,128)(2,1)S(1)}, u32[]{:S(2)}, u32[]{:S(2)}) collective-permute-start(bf16[128,1024]{1,0:T(8,128)(2,1)S(1)} %collective-permute-done.16), channel_id=1, source_target_pairs={{4,8},{5,9},{6,10},{7,11},{8,12},{9,13},{10,14},{11,15},{20,24},{2... | collective-permute-start | bytes 786440 | tf_op jit(solution)/shard_map/stream1/ppermute | solution.py:205
  110.6 22.8 %collective-permute-start.20 = (bf16[128,1024]{1,0:T(8,128)(2,1)S(1)}, bf16[128,1024]{1,0:T(8,128)(2,1)S(1)}, u32[]{:S(2)}, u32[]{:S(2)}) collective-permute-start(bf16[128,1024]{1,0:T(8,128)(2,1)S(1)} %collective-permute-done.19), channel_id=1, source_target_pairs={{4,0},{5,1},{6,2},{7,3},{8,4},{9,5},{10,6},{11,7},{20,16},{21,17},... | collective-permute-start | bytes 786440 | tf_op jit(solution)/shard_map/stream1/ppermute | solution.py:205
  112.6 22.3 %collective-permute-start.26 = (bf16[128,1024]{1,0:T(8,128)(2,1)S(1)}, bf16[128,1024]{1,0:T(8,128)(2,1)S(1)}, u32[]{:S(2)}, u32[]{:S(2)}) collective-permute-start(bf16[128,1024]{1,0:T(8,128)(2,1)S(1)} %collective-permute-done.25), channel_id=1, source_target_pairs={{8,12},{9,13},{10,14},{11,15},{24,28},{25,29},{26,30},{27,31}} | collective-permute-start | bytes 786440 | tf_op jit(solution)/shard_map/stream1/ppermute | solution.py:205
  131.3 55.8 %collective-permute-start.48 = (bf16[2,4,128,1024]{3,2,1,0:T(8,128)(2,1)S(1)}, bf16[2,4,128,1024]{3,2,1,0:T(8,128)(2,1)S(1)}, u32[]{:S(2)}, u32[]{:S(2)}) collective-permute-start(bf16[2,4,128,1024]{3,2,1,0:T(8,128)(2,1)S(1)} %bitcast.309), channel_id=1, source_target_pairs={{1,0},{0,1},{3,2},{2,3},{5,4},{4,5},{7,6},{6,7},{9,8},{8,9},{11,10... | collective-permute-start | bytes 6291464 | tf_op jit(solution)/shard_map/stream0/transpose()/ppermute | solution.py:205
  139.5 26.1 %collective-permute-start.30 = (bf16[4,128,1024]{2,1,0:T(8,128)(2,1)S(1)}, bf16[4,128,1024]{2,1,0:T(8,128)(2,1)S(1)}, u32[]{:S(2)}, u32[]{:S(2)}) collective-permute-start(bf16[4,128,1024]{2,1,0:T(8,128)(2,1)S(1)} %constant_dynamic-slice_fusion), channel_id=1, source_target_pairs={{0,2},{1,3},{2,0},{3,1},{4,6},{5,7},{6,4},{7,5},{8,10},{9,11},{10,... | collective-permute-start | bytes 3145736 | tf_op jit(solution)/shard_map/stream1/ppermute | solution.py:205
  144.9 41.9 %collective-permute-start.22 = (bf16[4,128,1024]{2,1,0:T(8,128)(2,1)S(1)}, bf16[4,128,1024]{2,1,0:T(8,128)(2,1)S(1)}, u32[]{:S(2)}, u32[]{:S(2)}) collective-permute-start(bf16[4,128,1024]{2,1,0:T(8,128)(2,1)S(1)} %constant_dynamic-slice_fusion.1), channel_id=1, source_target_pairs={{0,2},{1,3},{2,0},{3,1},{4,6},{5,7},{6,4},{7,5},{8,10},{9,11},{10,... | collective-permute-start | bytes 3145736 | tf_op jit(solution)/shard_map/stream1/ppermute | solution.py:205
  146.7 44.7 %collective-permute-start.32 = (bf16[2,4,128,1024]{3,2,1,0:T(8,128)(2,1)S(1)}, bf16[2,4,128,1024]{3,2,1,0:T(8,128)(2,1)S(1)}, u32[]{:S(2)}, u32[]{:S(2)}) collective-permute-start(bf16[2,4,128,1024]{3,2,1,0:T(8,128)(2,1)S(1)} %bitcast.312), channel_id=1, source_target_pairs={{1,0},{0,1},{3,2},{2,3},{5,4},{4,5},{7,6},{6,7},{9,8},{8,9},{11,10... | collective-permute-start | bytes 6291464 | tf_op jit(solution)/shard_map/stream0/transpose()/ppermute | solution.py:205
  165.8 53.7 %collective-permute-start.31 = (bf16[2,4,128,1024]{3,2,1,0:T(8,128)(2,1)S(1)}, bf16[2,4,128,1024]{3,2,1,0:T(8,128)(2,1)}, u32[]{:S(2)}, u32[]{:S(2)}) collective-permute-start(bf16[2,4,128,1024]{3,2,1,0:T(8,128)(2,1)S(1)} %get-tuple-element.33), channel_id=1, source_target_pairs={{0,1},{1,0},{2,3},{3,2},{4,5},{5,4},{6,7},{7,6},{8,9},{9,8},{10,11... | collective-permute-start | bytes 6291464 | tf_op jit(solution)/shard_map/stream1/ppermute | solution.py:205
  187.0 36.5 %collective-permute-start.23 = (bf16[2,4,128,1024]{3,2,1,0:T(8,128)(2,1)S(1)}, bf16[2,4,128,1024]{3,2,1,0:T(8,128)(2,1)}, u32[]{:S(2)}, u32[]{:S(2)}) collective-permute-start(bf16[2,4,128,1024]{3,2,1,0:T(8,128)(2,1)S(1)} %get-tuple-element.35), channel_id=1, source_target_pairs={{0,1},{1,0},{2,3},{3,2},{4,5},{5,4},{6,7},{7,6},{8,9},{9,8},{10,11... | collective-permute-start | bytes 6291464 | tf_op jit(solution)/shard_map/stream1/ppermute | solution.py:205
  189.3 26.3 %collective-permute-start.49 = (bf16[4,128,1024]{2,1,0:T(8,128)(2,1)}, bf16[4,128,1024]{2,1,0:T(8,128)(2,1)}, u32[]{:S(2)}, u32[]{:S(2)}) collective-permute-start(bf16[4,128,1024]{2,1,0:T(8,128)(2,1)} %fusion.10), channel_id=1, source_target_pairs={{2,0},{3,1},{0,2},{1,3},{6,4},{7,5},{4,6},{5,7},{10,8},{11,9},{8,1... | collective-permute-start | bytes 3145736 | tf_op jit(solution)/shard_map/stream0/transpose()/ppermute | solution.py:205
  192.6 53.9 %collective-permute-start.33 = (bf16[4,128,1024]{2,1,0:T(8,128)(2,1)S(1)}, bf16[4,128,1024]{2,1,0:T(8,128)(2,1)}, u32[]{:S(2)}, u32[]{:S(2)}) collective-permute-start(bf16[4,128,1024]{2,1,0:T(8,128)(2,1)S(1)} %fusion.8), channel_id=1, source_target_pairs={{2,0},{3,1},{0,2},{1,3},{6,4},{7,5},{4,6},{5,7},{10,8},{11,9},{8,1... | collective-permute-start | bytes 3145736 | tf_op jit(solution)/shard_map/stream0/transpose()/ppermute | solution.py:205
  244.9 37.7 %collective-permute-start.56 = (bf16[2,4,128,1024]{3,2,1,0:T(8,128)(2,1)S(1)}, bf16[2,4,128,1024]{3,2,1,0:T(8,128)(2,1)S(1)}, u32[]{:S(2)}, u32[]{:S(2)}) collective-permute-start(bf16[2,4,128,1024]{3,2,1,0:T(8,128)(2,1)S(1)} %bitcast.310), channel_id=1, source_target_pairs={{1,0},{0,1},{3,2},{2,3},{5,4},{4,5},{7,6},{6,7},{9,8},{8,9},{11,10... | collective-permute-start | bytes 6291464 | tf_op jit(solution)/shard_map/stream1/transpose()/ppermute | solution.py:205
  251.2 37.4 %collective-permute-start.40 = (bf16[2,4,128,1024]{3,2,1,0:T(8,128)(2,1)S(1)}, bf16[2,4,128,1024]{3,2,1,0:T(8,128)(2,1)S(1)}, u32[]{:S(2)}, u32[]{:S(2)}) collective-permute-start(bf16[2,4,128,1024]{3,2,1,0:T(8,128)(2,1)S(1)} %bitcast.311), channel_id=1, source_target_pairs={{1,0},{0,1},{3,2},{2,3},{5,4},{4,5},{7,6},{6,7},{9,8},{8,9},{11,10... | collective-permute-start | bytes 6291464 | tf_op jit(solution)/shard_map/stream1/transpose()/ppermute | solution.py:205
  269.5 21.9 %collective-permute-start.54 = (bf16[128,1024]{1,0:T(8,128)(2,1)}, bf16[128,1024]{1,0:T(8,128)(2,1)S(1)}, u32[]{:S(2)}, u32[]{:S(2)}) collective-permute-start(bf16[128,1024]{1,0:T(8,128)(2,1)} %get-tuple-element.25), channel_id=1, source_target_pairs={{8,4},{9,5},{10,6},{11,7},{12,8},{13,9},{14,10},{15,11},{24,20},{2... | collective-permute-start | bytes 786440 | tf_op jit(solution)/shard_map/stream0/transpose()/ppermute | solution.py:205
  270.8 72.7 %collective-permute-start.52 = (bf16[128,1024]{1,0:T(8,128)(2,1)}, bf16[128,1024]{1,0:T(8,128)(2,1)S(1)}, u32[]{:S(2)}, u32[]{:S(2)}) collective-permute-start(bf16[128,1024]{1,0:T(8,128)(2,1)} %get-tuple-element.24), channel_id=1, source_target_pairs={{0,4},{1,5},{2,6},{3,7},{4,8},{5,9},{6,10},{7,11},{8,12},{9,13},{1... | collective-permute-start | bytes 786440 | tf_op jit(solution)/shard_map/stream0/transpose()/ppermute | solution.py:205
  282.6 87.6 %collective-permute-start.36 = (bf16[128,1024]{1,0:T(8,128)(2,1)}, bf16[128,1024]{1,0:T(8,128)(2,1)S(1)}, u32[]{:S(2)}, u32[]{:S(2)}) collective-permute-start(bf16[128,1024]{1,0:T(8,128)(2,1)} %get-tuple-element.28), channel_id=1, source_target_pairs={{0,4},{1,5},{2,6},{3,7},{4,8},{5,9},{6,10},{7,11},{8,12},{9,13},{1... | collective-permute-start | bytes 786440 | tf_op jit(solution)/shard_map/stream0/transpose()/ppermute | solution.py:205
  288.6 26.1 %collective-permute-start.57 = (bf16[4,128,1024]{2,1,0:T(8,128)(2,1)S(1)}, bf16[4,128,1024]{2,1,0:T(8,128)(2,1)S(1)}, u32[]{:S(2)}, u32[]{:S(2)}) collective-permute-start(bf16[4,128,1024]{2,1,0:T(8,128)(2,1)S(1)} %fusion.11), channel_id=1, source_target_pairs={{2,0},{3,1},{0,2},{1,3},{6,4},{7,5},{4,6},{5,7},{10,8},{11,9},{8,1... | collective-permute-start | bytes 3145736 | tf_op jit(solution)/shard_map/stream1/transpose()/ppermute | solution.py:205
  291.4 42.5 %collective-permute-start.41 = (bf16[4,128,1024]{2,1,0:T(8,128)(2,1)S(1)}, bf16[4,128,1024]{2,1,0:T(8,128)(2,1)S(1)}, u32[]{:S(2)}, u32[]{:S(2)}) collective-permute-start(bf16[4,128,1024]{2,1,0:T(8,128)(2,1)S(1)} %fusion.9), channel_id=1, source_target_pairs={{2,0},{3,1},{0,2},{1,3},{6,4},{7,5},{4,6},{5,7},{10,8},{11,9},{8,1... | collective-permute-start | bytes 3145736 | tf_op jit(solution)/shard_map/stream1/transpose()/ppermute | solution.py:205
  292.0 52.2 %collective-permute-start.55 = (bf16[128,1024]{1,0:T(8,128)(2,1)S(1)}, bf16[128,1024]{1,0:T(8,128)(2,1)S(1)}, u32[]{:S(2)}, u32[]{:S(2)}) collective-permute-start(bf16[128,1024]{1,0:T(8,128)(2,1)S(1)} %fusion.26), channel_id=1, source_target_pairs={{4,0},{5,1},{6,2},{7,3},{8,4},{9,5},{10,6},{11,7},{12,8},{13,9},{1... | collective-permute-start | bytes 786440 | tf_op jit(solution)/shard_map/stream0/transpose()/ppermute | solution.py:205
  314.7 55.5 %collective-permute-start.39 = (bf16[128,1024]{1,0:T(8,128)(2,1)S(1)}, bf16[128,1024]{1,0:T(8,128)(2,1)S(1)}, u32[]{:S(2)}, u32[]{:S(2)}) collective-permute-start(bf16[128,1024]{1,0:T(8,128)(2,1)S(1)} %fusion.48), channel_id=1, source_target_pairs={{4,0},{5,1},{6,2},{7,3},{8,4},{9,5},{10,6},{11,7},{12,8},{13,9},{1... | collective-permute-start | bytes 786440 | tf_op jit(solution)/shard_map/stream0/transpose()/ppermute | solution.py:205
  358.4 17.9 %collective-permute-start.60 = (bf16[128,1024]{1,0:T(8,128)(2,1)S(1)}, bf16[128,1024]{1,0:T(8,128)(2,1)S(1)}, u32[]{:S(2)}, u32[]{:S(2)}) collective-permute-start(bf16[128,1024]{1,0:T(8,128)(2,1)S(1)} %get-tuple-element.26), channel_id=1, source_target_pairs={{0,4},{1,5},{2,6},{3,7},{4,8},{5,9},{6,10},{7,11},{8,12},{9,13},{1... | collective-permute-start | bytes 786440 | tf_op jit(solution)/shard_map/stream1/transpose()/ppermute | solution.py:205
  (58 other events, 695.2 us)

commit v11 on v10

--- a/solution.py
+++ b/solution.py
@@ -230,7 +230,7 @@
 def _attend_kernel(pos_ref, q_ref, g_ref, *refs):
     k_refs = refs[:SLOTS]
     v_refs = refs[SLOTS : 2 * SLOTS]
-    att_ref, gq_ref, dk_ref, dv_ref = refs[2 * SLOTS :]
+    att_ref, gq_ref, dk_ref, dv_ref, dk_acc, dv_acc = refs[2 * SLOTS :]
     scale = HD ** (-0.5)
     nt = (((1,), (1,)), ((), ()))
     q = q_ref[...]
@@ -253,13 +253,15 @@
     tn = (((0,), (0,)), ((), ()))
     gk = lax.dot_general(gs, q, tn, preferred_element_type=jnp.float32) * scale
     gv = lax.dot_general(w, g, tn, preferred_element_type=jnp.float32)
-    dk_ref[...] = jnp.zeros(dk_ref.shape, jnp.float32)
-    dv_ref[...] = jnp.zeros(dv_ref.shape, jnp.float32)
+    dk_acc[...] = jnp.zeros(dk_acc.shape, jnp.float32)
+    dv_acc[...] = jnp.zeros(dv_acc.shape, jnp.float32)
     rows = q.shape[0]
     for j in range(SLOTS):
         at = pos_ref[j]
-        dk_ref[at] = dk_ref[at] + gk[j * rows : (j + 1) * rows]
-        dv_ref[at] = dv_ref[at] + gv[j * rows : (j + 1) * rows]
+        dk_acc[at] = dk_acc[at] + gk[j * rows : (j + 1) * rows]
+        dv_acc[at] = dv_acc[at] + gv[j * rows : (j + 1) * rows]
+    dk_ref[...] = dk_acc[...].astype(dk_ref.dtype)
+    dv_ref[...] = dv_acc[...].astype(dv_ref.dtype)
 
 
 def attend_local(pos, query, grad_out, keys_local, values_local):
@@ -272,20 +274,21 @@
     ]
     part_spec = pl.BlockSpec((held, rows, HD), lambda h, pos: (0, 0, h))
     flops = 12 * rows * SLOTS * rows * HD * heads
-    moved = 2 * SLOTS * rows * width * 2 + 4 * rows * width * 2 + 2 * held * rows * width * 4
+    moved = 2 * SLOTS * rows * width * 2 + 4 * rows * width * 2 + 2 * held * rows * width * 2
     call = pl.pallas_call(
         _attend_kernel,
         out_shape=(
             jax.ShapeDtypeStruct((rows, width), jnp.bfloat16),
             jax.ShapeDtypeStruct((rows, width), jnp.bfloat16),
-            jax.ShapeDtypeStruct((held, rows, width), jnp.float32),
-            jax.ShapeDtypeStruct((held, rows, width), jnp.float32),
+            jax.ShapeDtypeStruct((held, rows, width), jnp.bfloat16),
+            jax.ShapeDtypeStruct((held, rows, width), jnp.bfloat16),
         ),
         grid_spec=pltpu.PrefetchScalarGridSpec(
             num_scalar_prefetch=1,
             grid=(heads,),
             in_specs=[head_spec, head_spec] + slot_specs + slot_specs,
             out_specs=(head_spec, head_spec, part_spec, part_spec),
+            scratch_shapes=[pltpu.VMEM((held, rows, HD), jnp.float32)] * 2,
         ),
         compiler_params=pltpu.CompilerParams(dimension_semantics=("arbitrary",)),
         cost_estimate=pl.CostEstimate(
@@ -314,8 +317,8 @@
     scatter = jax.linear_transpose(
         lambda t: gather_blocks(t, n), jax.ShapeDtypeStruct((rows, width), jnp.float32)
     )
-    (grad_keys,) = scatter(part_keys.reshape(2, 2, line_len, rows, width))
-    (grad_values,) = scatter(part_values.reshape(2, 2, line_len, rows, width))
+    (grad_keys,) = scatter(part_keys.astype(jnp.float32).reshape(2, 2, line_len, rows, width))
+    (grad_values,) = scatter(part_values.astype(jnp.float32).reshape(2, 2, line_len, rows, width))
     outs = (attended, grad_query, grad_keys.astype(jnp.bfloat16), grad_values.astype(jnp.bfloat16))
     return outs, (keys_local, values_local)
 

time: 388 us -> 378 us (0.974)
  other arithmetic: 29.8 us -> 23.1 us
  local copies, waits for them, and re-layouts: 25 us -> 18.8 us
    another operation x8 -> x2, local copies, waits for them, and re-layouts: 12.3 us -> 8.02 us  [gather_blocks(): return jnp.stack([pair, sibling])]
  transfers between devices with their start and end apart: 64 -> 64, of which waited for: 24 -> 24; matrix products, arithmetic and copies ran while one was open for 12% -> 9% of each run, Pallas kernels for 8% -> 8%
where the time goes in v11:
time: 378 us; the launch traced here: 375 us
  waiting for transfers between devices  185 us (49%)
  starting transfers between devices  116 us (31%)
  Pallas kernels  29.9 us (8%)
  other arithmetic  23.1 us (6%)
  local copies, waits for them, and re-layouts  18.8 us (5%)
    ppermute x64, waiting for transfers between devices, _send(): return lax.ppermute(v.astype(jnp.bfloat16), 'seq', pairs).astype(v.dtype)  185 us
    ppermute x64, starting transfers between devices, _send(): return lax.ppermute(v.astype(jnp.bfloat16), 'seq', pairs).astype(v.dtype)  116 us
    pallas_call x2, Pallas kernels, attend_local(): call(pos, query, grad_out, *[keys_local] * SLOTS, *[values_local] * SLOTS)  29.9 us
    another operation x8, other arithmetic, gather_blocks(): return jnp.stack([pair, sibling])  10.7 us
    another operation x2, local copies, waits for them, and re-layouts, gather_blocks(): return jnp.stack([pair, sibling])  8.02 us
  transfers between devices with their start and end apart: 64, of which 24 were waited for; matrix products, arithmetic and copies ran while one was open for 9% of the time, Pallas kernels for 8%

profile of v11, /device:TPU:10, one launch (start us, length us, event | category | flops | bytes accessed | tf_op | source)
XLA Modules:
  0.0 375.2 jit_solution(15878302170180375718)
XLA Ops:
  20.0 3.9 %collective-permute-start.1 = (bf16[128,1024]{1,0:T(8,128)(2,1)S(1)}, bf16[128,1024]{1,0:T(8,128)(2,1)S(1)}, u32[]{:S(2)}, u32[]{:S(2)}) collective-permute-start(bf16[128,1024]{1,0:T(8,128)(2,1)S(1)} %collective-permute-done), channel_id=1, source_target_pairs={{4,8},{5,9},{6,10},{7,11},{8,12},{9,13},{10,14},{11,15},{20,24},{2... | collective-permute-start | bytes 786440 | tf_op jit(solution)/shard_map/stream0/ppermute | solution.py:205
  32.6 4.4 %collective-permute-start.5 = (bf16[128,1024]{1,0:T(8,128)(2,1)S(1)}, bf16[128,1024]{1,0:T(8,128)(2,1)S(1)}, u32[]{:S(2)}, u32[]{:S(2)}) collective-permute-start(bf16[128,1024]{1,0:T(8,128)(2,1)S(1)} %collective-permute-done.4), channel_id=1, source_target_pairs={{4,0},{5,1},{6,2},{7,3},{20,16},{21,17},{22,18},{23,19}} | collective-permute-start | bytes 786440 | tf_op jit(solution)/shard_map/stream0/ppermute | solution.py:205
  43.5 20.9 %collective-permute-done.14 = bf16[4,128,1024]{2,1,0:T(8,128)(2,1)S(1)} collective-permute-done((bf16[4,128,1024]{2,1,0:T(8,128)(2,1)S(1)}, bf16[4,128,1024]{2,1,0:T(8,128)(2,1)S(1)}, u32[]{:S(2)}, u32[]{:S(2)}) %collective-permute-start.14) | collective-permute-done | bytes 1048608 | tf_op jit(solution)/shard_map/stream0/ppermute | solution.py:205
  64.9 17.0 %collective-permute-done.6 = bf16[4,128,1024]{2,1,0:T(8,128)(2,1)S(1)} collective-permute-done((bf16[4,128,1024]{2,1,0:T(8,128)(2,1)S(1)}, bf16[4,128,1024]{2,1,0:T(8,128)(2,1)S(1)}, u32[]{:S(2)}, u32[]{:S(2)}) %collective-permute-start.6) | collective-permute-done | bytes 1048608 | tf_op jit(solution)/shard_map/stream0/ppermute | solution.py:205
  92.7 3.9 %collective-permute-start.27 = (bf16[128,1024]{1,0:T(8,128)(2,1)S(1)}, bf16[128,1024]{1,0:T(8,128)(2,1)S(1)}, u32[]{:S(2)}, u32[]{:S(2)}) collective-permute-start(bf16[128,1024]{1,0:T(8,128)(2,1)S(1)} %get-tuple-element.16), channel_id=1, source_target_pairs={{4,0},{5,1},{6,2},{7,3},{8,4},{9,5},{10,6},{11,7},{12,8},{13,9},{1... | collective-permute-start | bytes 786440 | tf_op jit(solution)/shard_map/stream1/ppermute | solution.py:205
  105.3 15.0 %stream0.1 = (bf16[128,1024]{1,0:T(8,128)(2,1)}, bf16[128,1024]{1,0:T(8,128)(2,1)}, bf16[16,128,1024]{2,1,0:T(8,128)(2,1)}, bf16[16,128,1024]{2,1,0:T(8,128)(2,1)}) custom-call(s32[8]{0:T(128)} %multiply_add_fusion.pos_ref, bf16[128,1024]{1,0:T(8,128)(2,1)} %get-tuple-element.58.q_ref, bf16[128,1024]{1,0:T(8,128)(2,1)} %get-tuple-element.56.g_ref, ...), custom_call_target="tpu_custom_call" | custom-call | flops 1610612736 | bytes 13631488 | tf_op jit(solution)/shard_map/stream0/pallas_call | solution.py:298
  122.2 3.9 %collective-permute-start.17 = (bf16[128,1024]{1,0:T(8,128)(2,1)S(1)}, bf16[128,1024]{1,0:T(8,128)(2,1)S(1)}, u32[]{:S(2)}, u32[]{:S(2)}) collective-permute-start(bf16[128,1024]{1,0:T(8,128)(2,1)S(1)} %collective-permute-done.16), channel_id=1, source_target_pairs={{4,8},{5,9},{6,10},{7,11},{8,12},{9,13},{10,14},{11,15},{20,24},{2... | collective-permute-start | bytes 786440 | tf_op jit(solution)/shard_map/stream1/ppermute | solution.py:205
  128.8 4.1 %fusion.66 = (bf16[8,128,1024]{2,1,0:T(8,128)(2,1)S(1)}, bf16[8,128,1024]{2,1,0:T(8,128)(2,1)S(1)}, bf16[8,128,1024]{2,1,0:T(8,128)(2,1)S(1)}, bf16[8,128,1024]{2,1,0:T(8,128)(2,1)S(1)}) fusion(bf16[16,128,1024]{2,1,0:T(8,128)(2,1)} %get-tuple-element.22, bf16[16,128,1024]{2,1,0:T(8,128)(2,1)} %get-tuple-element.20), kind=kLoop, calls=%fused_computation.163 | loop fusion | bytes 16777216 | tf_op jit(solution)/shard_map/stream0/transpose()/unstack | solution.py:227
  148.3 18.9 %collective-permute-done.30 = bf16[4,128,1024]{2,1,0:T(8,128)(2,1)S(1)} collective-permute-done((bf16[4,128,1024]{2,1,0:T(8,128)(2,1)S(1)}, bf16[4,128,1024]{2,1,0:T(8,128)(2,1)S(1)}, u32[]{:S(2)}, u32[]{:S(2)}) %collective-permute-start.30) | collective-permute-done | bytes 1048608 | tf_op jit(solution)/shard_map/stream1/ppermute | solution.py:205
  167.5 20.8 %collective-permute-done.22 = bf16[4,128,1024]{2,1,0:T(8,128)(2,1)S(1)} collective-permute-done((bf16[4,128,1024]{2,1,0:T(8,128)(2,1)S(1)}, bf16[4,128,1024]{2,1,0:T(8,128)(2,1)S(1)}, u32[]{:S(2)}, u32[]{:S(2)}) %collective-permute-start.22) | collective-permute-done | bytes 1048608 | tf_op jit(solution)/shard_map/stream1/ppermute | solution.py:205
  194.4 21.5 %collective-permute-done.49 = bf16[4,128,1024]{2,1,0:T(8,128)(2,1)S(1)} collective-permute-done((bf16[4,128,1024]{2,1,0:T(8,128)(2,1)S(1)}, bf16[4,128,1024]{2,1,0:T(8,128)(2,1)S(1)}, u32[]{:S(2)}, u32[]{:S(2)}) %collective-permute-start.49) | collective-permute-done | bytes 1048608 | tf_op jit(solution)/shard_map/stream0/transpose()/ppermute | solution.py:205
  223.4 14.9 %stream1.1 = (bf16[128,1024]{1,0:T(8,128)(2,1)}, bf16[128,1024]{1,0:T(8,128)(2,1)}, bf16[16,128,1024]{2,1,0:T(8,128)(2,1)}, bf16[16,128,1024]{2,1,0:T(8,128)(2,1)}) custom-call(s32[8]{0:T(128)} %multiply_add_fusion.pos_ref, bf16[128,1024]{1,0:T(8,128)(2,1)} %get-tuple-element.59.q_ref, bf16[128,1024]{1,0:T(8,128)(2,1)} %get-tuple-element.57.g_ref, ...), custom_call_target="tpu_custom_call" | custom-call | flops 1610612736 | bytes 13631488 | tf_op jit(solution)/shard_map/stream1/pallas_call | solution.py:298
  238.4 3.9 %fusion.67 = (bf16[8,128,1024]{2,1,0:T(8,128)(2,1)S(1)}, bf16[8,128,1024]{2,1,0:T(8,128)(2,1)S(1)}, bf16[8,128,1024]{2,1,0:T(8,128)(2,1)S(1)}, bf16[8,128,1024]{2,1,0:T(8,128)(2,1)S(1)}) fusion(bf16[16,128,1024]{2,1,0:T(8,128)(2,1)} %get-tuple-element.23, bf16[16,128,1024]{2,1,0:T(8,128)(2,1)} %get-tuple-element.21), kind=kLoop, calls=%fused_computation.164 | loop fusion | bytes 16777216 | tf_op jit(solution)/shard_map/stream1/transpose()/unstack | solution.py:227
  249.2 4.7 %collective-permute-done.50 = bf16[128,1024]{1,0:T(8,128)(2,1)S(1)} collective-permute-done((bf16[128,1024]{1,0:T(8,128)(2,1)S(1)}, bf16[128,1024]{1,0:T(8,128)(2,1)S(1)}, u32[]{:S(2)}, u32[]{:S(2)}) %collective-permute-start.50) | collective-permute-done | bytes 262176 | tf_op jit(solution)/shard_map/stream0/transpose()/ppermute | solution.py:205
  266.6 4.6 %collective-permute-start.52 = (bf16[128,1024]{1,0:T(8,128)(2,1)S(1)}, bf16[128,1024]{1,0:T(8,128)(2,1)S(1)}, u32[]{:S(2)}, u32[]{:S(2)}) collective-permute-start(bf16[128,1024]{1,0:T(8,128)(2,1)S(1)} %get-tuple-element.32), channel_id=1, source_target_pairs={{0,4},{1,5},{2,6},{3,7},{4,8},{5,9},{6,10},{7,11},{8,12},{9,13},{1... | collective-permute-start | bytes 786440 | tf_op jit(solution)/shard_map/stream0/transpose()/ppermute | solution.py:205
  273.7 4.8 %collective-permute-start.36 = (bf16[128,1024]{1,0:T(8,128)(2,1)S(1)}, bf16[128,1024]{1,0:T(8,128)(2,1)S(1)}, u32[]{:S(2)}, u32[]{:S(2)}) collective-permute-start(bf16[128,1024]{1,0:T(8,128)(2,1)S(1)} %get-tuple-element.36), channel_id=1, source_target_pairs={{0,4},{1,5},{2,6},{3,7},{4,8},{5,9},{6,10},{7,11},{8,12},{9,13},{1... | collective-permute-start | bytes 786440 | tf_op jit(solution)/shard_map/stream0/transpose()/ppermute | solution.py:205
  284.9 20.8 %collective-permute-done.57 = bf16[4,128,1024]{2,1,0:T(8,128)(2,1)S(1)} collective-permute-done((bf16[4,128,1024]{2,1,0:T(8,128)(2,1)S(1)}, bf16[4,128,1024]{2,1,0:T(8,128)(2,1)S(1)}, u32[]{:S(2)}, u32[]{:S(2)}) %collective-permute-start.57) | collective-permute-done | bytes 1048608 | tf_op jit(solution)/shard_map/stream1/transpose()/ppermute | solution.py:205
  308.9 16.4 %collective-permute-done.41 = bf16[4,128,1024]{2,1,0:T(8,128)(2,1)S(1)} collective-permute-done((bf16[4,128,1024]{2,1,0:T(8,128)(2,1)S(1)}, bf16[4,128,1024]{2,1,0:T(8,128)(2,1)S(1)}, u32[]{:S(2)}, u32[]{:S(2)}) %collective-permute-start.41) | collective-permute-done | bytes 1048608 | tf_op jit(solution)/shard_map/stream1/transpose()/ppermute | solution.py:205
  327.8 5.7 %collective-permute-done.58 = bf16[128,1024]{1,0:T(8,128)(2,1)S(1)} collective-permute-done((bf16[128,1024]{1,0:T(8,128)(2,1)S(1)}, bf16[128,1024]{1,0:T(8,128)(2,1)S(1)}, u32[]{:S(2)}, u32[]{:S(2)}) %collective-permute-start.58) | collective-permute-done | bytes 262176 | tf_op jit(solution)/shard_map/stream1/transpose()/ppermute | solution.py:205
  337.6 5.4 %collective-permute-done.42 = bf16[128,1024]{1,0:T(8,128)(2,1)S(1)} collective-permute-done((bf16[128,1024]{1,0:T(8,128)(2,1)S(1)}, bf16[128,1024]{1,0:T(8,128)(2,1)S(1)}, u32[]{:S(2)}, u32[]{:S(2)}) %collective-permute-start.42) | collective-permute-done | bytes 262176 | tf_op jit(solution)/shard_map/stream1/transpose()/ppermute | solution.py:205
  350.1 4.6 %collective-permute-start.60 = (bf16[128,1024]{1,0:T(8,128)(2,1)S(1)}, bf16[128,1024]{1,0:T(8,128)(2,1)S(1)}, u32[]{:S(2)}, u32[]{:S(2)}) collective-permute-start(bf16[128,1024]{1,0:T(8,128)(2,1)S(1)} %get-tuple-element.34), channel_id=1, source_target_pairs={{0,4},{1,5},{2,6},{3,7},{4,8},{5,9},{6,10},{7,11},{8,12},{9,13},{1... | collective-permute-start | bytes 786440 | tf_op jit(solution)/shard_map/stream1/transpose()/ppermute | solution.py:205
  356.2 3.7 collective-permute-done.62
  362.0 3.9 %collective-permute-start.44 = (bf16[128,1024]{1,0:T(8,128)(2,1)S(1)}, bf16[128,1024]{1,0:T(8,128)(2,1)S(1)}, u32[]{:S(2)}, u32[]{:S(2)}) collective-permute-start(bf16[128,1024]{1,0:T(8,128)(2,1)S(1)} %get-tuple-element.38), channel_id=1, source_target_pairs={{0,4},{1,5},{2,6},{3,7},{4,8},{5,9},{6,10},{7,11},{8,12},{9,13},{1... | collective-permute-start | bytes 786440 | tf_op jit(solution)/shard_map/stream1/transpose()/ppermute | solution.py:205
  370.3 4.0 %collective-permute-done.47 = bf16[128,1024]{1,0:T(8,128)(2,1)S(1)} collective-permute-done((bf16[128,1024]{1,0:T(8,128)(2,1)S(1)}, bf16[128,1024]{1,0:T(8,128)(2,1)S(1)}, u32[]{:S(2)}, u32[]{:S(2)}) %collective-permute-start.47) | collective-permute-done | bytes 262176 | tf_op jit(solution)/shard_map/stream1/transpose()/ppermute | solution.py:205
  (232 shorter events, 141.2 us)
Async XLA Ops:
  38.3 26.1 %collective-permute-start.14 = (bf16[4,128,1024]{2,1,0:T(8,128)(2,1)S(1)}, bf16[4,128,1024]{2,1,0:T(8,128)(2,1)S(1)}, u32[]{:S(2)}, u32[]{:S(2)}) collective-permute-start(bf16[4,128,1024]{2,1,0:T(8,128)(2,1)S(1)} %constant_dynamic-slice_fusion.2), channel_id=1, source_target_pairs={{0,2},{1,3},{2,0},{3,1},{4,6},{5,7},{6,4},{7,5},{8,10},{9,11},{10,... | collective-permute-start | bytes 3145736 | tf_op jit(solution)/shard_map/stream0/ppermute | solution.py:205
  41.9 40.0 %collective-permute-start.6 = (bf16[4,128,1024]{2,1,0:T(8,128)(2,1)S(1)}, bf16[4,128,1024]{2,1,0:T(8,128)(2,1)S(1)}, u32[]{:S(2)}, u32[]{:S(2)}) collective-permute-start(bf16[4,128,1024]{2,1,0:T(8,128)(2,1)S(1)} %constant_dynamic-slice_fusion.3), channel_id=1, source_target_pairs={{0,2},{1,3},{2,0},{3,1},{4,6},{5,7},{6,4},{7,5},{8,10},{9,11},{10,... | collective-permute-start | bytes 3145736 | tf_op jit(solution)/shard_map/stream0/ppermute | solution.py:205
  64.7 17.6 %collective-permute-start.15 = (bf16[2,4,128,1024]{3,2,1,0:T(8,128)(2,1)S(1)}, bf16[2,4,128,1024]{3,2,1,0:T(8,128)(2,1)S(1)}, u32[]{:S(2)}, u32[]{:S(2)}) collective-permute-start(bf16[2,4,128,1024]{3,2,1,0:T(8,128)(2,1)S(1)} %get-tuple-element.45), channel_id=1, source_target_pairs={{0,1},{1,0},{2,3},{3,2},{4,5},{5,4},{6,7},{7,6},{8,9},{9,8},{10,11... | collective-permute-start | bytes 6291464 | tf_op jit(solution)/shard_map/stream0/ppermute | solution.py:205
  92.7 27.6 %collective-permute-start.27 = (bf16[128,1024]{1,0:T(8,128)(2,1)S(1)}, bf16[128,1024]{1,0:T(8,128)(2,1)S(1)}, u32[]{:S(2)}, u32[]{:S(2)}) collective-permute-start(bf16[128,1024]{1,0:T(8,128)(2,1)S(1)} %get-tuple-element.16), channel_id=1, source_target_pairs={{4,0},{5,1},{6,2},{7,3},{8,4},{9,5},{10,6},{11,7},{12,8},{13,9},{1... | collective-permute-start | bytes 786440 | tf_op jit(solution)/shard_map/stream1/ppermute | solution.py:205
  96.6 25.6 %collective-permute-start.16 = (bf16[128,1024]{1,0:T(8,128)(2,1)S(1)}, bf16[128,1024]{1,0:T(8,128)(2,1)S(1)}, u32[]{:S(2)}, u32[]{:S(2)}) collective-permute-start(bf16[128,1024]{1,0:T(8,128)(2,1)S(1)} %get-tuple-element.15), channel_id=1, source_target_pairs={{0,4},{1,5},{2,6},{3,7},{4,8},{5,9},{6,10},{7,11},{8,12},{9,13},{1... | collective-permute-start | bytes 786440 | tf_op jit(solution)/shard_map/stream1/ppermute | solution.py:205
  98.8 27.3 %collective-permute-start.19 = (bf16[128,1024]{1,0:T(8,128)(2,1)S(1)}, bf16[128,1024]{1,0:T(8,128)(2,1)S(1)}, u32[]{:S(2)}, u32[]{:S(2)}) collective-permute-start(bf16[128,1024]{1,0:T(8,128)(2,1)S(1)} %get-tuple-element.15), channel_id=1, source_target_pairs={{4,0},{5,1},{6,2},{7,3},{8,4},{9,5},{10,6},{11,7},{12,8},{13,9},{1... | collective-permute-start | bytes 786440 | tf_op jit(solution)/shard_map/stream1/ppermute | solution.py:205
  102.5 25.6 %collective-permute-start.25 = (bf16[128,1024]{1,0:T(8,128)(2,1)S(1)}, bf16[128,1024]{1,0:T(8,128)(2,1)S(1)}, u32[]{:S(2)}, u32[]{:S(2)}) collective-permute-start(bf16[128,1024]{1,0:T(8,128)(2,1)S(1)} %collective-permute-done.24), channel_id=1, source_target_pairs={{4,8},{5,9},{6,10},{7,11},{8,12},{9,13},{10,14},{11,15},{20,24},{2... | collective-permute-start | bytes 786440 | tf_op jit(solution)/shard_map/stream1/ppermute | solution.py:205
  132.9 55.8 %collective-permute-start.48 = (bf16[2,4,128,1024]{3,2,1,0:T(8,128)(2,1)S(1)}, bf16[2,4,128,1024]{3,2,1,0:T(8,128)(2,1)S(1)}, u32[]{:S(2)}, u32[]{:S(2)}) collective-permute-start(bf16[2,4,128,1024]{3,2,1,0:T(8,128)(2,1)S(1)} %bitcast.317), channel_id=1, source_target_pairs={{1,0},{0,1},{3,2},{2,3},{5,4},{4,5},{7,6},{6,7},{9,8},{8,9},{11,10... | collective-permute-start | bytes 6291464 | tf_op jit(solution)/shard_map/stream0/transpose()/ppermute | solution.py:205
  141.1 26.1 %collective-permute-start.30 = (bf16[4,128,1024]{2,1,0:T(8,128)(2,1)S(1)}, bf16[4,128,1024]{2,1,0:T(8,128)(2,1)S(1)}, u32[]{:S(2)}, u32[]{:S(2)}) collective-permute-start(bf16[4,128,1024]{2,1,0:T(8,128)(2,1)S(1)} %constant_dynamic-slice_fusion), channel_id=1, source_target_pairs={{0,2},{1,3},{2,0},{3,1},{4,6},{5,7},{6,4},{7,5},{8,10},{9,11},{10,... | collective-permute-start | bytes 3145736 | tf_op jit(solution)/shard_map/stream1/ppermute | solution.py:205
  146.5 41.9 %collective-permute-start.22 = (bf16[4,128,1024]{2,1,0:T(8,128)(2,1)S(1)}, bf16[4,128,1024]{2,1,0:T(8,128)(2,1)S(1)}, u32[]{:S(2)}, u32[]{:S(2)}) collective-permute-start(bf16[4,128,1024]{2,1,0:T(8,128)(2,1)S(1)} %constant_dynamic-slice_fusion.1), channel_id=1, source_target_pairs={{0,2},{1,3},{2,0},{3,1},{4,6},{5,7},{6,4},{7,5},{8,10},{9,11},{10,... | collective-permute-start | bytes 3145736 | tf_op jit(solution)/shard_map/stream1/ppermute | solution.py:205
  148.1 43.3 %collective-permute-start.32 = (bf16[2,4,128,1024]{3,2,1,0:T(8,128)(2,1)S(1)}, bf16[2,4,128,1024]{3,2,1,0:T(8,128)(2,1)S(1)}, u32[]{:S(2)}, u32[]{:S(2)}) collective-permute-start(bf16[2,4,128,1024]{3,2,1,0:T(8,128)(2,1)S(1)} %bitcast.315), channel_id=1, source_target_pairs={{1,0},{0,1},{3,2},{2,3},{5,4},{4,5},{7,6},{6,7},{9,8},{8,9},{11,10... | collective-permute-start | bytes 6291464 | tf_op jit(solution)/shard_map/stream0/transpose()/ppermute | solution.py:205
  167.5 51.1 %collective-permute-start.31 = (bf16[2,4,128,1024]{3,2,1,0:T(8,128)(2,1)S(1)}, bf16[2,4,128,1024]{3,2,1,0:T(8,128)(2,1)S(1)}, u32[]{:S(2)}, u32[]{:S(2)}) collective-permute-start(bf16[2,4,128,1024]{3,2,1,0:T(8,128)(2,1)S(1)} %get-tuple-element.41), channel_id=1, source_target_pairs={{0,1},{1,0},{2,3},{3,2},{4,5},{5,4},{6,7},{7,6},{8,9},{9,8},{10,11... | collective-permute-start | bytes 6291464 | tf_op jit(solution)/shard_map/stream1/ppermute | solution.py:205
  188.7 32.4 %collective-permute-start.23 = (bf16[2,4,128,1024]{3,2,1,0:T(8,128)(2,1)S(1)}, bf16[2,4,128,1024]{3,2,1,0:T(8,128)(2,1)S(1)}, u32[]{:S(2)}, u32[]{:S(2)}) collective-permute-start(bf16[2,4,128,1024]{3,2,1,0:T(8,128)(2,1)S(1)} %get-tuple-element.43), channel_id=1, source_target_pairs={{0,1},{1,0},{2,3},{3,2},{4,5},{5,4},{6,7},{7,6},{8,9},{9,8},{10,11... | collective-permute-start | bytes 6291464 | tf_op jit(solution)/shard_map/stream1/ppermute | solution.py:205
  189.8 26.1 %collective-permute-start.49 = (bf16[4,128,1024]{2,1,0:T(8,128)(2,1)S(1)}, bf16[4,128,1024]{2,1,0:T(8,128)(2,1)S(1)}, u32[]{:S(2)}, u32[]{:S(2)}) collective-permute-start(bf16[4,128,1024]{2,1,0:T(8,128)(2,1)S(1)} %fusion.10), channel_id=1, source_target_pairs={{2,0},{3,1},{0,2},{1,3},{6,4},{7,5},{4,6},{5,7},{10,8},{11,9},{8,1... | collective-permute-start | bytes 3145736 | tf_op jit(solution)/shard_map/stream0/transpose()/ppermute | solution.py:205
  192.5 51.4 %collective-permute-start.33 = (bf16[4,128,1024]{2,1,0:T(8,128)(2,1)S(1)}, bf16[4,128,1024]{2,1,0:T(8,128)(2,1)}, u32[]{:S(2)}, u32[]{:S(2)}) collective-permute-start(bf16[4,128,1024]{2,1,0:T(8,128)(2,1)S(1)} %fusion.8), channel_id=1, source_target_pairs={{2,0},{3,1},{0,2},{1,3},{6,4},{7,5},{4,6},{5,7},{10,8},{11,9},{8,1... | collective-permute-start | bytes 3145736 | tf_op jit(solution)/shard_map/stream0/transpose()/ppermute | solution.py:205
  242.3 31.4 %collective-permute-start.56 = (bf16[2,4,128,1024]{3,2,1,0:T(8,128)(2,1)S(1)}, bf16[2,4,128,1024]{3,2,1,0:T(8,128)(2,1)S(1)}, u32[]{:S(2)}, u32[]{:S(2)}) collective-permute-start(bf16[2,4,128,1024]{3,2,1,0:T(8,128)(2,1)S(1)} %bitcast.318), channel_id=1, source_target_pairs={{1,0},{0,1},{3,2},{2,3},{5,4},{4,5},{7,6},{6,7},{9,8},{8,9},{11,10... | collective-permute-start | bytes 6291464 | tf_op jit(solution)/shard_map/stream1/transpose()/ppermute | solution.py:205
  246.5 33.1 %collective-permute-start.40 = (bf16[2,4,128,1024]{3,2,1,0:T(8,128)(2,1)S(1)}, bf16[2,4,128,1024]{3,2,1,0:T(8,128)(2,1)S(1)}, u32[]{:S(2)}, u32[]{:S(2)}) collective-permute-start(bf16[2,4,128,1024]{3,2,1,0:T(8,128)(2,1)S(1)} %bitcast.316), channel_id=1, source_target_pairs={{1,0},{0,1},{3,2},{2,3},{5,4},{4,5},{7,6},{6,7},{9,8},{8,9},{11,10... | collective-permute-start | bytes 6291464 | tf_op jit(solution)/shard_map/stream1/transpose()/ppermute | solution.py:205
  266.6 68.3 %collective-permute-start.52 = (bf16[128,1024]{1,0:T(8,128)(2,1)S(1)}, bf16[128,1024]{1,0:T(8,128)(2,1)S(1)}, u32[]{:S(2)}, u32[]{:S(2)}) collective-permute-start(bf16[128,1024]{1,0:T(8,128)(2,1)S(1)} %get-tuple-element.32), channel_id=1, source_target_pairs={{0,4},{1,5},{2,6},{3,7},{4,8},{5,9},{6,10},{7,11},{8,12},{9,13},{1... | collective-permute-start | bytes 786440 | tf_op jit(solution)/shard_map/stream0/transpose()/ppermute | solution.py:205
  273.7 88.2 %collective-permute-start.36 = (bf16[128,1024]{1,0:T(8,128)(2,1)S(1)}, bf16[128,1024]{1,0:T(8,128)(2,1)S(1)}, u32[]{:S(2)}, u32[]{:S(2)}) collective-permute-start(bf16[128,1024]{1,0:T(8,128)(2,1)S(1)} %get-tuple-element.36), channel_id=1, source_target_pairs={{0,4},{1,5},{2,6},{3,7},{4,8},{5,9},{6,10},{7,11},{8,12},{9,13},{1... | collective-permute-start | bytes 786440 | tf_op jit(solution)/shard_map/stream0/transpose()/ppermute | solution.py:205
  279.6 26.1 %collective-permute-start.57 = (bf16[4,128,1024]{2,1,0:T(8,128)(2,1)S(1)}, bf16[4,128,1024]{2,1,0:T(8,128)(2,1)S(1)}, u32[]{:S(2)}, u32[]{:S(2)}) collective-permute-start(bf16[4,128,1024]{2,1,0:T(8,128)(2,1)S(1)} %fusion.11), channel_id=1, source_target_pairs={{2,0},{3,1},{0,2},{1,3},{6,4},{7,5},{4,6},{5,7},{10,8},{11,9},{8,1... | collective-permute-start | bytes 3145736 | tf_op jit(solution)/shard_map/stream1/transpose()/ppermute | solution.py:205
  282.3 43.0 %collective-permute-start.41 = (bf16[4,128,1024]{2,1,0:T(8,128)(2,1)S(1)}, bf16[4,128,1024]{2,1,0:T(8,128)(2,1)S(1)}, u32[]{:S(2)}, u32[]{:S(2)}) collective-permute-start(bf16[4,128,1024]{2,1,0:T(8,128)(2,1)S(1)} %fusion.9), channel_id=1, source_target_pairs={{2,0},{3,1},{0,2},{1,3},{6,4},{7,5},{4,6},{5,7},{10,8},{11,9},{8,1... | collective-permute-start | bytes 3145736 | tf_op jit(solution)/shard_map/stream1/transpose()/ppermute | solution.py:205
  282.9 52.6 %collective-permute-start.55 = (bf16[128,1024]{1,0:T(8,128)(2,1)S(1)}, bf16[128,1024]{1,0:T(8,128)(2,1)S(1)}, u32[]{:S(2)}, u32[]{:S(2)}) collective-permute-start(bf16[128,1024]{1,0:T(8,128)(2,1)S(1)} %fusion.26), channel_id=1, source_target_pairs={{4,0},{5,1},{6,2},{7,3},{8,4},{9,5},{10,6},{11,7},{12,8},{13,9},{1... | collective-permute-start | bytes 786440 | tf_op jit(solution)/shard_map/stream0/transpose()/ppermute | solution.py:205
  305.7 56.2 %collective-permute-start.39 = (bf16[128,1024]{1,0:T(8,128)(2,1)S(1)}, bf16[128,1024]{1,0:T(8,128)(2,1)S(1)}, u32[]{:S(2)}, u32[]{:S(2)}) collective-permute-start(bf16[128,1024]{1,0:T(8,128)(2,1)S(1)} %fusion.48), channel_id=1, source_target_pairs={{4,0},{5,1},{6,2},{7,3},{8,4},{9,5},{10,6},{11,7},{12,8},{13,9},{1... | collective-permute-start | bytes 786440 | tf_op jit(solution)/shard_map/stream0/transpose()/ppermute | solution.py:205
  350.1 17.8 %collective-permute-start.60 = (bf16[128,1024]{1,0:T(8,128)(2,1)S(1)}, bf16[128,1024]{1,0:T(8,128)(2,1)S(1)}, u32[]{:S(2)}, u32[]{:S(2)}) collective-permute-start(bf16[128,1024]{1,0:T(8,128)(2,1)S(1)} %get-tuple-element.34), channel_id=1, source_target_pairs={{0,4},{1,5},{2,6},{3,7},{4,8},{5,9},{6,10},{7,11},{8,12},{9,13},{1... | collective-permute-start | bytes 786440 | tf_op jit(solution)/shard_map/stream1/transpose()/ppermute | solution.py:205
  (55 other events, 634.1 us)

commit v12 on v11

--- a/solution.py
+++ b/solution.py
@@ -300,7 +300,7 @@
     )
 
 
-STREAMS = 2
+STREAMS = 3
 
 
 def _stream(pos, query, grad_out, keys, values, after=None):
@@ -339,11 +339,13 @@
     core = idx % 2
     ypos = (idx // 2) % 2
     pos = (((listed % 2) ^ core) * 2 + (((listed // 2) % 2) ^ ypos)) * line_len + listed // 4
-    cut = width // STREAMS
+    heads = width // HD
+    shares = [heads // STREAMS + (1 if s < heads % STREAMS else 0) for s in range(STREAMS)]
+    edges = [sum(shares[:s]) * HD for s in range(STREAMS + 1)]
     outs = []
     after = None
     for s in range(STREAMS):
-        cols = slice(s * cut, (s + 1) * cut)
+        cols = slice(edges[s], edges[s + 1])
         with jax.named_scope(f"stream{s}"):
             out, after = _stream(
                 pos, query[:, cols], grad_out[:, cols], keys[:, cols], values[:, cols], after

time: 378 us -> 446 us (1.18)
  starting transfers between devices: 116 us -> 174 us
    ppermute x64 -> x96, starting transfers between devices: 116 us -> 174 us  [_send(): return lax.ppermute(v.astype(jnp.bfloat16), 'seq', pairs).astype(v.dtype)]
    convert_element_type x12 -> x18, other arithmetic: 1.02 us -> 5.9 us  [_send(): return lax.ppermute(v.astype(jnp.bfloat16), 'seq', pairs).astype(v.dtype)]
    pallas_call x2 -> x3, Pallas kernels: 29.9 us -> 32.4 us  [attend_local(): call(pos, query, grad_out, *[keys_local] * SLOTS, *[values_local] * SLOTS)]
    another operation x2 -> x3, local copies, waits for them, and re-layouts: 8.02 us -> 10 us  [gather_blocks(): return jnp.stack([pair, sibling])]
    another operation x8 -> x12, other arithmetic: 10.7 us -> 12.3 us  [gather_blocks(): return jnp.stack([pair, sibling])]
    ppermute x64 -> x96, waiting for transfers between devices: 185 us -> 186 us  [_send(): return lax.ppermute(v.astype(jnp.bfloat16), 'seq', pairs).astype(v.dtype)]
  transfers between devices with their start and end apart: 64 -> 96, of which waited for: 24 -> 32; matrix products, arithmetic and copies ran while one was open for 9% -> 10% of each run, Pallas kernels for 8% -> 7%
where the time goes in v12:
time: 446 us; the launch traced here: 443 us
  waiting for transfers between devices  186 us (42%)
  starting transfers between devices  174 us (39%)
  Pallas kernels  32.4 us (7%)
  other arithmetic  25.5 us (6%)
  local copies, waits for them, and re-layouts  22.4 us (5%)
    ppermute x96, waiting for transfers between devices, _send(): return lax.ppermute(v.astype(jnp.bfloat16), 'seq', pairs).astype(v.dtype)  186 us
    ppermute x96, starting transfers between devices, _send(): return lax.ppermute(v.astype(jnp.bfloat16), 'seq', pairs).astype(v.dtype)  174 us
    pallas_call x3, Pallas kernels, attend_local(): call(pos, query, grad_out, *[keys_local] * SLOTS, *[values_local] * SLOTS)  32.4 us
    another operation x12, other arithmetic, gather_blocks(): return jnp.stack([pair, sibling])  12.3 us
    another operation x3, local copies, waits for them, and re-layouts, gather_blocks(): return jnp.stack([pair, sibling])  10 us
  transfers between devices with their start and end apart: 96, of which 32 were waited for; matrix products, arithmetic and copies ran while one was open for 10% of the time, Pallas kernels for 7%

profile of v12, /device:TPU:10, one launch (start us, length us, event | category | flops | bytes accessed | tf_op | source)
XLA Modules:
  0.0 443.5 jit_solution(8590024666171415306)
XLA Ops:
  39.5 15.9 %collective-permute-done.14 = bf16[4,128,768]{2,1,0:T(8,128)(2,1)S(1)} collective-permute-done((bf16[4,128,768]{2,1,0:T(8,128)(2,1)S(1)}, bf16[4,128,768]{2,1,0:T(8,128)(2,1)S(1)}, u32[]{:S(2)}, u32[]{:S(2)}) %collective-permute-start.14) | collective-permute-done | bytes 786464 | tf_op jit(solution)/shard_map/stream0/ppermute | solution.py:205
  55.7 10.9 %collective-permute-done.6 = bf16[4,128,768]{2,1,0:T(8,128)(2,1)S(1)} collective-permute-done((bf16[4,128,768]{2,1,0:T(8,128)(2,1)S(1)}, bf16[4,128,768]{2,1,0:T(8,128)(2,1)S(1)}, u32[]{:S(2)}, u32[]{:S(2)}) %collective-permute-start.6) | collective-permute-done | bytes 786464 | tf_op jit(solution)/shard_map/stream0/ppermute | solution.py:205
  88.2 11.9 %stream0.1 = (bf16[128,768]{1,0:T(8,128)(2,1)}, bf16[128,768]{1,0:T(8,128)(2,1)}, bf16[16,128,768]{2,1,0:T(8,128)(2,1)}, bf16[16,128,768]{2,1,0:T(8,128)(2,1)}) custom-call(s32[8]{0:T(128)} %multiply_add_fusion.pos_ref, bf16[128,768]{1,0:T(8,128)(2,1)} %slice.60.q_ref, bf16[128,768]{1,0:T(8,128)(2,1)} %slice.61.g_ref, bf16[16,128,768]{2,1,0:T(8,128)(2,1)} %bitcast.419, ...), custom_call_target="tpu_custom_call" | custom-call | flops 1207959552 | bytes 10223616 | tf_op jit(solution)/shard_map/stream0/pallas_call | solution.py:298
  124.0 12.3 %collective-permute-done.30 = bf16[4,128,640]{2,1,0:T(8,128)(2,1)S(1)} collective-permute-done((bf16[4,128,640]{2,1,0:T(8,128)(2,1)S(1)}, bf16[4,128,640]{2,1,0:T(8,128)(2,1)S(1)}, u32[]{:S(2)}, u32[]{:S(2)}) %collective-permute-start.30) | collective-permute-done | bytes 655392 | tf_op jit(solution)/shard_map/stream1/ppermute | solution.py:205
  136.5 11.7 %collective-permute-done.22 = bf16[4,128,640]{2,1,0:T(8,128)(2,1)S(1)} collective-permute-done((bf16[4,128,640]{2,1,0:T(8,128)(2,1)S(1)}, bf16[4,128,640]{2,1,0:T(8,128)(2,1)S(1)}, u32[]{:S(2)}, u32[]{:S(2)}) %collective-permute-start.22) | collective-permute-done | bytes 655392 | tf_op jit(solution)/shard_map/stream1/ppermute | solution.py:205
  152.3 17.1 %collective-permute-done.73 = bf16[4,128,768]{2,1,0:T(8,128)(2,1)S(1)} collective-permute-done((bf16[4,128,768]{2,1,0:T(8,128)(2,1)S(1)}, bf16[4,128,768]{2,1,0:T(8,128)(2,1)S(1)}, u32[]{:S(2)}, u32[]{:S(2)}) %collective-permute-start.73) | collective-permute-done | bytes 786464 | tf_op jit(solution)/shard_map/stream0/transpose()/ppermute | solution.py:205
  172.8 13.0 %collective-permute-done.49 = bf16[4,128,768]{2,1,0:T(8,128)(2,1)S(1)} collective-permute-done((bf16[4,128,768]{2,1,0:T(8,128)(2,1)S(1)}, bf16[4,128,768]{2,1,0:T(8,128)(2,1)S(1)}, u32[]{:S(2)}, u32[]{:S(2)}) %collective-permute-start.49) | collective-permute-done | bytes 786464 | tf_op jit(solution)/shard_map/stream0/transpose()/ppermute | solution.py:205
  197.7 10.3 %stream1.1 = (bf16[128,640]{1,0:T(8,128)(2,1)}, bf16[128,640]{1,0:T(8,128)(2,1)}, bf16[16,128,640]{2,1,0:T(8,128)(2,1)}, bf16[16,128,640]{2,1,0:T(8,128)(2,1)}) custom-call(s32[8]{0:T(128)} %multiply_add_fusion.pos_ref, bf16[128,640]{1,0:T(8,128)(2,1)} %get-tuple-element.86.q_ref, bf16[128,640]{1,0:T(8,128)(2,1)} %get-tuple-element.84.g_ref, ...), custom_call_target="tpu_custom_call" | custom-call | flops 1006632960 | bytes 8519680 | tf_op jit(solution)/shard_map/stream1/pallas_call | solution.py:298
  235.2 6.2 %collective-permute-done.78 = bf16[128,768]{1,0:T(8,128)(2,1)S(1)} collective-permute-done((bf16[128,768]{1,0:T(8,128)(2,1)S(1)}, bf16[128,768]{1,0:T(8,128)(2,1)S(1)}, u32[]{:S(2)}, u32[]{:S(2)}) %collective-permute-start.78) | collective-permute-done | bytes 196640 | tf_op jit(solution)/shard_map/stream0/transpose()/ppermute | solution.py:205
  242.8 4.6 %collective-permute-start.33 = (bf16[128,640]{1,0:T(8,128)(2,1)S(1)}, bf16[128,640]{1,0:T(8,128)(2,1)S(1)}, u32[]{:S(2)}, u32[]{:S(2)}) collective-permute-start(bf16[128,640]{1,0:T(8,128)(2,1)S(1)} %collective-permute-done.32), channel_id=1, source_target_pairs={{4,8},{5,9},{6,10},{7,11},{8,12},{9,13},{10,14},{11,15},{20,24},{2... | collective-permute-start | bytes 491528 | tf_op jit(solution)/shard_map/stream2/ppermute | solution.py:205
  258.7 3.9 collective-permute-start.76
  269.2 4.4 collective-permute-start.79
  285.1 6.2 %collective-permute-done.46 = bf16[4,128,640]{2,1,0:T(8,128)(2,1)S(1)} collective-permute-done((bf16[4,128,640]{2,1,0:T(8,128)(2,1)S(1)}, bf16[4,128,640]{2,1,0:T(8,128)(2,1)S(1)}, u32[]{:S(2)}, u32[]{:S(2)}) %collective-permute-start.46) | collective-permute-done | bytes 655392 | tf_op jit(solution)/shard_map/stream2/ppermute | solution.py:205
  294.6 10.9 %collective-permute-done.38 = bf16[4,128,640]{2,1,0:T(8,128)(2,1)S(1)} collective-permute-done((bf16[4,128,640]{2,1,0:T(8,128)(2,1)S(1)}, bf16[4,128,640]{2,1,0:T(8,128)(2,1)S(1)}, u32[]{:S(2)}, u32[]{:S(2)}) %collective-permute-start.38) | collective-permute-done | bytes 655392 | tf_op jit(solution)/shard_map/stream2/ppermute | solution.py:205
  305.7 13.8 %collective-permute-done.81 = bf16[4,128,640]{2,1,0:T(8,128)(2,1)S(1)} collective-permute-done((bf16[4,128,640]{2,1,0:T(8,128)(2,1)S(1)}, bf16[4,128,640]{2,1,0:T(8,128)(2,1)S(1)}, u32[]{:S(2)}, u32[]{:S(2)}) %collective-permute-start.81) | collective-permute-done | bytes 655392 | tf_op jit(solution)/shard_map/stream1/transpose()/ppermute | solution.py:205
  322.0 7.0 %collective-permute-done.57 = bf16[4,128,640]{2,1,0:T(8,128)(2,1)S(1)} collective-permute-done((bf16[4,128,640]{2,1,0:T(8,128)(2,1)S(1)}, bf16[4,128,640]{2,1,0:T(8,128)(2,1)S(1)}, u32[]{:S(2)}, u32[]{:S(2)}) %collective-permute-start.57) | collective-permute-done | bytes 655392 | tf_op jit(solution)/shard_map/stream1/transpose()/ppermute | solution.py:205
  332.1 4.8 %collective-permute-done.58 = bf16[128,640]{1,0:T(8,128)(2,1)S(1)} collective-permute-done((bf16[128,640]{1,0:T(8,128)(2,1)S(1)}, bf16[128,640]{1,0:T(8,128)(2,1)S(1)}, u32[]{:S(2)}, u32[]{:S(2)}) %collective-permute-start.58) | collective-permute-done | bytes 163872 | tf_op jit(solution)/shard_map/stream1/transpose()/ppermute | solution.py:205
  345.0 10.2 %stream2.1 = (bf16[128,640]{1,0:T(8,128)(2,1)}, bf16[128,640]{1,0:T(8,128)(2,1)}, bf16[16,128,640]{2,1,0:T(8,128)(2,1)}, bf16[16,128,640]{2,1,0:T(8,128)(2,1)}) custom-call(s32[8]{0:T(128)} %multiply_add_fusion.pos_ref, bf16[128,640]{1,0:T(8,128)(2,1)} %get-tuple-element.87.q_ref, bf16[128,640]{1,0:T(8,128)(2,1)} %get-tuple-element.85.g_ref, ...), custom_call_target="tpu_custom_call" | custom-call | flops 1006632960 | bytes 8519680 | tf_op jit(solution)/shard_map/stream2/pallas_call | solution.py:298
  361.2 4.6 %collective-permute-start.84 = (bf16[128,640]{1,0:T(8,128)(2,1)S(1)}, bf16[128,640]{1,0:T(8,128)(2,1)S(1)}, u32[]{:S(2)}, u32[]{:S(2)}) collective-permute-start(bf16[128,640]{1,0:T(8,128)(2,1)S(1)} %get-tuple-element.52), channel_id=1, source_target_pairs={{0,4},{1,5},{2,6},{3,7},{4,8},{5,9},{6,10},{7,11},{8,12},{9,13},{1... | collective-permute-start | bytes 491528 | tf_op jit(solution)/shard_map/stream1/transpose()/ppermute | solution.py:205
  368.1 4.6 %collective-permute-start.60 = (bf16[128,640]{1,0:T(8,128)(2,1)S(1)}, bf16[128,640]{1,0:T(8,128)(2,1)S(1)}, u32[]{:S(2)}, u32[]{:S(2)}) collective-permute-start(bf16[128,640]{1,0:T(8,128)(2,1)S(1)} %get-tuple-element.56), channel_id=1, source_target_pairs={{0,4},{1,5},{2,6},{3,7},{4,8},{5,9},{6,10},{7,11},{8,12},{9,13},{1... | collective-permute-start | bytes 491528 | tf_op jit(solution)/shard_map/stream1/transpose()/ppermute | solution.py:205
  384.7 13.4 %collective-permute-done.89 = bf16[4,128,640]{2,1,0:T(8,128)(2,1)S(1)} collective-permute-done((bf16[4,128,640]{2,1,0:T(8,128)(2,1)S(1)}, bf16[4,128,640]{2,1,0:T(8,128)(2,1)S(1)}, u32[]{:S(2)}, u32[]{:S(2)}) %collective-permute-start.89) | collective-permute-done | bytes 655392 | tf_op jit(solution)/shard_map/stream2/transpose()/ppermute | solution.py:205
  400.6 9.1 %collective-permute-done.65 = bf16[4,128,640]{2,1,0:T(8,128)(2,1)S(1)} collective-permute-done((bf16[4,128,640]{2,1,0:T(8,128)(2,1)S(1)}, bf16[4,128,640]{2,1,0:T(8,128)(2,1)S(1)}, u32[]{:S(2)}, u32[]{:S(2)}) %collective-permute-start.65) | collective-permute-done | bytes 655392 | tf_op jit(solution)/shard_map/stream2/transpose()/ppermute | solution.py:205
  422.0 5.0 %collective-permute-start.92 = (bf16[128,640]{1,0:T(8,128)(2,1)S(1)}, bf16[128,640]{1,0:T(8,128)(2,1)S(1)}, u32[]{:S(2)}, u32[]{:S(2)}) collective-permute-start(bf16[128,640]{1,0:T(8,128)(2,1)S(1)} %get-tuple-element.54), channel_id=1, source_target_pairs={{0,4},{1,5},{2,6},{3,7},{4,8},{5,9},{6,10},{7,11},{8,12},{9,13},{1... | collective-permute-start | bytes 491528 | tf_op jit(solution)/shard_map/stream2/transpose()/ppermute | solution.py:205
  428.5 4.6 %collective-permute-start.68 = (bf16[128,640]{1,0:T(8,128)(2,1)S(1)}, bf16[128,640]{1,0:T(8,128)(2,1)S(1)}, u32[]{:S(2)}, u32[]{:S(2)}) collective-permute-start(bf16[128,640]{1,0:T(8,128)(2,1)S(1)} %get-tuple-element.58), channel_id=1, source_target_pairs={{0,4},{1,5},{2,6},{3,7},{4,8},{5,9},{6,10},{7,11},{8,12},{9,13},{1... | collective-permute-start | bytes 491528 | tf_op jit(solution)/shard_map/stream2/transpose()/ppermute | solution.py:205
  (348 shorter events, 224.6 us)
Async XLA Ops:
  37.9 28.7 %collective-permute-start.6 = (bf16[4,128,768]{2,1,0:T(8,128)(2,1)S(1)}, bf16[4,128,768]{2,1,0:T(8,128)(2,1)S(1)}, u32[]{:S(2)}, u32[]{:S(2)}) collective-permute-start(bf16[4,128,768]{2,1,0:T(8,128)(2,1)S(1)} %constant_dynamic-slice_fusion.5), channel_id=1, source_target_pairs={{0,2},{1,3},{2,0},{3,1},{4,6},{5,7},{6,4},{7,5},{8,10},{9,11},{10,... | collective-permute-start | bytes 2359304 | tf_op jit(solution)/shard_map/stream0/ppermute | solution.py:205
  80.3 25.6 %collective-permute-start.19 = (bf16[128,640]{1,0:T(8,128)(2,1)S(1)}, bf16[128,640]{1,0:T(8,128)(2,1)S(1)}, u32[]{:S(2)}, u32[]{:S(2)}) collective-permute-start(bf16[128,640]{1,0:T(8,128)(2,1)S(1)} %get-tuple-element.21), channel_id=1, source_target_pairs={{4,0},{5,1},{6,2},{7,3},{8,4},{9,5},{10,6},{11,7},{12,8},{13,9},{1... | collective-permute-start | bytes 491528 | tf_op jit(solution)/shard_map/stream1/ppermute | solution.py:205
  112.0 36.5 %collective-permute-start.72 = (bf16[2,4,128,768]{3,2,1,0:T(8,128)(2,1)S(1)}, bf16[2,4,128,768]{3,2,1,0:T(8,128)(2,1)S(1)}, u32[]{:S(2)}, u32[]{:S(2)}) collective-permute-start(bf16[2,4,128,768]{3,2,1,0:T(8,128)(2,1)S(1)} %bitcast.466), channel_id=1, source_target_pairs={{1,0},{0,1},{3,2},{2,3},{5,4},{4,5},{7,6},{6,7},{9,8},{8,9},{11,10... | collective-permute-start | bytes 4718600 | tf_op jit(solution)/shard_map/stream0/transpose()/ppermute | solution.py:205
  112.1 38.4 %collective-permute-start.48 = (bf16[2,4,128,768]{3,2,1,0:T(8,128)(2,1)S(1)}, bf16[2,4,128,768]{3,2,1,0:T(8,128)(2,1)S(1)}, u32[]{:S(2)}, u32[]{:S(2)}) collective-permute-start(bf16[2,4,128,768]{3,2,1,0:T(8,128)(2,1)S(1)} %bitcast.465), channel_id=1, source_target_pairs={{1,0},{0,1},{3,2},{2,3},{5,4},{4,5},{7,6},{6,7},{9,8},{8,9},{11,10... | collective-permute-start | bytes 4718600 | tf_op jit(solution)/shard_map/stream0/transpose()/ppermute | solution.py:205
  121.5 26.7 %collective-permute-start.22 = (bf16[4,128,640]{2,1,0:T(8,128)(2,1)S(1)}, bf16[4,128,640]{2,1,0:T(8,128)(2,1)S(1)}, u32[]{:S(2)}, u32[]{:S(2)}) collective-permute-start(bf16[4,128,640]{2,1,0:T(8,128)(2,1)S(1)} %constant_dynamic-slice_fusion.3), channel_id=1, source_target_pairs={{0,2},{1,3},{2,0},{3,1},{4,6},{5,7},{6,4},{7,5},{8,10},{9,11},{10,... | collective-permute-start | bytes 1966088 | tf_op jit(solution)/shard_map/stream1/ppermute | solution.py:205
  136.4 53.4 %collective-permute-start.31 = (bf16[2,4,128,640]{3,2,1,0:T(8,128)(2,1)S(1)}, bf16[2,4,128,640]{3,2,1,0:T(8,128)(2,1)S(1)}, u32[]{:S(2)}, u32[]{:S(2)}) collective-permute-start(bf16[2,4,128,640]{3,2,1,0:T(8,128)(2,1)S(1)} %get-tuple-element.73), channel_id=1, source_target_pairs={{0,1},{1,0},{2,3},{3,2},{4,5},{5,4},{6,7},{7,6},{8,9},{9,8},{10,11... | collective-permute-start | bytes 3932168 | tf_op jit(solution)/shard_map/stream1/ppermute | solution.py:205
  148.4 43.9 %collective-permute-start.23 = (bf16[2,4,128,640]{3,2,1,0:T(8,128)(2,1)S(1)}, bf16[2,4,128,640]{3,2,1,0:T(8,128)(2,1)S(1)}, u32[]{:S(2)}, u32[]{:S(2)}) collective-permute-start(bf16[2,4,128,640]{3,2,1,0:T(8,128)(2,1)S(1)} %get-tuple-element.75), channel_id=1, source_target_pairs={{0,1},{1,0},{2,3},{3,2},{4,5},{5,4},{6,7},{7,6},{8,9},{9,8},{10,11... | collective-permute-start | bytes 3932168 | tf_op jit(solution)/shard_map/stream1/ppermute | solution.py:205
  151.0 34.8 %collective-permute-start.49 = (bf16[4,128,768]{2,1,0:T(8,128)(2,1)S(1)}, bf16[4,128,768]{2,1,0:T(8,128)(2,1)S(1)}, u32[]{:S(2)}, u32[]{:S(2)}) collective-permute-start(bf16[4,128,768]{2,1,0:T(8,128)(2,1)S(1)} %fusion.12), channel_id=1, source_target_pairs={{2,0},{3,1},{0,2},{1,3},{6,4},{7,5},{4,6},{5,7},{10,8},{11,9},{8,1... | collective-permute-start | bytes 2359304 | tf_op jit(solution)/shard_map/stream0/transpose()/ppermute | solution.py:205
  170.8 40.5 %collective-permute-start.74 = (bf16[128,768]{1,0:T(8,128)(2,1)}, bf16[128,768]{1,0:T(8,128)(2,1)}, u32[]{:S(2)}, u32[]{:S(2)}) collective-permute-start(bf16[128,768]{1,0:T(8,128)(2,1)} %get-tuple-element.64), channel_id=1, source_target_pairs={{0,4},{1,5},{2,6},{3,7},{16,20},{17,21},{18,22},{19,23}} | collective-permute-start | bytes 589832 | tf_op jit(solution)/shard_map/stream0/transpose()/ppermute | solution.py:205
  172.1 47.7 %collective-permute-start.77 = (bf16[128,768]{1,0:T(8,128)(2,1)}, bf16[128,768]{1,0:T(8,128)(2,1)S(1)}, u32[]{:S(2)}, u32[]{:S(2)}) collective-permute-start(bf16[128,768]{1,0:T(8,128)(2,1)} %get-tuple-element.65), channel_id=1, source_target_pairs={{12,8},{13,9},{14,10},{15,11},{28,24},{29,25},{30,26},{31,27}} | collective-permute-start | bytes 589832 | tf_op jit(solution)/shard_map/stream0/transpose()/ppermute | solution.py:205
  188.6 27.3 %collective-permute-start.50 = (bf16[128,768]{1,0:T(8,128)(2,1)}, bf16[128,768]{1,0:T(8,128)(2,1)}, u32[]{:S(2)}, u32[]{:S(2)}) collective-permute-start(bf16[128,768]{1,0:T(8,128)(2,1)} %get-tuple-element.66), channel_id=1, source_target_pairs={{0,4},{1,5},{2,6},{3,7},{16,20},{17,21},{18,22},{19,23}} | collective-permute-start | bytes 589832 | tf_op jit(solution)/shard_map/stream0/transpose()/ppermute | solution.py:205
  189.8 38.1 %collective-permute-start.53 = (bf16[128,768]{1,0:T(8,128)(2,1)}, bf16[128,768]{1,0:T(8,128)(2,1)S(1)}, u32[]{:S(2)}, u32[]{:S(2)}) collective-permute-start(bf16[128,768]{1,0:T(8,128)(2,1)} %get-tuple-element.67), channel_id=1, source_target_pairs={{12,8},{13,9},{14,10},{15,11},{28,24},{29,25},{30,26},{31,27}} | collective-permute-start | bytes 589832 | tf_op jit(solution)/shard_map/stream0/transpose()/ppermute | solution.py:205
  194.2 36.3 %collective-permute-start.40 = (bf16[128,640]{1,0:T(8,128)(2,1)S(1)}, bf16[128,640]{1,0:T(8,128)(2,1)}, u32[]{:S(2)}, u32[]{:S(2)}) collective-permute-start(bf16[128,640]{1,0:T(8,128)(2,1)S(1)} %get-tuple-element.25), channel_id=1, source_target_pairs={{0,4},{1,5},{2,6},{3,7},{4,8},{5,9},{6,10},{7,11},{8,12},{9,13},{1... | collective-permute-start | bytes 491528 | tf_op jit(solution)/shard_map/stream2/ppermute | solution.py:205
  211.3 38.3 %collective-permute-start.43 = (bf16[128,640]{1,0:T(8,128)(2,1)S(1)}, bf16[128,640]{1,0:T(8,128)(2,1)S(1)}, u32[]{:S(2)}, u32[]{:S(2)}) collective-permute-start(bf16[128,640]{1,0:T(8,128)(2,1)S(1)} %get-tuple-element.25), channel_id=1, source_target_pairs={{4,0},{5,1},{6,2},{7,3},{8,4},{9,5},{10,6},{11,7},{12,8},{13,9},{1... | collective-permute-start | bytes 491528 | tf_op jit(solution)/shard_map/stream2/ppermute | solution.py:205
  242.7 49.0 %collective-permute-start.80 = (bf16[2,4,128,640]{3,2,1,0:T(8,128)(2,1)S(1)}, bf16[2,4,128,640]{3,2,1,0:T(8,128)(2,1)S(1)}, u32[]{:S(2)}, u32[]{:S(2)}) collective-permute-start(bf16[2,4,128,640]{3,2,1,0:T(8,128)(2,1)S(1)} %bitcast.470), channel_id=1, source_target_pairs={{1,0},{0,1},{3,2},{2,3},{5,4},{4,5},{7,6},{6,7},{9,8},{8,9},{11,10... | collective-permute-start | bytes 3932168 | tf_op jit(solution)/shard_map/stream1/transpose()/ppermute | solution.py:205
  249.7 44.0 %collective-permute-start.56 = (bf16[2,4,128,640]{3,2,1,0:T(8,128)(2,1)S(1)}, bf16[2,4,128,640]{3,2,1,0:T(8,128)(2,1)S(1)}, u32[]{:S(2)}, u32[]{:S(2)}) collective-permute-start(bf16[2,4,128,640]{3,2,1,0:T(8,128)(2,1)S(1)} %bitcast.469), channel_id=1, source_target_pairs={{1,0},{0,1},{3,2},{2,3},{5,4},{4,5},{7,6},{6,7},{9,8},{8,9},{11,10... | collective-permute-start | bytes 3932168 | tf_op jit(solution)/shard_map/stream1/transpose()/ppermute | solution.py:205
  291.6 48.0 %collective-permute-start.47 = (bf16[2,4,128,640]{3,2,1,0:T(8,128)(2,1)S(1)}, bf16[2,4,128,640]{3,2,1,0:T(8,128)(2,1)S(1)}, u32[]{:S(2)}, u32[]{:S(2)}) collective-permute-start(bf16[2,4,128,640]{3,2,1,0:T(8,128)(2,1)S(1)} %get-tuple-element.69), channel_id=1, source_target_pairs={{0,1},{1,0},{2,3},{3,2},{4,5},{5,4},{6,7},{7,6},{8,9},{9,8},{10,11... | collective-permute-start | bytes 3932168 | tf_op jit(solution)/shard_map/stream2/ppermute | solution.py:205
  292.0 27.4 %collective-permute-start.81 = (bf16[4,128,640]{2,1,0:T(8,128)(2,1)S(1)}, bf16[4,128,640]{2,1,0:T(8,128)(2,1)S(1)}, u32[]{:S(2)}, u32[]{:S(2)}) collective-permute-start(bf16[4,128,640]{2,1,0:T(8,128)(2,1)S(1)} %fusion.16), channel_id=1, source_target_pairs={{2,0},{3,1},{0,2},{1,3},{6,4},{7,5},{4,6},{5,7},{10,8},{11,9},{8,1... | collective-permute-start | bytes 1966088 | tf_op jit(solution)/shard_map/stream1/transpose()/ppermute | solution.py:205
  294.1 34.9 %collective-permute-start.57 = (bf16[4,128,640]{2,1,0:T(8,128)(2,1)S(1)}, bf16[4,128,640]{2,1,0:T(8,128)(2,1)S(1)}, u32[]{:S(2)}, u32[]{:S(2)}) collective-permute-start(bf16[4,128,640]{2,1,0:T(8,128)(2,1)S(1)} %fusion.14), channel_id=1, source_target_pairs={{2,0},{3,1},{0,2},{1,3},{6,4},{7,5},{4,6},{5,7},{10,8},{11,9},{8,1... | collective-permute-start | bytes 1966088 | tf_op jit(solution)/shard_map/stream1/transpose()/ppermute | solution.py:205
  305.6 37.6 %collective-permute-start.39 = (bf16[2,4,128,640]{3,2,1,0:T(8,128)(2,1)S(1)}, bf16[2,4,128,640]{3,2,1,0:T(8,128)(2,1)S(1)}, u32[]{:S(2)}, u32[]{:S(2)}) collective-permute-start(bf16[2,4,128,640]{3,2,1,0:T(8,128)(2,1)S(1)} %get-tuple-element.71), channel_id=1, source_target_pairs={{0,1},{1,0},{2,3},{3,2},{4,5},{5,4},{6,7},{7,6},{8,9},{9,8},{10,11... | collective-permute-start | bytes 3932168 | tf_op jit(solution)/shard_map/stream2/ppermute | solution.py:205
  321.3 37.4 %collective-permute-start.85 = (bf16[128,640]{1,0:T(8,128)(2,1)S(1)}, bf16[128,640]{1,0:T(8,128)(2,1)S(1)}, u32[]{:S(2)}, u32[]{:S(2)}) collective-permute-start(bf16[128,640]{1,0:T(8,128)(2,1)S(1)} %get-tuple-element.77), channel_id=1, source_target_pairs={{12,8},{13,9},{14,10},{15,11},{28,24},{29,25},{30,26},{31,27}} | collective-permute-start | bytes 491528 | tf_op jit(solution)/shard_map/stream1/transpose()/ppermute | solution.py:205
  330.8 35.0 %collective-permute-start.61 = (bf16[128,640]{1,0:T(8,128)(2,1)S(1)}, bf16[128,640]{1,0:T(8,128)(2,1)S(1)}, u32[]{:S(2)}, u32[]{:S(2)}) collective-permute-start(bf16[128,640]{1,0:T(8,128)(2,1)S(1)} %get-tuple-element.81), channel_id=1, source_target_pairs={{12,8},{13,9},{14,10},{15,11},{28,24},{29,25},{30,26},{31,27}} | collective-permute-start | bytes 491528 | tf_op jit(solution)/shard_map/stream1/transpose()/ppermute | solution.py:205
  339.6 26.2 %collective-permute-start.59 = (bf16[128,640]{1,0:T(8,128)(2,1)}, bf16[128,640]{1,0:T(8,128)(2,1)}, u32[]{:S(2)}, u32[]{:S(2)}) collective-permute-start(bf16[128,640]{1,0:T(8,128)(2,1)} %fusion.78), channel_id=1, source_target_pairs={{0,4},{1,5},{2,6},{3,7},{4,8},{5,9},{6,10},{7,11},{16,20},{17,21},... | collective-permute-start | bytes 491528 | tf_op jit(solution)/shard_map/stream1/transpose()/ppermute | solution.py:205
  382.5 27.3 %collective-permute-start.65 = (bf16[4,128,640]{2,1,0:T(8,128)(2,1)S(1)}, bf16[4,128,640]{2,1,0:T(8,128)(2,1)S(1)}, u32[]{:S(2)}, u32[]{:S(2)}) collective-permute-start(bf16[4,128,640]{2,1,0:T(8,128)(2,1)S(1)} %fusion.15), channel_id=1, source_target_pairs={{2,0},{3,1},{0,2},{1,3},{6,4},{7,5},{4,6},{5,7},{10,8},{11,9},{8,1... | collective-permute-start | bytes 1966088 | tf_op jit(solution)/shard_map/stream2/transpose()/ppermute | solution.py:205
  (89 other events, 1124.5 us)

commit v13 on v11

--- a/solution.py
+++ b/solution.py
@@ -208,6 +208,8 @@
 def gather_blocks(x, n):
     line_len = n // 4
     z = lax.axis_index("seq") // 4
+    y_swap = [(i, i ^ 2) for i in range(n)]
+    other_own = _send(x, y_swap)
     ups, downs = [], []
     up, down = x, x
     for k in range(1, line_len):
@@ -219,10 +221,12 @@
         )
         ups.append(up)
         downs.append(down)
-    rel = jnp.stack(ups[::-1] + [x] + downs)
-    line = lax.dynamic_slice_in_dim(rel, line_len - 1 - z, line_len, axis=0)
-    other = _send(line, [(i, i ^ 2) for i in range(n)])
-    pair = jnp.stack([line, other])
+    rest = lax.dynamic_slice_in_dim(
+        jnp.stack(ups[::-1] + downs), line_len - 1 - z, line_len - 1, axis=0
+    )
+    mine = jnp.concatenate([x[None], rest])
+    other = jnp.concatenate([other_own[None], _send(rest, y_swap)])
+    pair = jnp.stack([mine, other])
     sibling = _send(pair, [(i, i ^ 1) for i in range(n)])
     return jnp.stack([pair, sibling])
 
@@ -338,7 +342,10 @@
     listed = jnp.clip(listed, 0, n - 1)
     core = idx % 2
     ypos = (idx // 2) % 2
-    pos = (((listed % 2) ^ core) * 2 + (((listed // 2) % 2) ^ ypos)) * line_len + listed // 4
+    zpos = idx // 4
+    plane = listed // 4
+    in_line = jnp.where(plane == zpos, 0, jnp.where(plane < zpos, plane + 1, plane))
+    pos = (((listed % 2) ^ core) * 2 + (((listed // 2) % 2) ^ ypos)) * line_len + in_line
     cut = width // STREAMS
     outs = []
     after = None

time: 378 us -> 383 us (1.013)
  waiting for transfers between devices: 185 us -> 167 us
  starting transfers between devices: 116 us -> 131 us
  other arithmetic: 23.1 us -> 27.4 us
    ppermute x64 -> x72, waiting for transfers between devices: 185 us -> 167 us  [_send(): return lax.ppermute(v.astype(jnp.bfloat16), 'seq', pairs).astype(v.dtype)]
    ppermute x64 -> x72, starting transfers between devices: 116 us -> 131 us  [_send(): return lax.ppermute(v.astype(jnp.bfloat16), 'seq', pairs).astype(v.dtype)]
    another operation x4 -> x16, other arithmetic: 1.16 us -> 6.1 us
  transfers between devices with their start and end apart: 64 -> 72, of which waited for: 24 -> 25; matrix products, arithmetic and copies ran while one was open for 9% -> 11% of each run, Pallas kernels for 8% -> 8%
where the time goes in v13:
time: 383 us; the launch traced here: 379 us
  waiting for transfers between devices  167 us (44%)
  starting transfers between devices  131 us (34%)
  Pallas kernels  29.9 us (8%)
  other arithmetic  27.4 us (7%)
  local copies, waits for them, and re-layouts  20.9 us (5%)
    ppermute x72, waiting for transfers between devices, _send(): return lax.ppermute(v.astype(jnp.bfloat16), 'seq', pairs).astype(v.dtype)  167 us
    ppermute x72, starting transfers between devices, _send(): return lax.ppermute(v.astype(jnp.bfloat16), 'seq', pairs).astype(v.dtype)  131 us
    pallas_call x2, Pallas kernels, attend_local(): call(pos, query, grad_out, *[keys_local] * SLOTS, *[values_local] * SLOTS)  29.9 us
    another operation x8, other arithmetic, gather_blocks(): return jnp.stack([pair, sibling])  10.6 us
    another operation x2, local copies, waits for them, and re-layouts, gather_blocks(): return jnp.stack([pair, sibling])  7.99 us
  transfers between devices with their start and end apart: 72, of which 25 were waited for; matrix products, arithmetic and copies ran while one was open for 11% of the time, Pallas kernels for 8%

profile of v13, /device:TPU:10, one launch (start us, length us, event | category | flops | bytes accessed | tf_op | source)
XLA Modules:
  0.0 379.3 jit_solution(5839347621305541321)
XLA Ops:
  14.7 4.2 %collective-permute-start.1 = (bf16[128,1024]{1,0:T(8,128)(2,1)S(1)}, bf16[128,1024]{1,0:T(8,128)(2,1)}, u32[]{:S(2)}, u32[]{:S(2)}) collective-permute-start(bf16[128,1024]{1,0:T(8,128)(2,1)S(1)} %collective-permute-done), channel_id=1, source_target_pairs={{4,8},{5,9},{6,10},{7,11},{8,12},{9,13},{10,14},{11,15},{20,24},{2... | collective-permute-start | bytes 786440 | tf_op jit(solution)/shard_map/stream0/ppermute | solution.py:205
  20.8 3.9 %collective-permute-start.10 = (bf16[128,1024]{1,0:T(8,128)(2,1)S(1)}, bf16[128,1024]{1,0:T(8,128)(2,1)S(1)}, u32[]{:S(2)}, u32[]{:S(2)}) collective-permute-start(bf16[128,1024]{1,0:T(8,128)(2,1)S(1)} %collective-permute-done.9), channel_id=1, source_target_pairs={{4,8},{5,9},{6,10},{7,11},{8,12},{9,13},{10,14},{11,15},{20,24},{2... | collective-permute-start | bytes 786440 | tf_op jit(solution)/shard_map/stream0/ppermute | solution.py:205
  33.3 4.4 %collective-permute-start.14 = (bf16[128,1024]{1,0:T(8,128)(2,1)S(1)}, bf16[128,1024]{1,0:T(8,128)(2,1)S(1)}, u32[]{:S(2)}, u32[]{:S(2)}) collective-permute-start(bf16[128,1024]{1,0:T(8,128)(2,1)S(1)} %collective-permute-done.13), channel_id=1, source_target_pairs={{4,0},{5,1},{6,2},{7,3},{20,16},{21,17},{22,18},{23,19}} | collective-permute-start | bytes 786440 | tf_op jit(solution)/shard_map/stream0/ppermute | solution.py:205
  45.9 33.5 %collective-permute-done.6 = bf16[128,1024]{1,0:T(8,128)(2,1)S(1)} collective-permute-done((bf16[128,1024]{1,0:T(8,128)(2,1)S(1)}, bf16[128,1024]{1,0:T(8,128)(2,1)S(1)}, u32[]{:S(2)}, u32[]{:S(2)}) %collective-permute-start.6) | collective-permute-done | bytes 262176 | tf_op jit(solution)/shard_map/stream0/ppermute | solution.py:205
  89.4 4.0 %collective-permute-start.18 = (bf16[128,1024]{1,0:T(8,128)(2,1)S(1)}, bf16[128,1024]{1,0:T(8,128)(2,1)S(1)}, u32[]{:S(2)}, u32[]{:S(2)}) collective-permute-start(bf16[128,1024]{1,0:T(8,128)(2,1)S(1)} %get-tuple-element.15), channel_id=1, source_target_pairs={{0,4},{1,5},{2,6},{3,7},{4,8},{5,9},{6,10},{7,11},{8,12},{9,13},{1... | collective-permute-start | bytes 786440 | tf_op jit(solution)/shard_map/stream1/ppermute | solution.py:205
  97.2 4.4 %collective-permute-start.27 = (bf16[128,1024]{1,0:T(8,128)(2,1)S(1)}, bf16[128,1024]{1,0:T(8,128)(2,1)S(1)}, u32[]{:S(2)}, u32[]{:S(2)}) collective-permute-start(bf16[128,1024]{1,0:T(8,128)(2,1)S(1)} %get-tuple-element.16), channel_id=1, source_target_pairs={{0,4},{1,5},{2,6},{3,7},{4,8},{5,9},{6,10},{7,11},{8,12},{9,13},{1... | collective-permute-start | bytes 786440 | tf_op jit(solution)/shard_map/stream1/ppermute | solution.py:205
  103.6 3.9 %collective-permute-start.19 = (bf16[128,1024]{1,0:T(8,128)(2,1)S(1)}, bf16[128,1024]{1,0:T(8,128)(2,1)S(1)}, u32[]{:S(2)}, u32[]{:S(2)}) collective-permute-start(bf16[128,1024]{1,0:T(8,128)(2,1)S(1)} %collective-permute-done.18), channel_id=1, source_target_pairs={{4,8},{5,9},{6,10},{7,11},{8,12},{9,13},{10,14},{11,15},{20,24},{2... | collective-permute-start | bytes 786440 | tf_op jit(solution)/shard_map/stream1/ppermute | solution.py:205
  108.1 15.0 %stream0.1 = (bf16[128,1024]{1,0:T(8,128)(2,1)}, bf16[128,1024]{1,0:T(8,128)(2,1)}, bf16[16,128,1024]{2,1,0:T(8,128)(2,1)}, bf16[16,128,1024]{2,1,0:T(8,128)(2,1)}) custom-call(s32[8]{0:T(128)} %fusion.57.pos_ref, bf16[128,1024]{1,0:T(8,128)(2,1)} %get-tuple-element.66.q_ref, bf16[128,1024]{1,0:T(8,128)(2,1)} %get-tuple-element.64.g_ref, ...), custom_call_target="tpu_custom_call" | custom-call | flops 1610612736 | bytes 13631488 | tf_op jit(solution)/shard_map/stream0/pallas_call | solution.py:302
  125.0 3.9 %collective-permute-start.28 = (bf16[128,1024]{1,0:T(8,128)(2,1)S(1)}, bf16[128,1024]{1,0:T(8,128)(2,1)S(1)}, u32[]{:S(2)}, u32[]{:S(2)}) collective-permute-start(bf16[128,1024]{1,0:T(8,128)(2,1)S(1)} %collective-permute-done.27), channel_id=1, source_target_pairs={{4,8},{5,9},{6,10},{7,11},{8,12},{9,13},{10,14},{11,15},{20,24},{2... | collective-permute-start | bytes 786440 | tf_op jit(solution)/shard_map/stream1/ppermute | solution.py:205
  131.6 3.9 %fusion.71 = (bf16[8,128,1024]{2,1,0:T(8,128)(2,1)S(1)}, bf16[8,128,1024]{2,1,0:T(8,128)(2,1)S(1)}, bf16[8,128,1024]{2,1,0:T(8,128)(2,1)S(1)}, bf16[8,128,1024]{2,1,0:T(8,128)(2,1)S(1)}) fusion(bf16[16,128,1024]{2,1,0:T(8,128)(2,1)} %get-tuple-element.22, bf16[16,128,1024]{2,1,0:T(8,128)(2,1)} %get-tuple-element.20), kind=kLoop, calls=%fused_computation.179 | loop fusion | bytes 16777216 | tf_op jit(solution)/shard_map/stream0/transpose()/unstack | solution.py:231
  151.5 33.6 %collective-permute-done.24 = bf16[128,1024]{1,0:T(8,128)(2,1)S(1)} collective-permute-done((bf16[128,1024]{1,0:T(8,128)(2,1)S(1)}, bf16[128,1024]{1,0:T(8,128)(2,1)S(1)}, u32[]{:S(2)}, u32[]{:S(2)}) %collective-permute-start.24) | collective-permute-done | bytes 262176 | tf_op jit(solution)/shard_map/stream1/ppermute | solution.py:205
  187.0 4.4 %collective-permute-done.33 = bf16[128,1024]{1,0:T(8,128)(2,1)S(1)} collective-permute-done((bf16[128,1024]{1,0:T(8,128)(2,1)S(1)}, bf16[128,1024]{1,0:T(8,128)(2,1)S(1)}, u32[]{:S(2)}, u32[]{:S(2)}) %collective-permute-start.33) | collective-permute-done | bytes 262176 | tf_op jit(solution)/shard_map/stream1/ppermute | solution.py:205
  197.1 16.4 %collective-permute-done.37 = bf16[3,128,1024]{2,1,0:T(8,128)(2,1)S(1)} collective-permute-done((bf16[3,128,1024]{2,1,0:T(8,128)(2,1)S(1)}, bf16[3,128,1024]{2,1,0:T(8,128)(2,1)S(1)}, u32[]{:S(2)}, u32[]{:S(2)}) %collective-permute-start.37) | collective-permute-done | bytes 786464 | tf_op jit(solution)/shard_map/stream0/transpose()/ppermute | solution.py:205
  217.2 12.7 %collective-permute-done.55 = bf16[3,128,1024]{2,1,0:T(8,128)(2,1)S(1)} collective-permute-done((bf16[3,128,1024]{2,1,0:T(8,128)(2,1)S(1)}, bf16[3,128,1024]{2,1,0:T(8,128)(2,1)S(1)}, u32[]{:S(2)}, u32[]{:S(2)}) %collective-permute-start.55) | collective-permute-done | bytes 786464 | tf_op jit(solution)/shard_map/stream0/transpose()/ppermute | solution.py:205
  241.9 14.9 %stream1.1 = (bf16[128,1024]{1,0:T(8,128)(2,1)}, bf16[128,1024]{1,0:T(8,128)(2,1)}, bf16[16,128,1024]{2,1,0:T(8,128)(2,1)}, bf16[16,128,1024]{2,1,0:T(8,128)(2,1)}) custom-call(s32[8]{0:T(128)} %fusion.57.pos_ref, bf16[128,1024]{1,0:T(8,128)(2,1)} %get-tuple-element.67.q_ref, bf16[128,1024]{1,0:T(8,128)(2,1)} %get-tuple-element.65.g_ref, ...), custom_call_target="tpu_custom_call" | custom-call | flops 1610612736 | bytes 13631488 | tf_op jit(solution)/shard_map/stream1/pallas_call | solution.py:302
  256.9 4.1 %fusion.72 = (bf16[8,128,1024]{2,1,0:T(8,128)(2,1)S(1)}, bf16[8,128,1024]{2,1,0:T(8,128)(2,1)S(1)}, bf16[8,128,1024]{2,1,0:T(8,128)(2,1)S(1)}, bf16[8,128,1024]{2,1,0:T(8,128)(2,1)S(1)}) fusion(bf16[16,128,1024]{2,1,0:T(8,128)(2,1)} %get-tuple-element.23, bf16[16,128,1024]{2,1,0:T(8,128)(2,1)} %get-tuple-element.21), kind=kLoop, calls=%fused_computation.180 | loop fusion | bytes 16777216 | tf_op jit(solution)/shard_map/stream1/transpose()/unstack | solution.py:231
  268.9 6.5 %collective-permute-done.57 = bf16[128,1024]{1,0:T(8,128)(2,1)S(1)} collective-permute-done((bf16[128,1024]{1,0:T(8,128)(2,1)S(1)}, bf16[128,1024]{1,0:T(8,128)(2,1)S(1)}, u32[]{:S(2)}, u32[]{:S(2)}) %collective-permute-start.57) | collective-permute-done | bytes 262176 | tf_op jit(solution)/shard_map/stream0/transpose()/ppermute | solution.py:205
  279.4 4.5 %collective-permute-start.40 = (bf16[128,1024]{1,0:T(8,128)(2,1)S(1)}, bf16[128,1024]{1,0:T(8,128)(2,1)S(1)}, u32[]{:S(2)}, u32[]{:S(2)}) collective-permute-start(bf16[128,1024]{1,0:T(8,128)(2,1)S(1)} %get-tuple-element.44), channel_id=1, source_target_pairs={{0,4},{1,5},{2,6},{3,7},{4,8},{5,9},{6,10},{7,11},{8,12},{9,13},{1... | collective-permute-start | bytes 786440 | tf_op jit(solution)/shard_map/stream0/transpose()/ppermute | solution.py:205
  290.2 3.9 %collective-permute-start.58 = (bf16[128,1024]{1,0:T(8,128)(2,1)S(1)}, bf16[128,1024]{1,0:T(8,128)(2,1)S(1)}, u32[]{:S(2)}, u32[]{:S(2)}) collective-permute-start(bf16[128,1024]{1,0:T(8,128)(2,1)S(1)} %get-tuple-element.40), channel_id=1, source_target_pairs={{0,4},{1,5},{2,6},{3,7},{4,8},{5,9},{6,10},{7,11},{8,12},{9,13},{1... | collective-permute-start | bytes 786440 | tf_op jit(solution)/shard_map/stream0/transpose()/ppermute | solution.py:205
  304.2 15.8 %collective-permute-done.46 = bf16[3,128,1024]{2,1,0:T(8,128)(2,1)S(1)} collective-permute-done((bf16[3,128,1024]{2,1,0:T(8,128)(2,1)S(1)}, bf16[3,128,1024]{2,1,0:T(8,128)(2,1)S(1)}, u32[]{:S(2)}, u32[]{:S(2)}) %collective-permute-start.46) | collective-permute-done | bytes 786464 | tf_op jit(solution)/shard_map/stream1/transpose()/ppermute | solution.py:205
  322.9 11.2 %collective-permute-done.64 = bf16[3,128,1024]{2,1,0:T(8,128)(2,1)S(1)} collective-permute-done((bf16[3,128,1024]{2,1,0:T(8,128)(2,1)S(1)}, bf16[3,128,1024]{2,1,0:T(8,128)(2,1)S(1)}, u32[]{:S(2)}, u32[]{:S(2)}) %collective-permute-start.64) | collective-permute-done | bytes 786464 | tf_op jit(solution)/shard_map/stream1/transpose()/ppermute | solution.py:205
  341.4 4.7 %collective-permute-done.65 = bf16[128,1024]{1,0:T(8,128)(2,1)S(1)} collective-permute-done((bf16[128,1024]{1,0:T(8,128)(2,1)S(1)}, bf16[128,1024]{1,0:T(8,128)(2,1)S(1)}, u32[]{:S(2)}, u32[]{:S(2)}) %collective-permute-start.65) | collective-permute-done | bytes 262176 | tf_op jit(solution)/shard_map/stream1/transpose()/ppermute | solution.py:205
  352.7 4.6 %collective-permute-start.49 = (bf16[128,1024]{1,0:T(8,128)(2,1)S(1)}, bf16[128,1024]{1,0:T(8,128)(2,1)S(1)}, u32[]{:S(2)}, u32[]{:S(2)}) collective-permute-start(bf16[128,1024]{1,0:T(8,128)(2,1)S(1)} %get-tuple-element.46), channel_id=1, source_target_pairs={{0,4},{1,5},{2,6},{3,7},{4,8},{5,9},{6,10},{7,11},{8,12},{9,13},{1... | collective-permute-start | bytes 786440 | tf_op jit(solution)/shard_map/stream1/transpose()/ppermute | solution.py:205
  358.7 3.7 collective-permute-done.51
  (254 shorter events, 155.2 us)
Async XLA Ops:
  39.9 39.5 %collective-permute-start.7 = (bf16[3,128,1024]{2,1,0:T(8,128)(2,1)S(1)}, bf16[3,128,1024]{2,1,0:T(8,128)(2,1)S(1)}, u32[]{:S(2)}, u32[]{:S(2)}) collective-permute-start(bf16[3,128,1024]{2,1,0:T(8,128)(2,1)S(1)} %constant_dynamic-slice_fusion.3), channel_id=1, source_target_pairs={{0,2},{1,3},{2,0},{3,1},{4,6},{5,7},{6,4},{7,5},{8,10},{9,11},{10,... | collective-permute-start | bytes 2359304 | tf_op jit(solution)/shard_map/stream0/ppermute | solution.py:205
  42.1 40.1 %collective-permute-start.16 = (bf16[3,128,1024]{2,1,0:T(8,128)(2,1)S(1)}, bf16[3,128,1024]{2,1,0:T(8,128)(2,1)S(1)}, u32[]{:S(2)}, u32[]{:S(2)}) collective-permute-start(bf16[3,128,1024]{2,1,0:T(8,128)(2,1)S(1)} %constant_dynamic-slice_fusion.2), channel_id=1, source_target_pairs={{0,2},{1,3},{2,0},{3,1},{4,6},{5,7},{6,4},{7,5},{8,10},{9,11},{10,... | collective-permute-start | bytes 2359304 | tf_op jit(solution)/shard_map/stream0/ppermute | solution.py:205
  43.7 35.7 %collective-permute-start.6 = (bf16[128,1024]{1,0:T(8,128)(2,1)S(1)}, bf16[128,1024]{1,0:T(8,128)(2,1)S(1)}, u32[]{:S(2)}, u32[]{:S(2)}) collective-permute-start(bf16[128,1024]{1,0:T(8,128)(2,1)S(1)} %get-tuple-element.73), channel_id=1, source_target_pairs={{0,2},{1,3},{2,0},{3,1},{4,6},{5,7},{6,4},{7,5},{8,10},{9,11},{10,... | collective-permute-start | bytes 786440 | tf_op jit(solution)/shard_map/stream0/ppermute | solution.py:205
  44.2 38.0 %collective-permute-start.15 = (bf16[128,1024]{1,0:T(8,128)(2,1)S(1)}, bf16[128,1024]{1,0:T(8,128)(2,1)S(1)}, u32[]{:S(2)}, u32[]{:S(2)}) collective-permute-start(bf16[128,1024]{1,0:T(8,128)(2,1)S(1)} %get-tuple-element.70), channel_id=1, source_target_pairs={{0,2},{1,3},{2,0},{3,1},{4,6},{5,7},{6,4},{7,5},{8,10},{9,11},{10,... | collective-permute-start | bytes 786440 | tf_op jit(solution)/shard_map/stream0/ppermute | solution.py:205
  95.3 27.7 %collective-permute-start.21 = (bf16[128,1024]{1,0:T(8,128)(2,1)S(1)}, bf16[128,1024]{1,0:T(8,128)(2,1)S(1)}, u32[]{:S(2)}, u32[]{:S(2)}) collective-permute-start(bf16[128,1024]{1,0:T(8,128)(2,1)S(1)} %get-tuple-element.15), channel_id=1, source_target_pairs={{4,0},{5,1},{6,2},{7,3},{8,4},{9,5},{10,6},{11,7},{12,8},{13,9},{1... | collective-permute-start | bytes 786440 | tf_op jit(solution)/shard_map/stream1/ppermute | solution.py:205
  97.2 27.7 %collective-permute-start.27 = (bf16[128,1024]{1,0:T(8,128)(2,1)S(1)}, bf16[128,1024]{1,0:T(8,128)(2,1)S(1)}, u32[]{:S(2)}, u32[]{:S(2)}) collective-permute-start(bf16[128,1024]{1,0:T(8,128)(2,1)S(1)} %get-tuple-element.16), channel_id=1, source_target_pairs={{0,4},{1,5},{2,6},{3,7},{4,8},{5,9},{6,10},{7,11},{8,12},{9,13},{1... | collective-permute-start | bytes 786440 | tf_op jit(solution)/shard_map/stream1/ppermute | solution.py:205
  101.6 27.3 %collective-permute-start.30 = (bf16[128,1024]{1,0:T(8,128)(2,1)S(1)}, bf16[128,1024]{1,0:T(8,128)(2,1)S(1)}, u32[]{:S(2)}, u32[]{:S(2)}) collective-permute-start(bf16[128,1024]{1,0:T(8,128)(2,1)S(1)} %get-tuple-element.16), channel_id=1, source_target_pairs={{4,0},{5,1},{6,2},{7,3},{8,4},{9,5},{10,6},{11,7},{12,8},{13,9},{1... | collective-permute-start | bytes 786440 | tf_op jit(solution)/shard_map/stream1/ppermute | solution.py:205
  103.6 27.3 %collective-permute-start.19 = (bf16[128,1024]{1,0:T(8,128)(2,1)S(1)}, bf16[128,1024]{1,0:T(8,128)(2,1)S(1)}, u32[]{:S(2)}, u32[]{:S(2)}) collective-permute-start(bf16[128,1024]{1,0:T(8,128)(2,1)S(1)} %collective-permute-done.18), channel_id=1, source_target_pairs={{4,8},{5,9},{6,10},{7,11},{8,12},{9,13},{10,14},{11,15},{20,24},{2... | collective-permute-start | bytes 786440 | tf_op jit(solution)/shard_map/stream1/ppermute | solution.py:205
  135.5 56.4 %collective-permute-start.36 = (bf16[2,4,128,1024]{3,2,1,0:T(8,128)(2,1)S(1)}, bf16[2,4,128,1024]{3,2,1,0:T(8,128)(2,1)S(1)}, u32[]{:S(2)}, u32[]{:S(2)}) collective-permute-start(bf16[2,4,128,1024]{3,2,1,0:T(8,128)(2,1)S(1)} %bitcast.339), channel_id=1, source_target_pairs={{1,0},{0,1},{3,2},{2,3},{5,4},{4,5},{7,6},{6,7},{9,8},{8,9},{11,10... | collective-permute-start | bytes 6291464 | tf_op jit(solution)/shard_map/stream0/transpose()/ppermute | solution.py:205
  135.6 59.1 %collective-permute-start.54 = (bf16[2,4,128,1024]{3,2,1,0:T(8,128)(2,1)S(1)}, bf16[2,4,128,1024]{3,2,1,0:T(8,128)(2,1)S(1)}, u32[]{:S(2)}, u32[]{:S(2)}) collective-permute-start(bf16[2,4,128,1024]{3,2,1,0:T(8,128)(2,1)S(1)} %bitcast.337), channel_id=1, source_target_pairs={{1,0},{0,1},{3,2},{2,3},{5,4},{4,5},{7,6},{6,7},{9,8},{8,9},{11,10... | collective-permute-start | bytes 6291464 | tf_op jit(solution)/shard_map/stream0/transpose()/ppermute | solution.py:205
  144.2 42.4 %collective-permute-start.25 = (bf16[3,128,1024]{2,1,0:T(8,128)(2,1)S(1)}, bf16[3,128,1024]{2,1,0:T(8,128)(2,1)S(1)}, u32[]{:S(2)}, u32[]{:S(2)}) collective-permute-start(bf16[3,128,1024]{2,1,0:T(8,128)(2,1)S(1)} %constant_dynamic-slice_fusion.1), channel_id=1, source_target_pairs={{0,2},{1,3},{2,0},{3,1},{4,6},{5,7},{6,4},{7,5},{8,10},{9,11},{10,... | collective-permute-start | bytes 2359304 | tf_op jit(solution)/shard_map/stream1/ppermute | solution.py:205
  149.2 42.2 %collective-permute-start.34 = (bf16[3,128,1024]{2,1,0:T(8,128)(2,1)S(1)}, bf16[3,128,1024]{2,1,0:T(8,128)(2,1)S(1)}, u32[]{:S(2)}, u32[]{:S(2)}) collective-permute-start(bf16[3,128,1024]{2,1,0:T(8,128)(2,1)S(1)} %constant_dynamic-slice_fusion), channel_id=1, source_target_pairs={{0,2},{1,3},{2,0},{3,1},{4,6},{5,7},{6,4},{7,5},{8,10},{9,11},{10,... | collective-permute-start | bytes 2359304 | tf_op jit(solution)/shard_map/stream1/ppermute | solution.py:205
  150.8 34.3 %collective-permute-start.24 = (bf16[128,1024]{1,0:T(8,128)(2,1)S(1)}, bf16[128,1024]{1,0:T(8,128)(2,1)S(1)}, u32[]{:S(2)}, u32[]{:S(2)}) collective-permute-start(bf16[128,1024]{1,0:T(8,128)(2,1)S(1)} %get-tuple-element.15), channel_id=1, source_target_pairs={{0,2},{1,3},{2,0},{3,1},{4,6},{5,7},{6,4},{7,5},{8,10},{9,11},{10,... | collective-permute-start | bytes 786440 | tf_op jit(solution)/shard_map/stream1/ppermute | solution.py:205
  186.9 50.2 %collective-permute-start.26 = (bf16[2,4,128,1024]{3,2,1,0:T(8,128)(2,1)S(1)}, bf16[2,4,128,1024]{3,2,1,0:T(8,128)(2,1)S(1)}, u32[]{:S(2)}, u32[]{:S(2)}) collective-permute-start(bf16[2,4,128,1024]{3,2,1,0:T(8,128)(2,1)S(1)} %get-tuple-element.51), channel_id=1, source_target_pairs={{0,1},{1,0},{2,3},{3,2},{4,5},{5,4},{6,7},{7,6},{8,9},{9,8},{10,11... | collective-permute-start | bytes 6291464 | tf_op jit(solution)/shard_map/stream1/ppermute | solution.py:205
  191.8 47.8 %collective-permute-start.35 = (bf16[2,4,128,1024]{3,2,1,0:T(8,128)(2,1)S(1)}, bf16[2,4,128,1024]{3,2,1,0:T(8,128)(2,1)S(1)}, u32[]{:S(2)}, u32[]{:S(2)}) collective-permute-start(bf16[2,4,128,1024]{3,2,1,0:T(8,128)(2,1)S(1)} %get-tuple-element.49), channel_id=1, source_target_pairs={{0,1},{1,0},{2,3},{3,2},{4,5},{5,4},{6,7},{7,6},{8,9},{9,8},{10,11... | collective-permute-start | bytes 6291464 | tf_op jit(solution)/shard_map/stream1/ppermute | solution.py:205
  195.9 34.1 %collective-permute-start.55 = (bf16[3,128,1024]{2,1,0:T(8,128)(2,1)S(1)}, bf16[3,128,1024]{2,1,0:T(8,128)(2,1)S(1)}, u32[]{:S(2)}, u32[]{:S(2)}) collective-permute-start(bf16[3,128,1024]{2,1,0:T(8,128)(2,1)S(1)} %slice_bitcast_fusion.5), channel_id=1, source_target_pairs={{2,0},{3,1},{0,2},{1,3},{6,4},{7,5},{4,6},{5,7},{10,8},{11,9},{8,1... | collective-permute-start | bytes 2359304 | tf_op jit(solution)/shard_map/stream0/transpose()/ppermute | solution.py:205
  215.8 49.9 %collective-permute-start.41 = (bf16[128,1024]{1,0:T(8,128)(2,1)S(1)}, bf16[128,1024]{1,0:T(8,128)(2,1)}, u32[]{:S(2)}, u32[]{:S(2)}) collective-permute-start(bf16[128,1024]{1,0:T(8,128)(2,1)S(1)} %get-tuple-element.61), channel_id=1, source_target_pairs={{12,8},{13,9},{14,10},{15,11},{28,24},{29,25},{30,26},{31,27}} | collective-permute-start | bytes 786440 | tf_op jit(solution)/shard_map/stream0/transpose()/ppermute | solution.py:205
  233.2 29.5 %collective-permute-start.56 = (bf16[128,1024]{1,0:T(8,128)(2,1)}, bf16[128,1024]{1,0:T(8,128)(2,1)}, u32[]{:S(2)}, u32[]{:S(2)}) collective-permute-start(bf16[128,1024]{1,0:T(8,128)(2,1)} %get-tuple-element.56), channel_id=1, source_target_pairs={{0,4},{1,5},{2,6},{3,7},{16,20},{17,21},{18,22},{19,23}} | collective-permute-start | bytes 786440 | tf_op jit(solution)/shard_map/stream0/transpose()/ppermute | solution.py:205
  235.2 30.5 %collective-permute-start.39 = (bf16[128,1024]{1,0:T(8,128)(2,1)}, bf16[128,1024]{1,0:T(8,128)(2,1)}, u32[]{:S(2)}, u32[]{:S(2)}) collective-permute-start(bf16[128,1024]{1,0:T(8,128)(2,1)} %fusion.49), channel_id=1, source_target_pairs={{0,4},{1,5},{2,6},{3,7},{4,8},{5,9},{6,10},{7,11},{16,20},{17,21},... | collective-permute-start | bytes 786440 | tf_op jit(solution)/shard_map/stream0/transpose()/ppermute | solution.py:205
  260.9 37.4 %collective-permute-start.45 = (bf16[2,4,128,1024]{3,2,1,0:T(8,128)(2,1)S(1)}, bf16[2,4,128,1024]{3,2,1,0:T(8,128)(2,1)S(1)}, u32[]{:S(2)}, u32[]{:S(2)}) collective-permute-start(bf16[2,4,128,1024]{3,2,1,0:T(8,128)(2,1)S(1)} %bitcast.340), channel_id=1, source_target_pairs={{1,0},{0,1},{3,2},{2,3},{5,4},{4,5},{7,6},{6,7},{9,8},{8,9},{11,10... | collective-permute-start | bytes 6291464 | tf_op jit(solution)/shard_map/stream1/transpose()/ppermute | solution.py:205
  268.4 32.7 %collective-permute-start.63 = (bf16[2,4,128,1024]{3,2,1,0:T(8,128)(2,1)S(1)}, bf16[2,4,128,1024]{3,2,1,0:T(8,128)(2,1)S(1)}, u32[]{:S(2)}, u32[]{:S(2)}) collective-permute-start(bf16[2,4,128,1024]{3,2,1,0:T(8,128)(2,1)S(1)} %bitcast.338), channel_id=1, source_target_pairs={{1,0},{0,1},{3,2},{2,3},{5,4},{4,5},{7,6},{6,7},{9,8},{8,9},{11,10... | collective-permute-start | bytes 6291464 | tf_op jit(solution)/shard_map/stream1/transpose()/ppermute | solution.py:205
  302.2 31.8 %collective-permute-start.64 = (bf16[3,128,1024]{2,1,0:T(8,128)(2,1)S(1)}, bf16[3,128,1024]{2,1,0:T(8,128)(2,1)S(1)}, u32[]{:S(2)}, u32[]{:S(2)}) collective-permute-start(bf16[3,128,1024]{2,1,0:T(8,128)(2,1)S(1)} %slice_bitcast_fusion.4), channel_id=1, source_target_pairs={{2,0},{3,1},{0,2},{1,3},{6,4},{7,5},{4,6},{5,7},{10,8},{11,9},{8,1... | collective-permute-start | bytes 2359304 | tf_op jit(solution)/shard_map/stream1/transpose()/ppermute | solution.py:205
  322.2 25.9 %collective-permute-start.50 = (bf16[128,1024]{1,0:T(8,128)(2,1)S(1)}, bf16[128,1024]{1,0:T(8,128)(2,1)S(1)}, u32[]{:S(2)}, u32[]{:S(2)}) collective-permute-start(bf16[128,1024]{1,0:T(8,128)(2,1)S(1)} %get-tuple-element.63), channel_id=1, source_target_pairs={{12,8},{13,9},{14,10},{15,11},{28,24},{29,25},{30,26},{31,27}} | collective-permute-start | bytes 786440 | tf_op jit(solution)/shard_map/stream1/transpose()/ppermute | solution.py:205
  339.2 30.9 %collective-permute-start.53 = (bf16[128,1024]{1,0:T(8,128)(2,1)S(1)}, bf16[128,1024]{1,0:T(8,128)(2,1)S(1)}, u32[]{:S(2)}, u32[]{:S(2)}) collective-permute-start(bf16[128,1024]{1,0:T(8,128)(2,1)S(1)} %slice_bitcast_fusion.34), channel_id=1, source_target_pairs={{2,0},{3,1},{0,2},{1,3},{6,4},{7,5},{4,6},{5,7},{10,8},{11,9},{8,1... | collective-permute-start | bytes 786440 | tf_op jit(solution)/shard_map/stream1/transpose()/ppermute | solution.py:205
  (64 other events, 835.1 us)
